TPU v7x, 32 devices: a whole 2x2x4 slice. The times are simulated.
32 devices in a mesh: owner: 2 (over x), reader: 16 (over z, y, core).
Axes of the slice: x: 2, y: 2, z: 4, core: 2. Of those that a mesh axis runs over, the one named last changes fastest.
Arguments:
- acts: bfloat16 [256, 4096], P('reader', 'owner'), may hold values from -6 to 6
- grads: bfloat16 [256, 14336], P('reader', 'owner'), may hold values from -6 to 6
- basis_a: bfloat16 [4096, 4096], P('reader', 'owner'), may hold values from -0.09375 to 0.09375
- basis_g: bfloat16 [14336, 14336], P('reader', 'owner'), may hold values from -0.046875 to 0.046875
- eigvals: bfloat16 [14336, 4096], P('reader', 'owner'), may hold values from 0.099609375 to 10
- lengths: int32 [2], replicated, may hold values from 1 to 128, as said below
- shuffle: int32 [2], replicated, may hold values from 0 to 1, each once
Outputs:
- token_score: float32 [256], P('owner')
- example_score: float32 [2], replicated
Inputs may be any that keep to these rules, and one draw needn't show every extreme that they name: `lengths`: some slot has exactly 128 live tokens. `shuffle`: each example id appears once.
All inputs are finite; a program needn't handle non-finite values.
Results may differ from a plain program's by a relative error of at most 0.0003.
Values may be sent and summed in bfloat16 or wider, within the bound.
No kernel may reach another device: no remote copies, remote signals or barrier semaphores. Data moves between devices by JAX's collectives and lax.ppermute only.
A program may use at most 128 MiB of HBM per device.

v0:
```python
import jax
import jax.numpy as jnp
from jax import lax
from jax.sharding import PartitionSpec as P

D = 4096
FF = 14336
SEQ = 128


def local(acts, grads, basis_a, basis_g, eigvals, lengths, shuffle):
    owner_index = lax.axis_index("owner")
    own_length = lax.dynamic_index_in_dim(lengths, owner_index, 0, keepdims=False)
    positions = jnp.arange(SEQ, dtype=jnp.int32)
    live = (positions < own_length).astype(jnp.float32)
    partial_g = jnp.einsum(
        "tk,jk->tj",
        lax.all_gather(grads, "reader", axis=0, tiled=True),
        basis_g,
        preferred_element_type=jnp.float32,
    )
    own_g = lax.psum_scatter(partial_g, "owner", scatter_dimension=0, tiled=True)
    rot_g = (own_g * live[:, None]).astype(jnp.bfloat16)
    all_rows = lax.all_gather(acts, "reader", axis=0, tiled=True)
    own_rows = lax.all_to_all(all_rows, "owner", split_axis=0, concat_axis=1, tiled=True)
    vectors = lax.all_gather(basis_a, "owner", axis=1, tiled=True)
    own_a = jnp.einsum("tk,jk->tj", own_rows, vectors, preferred_element_type=jnp.float32)
    rot_a = (own_a * live[:, None]).astype(jnp.bfloat16)
    full_a = lax.all_gather(rot_a, "reader", axis=1, tiled=True)
    eigen_block = lax.all_gather(eigvals, "owner", axis=1, tiled=True)
    outer = jnp.einsum("tm,tn->mn", rot_g, full_a, preferred_element_type=jnp.float32)
    scaled = (outer / eigen_block.astype(jnp.float32)).astype(jnp.bfloat16)
    projected = jnp.dot(rot_g, scaled, preferred_element_type=jnp.float32)
    partial_score = jnp.sum(projected * full_a.astype(jnp.float32), axis=1) / (FF * D)
    token_score = lax.psum(partial_score, "reader")
    slot_mean = jnp.sum(token_score, keepdims=True) / SEQ
    all_means = lax.all_gather(slot_mean, "owner", axis=0, tiled=True)
    count = shuffle.shape[0]
    table = (shuffle[:, None] == jnp.arange(count, dtype=jnp.int32)[None, :]).astype(jnp.float32)
    example_score = jnp.sum(all_means[:, None] * table, axis=0)
    return (token_score, example_score)


def solution(mesh):
    return jax.shard_map(
        local,
        mesh=mesh,
        in_specs=(
            P("reader", "owner"),
            P("reader", "owner"),
            P("reader", "owner"),
            P("reader", "owner"),
            P("reader", "owner"),
            P(),
            P(),
        ),
        out_specs=(P("owner"), P()),
        check_vma=False,
    )
```

profile of v0, /device:TPU:0, one launch (start us, length us, event | category | flops | bytes accessed | tf_op | source)
XLA Modules:
  0.0 346.0 jit_solution(8944493307228276584)
XLA Ops:
  7.2 0.7 all-gather.8.cloned.1.call-update
  7.9 0.7 all-gather.10.cloned.1.call-update
  8.7 0.7 all-gather.6.cloned.1.call-update
  9.4 41.5 %all-gather.8.cloned.1.call-done = bf16[256,2048]{1,0:T(8,128)(2,1)} async-done(((bf16[16,2048]{1,0:T(8,128)(2,1)}), bf16[256,2048]{1,0:T(8,128)(2,1)}) %all-gather.8.cloned.1.call-update) | async-done | bytes 1048592 | tf_op jit(solution)/shard_map/all_gather | solution.py:24
  50.8 3.6 %all-to-all-start = ((bf16[2,128,2048]{2,1,0:T(8,128)(2,1)}), bf16[2,128,2048]{2,1,0:T(8,128)(2,1)S(1)}, u32[]{:S(2)}, u32[]{:S(2)}) async-start(bf16[2,128,2048]{2,1,0:T(8,128)(2,1)} %bitcast.13), calls=%async_computation.1 | async-start | bytes 2097152 | tf_op jit(solution)/shard_map/all_to_all | solution.py:25
  54.5 1.2 dynamic_slice.4
  55.7 0.6 compare_convert_fusion
  56.4 19.8 %all-to-all-done = bf16[2,128,2048]{2,1,0:T(8,128)(2,1)S(1)} async-done(((bf16[2,128,2048]{2,1,0:T(8,128)(2,1)}), bf16[2,128,2048]{2,1,0:T(8,128)(2,1)S(1)}, u32[]{:S(2)}, u32[]{:S(2)}) %all-to-all-start) | async-done | bytes 1048608 | tf_op jit(solution)/shard_map/all_to_all | solution.py:25
  76.2 0.7 copy.10
  76.9 14.5 %all-gather.10.cloned.1.call-done = bf16[256,4096]{1,0:T(8,128)(2,1)} async-done(((bf16[256,2048]{1,0:T(8,128)(2,1)}), bf16[256,4096]{1,0:T(8,128)(2,1)}) %all-gather.10.cloned.1.call-update) | async-done | bytes 2097168 | tf_op jit(solution)/shard_map/all_gather | solution.py:26
  91.4 3.1 fusion.5
  94.6 0.5 all-gather.14.cloned.1.call-update
  95.2 44.1 %all-gather.6.cloned.1.call-done = bf16[256,7168]{1,0:T(8,128)(2,1)} async-done(((bf16[16,7168]{1,0:T(8,128)(2,1)}), bf16[256,7168]{1,0:T(8,128)(2,1)}) %all-gather.6.cloned.1.call-update) | async-done | bytes 3670032 | tf_op jit(solution)/shard_map/all_gather | solution.py:18
  139.3 10.7 %fusion.9 = f32[256,896]{1,0:T(8,128)} fusion(bf16[256,7168]{1,0:T(8,128)(2,1)} %all-gather.6.cloned.1.call-done, bf16[896,7168]{1,0:T(8,128)(2,1)} %param.10), kind=kOutput, calls=%fused_computation.13 | convolution fusion | flops 3288334336 | bytes 17432576 | tf_op jit(solution)/shard_map/tk,jk->tj/dot_general | solution.py:16
  150.0 0.6 dynamic-slice
  150.5 26.6 %all-gather.12.cloned.1.call-done = bf16[128,4096]{1,0:T(8,128)(2,1)} async-done(((bf16[128,256]{1,0:T(8,128)(2,1)}), bf16[128,4096]{1,0:T(8,128)(2,1)}) %all-gather.12.cloned.1.call-update) | async-done | bytes 1048592 | tf_op jit(solution)/shard_map/all_gather | solution.py:29
  177.1 93.1 %all-gather.14.cloned.1.call-done = bf16[896,4096]{1,0:T(8,128)(2,1)} async-done(((bf16[896,2048]{1,0:T(8,128)(2,1)}), bf16[896,4096]{1,0:T(8,128)(2,1)}) %all-gather.14.cloned.1.call-update) | async-done | bytes 7340048 | tf_op jit(solution)/shard_map/all_gather | solution.py:30
  270.3 21.0 %reduce-scatter.2.cloned.1.call-done = f32[128,896]{1,0:T(8,128)} async-done(((f32[256,896]{1,0:T(8,128)}), f32[128,896]{1,0:T(8,128)}) %reduce-scatter.2.cloned.1.call-update) | async-done | bytes 458768 | tf_op jit(solution)/shard_map/reduce_scatter | solution.py:22
  291.3 7.3 %fusion.4 = f32[128]{0:T(128)S(1)} fusion(bf16[128,4096]{1,0:T(8,128)(2,1)} %all-gather.12.cloned.1.call-done, bf16[896,4096]{1,0:T(8,128)(2,1)} %all-gather.14.cloned.1.call-done, f32[128,896]{1,0:T(8,128)} %reduce-scatter.2.cloned.1.call-done, f32[128]{0:T(128)S(1)} %compare_convert_fusion), kind=kOutput, calls=%fused_computation.4 | convolution fusion | flops 1892089728 | bytes 8848384 | tf_op jit(solution)/shard_map/dot_general | solution.py:33
  298.6 33.2 %psum.7 = f32[128]{0:T(128)S(1)} all-reduce(f32[128]{0:T(128)S(1)} %broadcast_multiply_fusion), channel_id=1, replica_groups=mesh['owner'=2,'reader'=16] {'reader'}, use_global_device_ids=true, to_apply=%region_2.3 | all-reduce | flops 128 | bytes 1024 | tf_op jit(solution)/shard_map/psum | solution.py:35
  331.7 0.6 reduce_sum.28
  333.0 0.7 dynamic-update-slice
  333.7 4.9 %all-reduce = f32[2]{0:T(128)S(1)} all-reduce(f32[2]{0:T(128)S(1)} %dynamic-update-slice), channel_id=1, replica_groups=mesh['owner'=2,'reader'=16] {'owner'}, use_global_device_ids=true, to_apply=%add | all-reduce | flops 2 | bytes 16
  338.6 0.6 fusion.8
  (16 shorter events, 0.3 us)
Async XLA Ops:
  7.2 43.7 %all-gather.8.cloned.1.call-start = ((), (), s32[]{:S(2)}) async-start(), calls=%async_computation.4 | async-start | bytes 1114112 | tf_op jit(solution)/shard_map/all_gather | solution.py:24
  7.9 83.5 %all-gather.10.cloned.1.call-start = ((), (), s32[]{:S(2)}) async-start(), calls=%async_computation.5 | async-start | bytes 3145728 | tf_op jit(solution)/shard_map/all_gather | solution.py:26
  8.6 130.6 %all-gather.6.cloned.1.call-start = ((), (), s32[]{:S(2)}) async-start(), calls=%async_computation.2 | async-start | bytes 3899392 | tf_op jit(solution)/shard_map/all_gather | solution.py:18
  50.8 25.4 %all-to-all-start = ((bf16[2,128,2048]{2,1,0:T(8,128)(2,1)}), bf16[2,128,2048]{2,1,0:T(8,128)(2,1)S(1)}, u32[]{:S(2)}, u32[]{:S(2)}) async-start(bf16[2,128,2048]{2,1,0:T(8,128)(2,1)} %bitcast.13), calls=%async_computation.1 | async-start | bytes 2097152 | tf_op jit(solution)/shard_map/all_to_all | solution.py:25
  54.4 122.7 %all-gather.12.cloned.1.call-start = ((), (), s32[]{:S(2)}) async-start(), calls=%async_computation.6 | async-start | bytes 1114112 | tf_op jit(solution)/shard_map/all_gather | solution.py:29
  94.5 175.7 %all-gather.14.cloned.1.call-start = ((), (), s32[]{:S(2)}) async-start(), calls=%async_computation.7 | async-start | bytes 11010048 | tf_op jit(solution)/shard_map/all_gather | solution.py:30
  95.1 54.9 %copy-start.1 = (u32[32]{0:T(128)S(1)}, u32[32]{0:T(128)}, u32[]{:S(2)}) copy-start(u32[32]{0:T(128)} %constant.24) | copy-start | bytes 388
  95.1 196.1 %reduce-scatter.2.cloned.1.call-start = ((), (), s32[]{:S(2)}) async-start(), calls=%async_computation.3 | async-start | bytes 1376256 | tf_op jit(solution)/shard_map/reduce_scatter | solution.py:22
  150.5 188.0 %copy-start = (s32[2]{0:T(128)S(1)}, s32[2]{0:T(128)}, u32[]{:S(2)}) copy-start(s32[2]{0:T(128)} %param.13) | copy-start | bytes 28
  331.7 7.4 %copy-start.2 = (f32[128]{0:T(128)}, f32[128]{0:T(128)S(1)}, u32[]{:S(2)}) copy-start(f32[128]{0:T(128)S(1)} %psum.7) | copy-start | bytes 1540
Sparse Core Ops, SparseCore 0:
  10.2 40.6 all-gather.7
  52.4 39.0 all-gather.9
  93.7 45.4 all-gather.5
  141.3 35.8 all-gather.11
  178.5 91.6 all-gather.13
  272.4 18.8 reduce-scatter.1
where the time goes:
time: 346 us
  waiting for transfers between devices  263 us (76%)
  blocking collectives  38.1 us (11%)
  matrix products  21.1 us (6%)
  between operations  14.8 us (4%)
  starting transfers between devices  3.81 us (1%)
    all_gather x1, waiting for transfers between devices, local(): eigen_block = lax.all_gather(eigvals, 'owner', axis=1, tiled=True)  93.1 us
    all_gather x1, waiting for transfers between devices, local(): lax.all_gather(grads, 'reader', axis=0, tiled=True)  44.1 us
    all_gather x1, waiting for transfers between devices, local(): all_rows = lax.all_gather(acts, 'reader', axis=0, tiled=True)  41.5 us
    psum x1, blocking collectives, local(): token_score = lax.psum(partial_score, 'reader')  33.2 us
    all_gather x1, waiting for transfers between devices, local(): full_a = lax.all_gather(rot_a, 'reader', axis=1, tiled=True)  26.6 us
    reduce_scatter x1, waiting for transfers between devices, local(): lax.psum_scatter(partial_g, 'owner', scatter_dimension=0, tiled=True)  21 us
    all_to_all x1, waiting for transfers between devices, local(): lax.all_to_all(all_rows, 'owner', split_axis=0, concat_axis=1, tiled=True)  19.8 us
    all_gather x1, waiting for transfers between devices, local(): vectors = lax.all_gather(basis_a, 'owner', axis=1, tiled=True)  14.5 us
  transfers between devices with their start and end apart: 7, of which 7 were waited for; matrix products, arithmetic and copies ran while one was open for 5% of the time, Pallas kernels for 0%

commit v1 on v0

v1 whole, which is shorter than its diff:
```python
import jax
import jax.numpy as jnp
from jax import lax
from jax.sharding import PartitionSpec as P

SEQ = 128


def local(acts, grads, basis_a, basis_g, eigvals, lengths, shuffle):
    owners = lax.axis_size("owner")
    readers = lax.axis_size("reader")
    owner_index = lax.axis_index("owner")
    rows = acts.shape[0] * readers
    slots = rows // SEQ
    m_block = basis_g.shape[0]
    n_block = basis_a.shape[0]
    width = eigvals.shape[1]
    dim_ff = m_block * readers
    dim_d = width * owners

    joined = jnp.concatenate([grads, acts], axis=1)
    joined = lax.all_gather(joined, "reader", axis=0, tiled=True)
    all_g = joined[:, : grads.shape[1]]
    all_a = joined[:, grads.shape[1]:]

    part_g = jnp.einsum("tk,jk->tj", all_g, basis_g, preferred_element_type=jnp.float32)
    part_a = jnp.einsum("tk,jk->tj", all_a, basis_a, preferred_element_type=jnp.float32)
    part = jnp.concatenate([part_g, part_a], axis=1)
    whole = lax.psum(part, "owner")

    token = jnp.arange(rows, dtype=jnp.int32)
    live = ((token % SEQ) < lengths[token // SEQ]).astype(jnp.float32)
    rot = (whole * live[:, None]).astype(jnp.bfloat16)
    rot_g = rot[:, :m_block]
    rot_a_block = rot[:, m_block:]

    rot_a_all = lax.all_gather(rot_a_block, "reader", axis=1, tiled=True)
    rot_a = lax.dynamic_slice_in_dim(rot_a_all, owner_index * width, width, axis=1)

    denom = eigvals.astype(jnp.float32)
    g_rows = rot_g.reshape(slots, SEQ, m_block)
    a_rows = rot_a.reshape(slots, SEQ, width)
    outer = jnp.einsum("smt,smn->stn", g_rows, a_rows, preferred_element_type=jnp.float32)
    scaled = (outer / denom[None]).astype(jnp.bfloat16)
    projected = jnp.einsum("stm,smn->stn", g_rows, scaled, preferred_element_type=jnp.float32)
    partial = jnp.sum(projected * a_rows.astype(jnp.float32), axis=2) / (dim_ff * dim_d)
    scores = lax.psum(partial, ("owner", "reader"))

    token_score = lax.dynamic_index_in_dim(scores, owner_index, 0, keepdims=False)
    slot_mean = jnp.sum(scores, axis=1) / SEQ
    table = (shuffle[:, None] == jnp.arange(slots, dtype=jnp.int32)[None, :]).astype(jnp.float32)
    example_score = jnp.sum(slot_mean[:, None] * table, axis=0)
    return (token_score, example_score)


def solution(mesh):
    return jax.shard_map(
        local,
        mesh=mesh,
        in_specs=(
            P("reader", "owner"),
            P("reader", "owner"),
            P("reader", "owner"),
            P("reader", "owner"),
            P("reader", "owner"),
            P(),
            P(),
        ),
        out_specs=(P("owner"), P()),
        check_vma=False,
    )
```

time: 346 us -> 220 us (0.64)
  waiting for transfers between devices: 263 us -> 133 us
  other arithmetic: 1.85 us -> 12.3 us
  starting transfers between devices: 3.81 us -> 0.12 us
    all_gather x5 -> x2, waiting for transfers between devices: 220 us -> 92.9 us  [the longest x1 57.3 us: local(): joined = lax.all_gather(joined, 'reader', axis=0, tiled=True)]
    psum x0 -> x1, waiting for transfers between devices: none -> 39.7 us  [local(): whole = lax.psum(part, 'owner')]
    reduce_scatter x1 -> x0, waiting for transfers between devices: 21 us -> none  [local(): lax.psum_scatter(partial_g, 'owner', scatter_dimension=0, tiled=True)]
    all_to_all x1 -> x0, waiting for transfers between devices: 19.8 us -> none  [local(): lax.all_to_all(all_rows, 'owner', split_axis=0, concat_axis=1, tiled=True)]
    convert_element_type x1 -> x3, other arithmetic: 0.65 us -> 7.35 us  [the longest x1 5.94 us: local(): denom = eigvals.astype(jnp.float32)]
    psum x1, blocking collectives: 33.2 us -> 39.7 us  [local(): scores = lax.psum(partial, ('owner', 'reader'))]
    unnamed x1 -> x0, blocking collectives: 4.92 us -> none
    all_to_all x1 -> x0, starting transfers between devices: 3.58 us -> none  [local(): lax.all_to_all(all_rows, 'owner', split_axis=0, concat_axis=1, tiled=True)]
  transfers between devices with their start and end apart: 7 -> 3, of which waited for: 7 -> 3; matrix products, arithmetic and copies ran while one was open for 5% -> 4% of each run, Pallas kernels for 0% -> 0%
where the time goes in v1:
time: 220 us
  waiting for transfers between devices  133 us (60%)
  blocking collectives  39.7 us (18%)
  matrix products  18.4 us (8%)
  between operations  13.8 us (6%)
  other arithmetic  12.3 us (6%)
  local copies, waits for them, and re-layouts  3.11 us (1%)
    all_gather x1, waiting for transfers between devices, local(): joined = lax.all_gather(joined, 'reader', axis=0, tiled=True)  57.3 us
    psum x1, blocking collectives, local(): scores = lax.psum(partial, ('owner', 'reader'))  39.7 us
    psum x1, waiting for transfers between devices, local(): whole = lax.psum(part, 'owner')  39.7 us
    all_gather x1, waiting for transfers between devices, local(): rot_a_all = lax.all_gather(rot_a_block, 'reader', axis=1, tiled=True)  35.5 us
    dot_general x1, matrix products, local(): jnp.einsum('tk,jk->tj', all_g, basis_g, preferred_element_type=jnp.float32)  10.2 us
    dot_general x1, matrix products, local(): jnp.einsum('stm,smn->stn', g_rows, scaled, preferred_element_type=jnp.flo...  6.41 us
    convert_element_type x1, other arithmetic, local(): denom = eigvals.astype(jnp.float32)  5.94 us
  transfers between devices with their start and end apart: 3, of which 3 were waited for; matrix products, arithmetic and copies ran while one was open for 4% of the time, Pallas kernels for 0%

profile of v1, /device:TPU:0, one launch (start us, length us, event | category | flops | bytes accessed | tf_op | source)
XLA Modules:
  0.0 220.0 jit_solution(6955430692185103928)
XLA Ops:
  7.2 0.0 all-gather.3.cloned.1.call-start
  7.2 1.8 pad_maximum_fusion.1
  9.0 0.0 all-gather.3.cloned.1.call-update
  9.0 0.0 all-reduce.2.cloned.1.call-start
  9.1 57.3 %all-gather.3.cloned.1.call-done = bf16[256,9216]{1,0:T(8,128)(2,1)} async-done(((bf16[16,9216]{1,0:T(8,128)(2,1)}), bf16[256,9216]{1,0:T(8,128)(2,1)}) %all-gather.3.cloned.1.call-update) | async-done | bytes 4718608 | tf_op jit(solution)/shard_map/all_gather | solution.py:22
  66.4 1.7 fusion.7
  68.1 10.2 %fusion.3 = f32[256,896]{1,0:T(8,128)S(1)} fusion(bf16[896,7168]{1,0:T(8,128)(2,1)} %param.10, bf16[256,9216]{1,0:T(8,128)(2,1)} %all-gather.3.cloned.1.call-done), kind=kOutput, calls=%fused_computation.3 | convolution fusion | flops 3288334336 | bytes 17432576 | tf_op jit(solution)/shard_map/tk,jk->tj/dot_general | solution.py:26
  78.4 1.1 pad_maximum_fusion
  79.5 0.0 all-reduce.2.cloned.1.call-update
  79.5 0.0 all-gather.5.cloned.1.call-start
  79.6 0.6 fusion.10
  80.2 1.3 compare_select_fusion.1
  81.5 39.7 %all-reduce.2.cloned.1.call-done = f32[256,1152]{1,0:T(8,128)} async-done(((f32[256,1152]{1,0:T(8,128)}), f32[256,1152]{1,0:T(8,128)}) %all-reduce.2.cloned.1.call-update) | async-done | bytes 1179664 | tf_op jit(solution)/shard_map/psum | solution.py:29
  121.2 1.4 multiply_convert_fusion
  122.6 0.7 slice.22
  123.2 0.0 all-gather.5.cloned.1.call-update
  123.3 5.9 %convert_element_type.22 = f32[896,2048]{1,0:T(8,128)} convert(bf16[896,2048]{1,0:T(8,128)(2,1)} %param.11) | non-fusion elementwise | flops 1835008 | bytes 11010048 | tf_op jit(solution)/shard_map/convert_element_type | solution.py:40
  129.2 35.5 %all-gather.5.cloned.1.call-done = bf16[256,4096]{1,0:T(8,128)(2,1)} async-done(((bf16[256,256]{1,0:T(8,128)(2,1)}), bf16[256,4096]{1,0:T(8,128)(2,1)}) %all-gather.5.cloned.1.call-update) | async-done | bytes 2097168 | tf_op jit(solution)/shard_map/all_gather | solution.py:37
  164.8 1.3 constant_dynamic-slice_fusion
  166.1 6.4 %fusion.6 = f32[2,128]{1,0:T(2,128)S(1)} fusion(bf16[2,128,2048]{2,1,0:T(8,128)(2,1)S(1)} %bitcast.12, bf16[2,128,896]{2,1,0:T(8,128)(2,1)S(1)} %bitcast.13, f32[896,2048]{1,0:T(8,128)} %convert_element_type.22), kind=kOutput, calls=%fused_computation.6 | convolution fusion | flops 1887960832 | bytes 8848384 | tf_op jit(solution)/shard_map/stm,smn->stn/dot_general | solution.py:45
  172.5 39.7 %psum.15 = f32[2,128]{1,0:T(2,128)S(1)} all-reduce(f32[2,128]{1,0:T(2,128)S(1)} %broadcast_multiply_fusion), channel_id=1, replica_groups=mesh['owner'=2,'reader'=16] {'owner','reader'}, use_global_device_ids=true, to_apply=%region_2.3 | all-reduce | flops 256 | bytes 2048 | tf_op jit(solution)/shard_map/psum | solution.py:47
  212.2 0.5 dynamic-slice_bitcast_fusion
  212.7 0.1 reduce_sum.28
  212.9 0.6 fusion.9
  (10 shorter events, 0.1 us)
Async XLA Ops:
  7.2 59.3 %copy-start = (bf16[256,2048]{1,0:T(8,128)(2,1)S(1)}, bf16[256,2048]{1,0:T(8,128)(2,1)}, u32[]{:S(2)}) copy-start(bf16[256,2048]{1,0:T(8,128)(2,1)} %param.9) | copy-start | bytes 3145732
  7.2 59.2 %all-gather.3.cloned.1.call-start = ((), (), s32[]{:S(2)}) async-start(), calls=%async_computation | async-start | bytes 5013504 | tf_op jit(solution)/shard_map/all_gather | solution.py:22
  9.0 112.1 %all-reduce.2.cloned.1.call-start = ((), (), s32[]{:S(2)}) async-start(), calls=%async_computation.1 | async-start | bytes 2359296 | tf_op jit(solution)/shard_map/psum | solution.py:29
  68.1 11.5 %copy-start.1 = (s32[2]{0:T(128)S(1)}, s32[2]{0:T(128)}, u32[]{:S(2)}) copy-start(s32[2]{0:T(128)} %param.12) | copy-start | bytes 28
  79.5 85.2 %all-gather.5.cloned.1.call-start = ((), (), s32[]{:S(2)}) async-start(), calls=%async_computation.2 | async-start | bytes 2228224 | tf_op jit(solution)/shard_map/all_gather | solution.py:37
  166.1 46.8 %copy-start.2 = (s32[2]{0:T(128)S(1)}, s32[2]{0:T(128)}, u32[]{:S(2)}) copy-start(s32[2]{0:T(128)} %param.13) | copy-start | bytes 28
Sparse Core Ops, SparseCore 0:
  10.3 56.0 all-gather.2
  79.7 41.4 all-reduce.1
  123.5 41.1 all-gather.4

commit v2 on v1

--- a/solution.py
+++ b/solution.py
@@ -4,6 +4,16 @@
 from jax.sharding import PartitionSpec as P
 
 SEQ = 128
+
+
+def butterfly_sum(x, axis, size):
+    if size & (size - 1):
+        return lax.psum(x, axis)
+    bit = 1
+    while bit < size:
+        x = x + lax.ppermute(x, axis, [(i, i ^ bit) for i in range(size)])
+        bit *= 2
+    return x
 
 
 def local(acts, grads, basis_a, basis_g, eigvals, lengths, shuffle):
@@ -23,16 +33,13 @@
     all_g = joined[:, : grads.shape[1]]
     all_a = joined[:, grads.shape[1]:]
 
-    part_g = jnp.einsum("tk,jk->tj", all_g, basis_g, preferred_element_type=jnp.float32)
-    part_a = jnp.einsum("tk,jk->tj", all_a, basis_a, preferred_element_type=jnp.float32)
-    part = jnp.concatenate([part_g, part_a], axis=1)
-    whole = lax.psum(part, "owner")
-
     token = jnp.arange(rows, dtype=jnp.int32)
     live = ((token % SEQ) < lengths[token // SEQ]).astype(jnp.float32)
-    rot = (whole * live[:, None]).astype(jnp.bfloat16)
-    rot_g = rot[:, :m_block]
-    rot_a_block = rot[:, m_block:]
+
+    part_a = jnp.einsum("tk,jk->tj", all_a, basis_a, preferred_element_type=jnp.float32)
+    rot_a_block = (butterfly_sum(part_a, "owner", owners) * live[:, None]).astype(jnp.bfloat16)
+    part_g = jnp.einsum("tk,jk->tj", all_g, basis_g, preferred_element_type=jnp.float32)
+    rot_g = (butterfly_sum(part_g, "owner", owners) * live[:, None]).astype(jnp.bfloat16)
 
     rot_a_all = lax.all_gather(rot_a_block, "reader", axis=1, tiled=True)
     rot_a = lax.dynamic_slice_in_dim(rot_a_all, owner_index * width, width, axis=1)
@@ -44,7 +51,7 @@
     scaled = (outer / denom[None]).astype(jnp.bfloat16)
     projected = jnp.einsum("stm,smn->stn", g_rows, scaled, preferred_element_type=jnp.float32)
     partial = jnp.sum(projected * a_rows.astype(jnp.float32), axis=2) / (dim_ff * dim_d)
-    scores = lax.psum(partial, ("owner", "reader"))
+    scores = butterfly_sum(butterfly_sum(partial, "reader", readers), "owner", owners)
 
     token_score = lax.dynamic_index_in_dim(scores, owner_index, 0, keepdims=False)
     slot_mean = jnp.sum(scores, axis=1) / SEQ

time: 220 us -> 150 us (0.68)
  blocking collectives: 39.7 us -> 0 us
  waiting for transfers between devices: 133 us -> 95.1 us
  starting transfers between devices: 0.12 us -> 8.25 us
    psum x1 -> x0, blocking collectives: 39.7 us -> none  [local(): scores = lax.psum(partial, ('owner', 'reader'))]
    psum x1 -> x0, waiting for transfers between devices: 39.7 us -> none  [local(): whole = lax.psum(part, 'owner')]
    ppermute x0 -> x7, waiting for transfers between devices: none -> 31.3 us  [butterfly_sum(): x = x + lax.ppermute(x, axis, [(i, i ^ bit) for i in range(size)])]
    all_gather x1, waiting for transfers between devices: 35.5 us -> 7.74 us  [local(): rot_a_all = lax.all_gather(rot_a_block, 'reader', axis=1, tiled=True)]
    ppermute x0 -> x7, starting transfers between devices: none -> 8.17 us  [butterfly_sum(): x = x + lax.ppermute(x, axis, [(i, i ^ bit) for i in range(size)])]
  transfers between devices with their start and end apart: 3 -> 9, of which waited for: 3 -> 9; matrix products, arithmetic and copies ran while one was open for 4% -> 13% of each run, Pallas kernels for 0% -> 0%
where the time goes in v2:
time: 150 us
  waiting for transfers between devices  95.1 us (63%)
  matrix products  18.5 us (12%)
  between operations  14.1 us (9%)
  other arithmetic  10.7 us (7%)
  starting transfers between devices  8.25 us (6%)
  local copies, waits for them, and re-layouts  3.14 us (2%)
    all_gather x1, waiting for transfers between devices, local(): joined = lax.all_gather(joined, 'reader', axis=0, tiled=True)  56 us
    ppermute x7, waiting for transfers between devices, butterfly_sum(): x = x + lax.ppermute(x, axis, [(i, i ^ bit) for i in range(size)])  31.3 us
    dot_general x1, matrix products, local(): jnp.einsum('tk,jk->tj', all_g, basis_g, preferred_element_type=jnp.float32)  10.2 us
    ppermute x7, starting transfers between devices, butterfly_sum(): x = x + lax.ppermute(x, axis, [(i, i ^ bit) for i in range(size)])  8.17 us
    all_gather x1, waiting for transfers between devices, local(): rot_a_all = lax.all_gather(rot_a_block, 'reader', axis=1, tiled=True)  7.74 us
    dot_general x1, matrix products, local(): jnp.einsum('stm,smn->stn', g_rows, scaled, preferred_element_type=jnp.flo...  6.59 us
    convert_element_type x1, other arithmetic, local(): denom = eigvals.astype(jnp.float32)  5.92 us
  transfers between devices with their start and end apart: 9, of which 9 were waited for; matrix products, arithmetic and copies ran while one was open for 13% of the time, Pallas kernels for 0%

profile of v2, /device:TPU:0, one launch (start us, length us, event | category | flops | bytes accessed | tf_op | source)
XLA Modules:
  0.0 149.7 jit_solution(16620412276112927531)
XLA Ops:
  7.2 1.8 %pad_maximum_fusion = bf16[16,9216]{1,0:T(8,128)(2,1)} fusion(bf16[16,2048]{1,0:T(8,128)(2,1)} %param.7, bf16[16,7168]{1,0:T(8,128)(2,1)} %param.8), kind=kLoop, calls=%fused_computation.10 | loop fusion | flops 589824 | bytes 589824 | tf_op jit(solution)/shard_map/concatenate | solution.py:31
  9.1 1.3 fusion.12
  10.4 56.0 %all-gather.3.cloned.1.call-done = bf16[256,9216]{1,0:T(8,128)(2,1)} async-done(((bf16[16,9216]{1,0:T(8,128)(2,1)}), bf16[256,9216]{1,0:T(8,128)(2,1)}) %all-gather.3.cloned.1.call-update) | async-done | bytes 4718608 | tf_op jit(solution)/shard_map/all_gather | solution.py:32
  66.4 1.7 %fusion.7 = f32[256,256]{1,0:T(8,128)S(1)} fusion(bf16[256,2048]{1,0:T(8,128)(2,1)S(1)} %copy-done, bf16[256,9216]{1,0:T(8,128)(2,1)} %all-gather.3.cloned.1.call-done), kind=kOutput, calls=%fused_computation.7 | convolution fusion | flops 268435456 | bytes 2359296 | tf_op jit(solution)/shard_map/tk,jk->tj/dot_general | solution.py:39
  68.1 1.5 %collective-permute-start.1 = (f32[256,256]{1,0:T(8,128)S(1)}, f32[256,256]{1,0:T(8,128)S(1)}, u32[]{:S(2)}, u32[]{:S(2)}) collective-permute-start(f32[256,256]{1,0:T(8,128)S(1)} %fusion.7), channel_id=1, source_target_pairs={{0,16},{16,0},{1,17},{17,1},{2,18},{18,2},{3,19},{19,3},{4,20},{20... | collective-permute-start | bytes 786440 | tf_op jit(solution)/shard_map/ppermute | solution.py:14
  69.7 1.3 compare_select_fusion.1
  71.0 5.7 %collective-permute-done.1 = f32[256,256]{1,0:T(8,128)S(1)} collective-permute-done((f32[256,256]{1,0:T(8,128)S(1)}, f32[256,256]{1,0:T(8,128)S(1)}, u32[]{:S(2)}, u32[]{:S(2)}) %collective-permute-start.1) | collective-permute-done | bytes 262176 | tf_op jit(solution)/shard_map/ppermute | solution.py:14
  76.7 0.8 multiply_convert_fusion.1
  77.5 10.2 %fusion.3 = f32[256,896]{1,0:T(8,128)S(1)} fusion(bf16[896,7168]{1,0:T(8,128)(2,1)} %param.10, bf16[256,9216]{1,0:T(8,128)(2,1)} %all-gather.3.cloned.1.call-done), kind=kOutput, calls=%fused_computation.3 | convolution fusion | flops 3288334336 | bytes 17432576 | tf_op jit(solution)/shard_map/tk,jk->tj/dot_general | solution.py:41
  87.7 1.5 %collective-permute-start = (f32[256,896]{1,0:T(8,128)S(1)}, f32[256,896]{1,0:T(8,128)S(1)}, u32[]{:S(2)}, u32[]{:S(2)}) collective-permute-start(f32[256,896]{1,0:T(8,128)S(1)} %fusion.3), channel_id=1, source_target_pairs={{0,16},{16,0},{1,17},{17,1},{2,18},{18,2},{3,19},{19,3},{4,20},{20... | collective-permute-start | bytes 2752520 | tf_op jit(solution)/shard_map/ppermute | solution.py:14
  89.2 5.9 %convert_element_type.26 = f32[896,2048]{1,0:T(8,128)} convert(bf16[896,2048]{1,0:T(8,128)(2,1)} %param.11) | non-fusion elementwise | flops 1835008 | bytes 11010048 | tf_op jit(solution)/shard_map/convert_element_type | solution.py:47
  95.1 14.3 %collective-permute-done = f32[256,896]{1,0:T(8,128)S(1)} collective-permute-done((f32[256,896]{1,0:T(8,128)S(1)}, f32[256,896]{1,0:T(8,128)S(1)}, u32[]{:S(2)}, u32[]{:S(2)}) %collective-permute-start) | collective-permute-done | bytes 917536 | tf_op jit(solution)/shard_map/ppermute | solution.py:14
  109.6 7.7 %all-gather.5.cloned.1.call-done = bf16[256,4096]{1,0:T(8,128)(2,1)} async-done(((bf16[256,256]{1,0:T(8,128)(2,1)}), bf16[256,4096]{1,0:T(8,128)(2,1)}) %all-gather.5.cloned.1.call-update) | async-done | bytes 2097168 | tf_op jit(solution)/shard_map/all_gather | solution.py:44
  117.4 1.3 constant_dynamic-slice_fusion
  118.7 6.6 %fusion.6 = f32[2,128]{1,0:T(2,128)S(1)} fusion(bf16[2,128,2048]{2,1,0:T(8,128)(2,1)S(1)} %bitcast.12, bf16[2,128,896]{2,1,0:T(8,128)(2,1)S(1)} %bitcast.13, f32[896,2048]{1,0:T(8,128)} %convert_element_type.26), kind=kOutput, calls=%fused_computation.6 | convolution fusion | flops 1887960832 | bytes 8848384 | tf_op jit(solution)/shard_map/stm,smn->stn/dot_general | solution.py:52
  125.6 0.9 collective-permute-done.2
  126.5 1.2 collective-permute-start.3
  127.7 2.4 %collective-permute-done.3 = f32[2,128]{1,0:T(2,128)S(1)} collective-permute-done((f32[2,128]{1,0:T(2,128)S(1)}, f32[2,128]{1,0:T(2,128)S(1)}, u32[]{:S(2)}, u32[]{:S(2)}) %collective-permute-start.3) | collective-permute-done | bytes 1056 | tf_op jit(solution)/shard_map/ppermute | solution.py:14
  130.0 0.8 collective-permute-start.4
  130.8 2.8 %collective-permute-done.4 = f32[2,128]{1,0:T(2,128)S(1)} collective-permute-done((f32[2,128]{1,0:T(2,128)S(1)}, f32[2,128]{1,0:T(2,128)S(1)}, u32[]{:S(2)}, u32[]{:S(2)}) %collective-permute-start.4) | collective-permute-done | bytes 1056 | tf_op jit(solution)/shard_map/ppermute | solution.py:14
  133.6 1.3 collective-permute-start.5
  134.9 3.2 %collective-permute-done.5 = f32[2,128]{1,0:T(2,128)S(1)} collective-permute-done((f32[2,128]{1,0:T(2,128)S(1)}, f32[2,128]{1,0:T(2,128)S(1)}, u32[]{:S(2)}, u32[]{:S(2)}) %collective-permute-start.5) | collective-permute-done | bytes 1056 | tf_op jit(solution)/shard_map/ppermute | solution.py:14
  138.1 1.5 %collective-permute-start.6 = (f32[2,128]{1,0:T(2,128)S(1)}, f32[2,128]{1,0:T(2,128)S(1)}, u32[]{:S(2)}, u32[]{:S(2)}) collective-permute-start(f32[2,128]{1,0:T(2,128)S(1)} %add.68), channel_id=1, source_target_pairs={{0,16},{16,0},{1,17},{17,1},{2,18},{18,2},{3,19},{19,3},{4,20},{20... | collective-permute-start | bytes 3080 | tf_op jit(solution)/shard_map/ppermute | solution.py:14
  139.6 2.1 %collective-permute-done.6 = f32[2,128]{1,0:T(2,128)S(1)} collective-permute-done((f32[2,128]{1,0:T(2,128)S(1)}, f32[2,128]{1,0:T(2,128)S(1)}, u32[]{:S(2)}, u32[]{:S(2)}) %collective-permute-start.6) | collective-permute-done | bytes 1056 | tf_op jit(solution)/shard_map/ppermute | solution.py:14
  (20 shorter events, 1.9 us)
Async XLA Ops:
  7.2 59.3 %copy-start = (bf16[256,2048]{1,0:T(8,128)(2,1)S(1)}, bf16[256,2048]{1,0:T(8,128)(2,1)}, u32[]{:S(2)}) copy-start(bf16[256,2048]{1,0:T(8,128)(2,1)} %param.9) | copy-start | bytes 3145732
  7.2 59.2 %all-gather.3.cloned.1.call-start = ((), (), s32[]{:S(2)}) async-start(), calls=%async_computation | async-start | bytes 5013504 | tf_op jit(solution)/shard_map/all_gather | solution.py:32
  9.0 108.3 %all-gather.5.cloned.1.call-start = ((), (), s32[]{:S(2)}) async-start(), calls=%async_computation.1 | async-start | bytes 2228224 | tf_op jit(solution)/shard_map/all_gather | solution.py:44
  68.1 8.5 %collective-permute-start.1 = (f32[256,256]{1,0:T(8,128)S(1)}, f32[256,256]{1,0:T(8,128)S(1)}, u32[]{:S(2)}, u32[]{:S(2)}) collective-permute-start(f32[256,256]{1,0:T(8,128)S(1)} %fusion.7), channel_id=1, source_target_pairs={{0,16},{16,0},{1,17},{17,1},{2,18},{18,2},{3,19},{19,3},{4,20},{20... | collective-permute-start | bytes 786440 | tf_op jit(solution)/shard_map/ppermute | solution.py:14
  87.7 21.8 %collective-permute-start = (f32[256,896]{1,0:T(8,128)S(1)}, f32[256,896]{1,0:T(8,128)S(1)}, u32[]{:S(2)}, u32[]{:S(2)}) collective-permute-start(f32[256,896]{1,0:T(8,128)S(1)} %fusion.3), channel_id=1, source_target_pairs={{0,16},{16,0},{1,17},{17,1},{2,18},{18,2},{3,19},{19,3},{4,20},{20... | collective-permute-start | bytes 2752520 | tf_op jit(solution)/shard_map/ppermute | solution.py:14
  118.7 23.1 %copy-start.1 = (s32[2]{0:T(128)S(1)}, s32[2]{0:T(128)}, u32[]{:S(2)}) copy-start(s32[2]{0:T(128)} %param.13) | copy-start | bytes 28
  125.3 1.2 collective-permute-start.2
  126.5 3.6 %collective-permute-start.3 = (f32[2,128]{1,0:T(2,128)S(1)}, f32[2,128]{1,0:T(2,128)S(1)}, u32[]{:S(2)}, u32[]{:S(2)}) collective-permute-start(f32[2,128]{1,0:T(2,128)S(1)} %fusion.10), channel_id=1, source_target_pairs={{0,2},{1,3},{2,0},{3,1},{4,6},{5,7},{6,4},{7,5},{8,10},{9,11},{10,... | collective-permute-start | bytes 3080 | tf_op jit(solution)/shard_map/ppermute | solution.py:14
  130.0 3.6 %collective-permute-start.4 = (f32[2,128]{1,0:T(2,128)S(1)}, f32[2,128]{1,0:T(2,128)S(1)}, u32[]{:S(2)}, u32[]{:S(2)}) collective-permute-start(f32[2,128]{1,0:T(2,128)S(1)} %add.66), channel_id=1, source_target_pairs={{0,4},{1,5},{2,6},{3,7},{4,0},{5,1},{6,2},{7,3},{8,12},{9,13},{10,... | collective-permute-start | bytes 3080 | tf_op jit(solution)/shard_map/ppermute | solution.py:14
  133.6 4.5 %collective-permute-start.5 = (f32[2,128]{1,0:T(2,128)S(1)}, f32[2,128]{1,0:T(2,128)S(1)}, u32[]{:S(2)}, u32[]{:S(2)}) collective-permute-start(f32[2,128]{1,0:T(2,128)S(1)} %add.67), channel_id=1, source_target_pairs={{0,8},{1,9},{2,10},{3,11},{4,12},{5,13},{6,14},{7,15},{8,0},{9,1},... | collective-permute-start | bytes 3080 | tf_op jit(solution)/shard_map/ppermute | solution.py:14
  138.1 3.6 %collective-permute-start.6 = (f32[2,128]{1,0:T(2,128)S(1)}, f32[2,128]{1,0:T(2,128)S(1)}, u32[]{:S(2)}, u32[]{:S(2)}) collective-permute-start(f32[2,128]{1,0:T(2,128)S(1)} %add.68), channel_id=1, source_target_pairs={{0,16},{16,0},{1,17},{17,1},{2,18},{18,2},{3,19},{19,3},{4,20},{20... | collective-permute-start | bytes 3080 | tf_op jit(solution)/shard_map/ppermute | solution.py:14
Sparse Core Ops, SparseCore 0:
  10.3 56.0 all-gather.2
  77.6 39.7 all-gather.4

commit v3 on v2

--- a/solution.py
+++ b/solution.py
@@ -14,6 +14,28 @@
         x = x + lax.ppermute(x, axis, [(i, i ^ bit) for i in range(size)])
         bit *= 2
     return x
+
+
+def half_gather(block, owners, readers):
+    reader_index = lax.axis_index("reader")
+    owner_index = lax.axis_index("owner")
+    group = readers // owners
+    held = block
+    bit = readers // 2
+    while bit >= group:
+        other = lax.ppermute(held, "reader", [(i, i ^ bit) for i in range(readers)])
+        keep = (reader_index & bit) == ((owner_index * group) & bit)
+        held = jnp.where(keep, held, other)
+        bit //= 2
+    held = held[None]
+    while bit >= 1:
+        other = lax.ppermute(held, "reader", [(i, i ^ bit) for i in range(readers)])
+        low = (reader_index & bit) == 0
+        first = jnp.where(low, held, other)
+        second = jnp.where(low, other, held)
+        held = jnp.stack([first, second], axis=1).reshape((-1,) + block.shape)
+        bit //= 2
+    return jnp.transpose(held, (1, 0, 2)).reshape(block.shape[0], -1)
 
 
 def local(acts, grads, basis_a, basis_g, eigvals, lengths, shuffle):
@@ -41,8 +63,7 @@
     part_g = jnp.einsum("tk,jk->tj", all_g, basis_g, preferred_element_type=jnp.float32)
     rot_g = (butterfly_sum(part_g, "owner", owners) * live[:, None]).astype(jnp.bfloat16)
 
-    rot_a_all = lax.all_gather(rot_a_block, "reader", axis=1, tiled=True)
-    rot_a = lax.dynamic_slice_in_dim(rot_a_all, owner_index * width, width, axis=1)
+    rot_a = half_gather(rot_a_block, owners, readers)
 
     denom = eigvals.astype(jnp.float32)
     g_rows = rot_g.reshape(slots, SEQ, m_block)

time: 150 us -> 152 us (1.013)
  waiting for transfers between devices: 95.1 us -> 90.8 us
  starting transfers between devices: 8.25 us -> 11.8 us
  other arithmetic: 10.7 us -> 13.2 us
    ppermute x0 -> x4, waiting for transfers between devices: none -> 13.2 us  [half_gather(): other = lax.ppermute(held, 'reader', [(i, i ^ bit) for i in range(readers)])]
    ppermute x7, waiting for transfers between devices: 31.3 us -> 21.6 us  [butterfly_sum(): x = x + lax.ppermute(x, axis, [(i, i ^ bit) for i in range(size)])]
    all_gather x1 -> x0, waiting for transfers between devices: 7.74 us -> none  [local(): rot_a_all = lax.all_gather(rot_a_block, 'reader', axis=1, tiled=True)]
    ppermute x0 -> x4, starting transfers between devices: none -> 2.68 us  [half_gather(): other = lax.ppermute(held, 'reader', [(i, i ^ bit) for i in range(readers)])]
    another operation x0 -> x5, other arithmetic: none -> 2.28 us  [half_gather(): held = jnp.stack([first, second], axis=1).reshape((-1,) + block.shape)]
  transfers between devices with their start and end apart: 9 -> 12, of which waited for: 9 -> 10; matrix products, arithmetic and copies ran while one was open for 13% -> 14% of each run, Pallas kernels for 0% -> 0%
where the time goes in v3:
time: 152 us
  waiting for transfers between devices  90.8 us (60%)
  matrix products  18.7 us (12%)
  between operations  14.2 us (9%)
  other arithmetic  13.2 us (9%)
  starting transfers between devices  11.8 us (8%)
  local copies, waits for them, and re-layouts  3.06 us (2%)
    all_gather x1, waiting for transfers between devices, local(): joined = lax.all_gather(joined, 'reader', axis=0, tiled=True)  56 us
    ppermute x7, waiting for transfers between devices, butterfly_sum(): x = x + lax.ppermute(x, axis, [(i, i ^ bit) for i in range(size)])  21.6 us
    ppermute x4, waiting for transfers between devices, half_gather(): other = lax.ppermute(held, 'reader', [(i, i ^ bit) for i in range(readers)])  13.2 us
    dot_general x1, matrix products, local(): jnp.einsum('tk,jk->tj', all_g, basis_g, preferred_element_type=jnp.float32)  10.2 us
    ppermute x7, starting transfers between devices, butterfly_sum(): x = x + lax.ppermute(x, axis, [(i, i ^ bit) for i in range(size)])  9.05 us
    dot_general x1, matrix products, local(): jnp.einsum('stm,smn->stn', g_rows, scaled, preferred_element_type=jnp.flo...  6.78 us
    convert_element_type x1, other arithmetic, local(): denom = eigvals.astype(jnp.float32)  5.92 us
  transfers between devices with their start and end apart: 12, of which 10 were waited for; matrix products, arithmetic and copies ran while one was open for 14% of the time, Pallas kernels for 0%

profile of v3, /device:TPU:0, one launch (start us, length us, event | category | flops | bytes accessed | tf_op | source)
XLA Modules:
  0.0 151.7 jit_solution(7481116946303128068)
XLA Ops:
  7.2 1.8 %pad_maximum_fusion.2 = bf16[16,9216]{1,0:T(8,128)(2,1)} fusion(bf16[16,2048]{1,0:T(8,128)(2,1)} %param.7, bf16[16,7168]{1,0:T(8,128)(2,1)} %param.8), kind=kLoop, calls=%fused_computation.14 | loop fusion | flops 589824 | bytes 589824 | tf_op jit(solution)/shard_map/concatenate | solution.py:53
  9.1 1.3 fusion.12
  10.4 56.0 %all-gather.2.cloned.1.call-done = bf16[256,9216]{1,0:T(8,128)(2,1)} async-done(((bf16[16,9216]{1,0:T(8,128)(2,1)}), bf16[256,9216]{1,0:T(8,128)(2,1)}) %all-gather.2.cloned.1.call-update) | async-done | bytes 4718608 | tf_op jit(solution)/shard_map/all_gather | solution.py:54
  66.4 1.7 %fusion.7 = f32[256,256]{1,0:T(8,128)S(1)} fusion(bf16[256,2048]{1,0:T(8,128)(2,1)S(1)} %copy-done, bf16[256,9216]{1,0:T(8,128)(2,1)} %all-gather.2.cloned.1.call-done), kind=kOutput, calls=%fused_computation.7 | convolution fusion | flops 268435456 | bytes 2359296 | tf_op jit(solution)/shard_map/tk,jk->tj/dot_general | solution.py:61
  68.1 1.5 %collective-permute-start.1 = (f32[256,256]{1,0:T(8,128)S(1)}, f32[256,256]{1,0:T(8,128)S(1)}, u32[]{:S(2)}, u32[]{:S(2)}) collective-permute-start(f32[256,256]{1,0:T(8,128)S(1)} %fusion.7), channel_id=1, source_target_pairs={{0,16},{16,0},{1,17},{17,1},{2,18},{18,2},{3,19},{19,3},{4,20},{20... | collective-permute-start | bytes 786440 | tf_op jit(solution)/shard_map/ppermute | solution.py:14
  69.7 1.3 compare_select_fusion.1
  71.0 5.7 %collective-permute-done.1 = f32[256,256]{1,0:T(8,128)S(1)} collective-permute-done((f32[256,256]{1,0:T(8,128)S(1)}, f32[256,256]{1,0:T(8,128)S(1)}, u32[]{:S(2)}, u32[]{:S(2)}) %collective-permute-start.1) | collective-permute-done | bytes 262176 | tf_op jit(solution)/shard_map/ppermute | solution.py:14
  76.8 1.9 %collective-permute-start.2 = (bf16[256,256]{1,0:T(8,128)(2,1)S(1)}, bf16[256,256]{1,0:T(8,128)(2,1)S(1)}, u32[]{:S(2)}, u32[]{:S(2)}) collective-permute-start(bf16[256,256]{1,0:T(8,128)(2,1)S(1)} %multiply_convert_fusion.1), channel_id=1, source_target_pairs={{0,8},{1,9},{2,10},{3,11},{4,12},{5,13},{6,14},{7,15},{8,0},{9,1},... | collective-permute-start | bytes 393224 | tf_op jit(solution)/shard_map/ppermute | solution.py:26
  78.7 6.7 %collective-permute-done.2 = bf16[256,256]{1,0:T(8,128)(2,1)S(1)} collective-permute-done((bf16[256,256]{1,0:T(8,128)(2,1)S(1)}, bf16[256,256]{1,0:T(8,128)(2,1)S(1)}, u32[]{:S(2)}, u32[]{:S(2)}) %collective-permute-start.2) | collective-permute-done | bytes 131104 | tf_op jit(solution)/shard_map/ppermute | solution.py:26
  85.5 10.2 %fusion.3 = f32[256,896]{1,0:T(8,128)S(1)} fusion(bf16[896,7168]{1,0:T(8,128)(2,1)} %param.10, bf16[256,9216]{1,0:T(8,128)(2,1)} %all-gather.2.cloned.1.call-done), kind=kOutput, calls=%fused_computation.3 | convolution fusion | flops 3288334336 | bytes 17432576 | tf_op jit(solution)/shard_map/tk,jk->tj/dot_general | solution.py:63
  95.7 1.5 %collective-permute-start = (f32[256,896]{1,0:T(8,128)S(1)}, f32[256,896]{1,0:T(8,128)S(1)}, u32[]{:S(2)}, u32[]{:S(2)}) collective-permute-start(f32[256,896]{1,0:T(8,128)S(1)} %fusion.3), channel_id=1, source_target_pairs={{0,16},{16,0},{1,17},{17,1},{2,18},{18,2},{3,19},{19,3},{4,20},{20... | collective-permute-start | bytes 2752520 | tf_op jit(solution)/shard_map/ppermute | solution.py:14
  97.9 6.5 %collective-permute-done.4 = bf16[2,256,256]{2,1,0:T(8,128)(2,1)} collective-permute-done((bf16[2,256,256]{2,1,0:T(8,128)(2,1)S(1)}, bf16[2,256,256]{2,1,0:T(8,128)(2,1)}, u32[]{:S(2)}, u32[]{:S(2)}) %collective-permute-start.4) | collective-permute-done | bytes 262176 | tf_op jit(solution)/shard_map/ppermute | solution.py:32
  105.6 5.9 %convert_element_type.26 = f32[896,2048]{1,0:T(8,128)} convert(bf16[896,2048]{1,0:T(8,128)(2,1)} %param.11) | non-fusion elementwise | flops 1835008 | bytes 11010048 | tf_op jit(solution)/shard_map/convert_element_type | solution.py:68
  111.5 5.5 %collective-permute-done = f32[256,896]{1,0:T(8,128)S(1)} collective-permute-done((f32[256,896]{1,0:T(8,128)S(1)}, f32[256,896]{1,0:T(8,128)S(1)}, u32[]{:S(2)}, u32[]{:S(2)}) %collective-permute-start) | collective-permute-done | bytes 917536 | tf_op jit(solution)/shard_map/ppermute | solution.py:14
  118.0 1.1 select_bitcast_fusion.1
  120.4 6.8 %fusion.6 = f32[2,128]{1,0:T(2,128)S(1)} fusion(bf16[2,128,2048]{2,1,0:T(8,128)(2,1)S(1)} %reshape_reshape.3, bf16[2,128,896]{2,1,0:T(8,128)(2,1)} %bitcast.39, f32[896,2048]{1,0:T(8,128)} %convert_element_type.26), kind=kOutput, calls=%fused_computation.6 | convolution fusion | flops 1887960832 | bytes 8848384 | tf_op jit(solution)/shard_map/stm,smn->stn/dot_general | solution.py:73
  127.3 1.1 collective-permute-done.6
  129.0 3.0 %collective-permute-done.7 = f32[2,128]{1,0:T(2,128)S(1)} collective-permute-done((f32[2,128]{1,0:T(2,128)S(1)}, f32[2,128]{1,0:T(2,128)S(1)}, u32[]{:S(2)}, u32[]{:S(2)}) %collective-permute-start.7) | collective-permute-done | bytes 1056 | tf_op jit(solution)/shard_map/ppermute | solution.py:14
  132.0 1.7 %collective-permute-start.8 = (f32[2,128]{1,0:T(2,128)S(1)}, f32[2,128]{1,0:T(2,128)S(1)}, u32[]{:S(2)}, u32[]{:S(2)}) collective-permute-start(f32[2,128]{1,0:T(2,128)S(1)} %add.62), channel_id=1, source_target_pairs={{0,4},{1,5},{2,6},{3,7},{4,0},{5,1},{6,2},{7,3},{8,12},{9,13},{10,... | collective-permute-start | bytes 3080 | tf_op jit(solution)/shard_map/ppermute | solution.py:14
  133.7 1.9 %collective-permute-done.8 = f32[2,128]{1,0:T(2,128)S(1)} collective-permute-done((f32[2,128]{1,0:T(2,128)S(1)}, f32[2,128]{1,0:T(2,128)S(1)}, u32[]{:S(2)}, u32[]{:S(2)}) %collective-permute-start.8) | collective-permute-done | bytes 1056 | tf_op jit(solution)/shard_map/ppermute | solution.py:14
  135.6 2.2 %collective-permute-start.9 = (f32[2,128]{1,0:T(2,128)S(1)}, f32[2,128]{1,0:T(2,128)S(1)}, u32[]{:S(2)}, u32[]{:S(2)}) collective-permute-start(f32[2,128]{1,0:T(2,128)S(1)} %add.63), channel_id=1, source_target_pairs={{0,8},{1,9},{2,10},{3,11},{4,12},{5,13},{6,14},{7,15},{8,0},{9,1},... | collective-permute-start | bytes 3080 | tf_op jit(solution)/shard_map/ppermute | solution.py:14
  137.8 2.3 %collective-permute-done.9 = f32[2,128]{1,0:T(2,128)S(1)} collective-permute-done((f32[2,128]{1,0:T(2,128)S(1)}, f32[2,128]{1,0:T(2,128)S(1)}, u32[]{:S(2)}, u32[]{:S(2)}) %collective-permute-start.9) | collective-permute-done | bytes 1056 | tf_op jit(solution)/shard_map/ppermute | solution.py:14
  140.1 1.5 collective-permute-start.10
  141.5 2.1 %collective-permute-done.10 = f32[2,128]{1,0:T(2,128)S(1)} collective-permute-done((f32[2,128]{1,0:T(2,128)S(1)}, f32[2,128]{1,0:T(2,128)S(1)}, u32[]{:S(2)}, u32[]{:S(2)}) %collective-permute-start.10) | collective-permute-done | bytes 1056 | tf_op jit(solution)/shard_map/ppermute | solution.py:14
  (35 shorter events, 6.2 us)
Async XLA Ops:
  7.2 59.3 %copy-start = (bf16[256,2048]{1,0:T(8,128)(2,1)S(1)}, bf16[256,2048]{1,0:T(8,128)(2,1)}, u32[]{:S(2)}) copy-start(bf16[256,2048]{1,0:T(8,128)(2,1)} %param.9) | copy-start | bytes 3145732
  7.2 59.2 %all-gather.2.cloned.1.call-start = ((), (), s32[]{:S(2)}) async-start(), calls=%async_computation | async-start | bytes 5013504 | tf_op jit(solution)/shard_map/all_gather | solution.py:54
  68.1 8.5 %collective-permute-start.1 = (f32[256,256]{1,0:T(8,128)S(1)}, f32[256,256]{1,0:T(8,128)S(1)}, u32[]{:S(2)}, u32[]{:S(2)}) collective-permute-start(f32[256,256]{1,0:T(8,128)S(1)} %fusion.7), channel_id=1, source_target_pairs={{0,16},{16,0},{1,17},{17,1},{2,18},{18,2},{3,19},{19,3},{4,20},{20... | collective-permute-start | bytes 786440 | tf_op jit(solution)/shard_map/ppermute | solution.py:14
  76.8 8.6 %collective-permute-start.2 = (bf16[256,256]{1,0:T(8,128)(2,1)S(1)}, bf16[256,256]{1,0:T(8,128)(2,1)S(1)}, u32[]{:S(2)}, u32[]{:S(2)}) collective-permute-start(bf16[256,256]{1,0:T(8,128)(2,1)S(1)} %multiply_convert_fusion.1), channel_id=1, source_target_pairs={{0,8},{1,9},{2,10},{3,11},{4,12},{5,13},{6,14},{7,15},{8,0},{9,1},... | collective-permute-start | bytes 393224 | tf_op jit(solution)/shard_map/ppermute | solution.py:26
  85.4 11.8 %collective-permute-start.3 = (bf16[1,256,256]{2,1,0:T(8,128)(2,1)S(1)}, bf16[1,256,256]{2,1,0:T(8,128)(2,1)S(1)}, u32[]{:S(2)}, u32[]{:S(2)}) collective-permute-start(bf16[1,256,256]{2,1,0:T(8,128)(2,1)S(1)} %select_bitcast_fusion.6), channel_id=1, source_target_pairs={{0,4},{1,5},{2,6},{3,7},{4,0},{5,1},{6,2},{7,3},{8,12},{9,13},{10,... | collective-permute-start | bytes 393224 | tf_op jit(solution)/shard_map/ppermute | solution.py:32
  95.7 21.3 %collective-permute-start = (f32[256,896]{1,0:T(8,128)S(1)}, f32[256,896]{1,0:T(8,128)S(1)}, u32[]{:S(2)}, u32[]{:S(2)}) collective-permute-start(f32[256,896]{1,0:T(8,128)S(1)} %fusion.3), channel_id=1, source_target_pairs={{0,16},{16,0},{1,17},{17,1},{2,18},{18,2},{3,19},{19,3},{4,20},{20... | collective-permute-start | bytes 2752520 | tf_op jit(solution)/shard_map/ppermute | solution.py:14
  97.3 7.1 %collective-permute-start.4 = (bf16[2,256,256]{2,1,0:T(8,128)(2,1)S(1)}, bf16[2,256,256]{2,1,0:T(8,128)(2,1)}, u32[]{:S(2)}, u32[]{:S(2)}) collective-permute-start(bf16[2,256,256]{2,1,0:T(8,128)(2,1)S(1)} %maximum_bitcast_fusion), channel_id=1, source_target_pairs={{0,2},{1,3},{2,0},{3,1},{4,6},{5,7},{6,4},{7,5},{8,10},{9,11},{10,... | collective-permute-start | bytes 786440 | tf_op jit(solution)/shard_map/ppermute | solution.py:32
  105.5 12.5 %collective-permute-start.5 = (bf16[4,256,256]{2,1,0:T(8,128)(2,1)S(1)}, bf16[4,256,256]{2,1,0:T(8,128)(2,1)}, u32[]{:S(2)}, u32[]{:S(2)}) collective-permute-start(bf16[4,256,256]{2,1,0:T(8,128)(2,1)S(1)} %bitcast.38), channel_id=1, source_target_pairs={{0,1},{1,0},{2,3},{3,2},{4,5},{5,4},{6,7},{7,6},{8,9},{9,8},{10,11... | collective-permute-start | bytes 1572872 | tf_op jit(solution)/shard_map/ppermute | solution.py:32
  120.4 23.3 %copy-start.1 = (s32[2]{0:T(128)S(1)}, s32[2]{0:T(128)}, u32[]{:S(2)}) copy-start(s32[2]{0:T(128)} %param.13) | copy-start | bytes 28
  127.2 1.2 collective-permute-start.6
  128.5 3.6 %collective-permute-start.7 = (f32[2,128]{1,0:T(2,128)S(1)}, f32[2,128]{1,0:T(2,128)S(1)}, u32[]{:S(2)}, u32[]{:S(2)}) collective-permute-start(f32[2,128]{1,0:T(2,128)S(1)} %fusion.10), channel_id=1, source_target_pairs={{0,2},{1,3},{2,0},{3,1},{4,6},{5,7},{6,4},{7,5},{8,10},{9,11},{10,... | collective-permute-start | bytes 3080 | tf_op jit(solution)/shard_map/ppermute | solution.py:14
  132.0 3.6 %collective-permute-start.8 = (f32[2,128]{1,0:T(2,128)S(1)}, f32[2,128]{1,0:T(2,128)S(1)}, u32[]{:S(2)}, u32[]{:S(2)}) collective-permute-start(f32[2,128]{1,0:T(2,128)S(1)} %add.62), channel_id=1, source_target_pairs={{0,4},{1,5},{2,6},{3,7},{4,0},{5,1},{6,2},{7,3},{8,12},{9,13},{10,... | collective-permute-start | bytes 3080 | tf_op jit(solution)/shard_map/ppermute | solution.py:14
  135.6 4.5 %collective-permute-start.9 = (f32[2,128]{1,0:T(2,128)S(1)}, f32[2,128]{1,0:T(2,128)S(1)}, u32[]{:S(2)}, u32[]{:S(2)}) collective-permute-start(f32[2,128]{1,0:T(2,128)S(1)} %add.63), channel_id=1, source_target_pairs={{0,8},{1,9},{2,10},{3,11},{4,12},{5,13},{6,14},{7,15},{8,0},{9,1},... | collective-permute-start | bytes 3080 | tf_op jit(solution)/shard_map/ppermute | solution.py:14
  140.1 3.6 %collective-permute-start.10 = (f32[2,128]{1,0:T(2,128)S(1)}, f32[2,128]{1,0:T(2,128)S(1)}, u32[]{:S(2)}, u32[]{:S(2)}) collective-permute-start(f32[2,128]{1,0:T(2,128)S(1)} %add.64), channel_id=1, source_target_pairs={{0,16},{16,0},{1,17},{17,1},{2,18},{18,2},{3,19},{19,3},{4,20},{20... | collective-permute-start | bytes 3080 | tf_op jit(solution)/shard_map/ppermute | solution.py:14
Sparse Core Ops, SparseCore 0:
  10.3 56.0 all-gather.1

commit v4 on v2

--- a/solution.py
+++ b/solution.py
@@ -6,14 +6,62 @@
 SEQ = 128
 
 
-def butterfly_sum(x, axis, size):
+def bit_groups(bits):
+    return [bits[i:i + 2] for i in range(0, len(bits), 2)]
+
+
+def xor_round(held, axis, size, group):
+    parts = [held]
+    for count in range(1, 1 << len(group)):
+        c = sum(bit for k, bit in enumerate(group) if count >> k & 1)
+        parts.append(lax.ppermute(held, axis, [(i, i ^ c) for i in range(size)]))
+    return jnp.stack(parts)
+
+
+def counter_of(c, group):
+    out = jnp.zeros_like(c)
+    for k, bit in enumerate(group):
+        out = out + (((c >> (bit.bit_length() - 1)) & 1) << k)
+    return out
+
+
+def xor_sum(x, axis, size):
     if size & (size - 1):
         return lax.psum(x, axis)
-    bit = 1
-    while bit < size:
-        x = x + lax.ppermute(x, axis, [(i, i ^ bit) for i in range(size)])
-        bit *= 2
+    index = lax.axis_index(axis)
+    bits = [1 << k for k in range(size.bit_length() - 1)][::-1]
+    for group in bit_groups(bits):
+        mask = sum(group)
+        stacked = xor_round(x, axis, size, group)
+        order = [counter_of((v ^ (index & mask)), group) for v in range(mask + 1) if v & ~mask == 0]
+        terms = [stacked[k] for k in order]
+        while len(terms) > 1:
+            terms = [terms[i] + terms[i + 1] for i in range(0, len(terms), 2)]
+        x = terms[0]
     return x
+
+
+def half_gather(block, owners, readers):
+    reader_index = lax.axis_index("reader")
+    owner_index = lax.axis_index("owner")
+    group_size = readers // owners
+    bits = [1 << k for k in range(readers.bit_length() - 1)][::-1]
+    target = owner_index * group_size
+    held = block[None]
+    for group in bit_groups(bits):
+        high = sum(bit for bit in group if bit >= group_size)
+        low = [bit for bit in group if bit < group_size]
+        stacked = xor_round(held, "reader", readers, group)
+        c_high = (reader_index ^ target) & high
+        picks = []
+        values = sorted(sum(bit for k, bit in enumerate(low) if count >> k & 1) for count in range(1 << len(low)))
+        for v in values:
+            c = c_high + (v ^ (reader_index & sum(low)))
+            picks.append(counter_of(c, group))
+        chosen = jnp.take(stacked, jnp.stack(picks), axis=0)
+        chosen = jnp.swapaxes(chosen, 0, 1)
+        held = chosen.reshape((-1,) + block.shape)
+    return jnp.transpose(held, (1, 0, 2)).reshape(block.shape[0], -1)
 
 
 def local(acts, grads, basis_a, basis_g, eigvals, lengths, shuffle):
@@ -37,12 +85,11 @@
     live = ((token % SEQ) < lengths[token // SEQ]).astype(jnp.float32)
 
     part_a = jnp.einsum("tk,jk->tj", all_a, basis_a, preferred_element_type=jnp.float32)
-    rot_a_block = (butterfly_sum(part_a, "owner", owners) * live[:, None]).astype(jnp.bfloat16)
+    rot_a_block = (xor_sum(part_a, "owner", owners) * live[:, None]).astype(jnp.bfloat16)
     part_g = jnp.einsum("tk,jk->tj", all_g, basis_g, preferred_element_type=jnp.float32)
-    rot_g = (butterfly_sum(part_g, "owner", owners) * live[:, None]).astype(jnp.bfloat16)
+    rot_g = (xor_sum(part_g, "owner", owners) * live[:, None]).astype(jnp.bfloat16)
 
-    rot_a_all = lax.all_gather(rot_a_block, "reader", axis=1, tiled=True)
-    rot_a = lax.dynamic_slice_in_dim(rot_a_all, owner_index * width, width, axis=1)
+    rot_a = half_gather(rot_a_block, owners, readers)
 
     denom = eigvals.astype(jnp.float32)
     g_rows = rot_g.reshape(slots, SEQ, m_block)
@@ -51,7 +98,7 @@
     scaled = (outer / denom[None]).astype(jnp.bfloat16)
     projected = jnp.einsum("stm,smn->stn", g_rows, scaled, preferred_element_type=jnp.float32)
     partial = jnp.sum(projected * a_rows.astype(jnp.float32), axis=2) / (dim_ff * dim_d)
-    scores = butterfly_sum(butterfly_sum(partial, "reader", readers), "owner", owners)
+    scores = xor_sum(xor_sum(partial, "reader", readers), "owner", owners)
 
     token_score = lax.dynamic_index_in_dim(scores, owner_index, 0, keepdims=False)
     slot_mean = jnp.sum(scores, axis=1) / SEQ

time: 150 us -> 145 us (0.967)
  waiting for transfers between devices: 95.1 us -> 76.9 us
  starting transfers between devices: 8.25 us -> 17.9 us
  other arithmetic: 10.7 us -> 12.6 us
    ppermute x7 -> x15, starting transfers between devices: 8.17 us -> 17.8 us  [xor_round(): parts.append(lax.ppermute(held, axis, [(i, i ^ c) for i in range(size)]))]
    ppermute x7 -> x15, waiting for transfers between devices: 31.3 us -> 22.4 us  [xor_round(): parts.append(lax.ppermute(held, axis, [(i, i ^ c) for i in range(size)]))]
    all_gather x1 -> x0, waiting for transfers between devices: 7.74 us -> none  [local(): rot_a_all = lax.all_gather(rot_a_block, 'reader', axis=1, tiled=True)]
    add x4 -> x5, other arithmetic: 0.01 us -> 1.71 us  [xor_sum(): terms = [terms[i] + terms[i + 1] for i in range(0, len(terms), 2)]]
  transfers between devices with their start and end apart: 9 -> 16, of which waited for: 9 -> 10; matrix products, arithmetic and copies ran while one was open for 13% -> 16% of each run, Pallas kernels for 0% -> 0%
where the time goes in v4:
time: 145 us
  waiting for transfers between devices  76.9 us (53%)
  matrix products  19 us (13%)
  starting transfers between devices  17.9 us (12%)
  between operations  14.2 us (10%)
  other arithmetic  12.6 us (9%)
  local copies, waits for them, and re-layouts  4.21 us (3%)
    all_gather x1, waiting for transfers between devices, local(): joined = lax.all_gather(joined, 'reader', axis=0, tiled=True)  54.5 us
    ppermute x15, waiting for transfers between devices, xor_round(): parts.append(lax.ppermute(held, axis, [(i, i ^ c) for i in range(size)]))  22.4 us
    ppermute x15, starting transfers between devices, xor_round(): parts.append(lax.ppermute(held, axis, [(i, i ^ c) for i in range(size)]))  17.8 us
    dot_general x1, matrix products, local(): jnp.einsum('tk,jk->tj', all_g, basis_g, preferred_element_type=jnp.float32)  10.7 us
    dot_general x1, matrix products, local(): jnp.einsum('stm,smn->stn', g_rows, scaled, preferred_element_type=jnp.flo...  6.61 us
    convert_element_type x1, other arithmetic, local(): denom = eigvals.astype(jnp.float32)  5.91 us
  transfers between devices with their start and end apart: 16, of which 10 were waited for; matrix products, arithmetic and copies ran while one was open for 16% of the time, Pallas kernels for 0%

profile of v4, /device:TPU:0, one launch (start us, length us, event | category | flops | bytes accessed | tf_op | source)
XLA Modules:
  0.0 144.8 jit_solution(15306244635436533846)
XLA Ops:
  7.2 1.8 %pad_maximum_fusion.1 = bf16[16,9216]{1,0:T(8,128)(2,1)} fusion(bf16[16,2048]{1,0:T(8,128)(2,1)} %param.7, bf16[16,7168]{1,0:T(8,128)(2,1)} %param.8), kind=kLoop, calls=%fused_computation.27 | loop fusion | flops 589824 | bytes 589824 | tf_op jit(solution)/shard_map/concatenate | solution.py:79
  9.2 1.3 fusion.35
  10.5 1.3 compare_select_fusion.1
  11.9 54.5 %all-gather.2.cloned.1.call-done = bf16[256,9216]{1,0:T(8,128)(2,1)} async-done(((bf16[16,9216]{1,0:T(8,128)(2,1)}), bf16[256,9216]{1,0:T(8,128)(2,1)}) %all-gather.2.cloned.1.call-update) | async-done | bytes 4718608 | tf_op jit(solution)/shard_map/all_gather | solution.py:80
  66.4 1.7 %fusion.7 = f32[256,256]{1,0:T(8,128)S(1)} fusion(bf16[256,2048]{1,0:T(8,128)(2,1)S(1)} %copy-done, bf16[256,9216]{1,0:T(8,128)(2,1)} %all-gather.2.cloned.1.call-done), kind=kOutput, calls=%fused_computation.13 | convolution fusion | flops 268435456 | bytes 2359296 | tf_op jit(solution)/shard_map/tk,jk->tj/dot_general | solution.py:87
  68.1 1.5 %collective-permute-start.1 = (f32[256,256]{1,0:T(8,128)S(1)}, f32[256,256]{1,0:T(8,128)S(1)}, u32[]{:S(2)}, u32[]{:S(2)}) collective-permute-start(f32[256,256]{1,0:T(8,128)S(1)} %fusion.7), channel_id=1, source_target_pairs={{0,16},{16,0},{1,17},{17,1},{2,18},{18,2},{3,19},{19,3},{4,20},{20... | collective-permute-start | bytes 786440 | tf_op jit(solution)/shard_map/ppermute | solution.py:17
  69.7 6.9 %collective-permute-done.1 = f32[256,256]{1,0:T(8,128)S(1)} collective-permute-done((f32[256,256]{1,0:T(8,128)S(1)}, f32[256,256]{1,0:T(8,128)S(1)}, u32[]{:S(2)}, u32[]{:S(2)}) %collective-permute-start.1) | collective-permute-done | bytes 262176 | tf_op jit(solution)/shard_map/ppermute | solution.py:17
  76.9 1.9 %collective-permute-start.2 = (bf16[1,256,256]{2,1,0:T(8,128)(2,1)S(1)}, bf16[1,256,256]{2,1,0:T(8,128)(2,1)S(1)}, u32[]{:S(2)}, u32[]{:S(2)}) collective-permute-start(bf16[1,256,256]{2,1,0:T(8,128)(2,1)S(1)} %multiply_convert_fusion.3), channel_id=1, source_target_pairs={{0,8},{1,9},{2,10},{3,11},{4,12},{5,13},{6,14},{7,15},{8,0},{9,1},... | collective-permute-start | bytes 393224 | tf_op jit(solution)/shard_map/ppermute | solution.py:17
  79.4 1.9 %collective-permute-start.4 = (bf16[1,256,256]{2,1,0:T(8,128)(2,1)S(1)}, bf16[1,256,256]{2,1,0:T(8,128)(2,1)S(1)}, u32[]{:S(2)}, u32[]{:S(2)}) collective-permute-start(bf16[1,256,256]{2,1,0:T(8,128)(2,1)S(1)} %multiply_convert_fusion.3), channel_id=1, source_target_pairs={{0,12},{1,13},{2,14},{3,15},{4,8},{5,9},{6,10},{7,11},{8,4},{9,5},... | collective-permute-start | bytes 393224 | tf_op jit(solution)/shard_map/ppermute | solution.py:17
  81.3 10.7 %fusion.3 = f32[256,896]{1,0:T(8,128)} fusion(bf16[896,7168]{1,0:T(8,128)(2,1)} %param.10, bf16[256,9216]{1,0:T(8,128)(2,1)} %all-gather.2.cloned.1.call-done), kind=kOutput, calls=%fused_computation.5 | convolution fusion | flops 3288334336 | bytes 17432576 | tf_op jit(solution)/shard_map/tk,jk->tj/dot_general | solution.py:89
  92.0 1.5 %collective-permute-start = (f32[256,896]{1,0:T(8,128)}, f32[256,896]{1,0:T(8,128)}, u32[]{:S(2)}, u32[]{:S(2)}) collective-permute-start(f32[256,896]{1,0:T(8,128)} %fusion.3), channel_id=1, source_target_pairs={{0,16},{16,0},{1,17},{17,1},{2,18},{18,2},{3,19},{19,3},{4,20},{20... | collective-permute-start | bytes 2752520 | tf_op jit(solution)/shard_map/ppermute | solution.py:17
  94.9 1.6 %collective-permute-start.7 = (bf16[2,256,256]{2,1,0:T(8,128)(2,1)S(1)}, bf16[2,256,256]{2,1,0:T(8,128)(2,1)S(1)}, u32[]{:S(2)}, u32[]{:S(2)}) collective-permute-start(bf16[2,256,256]{2,1,0:T(8,128)(2,1)S(1)} %broadcast_select_fusion), channel_id=1, source_target_pairs={{0,3},{1,2},{2,1},{3,0},{4,7},{5,6},{6,5},{7,4},{8,11},{9,10},{10,... | collective-permute-start | bytes 786440 | tf_op jit(solution)/shard_map/ppermute | solution.py:17
  96.6 5.9 %convert_element_type.42 = f32[896,2048]{1,0:T(8,128)} convert(bf16[896,2048]{1,0:T(8,128)(2,1)} %param.11) | non-fusion elementwise | flops 1835008 | bytes 11010048 | tf_op jit(solution)/shard_map/convert_element_type | solution.py:94
  106.7 6.5 %collective-permute-done = f32[256,896]{1,0:T(8,128)} collective-permute-done((f32[256,896]{1,0:T(8,128)}, f32[256,896]{1,0:T(8,128)}, u32[]{:S(2)}, u32[]{:S(2)}) %collective-permute-start) | collective-permute-done | bytes 917536 | tf_op jit(solution)/shard_map/ppermute | solution.py:17
  113.2 1.7 %fusion.10 = f32[1,256,896]{2,1,0:T(8,128)S(1)} fusion(s32[]{:T(128)S(6)} %select_n.131, f32[1,256,896]{2,1,0:T(8,128)} %bitcast, s32[]{:T(128)S(6)} %select_n.130, f32[1,256,896]{2,1,0:T(8,128)} %bitcast.1), kind=kLoop, calls=%fused_computation.18 | loop fusion | flops 688128 | bytes 2752520 | tf_op jit(solution)/shard_map/add | solution.py:39
  114.9 6.6 %fusion.6 = f32[2,128]{1,0:T(2,128)S(1)} fusion(bf16[2,128,2048]{2,1,0:T(8,128)(2,1)S(1)} %reshape_reshape.3, f32[896,2048]{1,0:T(8,128)} %convert_element_type.42, f32[2,128,896]{2,1,0:T(8,128)S(1)} %bitcast.63, f32[2,128]{1,0:T(2,128)S(1)} %compare_convert_fusion.1), kind=kOutput, calls=%fused_computation.12 | convolution fusion | flops 1888878336 | bytes 9308160 | tf_op jit(solution)/shard_map/stm,smn->stn/dot_general | solution.py:99
  121.5 1.0 collective-permute-start.8
  122.5 1.5 %collective-permute-start.9 = (f32[2,128]{1,0:T(2,128)S(1)}, f32[2,128]{1,0:T(2,128)S(1)}, u32[]{:S(2)}, u32[]{:S(2)}) collective-permute-start(f32[2,128]{1,0:T(2,128)S(1)} %get-tuple-element.7), channel_id=1, source_target_pairs={{0,4},{1,5},{2,6},{3,7},{4,0},{5,1},{6,2},{7,3},{8,12},{9,13},{10,... | collective-permute-start | bytes 3080 | tf_op jit(solution)/shard_map/ppermute | solution.py:17
  124.0 1.9 %collective-permute-start.10 = (f32[2,128]{1,0:T(2,128)S(1)}, f32[2,128]{1,0:T(2,128)S(1)}, u32[]{:S(2)}, u32[]{:S(2)}) collective-permute-start(f32[2,128]{1,0:T(2,128)S(1)} %get-tuple-element.7), channel_id=1, source_target_pairs={{0,12},{1,13},{2,14},{3,15},{4,8},{5,9},{6,10},{7,11},{8,4},{9,5},... | collective-permute-start | bytes 3080 | tf_op jit(solution)/shard_map/ppermute | solution.py:17
  126.1 3.3 %collective-permute-done.10 = f32[2,128]{1,0:T(2,128)S(1)} collective-permute-done((f32[2,128]{1,0:T(2,128)S(1)}, f32[2,128]{1,0:T(2,128)S(1)}, u32[]{:S(2)}, u32[]{:S(2)}) %collective-permute-start.10) | collective-permute-done | bytes 1056 | tf_op jit(solution)/shard_map/ppermute | solution.py:17
  130.0 1.6 %collective-permute-start.13 = (f32[2,128]{1,0:T(2,128)S(1)}, f32[2,128]{1,0:T(2,128)S(1)}, u32[]{:S(2)}, u32[]{:S(2)}) collective-permute-start(f32[2,128]{1,0:T(2,128)S(1)} %fusion.40), channel_id=1, source_target_pairs={{0,3},{1,2},{2,1},{3,0},{4,7},{5,6},{6,5},{7,4},{8,11},{9,10},{10,... | collective-permute-start | bytes 3080 | tf_op jit(solution)/shard_map/ppermute | solution.py:17
  131.6 1.4 collective-permute-done.11
  133.1 1.5 %collective-permute-start.14 = (f32[2,128]{1,0:T(2,128)S(1)}, f32[2,128]{1,0:T(2,128)S(1)}, u32[]{:S(2)}, u32[]{:S(2)}) collective-permute-start(f32[2,128]{1,0:T(2,128)S(1)} %fusion.39), channel_id=1, source_target_pairs={{0,16},{16,0},{1,17},{17,1},{2,18},{18,2},{3,19},{19,3},{4,20},{20... | collective-permute-start | bytes 3080 | tf_op jit(solution)/shard_map/ppermute | solution.py:17
  134.6 2.1 %collective-permute-done.14 = f32[2,128]{1,0:T(2,128)S(1)} collective-permute-done((f32[2,128]{1,0:T(2,128)S(1)}, f32[2,128]{1,0:T(2,128)S(1)}, u32[]{:S(2)}, u32[]{:S(2)}) %collective-permute-start.14) | collective-permute-done | bytes 1056 | tf_op jit(solution)/shard_map/ppermute | solution.py:17
  (52 shorter events, 8.8 us)
Async XLA Ops:
  7.2 59.3 %copy-start = (bf16[256,2048]{1,0:T(8,128)(2,1)S(1)}, bf16[256,2048]{1,0:T(8,128)(2,1)}, u32[]{:S(2)}) copy-start(bf16[256,2048]{1,0:T(8,128)(2,1)} %param.9) | copy-start | bytes 3145732
  7.2 59.2 %all-gather.2.cloned.1.call-start = ((), (), s32[]{:S(2)}) async-start(), calls=%async_computation | async-start | bytes 5013504 | tf_op jit(solution)/shard_map/all_gather | solution.py:80
  68.1 8.5 %collective-permute-start.1 = (f32[256,256]{1,0:T(8,128)S(1)}, f32[256,256]{1,0:T(8,128)S(1)}, u32[]{:S(2)}, u32[]{:S(2)}) collective-permute-start(f32[256,256]{1,0:T(8,128)S(1)} %fusion.7), channel_id=1, source_target_pairs={{0,16},{16,0},{1,17},{17,1},{2,18},{18,2},{3,19},{19,3},{4,20},{20... | collective-permute-start | bytes 786440 | tf_op jit(solution)/shard_map/ppermute | solution.py:17
  76.9 16.6 %collective-permute-start.2 = (bf16[1,256,256]{2,1,0:T(8,128)(2,1)S(1)}, bf16[1,256,256]{2,1,0:T(8,128)(2,1)S(1)}, u32[]{:S(2)}, u32[]{:S(2)}) collective-permute-start(bf16[1,256,256]{2,1,0:T(8,128)(2,1)S(1)} %multiply_convert_fusion.3), channel_id=1, source_target_pairs={{0,8},{1,9},{2,10},{3,11},{4,12},{5,13},{6,14},{7,15},{8,0},{9,1},... | collective-permute-start | bytes 393224 | tf_op jit(solution)/shard_map/ppermute | solution.py:17
  78.8 14.7 %collective-permute-start.3 = (bf16[1,256,256]{2,1,0:T(8,128)(2,1)S(1)}, bf16[1,256,256]{2,1,0:T(8,128)(2,1)S(1)}, u32[]{:S(2)}, u32[]{:S(2)}) collective-permute-start(bf16[1,256,256]{2,1,0:T(8,128)(2,1)S(1)} %multiply_convert_fusion.3), channel_id=1, source_target_pairs={{0,4},{1,5},{2,6},{3,7},{4,0},{5,1},{6,2},{7,3},{8,12},{9,13},{10,... | collective-permute-start | bytes 393224 | tf_op jit(solution)/shard_map/ppermute | solution.py:17
  79.4 14.1 %collective-permute-start.4 = (bf16[1,256,256]{2,1,0:T(8,128)(2,1)S(1)}, bf16[1,256,256]{2,1,0:T(8,128)(2,1)S(1)}, u32[]{:S(2)}, u32[]{:S(2)}) collective-permute-start(bf16[1,256,256]{2,1,0:T(8,128)(2,1)S(1)} %multiply_convert_fusion.3), channel_id=1, source_target_pairs={{0,12},{1,13},{2,14},{3,15},{4,8},{5,9},{6,10},{7,11},{8,4},{9,5},... | collective-permute-start | bytes 393224 | tf_op jit(solution)/shard_map/ppermute | solution.py:17
  92.0 21.2 %collective-permute-start = (f32[256,896]{1,0:T(8,128)}, f32[256,896]{1,0:T(8,128)}, u32[]{:S(2)}, u32[]{:S(2)}) collective-permute-start(f32[256,896]{1,0:T(8,128)} %fusion.3), channel_id=1, source_target_pairs={{0,16},{16,0},{1,17},{17,1},{2,18},{18,2},{3,19},{19,3},{4,20},{20... | collective-permute-start | bytes 2752520 | tf_op jit(solution)/shard_map/ppermute | solution.py:17
  94.3 9.3 %collective-permute-start.5 = (bf16[2,256,256]{2,1,0:T(8,128)(2,1)S(1)}, bf16[2,256,256]{2,1,0:T(8,128)(2,1)S(1)}, u32[]{:S(2)}, u32[]{:S(2)}) collective-permute-start(bf16[2,256,256]{2,1,0:T(8,128)(2,1)S(1)} %broadcast_select_fusion), channel_id=1, source_target_pairs={{0,2},{1,3},{2,0},{3,1},{4,6},{5,7},{6,4},{7,5},{8,10},{9,11},{10,... | collective-permute-start | bytes 786440 | tf_op jit(solution)/shard_map/ppermute | solution.py:17
  94.9 8.7 %collective-permute-start.6 = (bf16[2,256,256]{2,1,0:T(8,128)(2,1)S(1)}, bf16[2,256,256]{2,1,0:T(8,128)(2,1)S(1)}, u32[]{:S(2)}, u32[]{:S(2)}) collective-permute-start(bf16[2,256,256]{2,1,0:T(8,128)(2,1)S(1)} %broadcast_select_fusion), channel_id=1, source_target_pairs={{0,1},{1,0},{2,3},{3,2},{4,5},{5,4},{6,7},{7,6},{8,9},{9,8},{10,11... | collective-permute-start | bytes 786440 | tf_op jit(solution)/shard_map/ppermute | solution.py:17
  94.9 9.7 %collective-permute-start.7 = (bf16[2,256,256]{2,1,0:T(8,128)(2,1)S(1)}, bf16[2,256,256]{2,1,0:T(8,128)(2,1)S(1)}, u32[]{:S(2)}, u32[]{:S(2)}) collective-permute-start(bf16[2,256,256]{2,1,0:T(8,128)(2,1)S(1)} %broadcast_select_fusion), channel_id=1, source_target_pairs={{0,3},{1,2},{2,1},{3,0},{4,7},{5,6},{6,5},{7,4},{8,11},{9,10},{10,... | collective-permute-start | bytes 786440 | tf_op jit(solution)/shard_map/ppermute | solution.py:17
  114.9 22.5 %copy-start.1 = (s32[2]{0:T(128)S(1)}, s32[2]{0:T(128)}, u32[]{:S(2)}) copy-start(s32[2]{0:T(128)} %param.13) | copy-start | bytes 28
  121.5 4.5 %collective-permute-start.8 = (f32[2,128]{1,0:T(2,128)S(1)}, f32[2,128]{1,0:T(2,128)S(1)}, u32[]{:S(2)}, u32[]{:S(2)}) collective-permute-start(f32[2,128]{1,0:T(2,128)S(1)} %get-tuple-element.7), channel_id=1, source_target_pairs={{0,8},{1,9},{2,10},{3,11},{4,12},{5,13},{6,14},{7,15},{8,0},{9,1},... | collective-permute-start | bytes 3080 | tf_op jit(solution)/shard_map/ppermute | solution.py:17
  122.5 3.6 %collective-permute-start.9 = (f32[2,128]{1,0:T(2,128)S(1)}, f32[2,128]{1,0:T(2,128)S(1)}, u32[]{:S(2)}, u32[]{:S(2)}) collective-permute-start(f32[2,128]{1,0:T(2,128)S(1)} %get-tuple-element.7), channel_id=1, source_target_pairs={{0,4},{1,5},{2,6},{3,7},{4,0},{5,1},{6,2},{7,3},{8,12},{9,13},{10,... | collective-permute-start | bytes 3080 | tf_op jit(solution)/shard_map/ppermute | solution.py:17
  124.0 5.4 %collective-permute-start.10 = (f32[2,128]{1,0:T(2,128)S(1)}, f32[2,128]{1,0:T(2,128)S(1)}, u32[]{:S(2)}, u32[]{:S(2)}) collective-permute-start(f32[2,128]{1,0:T(2,128)S(1)} %get-tuple-element.7), channel_id=1, source_target_pairs={{0,12},{1,13},{2,14},{3,15},{4,8},{5,9},{6,10},{7,11},{8,4},{9,5},... | collective-permute-start | bytes 3080 | tf_op jit(solution)/shard_map/ppermute | solution.py:17
  129.4 3.6 %collective-permute-start.11 = (f32[2,128]{1,0:T(2,128)S(1)}, f32[2,128]{1,0:T(2,128)S(1)}, u32[]{:S(2)}, u32[]{:S(2)}) collective-permute-start(f32[2,128]{1,0:T(2,128)S(1)} %fusion.40), channel_id=1, source_target_pairs={{0,2},{1,3},{2,0},{3,1},{4,6},{5,7},{6,4},{7,5},{8,10},{9,11},{10,... | collective-permute-start | bytes 3080 | tf_op jit(solution)/shard_map/ppermute | solution.py:17
  130.0 3.0 %collective-permute-start.12 = (f32[2,128]{1,0:T(2,128)S(1)}, f32[2,128]{1,0:T(2,128)S(1)}, u32[]{:S(2)}, u32[]{:S(2)}) collective-permute-start(f32[2,128]{1,0:T(2,128)S(1)} %fusion.40), channel_id=1, source_target_pairs={{0,1},{1,0},{2,3},{3,2},{4,5},{5,4},{6,7},{7,6},{8,9},{9,8},{10,11... | collective-permute-start | bytes 3080 | tf_op jit(solution)/shard_map/ppermute | solution.py:17
  130.0 3.0 %collective-permute-start.13 = (f32[2,128]{1,0:T(2,128)S(1)}, f32[2,128]{1,0:T(2,128)S(1)}, u32[]{:S(2)}, u32[]{:S(2)}) collective-permute-start(f32[2,128]{1,0:T(2,128)S(1)} %fusion.40), channel_id=1, source_target_pairs={{0,3},{1,2},{2,1},{3,0},{4,7},{5,6},{6,5},{7,4},{8,11},{9,10},{10,... | collective-permute-start | bytes 3080 | tf_op jit(solution)/shard_map/ppermute | solution.py:17
  133.1 3.6 %collective-permute-start.14 = (f32[2,128]{1,0:T(2,128)S(1)}, f32[2,128]{1,0:T(2,128)S(1)}, u32[]{:S(2)}, u32[]{:S(2)}) collective-permute-start(f32[2,128]{1,0:T(2,128)S(1)} %fusion.39), channel_id=1, source_target_pairs={{0,16},{16,0},{1,17},{17,1},{2,18},{18,2},{3,19},{19,3},{4,20},{20... | collective-permute-start | bytes 3080 | tf_op jit(solution)/shard_map/ppermute | solution.py:17
Sparse Core Ops, SparseCore 0:
  10.3 56.0 all-gather.1

commit v5 on v4

--- a/solution.py
+++ b/solution.py
@@ -41,9 +41,9 @@
     return x
 
 
-def half_gather(block, owners, readers):
+def ordered_gather(block, owners, readers):
     reader_index = lax.axis_index("reader")
-    owner_index = lax.axis_index("owner")
+    owner_index = lax.axis_index("owner") if owners > 1 else 0
     group_size = readers // owners
     bits = [1 << k for k in range(readers.bit_length() - 1)][::-1]
     target = owner_index * group_size
@@ -61,6 +61,11 @@
         chosen = jnp.take(stacked, jnp.stack(picks), axis=0)
         chosen = jnp.swapaxes(chosen, 0, 1)
         held = chosen.reshape((-1,) + block.shape)
+    return held
+
+
+def half_gather(block, owners, readers):
+    held = ordered_gather(block, owners, readers)
     return jnp.transpose(held, (1, 0, 2)).reshape(block.shape[0], -1)
 
 
@@ -76,10 +81,8 @@
     dim_ff = m_block * readers
     dim_d = width * owners
 
-    joined = jnp.concatenate([grads, acts], axis=1)
-    joined = lax.all_gather(joined, "reader", axis=0, tiled=True)
-    all_g = joined[:, : grads.shape[1]]
-    all_a = joined[:, grads.shape[1]:]
+    all_g = lax.all_gather(grads, "reader", axis=0, tiled=True)
+    all_a = ordered_gather(acts, 1, readers).reshape(rows, acts.shape[1])
 
     token = jnp.arange(rows, dtype=jnp.int32)
     live = ((token % SEQ) < lengths[token // SEQ]).astype(jnp.float32)

time: 145 us -> 138 us (0.952)
  waiting for transfers between devices: 76.9 us -> 61.4 us
  starting transfers between devices: 17.9 us -> 26 us
  local copies, waits for them, and re-layouts: 4.21 us -> 5.67 us
    all_gather x1, waiting for transfers between devices: 54.5 us -> 0.02 us  [local(): all_g = lax.all_gather(grads, 'reader', axis=0, tiled=True)]
    ppermute x15 -> x21, waiting for transfers between devices: 22.4 us -> 60.7 us  [xor_round(): parts.append(lax.ppermute(held, axis, [(i, i ^ c) for i in range(size)]))]
    ppermute x15 -> x21, starting transfers between devices: 17.8 us -> 26 us  [xor_round(): parts.append(lax.ppermute(held, axis, [(i, i ^ c) for i in range(size)]))]
    concatenate x1 -> x0, other arithmetic: 1.79 us -> none  [local(): joined = jnp.concatenate([grads, acts], axis=1)]
  transfers between devices with their start and end apart: 16 -> 22, of which waited for: 10 -> 17; matrix products, arithmetic and copies ran while one was open for 16% -> 11% of each run, Pallas kernels for 0% -> 0%
where the time goes in v5:
time: 138 us; the launch traced here: 137 us
  waiting for transfers between devices  61.4 us (44%)
  starting transfers between devices  26 us (19%)
  matrix products  17.8 us (13%)
  between operations  14.3 us (10%)
  other arithmetic  12.2 us (9%)
  local copies, waits for them, and re-layouts  5.67 us (4%)
    ppermute x21, waiting for transfers between devices, xor_round(): parts.append(lax.ppermute(held, axis, [(i, i ^ c) for i in range(size)]))  60.7 us
    ppermute x21, starting transfers between devices, xor_round(): parts.append(lax.ppermute(held, axis, [(i, i ^ c) for i in range(size)]))  26 us
    dot_general x1, matrix products, local(): jnp.einsum('tk,jk->tj', all_g, basis_g, preferred_element_type=jnp.float32)  10.7 us
    dot_general x1, matrix products, local(): jnp.einsum('stm,smn->stn', g_rows, scaled, preferred_element_type=jnp.flo...  6.61 us
    convert_element_type x1, other arithmetic, local(): denom = eigvals.astype(jnp.float32)  5.92 us
  transfers between devices with their start and end apart: 22, of which 17 were waited for; matrix products, arithmetic and copies ran while one was open for 11% of the time, Pallas kernels for 0%

profile of v5, /device:TPU:0, one launch (start us, length us, event | category | flops | bytes accessed | tf_op | source)
XLA Modules:
  0.0 137.3 jit_solution(18173389456505906959)
XLA Ops:
  7.9 5.1 %collective-permute-start.3 = (bf16[1,16,2048]{2,1,0:T(8,128)(2,1)}, bf16[1,16,2048]{2,1,0:T(8,128)(2,1)S(1)}, u32[]{:S(2)}, u32[]{:S(2)}) collective-permute-start(bf16[1,16,2048]{2,1,0:T(8,128)(2,1)} %bitcast.103), channel_id=1, source_target_pairs={{0,12},{1,13},{2,14},{3,15},{4,8},{5,9},{6,10},{7,11},{8,4},{9,5},... | collective-permute-start | bytes 196616 | tf_op jit(solution)/shard_map/ppermute | solution.py:17
  20.5 1.6 %collective-permute-start.5 = (bf16[4,16,2048]{2,1,0:T(8,128)(2,1)S(1)}, bf16[4,16,2048]{2,1,0:T(8,128)(2,1)S(1)}, u32[]{:S(2)}, u32[]{:S(2)}) collective-permute-start(bf16[4,16,2048]{2,1,0:T(8,128)(2,1)S(1)} %broadcast_select_fusion.1), channel_id=1, source_target_pairs={{0,1},{1,0},{2,3},{3,2},{4,5},{5,4},{6,7},{7,6},{8,9},{9,8},{10,11... | collective-permute-start | bytes 786440 | tf_op jit(solution)/shard_map/ppermute | solution.py:17
  22.7 8.7 %collective-permute-done.6 = bf16[4,16,2048]{2,1,0:T(8,128)(2,1)S(1)} collective-permute-done((bf16[4,16,2048]{2,1,0:T(8,128)(2,1)S(1)}, bf16[4,16,2048]{2,1,0:T(8,128)(2,1)S(1)}, u32[]{:S(2)}, u32[]{:S(2)}) %collective-permute-start.6) | collective-permute-done | bytes 262176 | tf_op jit(solution)/shard_map/ppermute | solution.py:17
  31.5 5.7 %collective-permute-done.4 = bf16[4,16,2048]{2,1,0:T(8,128)(2,1)S(1)} collective-permute-done((bf16[4,16,2048]{2,1,0:T(8,128)(2,1)S(1)}, bf16[4,16,2048]{2,1,0:T(8,128)(2,1)S(1)}, u32[]{:S(2)}, u32[]{:S(2)}) %collective-permute-start.4) | collective-permute-done | bytes 262176 | tf_op jit(solution)/shard_map/ppermute | solution.py:17
  38.7 1.6 %collective-permute-start.7 = (f32[256,256]{1,0:T(8,128)S(1)}, f32[256,256]{1,0:T(8,128)S(1)}, u32[]{:S(2)}, u32[]{:S(2)}) collective-permute-start(f32[256,256]{1,0:T(8,128)S(1)} %fusion.34), channel_id=1, source_target_pairs={{0,16},{16,0},{1,17},{17,1},{2,18},{18,2},{3,19},{19,3},{4,20},{20... | collective-permute-start | bytes 786440 | tf_op jit(solution)/shard_map/ppermute | solution.py:17
  40.3 6.7 %collective-permute-done.7 = f32[256,256]{1,0:T(8,128)S(1)} collective-permute-done((f32[256,256]{1,0:T(8,128)S(1)}, f32[256,256]{1,0:T(8,128)S(1)}, u32[]{:S(2)}, u32[]{:S(2)}) %collective-permute-start.7) | collective-permute-done | bytes 262176 | tf_op jit(solution)/shard_map/ppermute | solution.py:17
  47.2 2.2 %collective-permute-start.10 = (bf16[1,256,256]{2,1,0:T(8,128)(2,1)S(1)}, bf16[1,256,256]{2,1,0:T(8,128)(2,1)S(1)}, u32[]{:S(2)}, u32[]{:S(2)}) collective-permute-start(bf16[1,256,256]{2,1,0:T(8,128)(2,1)S(1)} %multiply_convert_fusion.3), channel_id=1, source_target_pairs={{0,12},{1,13},{2,14},{3,15},{4,8},{5,9},{6,10},{7,11},{8,4},{9,5},... | collective-permute-start | bytes 393224 | tf_op jit(solution)/shard_map/ppermute | solution.py:17
  49.8 1.9 %collective-permute-start.8 = (bf16[1,256,256]{2,1,0:T(8,128)(2,1)S(1)}, bf16[1,256,256]{2,1,0:T(8,128)(2,1)S(1)}, u32[]{:S(2)}, u32[]{:S(2)}) collective-permute-start(bf16[1,256,256]{2,1,0:T(8,128)(2,1)S(1)} %multiply_convert_fusion.3), channel_id=1, source_target_pairs={{0,8},{1,9},{2,10},{3,11},{4,12},{5,13},{6,14},{7,15},{8,0},{9,1},... | collective-permute-start | bytes 393224 | tf_op jit(solution)/shard_map/ppermute | solution.py:17
  51.8 6.5 %collective-permute-done.10 = bf16[1,256,256]{2,1,0:T(8,128)(2,1)S(1)} collective-permute-done((bf16[1,256,256]{2,1,0:T(8,128)(2,1)S(1)}, bf16[1,256,256]{2,1,0:T(8,128)(2,1)S(1)}, u32[]{:S(2)}, u32[]{:S(2)}) %collective-permute-start.10) | collective-permute-done | bytes 131104 | tf_op jit(solution)/shard_map/ppermute | solution.py:17
  58.2 4.9 %collective-permute-done.9 = bf16[1,256,256]{2,1,0:T(8,128)(2,1)S(1)} collective-permute-done((bf16[1,256,256]{2,1,0:T(8,128)(2,1)S(1)}, bf16[1,256,256]{2,1,0:T(8,128)(2,1)S(1)}, u32[]{:S(2)}, u32[]{:S(2)}) %collective-permute-start.9) | collective-permute-done | bytes 131104 | tf_op jit(solution)/shard_map/ppermute | solution.py:17
  63.1 7.3 %collective-permute-done.8 = bf16[1,256,256]{2,1,0:T(8,128)(2,1)S(1)} collective-permute-done((bf16[1,256,256]{2,1,0:T(8,128)(2,1)S(1)}, bf16[1,256,256]{2,1,0:T(8,128)(2,1)S(1)}, u32[]{:S(2)}, u32[]{:S(2)}) %collective-permute-start.8) | collective-permute-done | bytes 131104 | tf_op jit(solution)/shard_map/ppermute | solution.py:17
  71.0 10.7 %fusion.33 = f32[256,896]{1,0:T(8,128)} fusion(bf16[256,7168]{1,0:T(8,128)(2,1)} %all-gather.2.cloned.1.call-done, bf16[896,7168]{1,0:T(8,128)(2,1)} %param.10), kind=kOutput, calls=%fused_computation.95 | convolution fusion | flops 3288334336 | bytes 17432576 | tf_op jit(solution)/shard_map/tk,jk->tj/dot_general | solution.py:92
  85.5 5.9 %convert_element_type.42 = f32[896,2048]{1,0:T(8,128)} convert(bf16[896,2048]{1,0:T(8,128)(2,1)} %param.11) | non-fusion elementwise | flops 1835008 | bytes 11010048 | tf_op jit(solution)/shard_map/convert_element_type | solution.py:97
  91.8 5.8 %collective-permute-done.11 = bf16[2,256,256]{2,1,0:T(8,128)(2,1)S(1)} collective-permute-done((bf16[2,256,256]{2,1,0:T(8,128)(2,1)S(1)}, bf16[2,256,256]{2,1,0:T(8,128)(2,1)S(1)}, u32[]{:S(2)}, u32[]{:S(2)}) %collective-permute-start.11) | collective-permute-done | bytes 262176 | tf_op jit(solution)/shard_map/ppermute | solution.py:17
  99.9 4.4 %collective-permute-done = f32[256,896]{1,0:T(8,128)} collective-permute-done((f32[256,896]{1,0:T(8,128)}, f32[256,896]{1,0:T(8,128)}, u32[]{:S(2)}, u32[]{:S(2)}) %collective-permute-start) | collective-permute-done | bytes 917536 | tf_op jit(solution)/shard_map/ppermute | solution.py:17
  104.4 1.7 %fusion.6 = f32[1,256,896]{2,1,0:T(8,128)S(1)} fusion(s32[]{:T(128)S(6)} %select_n.172, f32[1,256,896]{2,1,0:T(8,128)} %bitcast, s32[]{:T(128)S(6)} %select_n.171, f32[1,256,896]{2,1,0:T(8,128)} %bitcast.1), kind=kLoop, calls=%fused_computation.18 | loop fusion | flops 688128 | bytes 2752520 | tf_op jit(solution)/shard_map/add | solution.py:39
  106.1 6.6 %fusion.4 = f32[2,128]{1,0:T(2,128)S(1)} fusion(bf16[2,128,2048]{2,1,0:T(8,128)(2,1)S(1)} %reshape_reshape.7, f32[896,2048]{1,0:T(8,128)} %convert_element_type.42, f32[2,128,896]{2,1,0:T(8,128)S(1)} %bitcast.92, f32[2,128]{1,0:T(2,128)S(1)} %compare_convert_fusion.1), kind=kOutput, calls=%fused_computation.12 | convolution fusion | flops 1888878336 | bytes 9308160 | tf_op jit(solution)/shard_map/stm,smn->stn/dot_general | solution.py:102
  112.8 1.5 %collective-permute-start.14 = (f32[2,128]{1,0:T(2,128)S(1)}, f32[2,128]{1,0:T(2,128)S(1)}, u32[]{:S(2)}, u32[]{:S(2)}) collective-permute-start(f32[2,128]{1,0:T(2,128)S(1)} %get-tuple-element.7), channel_id=1, source_target_pairs={{0,8},{1,9},{2,10},{3,11},{4,12},{5,13},{6,14},{7,15},{8,0},{9,1},... | collective-permute-start | bytes 3080 | tf_op jit(solution)/shard_map/ppermute | solution.py:17
  114.3 2.8 %collective-permute-start.16 = (f32[2,128]{1,0:T(2,128)S(1)}, f32[2,128]{1,0:T(2,128)S(1)}, u32[]{:S(2)}, u32[]{:S(2)}) collective-permute-start(f32[2,128]{1,0:T(2,128)S(1)} %get-tuple-element.7), channel_id=1, source_target_pairs={{0,12},{1,13},{2,14},{3,15},{4,8},{5,9},{6,10},{7,11},{8,4},{9,5},... | collective-permute-start | bytes 3080 | tf_op jit(solution)/shard_map/ppermute | solution.py:17
  117.3 2.4 %collective-permute-done.16 = f32[2,128]{1,0:T(2,128)S(1)} collective-permute-done((f32[2,128]{1,0:T(2,128)S(1)}, f32[2,128]{1,0:T(2,128)S(1)}, u32[]{:S(2)}, u32[]{:S(2)}) %collective-permute-start.16) | collective-permute-done | bytes 1056 | tf_op jit(solution)/shard_map/ppermute | solution.py:17
  119.7 2.2 %collective-permute-start.18 = (f32[2,128]{1,0:T(2,128)S(1)}, f32[2,128]{1,0:T(2,128)S(1)}, u32[]{:S(2)}, u32[]{:S(2)}) collective-permute-start(f32[2,128]{1,0:T(2,128)S(1)} %fusion.41), channel_id=1, source_target_pairs={{0,1},{1,0},{2,3},{3,2},{4,5},{5,4},{6,7},{7,6},{8,9},{9,8},{10,11... | collective-permute-start | bytes 3080 | tf_op jit(solution)/shard_map/ppermute | solution.py:17
  122.8 2.7 %collective-permute-done.17 = f32[2,128]{1,0:T(2,128)S(1)} collective-permute-done((f32[2,128]{1,0:T(2,128)S(1)}, f32[2,128]{1,0:T(2,128)S(1)}, u32[]{:S(2)}, u32[]{:S(2)}) %collective-permute-start.17) | collective-permute-done | bytes 1056 | tf_op jit(solution)/shard_map/ppermute | solution.py:17
  125.6 1.5 %collective-permute-start.20 = (f32[2,128]{1,0:T(2,128)S(1)}, f32[2,128]{1,0:T(2,128)S(1)}, u32[]{:S(2)}, u32[]{:S(2)}) collective-permute-start(f32[2,128]{1,0:T(2,128)S(1)} %fusion.40), channel_id=1, source_target_pairs={{0,16},{16,0},{1,17},{17,1},{2,18},{18,2},{3,19},{19,3},{4,20},{20... | collective-permute-start | bytes 3080 | tf_op jit(solution)/shard_map/ppermute | solution.py:17
  127.1 2.1 %collective-permute-done.20 = f32[2,128]{1,0:T(2,128)S(1)} collective-permute-done((f32[2,128]{1,0:T(2,128)S(1)}, f32[2,128]{1,0:T(2,128)S(1)}, u32[]{:S(2)}, u32[]{:S(2)}) %collective-permute-start.20) | collective-permute-done | bytes 1056 | tf_op jit(solution)/shard_map/ppermute | solution.py:17
  (73 shorter events, 20.4 us)
Async XLA Ops:
  7.2 31.0 %copy-start = (bf16[256,2048]{1,0:T(8,128)(2,1)S(1)}, bf16[256,2048]{1,0:T(8,128)(2,1)}, u32[]{:S(2)}) copy-start(bf16[256,2048]{1,0:T(8,128)(2,1)} %param.9) | copy-start | bytes 3145732
  7.2 63.9 %all-gather.2.cloned.1.call-start = ((), (), s32[]{:S(2)}) async-start(), calls=%async_computation | async-start | bytes 3899392 | tf_op jit(solution)/shard_map/all_gather | solution.py:84
  7.9 8.6 %collective-permute-start.3 = (bf16[1,16,2048]{2,1,0:T(8,128)(2,1)}, bf16[1,16,2048]{2,1,0:T(8,128)(2,1)S(1)}, u32[]{:S(2)}, u32[]{:S(2)}) collective-permute-start(bf16[1,16,2048]{2,1,0:T(8,128)(2,1)} %bitcast.103), channel_id=1, source_target_pairs={{0,12},{1,13},{2,14},{3,15},{4,8},{5,9},{6,10},{7,11},{8,4},{9,5},... | collective-permute-start | bytes 196616 | tf_op jit(solution)/shard_map/ppermute | solution.py:17
  13.0 4.9 %collective-permute-start.2 = (bf16[1,16,2048]{2,1,0:T(8,128)(2,1)}, bf16[1,16,2048]{2,1,0:T(8,128)(2,1)S(1)}, u32[]{:S(2)}, u32[]{:S(2)}) collective-permute-start(bf16[1,16,2048]{2,1,0:T(8,128)(2,1)} %bitcast.104), channel_id=1, source_target_pairs={{0,4},{1,5},{2,6},{3,7},{4,0},{5,1},{6,2},{7,3},{8,12},{9,13},{10,... | collective-permute-start | bytes 196616 | tf_op jit(solution)/shard_map/ppermute | solution.py:17
  13.0 5.8 %collective-permute-start.1 = (bf16[1,16,2048]{2,1,0:T(8,128)(2,1)}, bf16[1,16,2048]{2,1,0:T(8,128)(2,1)S(1)}, u32[]{:S(2)}, u32[]{:S(2)}) collective-permute-start(bf16[1,16,2048]{2,1,0:T(8,128)(2,1)} %bitcast.105), channel_id=1, source_target_pairs={{0,8},{1,9},{2,10},{3,11},{4,12},{5,13},{6,14},{7,15},{8,0},{9,1},... | collective-permute-start | bytes 196616 | tf_op jit(solution)/shard_map/ppermute | solution.py:17
  20.4 11.1 %collective-permute-start.6 = (bf16[4,16,2048]{2,1,0:T(8,128)(2,1)S(1)}, bf16[4,16,2048]{2,1,0:T(8,128)(2,1)S(1)}, u32[]{:S(2)}, u32[]{:S(2)}) collective-permute-start(bf16[4,16,2048]{2,1,0:T(8,128)(2,1)S(1)} %broadcast_select_fusion.1), channel_id=1, source_target_pairs={{0,3},{1,2},{2,1},{3,0},{4,7},{5,6},{6,5},{7,4},{8,11},{9,10},{10,... | collective-permute-start | bytes 786440 | tf_op jit(solution)/shard_map/ppermute | solution.py:17
  20.5 11.0 %collective-permute-start.5 = (bf16[4,16,2048]{2,1,0:T(8,128)(2,1)S(1)}, bf16[4,16,2048]{2,1,0:T(8,128)(2,1)S(1)}, u32[]{:S(2)}, u32[]{:S(2)}) collective-permute-start(bf16[4,16,2048]{2,1,0:T(8,128)(2,1)S(1)} %broadcast_select_fusion.1), channel_id=1, source_target_pairs={{0,1},{1,0},{2,3},{3,2},{4,5},{5,4},{6,7},{7,6},{8,9},{9,8},{10,11... | collective-permute-start | bytes 786440 | tf_op jit(solution)/shard_map/ppermute | solution.py:17
  22.1 15.0 %collective-permute-start.4 = (bf16[4,16,2048]{2,1,0:T(8,128)(2,1)S(1)}, bf16[4,16,2048]{2,1,0:T(8,128)(2,1)S(1)}, u32[]{:S(2)}, u32[]{:S(2)}) collective-permute-start(bf16[4,16,2048]{2,1,0:T(8,128)(2,1)S(1)} %broadcast_select_fusion.1), channel_id=1, source_target_pairs={{0,2},{1,3},{2,0},{3,1},{4,6},{5,7},{6,4},{7,5},{8,10},{9,11},{10,... | collective-permute-start | bytes 786440 | tf_op jit(solution)/shard_map/ppermute | solution.py:17
  38.7 8.3 %collective-permute-start.7 = (f32[256,256]{1,0:T(8,128)S(1)}, f32[256,256]{1,0:T(8,128)S(1)}, u32[]{:S(2)}, u32[]{:S(2)}) collective-permute-start(f32[256,256]{1,0:T(8,128)S(1)} %fusion.34), channel_id=1, source_target_pairs={{0,16},{16,0},{1,17},{17,1},{2,18},{18,2},{3,19},{19,3},{4,20},{20... | collective-permute-start | bytes 786440 | tf_op jit(solution)/shard_map/ppermute | solution.py:17
  47.2 11.0 %collective-permute-start.10 = (bf16[1,256,256]{2,1,0:T(8,128)(2,1)S(1)}, bf16[1,256,256]{2,1,0:T(8,128)(2,1)S(1)}, u32[]{:S(2)}, u32[]{:S(2)}) collective-permute-start(bf16[1,256,256]{2,1,0:T(8,128)(2,1)S(1)} %multiply_convert_fusion.3), channel_id=1, source_target_pairs={{0,12},{1,13},{2,14},{3,15},{4,8},{5,9},{6,10},{7,11},{8,4},{9,5},... | collective-permute-start | bytes 393224 | tf_op jit(solution)/shard_map/ppermute | solution.py:17
  49.5 13.7 %collective-permute-start.9 = (bf16[1,256,256]{2,1,0:T(8,128)(2,1)S(1)}, bf16[1,256,256]{2,1,0:T(8,128)(2,1)S(1)}, u32[]{:S(2)}, u32[]{:S(2)}) collective-permute-start(bf16[1,256,256]{2,1,0:T(8,128)(2,1)S(1)} %multiply_convert_fusion.3), channel_id=1, source_target_pairs={{0,4},{1,5},{2,6},{3,7},{4,0},{5,1},{6,2},{7,3},{8,12},{9,13},{10,... | collective-permute-start | bytes 393224 | tf_op jit(solution)/shard_map/ppermute | solution.py:17
  49.8 20.6 %collective-permute-start.8 = (bf16[1,256,256]{2,1,0:T(8,128)(2,1)S(1)}, bf16[1,256,256]{2,1,0:T(8,128)(2,1)S(1)}, u32[]{:S(2)}, u32[]{:S(2)}) collective-permute-start(bf16[1,256,256]{2,1,0:T(8,128)(2,1)S(1)} %multiply_convert_fusion.3), channel_id=1, source_target_pairs={{0,8},{1,9},{2,10},{3,11},{4,12},{5,13},{6,14},{7,15},{8,0},{9,1},... | collective-permute-start | bytes 393224 | tf_op jit(solution)/shard_map/ppermute | solution.py:17
  81.8 22.6 %collective-permute-start = (f32[256,896]{1,0:T(8,128)}, f32[256,896]{1,0:T(8,128)}, u32[]{:S(2)}, u32[]{:S(2)}) collective-permute-start(f32[256,896]{1,0:T(8,128)} %fusion.33), channel_id=1, source_target_pairs={{0,16},{16,0},{1,17},{17,1},{2,18},{18,2},{3,19},{19,3},{4,20},{20... | collective-permute-start | bytes 2752520 | tf_op jit(solution)/shard_map/ppermute | solution.py:17
  83.3 8.5 %collective-permute-start.13 = (bf16[2,256,256]{2,1,0:T(8,128)(2,1)S(1)}, bf16[2,256,256]{2,1,0:T(8,128)(2,1)S(1)}, u32[]{:S(2)}, u32[]{:S(2)}) collective-permute-start(bf16[2,256,256]{2,1,0:T(8,128)(2,1)S(1)} %broadcast_select_fusion), channel_id=1, source_target_pairs={{0,3},{1,2},{2,1},{3,0},{4,7},{5,6},{6,5},{7,4},{8,11},{9,10},{10,... | collective-permute-start | bytes 786440 | tf_op jit(solution)/shard_map/ppermute | solution.py:17
  84.6 7.3 %collective-permute-start.12 = (bf16[2,256,256]{2,1,0:T(8,128)(2,1)S(1)}, bf16[2,256,256]{2,1,0:T(8,128)(2,1)S(1)}, u32[]{:S(2)}, u32[]{:S(2)}) collective-permute-start(bf16[2,256,256]{2,1,0:T(8,128)(2,1)S(1)} %broadcast_select_fusion), channel_id=1, source_target_pairs={{0,1},{1,0},{2,3},{3,2},{4,5},{5,4},{6,7},{7,6},{8,9},{9,8},{10,11... | collective-permute-start | bytes 786440 | tf_op jit(solution)/shard_map/ppermute | solution.py:17
  85.1 12.5 %collective-permute-start.11 = (bf16[2,256,256]{2,1,0:T(8,128)(2,1)S(1)}, bf16[2,256,256]{2,1,0:T(8,128)(2,1)S(1)}, u32[]{:S(2)}, u32[]{:S(2)}) collective-permute-start(bf16[2,256,256]{2,1,0:T(8,128)(2,1)S(1)} %broadcast_select_fusion), channel_id=1, source_target_pairs={{0,2},{1,3},{2,0},{3,1},{4,6},{5,7},{6,4},{7,5},{8,10},{9,11},{10,... | collective-permute-start | bytes 786440 | tf_op jit(solution)/shard_map/ppermute | solution.py:17
  106.0 23.3 %copy-start.1 = (s32[2]{0:T(128)S(1)}, s32[2]{0:T(128)}, u32[]{:S(2)}) copy-start(s32[2]{0:T(128)} %param.13) | copy-start | bytes 28
  112.7 4.5 %collective-permute-start.15 = (f32[2,128]{1,0:T(2,128)S(1)}, f32[2,128]{1,0:T(2,128)S(1)}, u32[]{:S(2)}, u32[]{:S(2)}) collective-permute-start(f32[2,128]{1,0:T(2,128)S(1)} %get-tuple-element.7), channel_id=1, source_target_pairs={{0,4},{1,5},{2,6},{3,7},{4,0},{5,1},{6,2},{7,3},{8,12},{9,13},{10,... | collective-permute-start | bytes 3080 | tf_op jit(solution)/shard_map/ppermute | solution.py:17
  112.8 4.5 %collective-permute-start.14 = (f32[2,128]{1,0:T(2,128)S(1)}, f32[2,128]{1,0:T(2,128)S(1)}, u32[]{:S(2)}, u32[]{:S(2)}) collective-permute-start(f32[2,128]{1,0:T(2,128)S(1)} %get-tuple-element.7), channel_id=1, source_target_pairs={{0,8},{1,9},{2,10},{3,11},{4,12},{5,13},{6,14},{7,15},{8,0},{9,1},... | collective-permute-start | bytes 3080 | tf_op jit(solution)/shard_map/ppermute | solution.py:17
  114.3 5.4 %collective-permute-start.16 = (f32[2,128]{1,0:T(2,128)S(1)}, f32[2,128]{1,0:T(2,128)S(1)}, u32[]{:S(2)}, u32[]{:S(2)}) collective-permute-start(f32[2,128]{1,0:T(2,128)S(1)} %get-tuple-element.7), channel_id=1, source_target_pairs={{0,12},{1,13},{2,14},{3,15},{4,8},{5,9},{6,10},{7,11},{8,4},{9,5},... | collective-permute-start | bytes 3080 | tf_op jit(solution)/shard_map/ppermute | solution.py:17
  119.7 3.1 %collective-permute-start.19 = (f32[2,128]{1,0:T(2,128)S(1)}, f32[2,128]{1,0:T(2,128)S(1)}, u32[]{:S(2)}, u32[]{:S(2)}) collective-permute-start(f32[2,128]{1,0:T(2,128)S(1)} %fusion.41), channel_id=1, source_target_pairs={{0,3},{1,2},{2,1},{3,0},{4,7},{5,6},{6,5},{7,4},{8,11},{9,10},{10,... | collective-permute-start | bytes 3080 | tf_op jit(solution)/shard_map/ppermute | solution.py:17
  119.7 3.1 %collective-permute-start.18 = (f32[2,128]{1,0:T(2,128)S(1)}, f32[2,128]{1,0:T(2,128)S(1)}, u32[]{:S(2)}, u32[]{:S(2)}) collective-permute-start(f32[2,128]{1,0:T(2,128)S(1)} %fusion.41), channel_id=1, source_target_pairs={{0,1},{1,0},{2,3},{3,2},{4,5},{5,4},{6,7},{7,6},{8,9},{9,8},{10,11... | collective-permute-start | bytes 3080 | tf_op jit(solution)/shard_map/ppermute | solution.py:17
  122.0 3.6 %collective-permute-start.17 = (f32[2,128]{1,0:T(2,128)S(1)}, f32[2,128]{1,0:T(2,128)S(1)}, u32[]{:S(2)}, u32[]{:S(2)}) collective-permute-start(f32[2,128]{1,0:T(2,128)S(1)} %fusion.41), channel_id=1, source_target_pairs={{0,2},{1,3},{2,0},{3,1},{4,6},{5,7},{6,4},{7,5},{8,10},{9,11},{10,... | collective-permute-start | bytes 3080 | tf_op jit(solution)/shard_map/ppermute | solution.py:17
  125.6 3.6 %collective-permute-start.20 = (f32[2,128]{1,0:T(2,128)S(1)}, f32[2,128]{1,0:T(2,128)S(1)}, u32[]{:S(2)}, u32[]{:S(2)}) collective-permute-start(f32[2,128]{1,0:T(2,128)S(1)} %fusion.40), channel_id=1, source_target_pairs={{0,16},{16,0},{1,17},{17,1},{2,18},{18,2},{3,19},{19,3},{4,20},{20... | collective-permute-start | bytes 3080 | tf_op jit(solution)/shard_map/ppermute | solution.py:17
Sparse Core Ops, SparseCore 0:
  10.3 60.4 all-gather.1

commit v6 on v5

--- a/solution.py
+++ b/solution.py
@@ -89,8 +89,14 @@
 
     part_a = jnp.einsum("tk,jk->tj", all_a, basis_a, preferred_element_type=jnp.float32)
     rot_a_block = (xor_sum(part_a, "owner", owners) * live[:, None]).astype(jnp.bfloat16)
-    part_g = jnp.einsum("tk,jk->tj", all_g, basis_g, preferred_element_type=jnp.float32)
-    rot_g = (xor_sum(part_g, "owner", owners) * live[:, None]).astype(jnp.bfloat16)
+    pieces = []
+    step = m_block // 2
+    for start in range(0, m_block, step):
+        part_g = jnp.einsum(
+            "tk,jk->tj", all_g, basis_g[start:start + step], preferred_element_type=jnp.float32
+        )
+        pieces.append(xor_sum(part_g, "owner", owners))
+    rot_g = (jnp.concatenate(pieces, axis=1) * live[:, None]).astype(jnp.bfloat16)
 
     rot_a = half_gather(rot_a_block, owners, readers)
 

time: 138 us -> 137 us (level)
  waiting for transfers between devices: 61.4 us -> 57.2 us
  matrix products: 17.8 us -> 19.5 us
    ppermute x21 -> x22, waiting for transfers between devices: 60.7 us -> 56.5 us  [xor_round(): parts.append(lax.ppermute(held, axis, [(i, i ^ c) for i in range(size)]))]
    dot_general x1 -> x2, matrix products: 10.7 us -> 12.2 us  [local(): jnp.einsum('tk,jk->tj', all_g, basis_g[start:start + step], preferred_ele...]
    ppermute x21 -> x22, starting transfers between devices: 26 us -> 26.4 us  [xor_round(): parts.append(lax.ppermute(held, axis, [(i, i ^ c) for i in range(size)]))]
  transfers between devices with their start and end apart: 22 -> 23, of which waited for: 17 -> 15; matrix products, arithmetic and copies ran while one was open for 11% -> 20% of each run, Pallas kernels for 0% -> 0%
where the time goes in v6:
time: 137 us; the launch traced here: 136 us
  waiting for transfers between devices  57.2 us (42%)
  starting transfers between devices  26.4 us (19%)
  matrix products  19.5 us (14%)
  between operations  14.3 us (10%)
  other arithmetic  12.2 us (9%)
  local copies, waits for them, and re-layouts  6.85 us (5%)
    ppermute x22, waiting for transfers between devices, xor_round(): parts.append(lax.ppermute(held, axis, [(i, i ^ c) for i in range(size)]))  56.5 us
    ppermute x22, starting transfers between devices, xor_round(): parts.append(lax.ppermute(held, axis, [(i, i ^ c) for i in range(size)]))  26.4 us
    dot_general x2, matrix products, local(): jnp.einsum('tk,jk->tj', all_g, basis_g[start:start + step], preferred_ele...  12.2 us
    dot_general x1, matrix products, local(): jnp.einsum('stm,smn->stn', g_rows, scaled, preferred_element_type=jnp.flo...  6.87 us
    convert_element_type x1, other arithmetic, local(): denom = eigvals.astype(jnp.float32)  5.91 us
  transfers between devices with their start and end apart: 23, of which 15 were waited for; matrix products, arithmetic and copies ran while one was open for 20% of the time, Pallas kernels for 0%

profile of v6, /device:TPU:0, one launch (start us, length us, event | category | flops | bytes accessed | tf_op | source)
XLA Modules:
  0.0 136.5 jit_solution(17714466674370785576)
XLA Ops:
  7.9 5.1 %collective-permute-start.4 = (bf16[1,16,2048]{2,1,0:T(8,128)(2,1)}, bf16[1,16,2048]{2,1,0:T(8,128)(2,1)S(1)}, u32[]{:S(2)}, u32[]{:S(2)}) collective-permute-start(bf16[1,16,2048]{2,1,0:T(8,128)(2,1)} %bitcast.107), channel_id=1, source_target_pairs={{0,12},{1,13},{2,14},{3,15},{4,8},{5,9},{6,10},{7,11},{8,4},{9,5},... | collective-permute-start | bytes 196616 | tf_op jit(solution)/shard_map/ppermute | solution.py:17
  20.5 1.6 %collective-permute-start.6 = (bf16[4,16,2048]{2,1,0:T(8,128)(2,1)S(1)}, bf16[4,16,2048]{2,1,0:T(8,128)(2,1)S(1)}, u32[]{:S(2)}, u32[]{:S(2)}) collective-permute-start(bf16[4,16,2048]{2,1,0:T(8,128)(2,1)S(1)} %broadcast_select_fusion.1), channel_id=1, source_target_pairs={{0,1},{1,0},{2,3},{3,2},{4,5},{5,4},{6,7},{7,6},{8,9},{9,8},{10,11... | collective-permute-start | bytes 786440 | tf_op jit(solution)/shard_map/ppermute | solution.py:17
  22.7 8.7 %collective-permute-done.7 = bf16[4,16,2048]{2,1,0:T(8,128)(2,1)S(1)} collective-permute-done((bf16[4,16,2048]{2,1,0:T(8,128)(2,1)S(1)}, bf16[4,16,2048]{2,1,0:T(8,128)(2,1)S(1)}, u32[]{:S(2)}, u32[]{:S(2)}) %collective-permute-start.7) | collective-permute-done | bytes 262176 | tf_op jit(solution)/shard_map/ppermute | solution.py:17
  31.5 5.7 %collective-permute-done.5 = bf16[4,16,2048]{2,1,0:T(8,128)(2,1)S(1)} collective-permute-done((bf16[4,16,2048]{2,1,0:T(8,128)(2,1)S(1)}, bf16[4,16,2048]{2,1,0:T(8,128)(2,1)S(1)}, u32[]{:S(2)}, u32[]{:S(2)}) %collective-permute-start.5) | collective-permute-done | bytes 262176 | tf_op jit(solution)/shard_map/ppermute | solution.py:17
  38.7 1.6 %collective-permute-start.8 = (f32[256,256]{1,0:T(8,128)S(1)}, f32[256,256]{1,0:T(8,128)S(1)}, u32[]{:S(2)}, u32[]{:S(2)}) collective-permute-start(f32[256,256]{1,0:T(8,128)S(1)} %fusion.45), channel_id=1, source_target_pairs={{0,16},{16,0},{1,17},{17,1},{2,18},{18,2},{3,19},{19,3},{4,20},{20... | collective-permute-start | bytes 786440 | tf_op jit(solution)/shard_map/ppermute | solution.py:17
  40.3 6.7 %collective-permute-done.8 = f32[256,256]{1,0:T(8,128)S(1)} collective-permute-done((f32[256,256]{1,0:T(8,128)S(1)}, f32[256,256]{1,0:T(8,128)S(1)}, u32[]{:S(2)}, u32[]{:S(2)}) %collective-permute-start.8) | collective-permute-done | bytes 262176 | tf_op jit(solution)/shard_map/ppermute | solution.py:17
  47.2 2.2 %collective-permute-start.11 = (bf16[1,256,256]{2,1,0:T(8,128)(2,1)S(1)}, bf16[1,256,256]{2,1,0:T(8,128)(2,1)S(1)}, u32[]{:S(2)}, u32[]{:S(2)}) collective-permute-start(bf16[1,256,256]{2,1,0:T(8,128)(2,1)S(1)} %multiply_convert_fusion), channel_id=1, source_target_pairs={{0,12},{1,13},{2,14},{3,15},{4,8},{5,9},{6,10},{7,11},{8,4},{9,5},... | collective-permute-start | bytes 393224 | tf_op jit(solution)/shard_map/ppermute | solution.py:17
  49.8 1.9 %collective-permute-start.9 = (bf16[1,256,256]{2,1,0:T(8,128)(2,1)S(1)}, bf16[1,256,256]{2,1,0:T(8,128)(2,1)S(1)}, u32[]{:S(2)}, u32[]{:S(2)}) collective-permute-start(bf16[1,256,256]{2,1,0:T(8,128)(2,1)S(1)} %multiply_convert_fusion), channel_id=1, source_target_pairs={{0,8},{1,9},{2,10},{3,11},{4,12},{5,13},{6,14},{7,15},{8,0},{9,1},... | collective-permute-start | bytes 393224 | tf_op jit(solution)/shard_map/ppermute | solution.py:17
  51.8 5.9 %convert_element_type.42 = f32[896,2048]{1,0:T(8,128)} convert(bf16[896,2048]{1,0:T(8,128)(2,1)} %param.11) | non-fusion elementwise | flops 1835008 | bytes 11010048 | tf_op jit(solution)/shard_map/convert_element_type | solution.py:103
  58.2 4.9 %collective-permute-done.10 = bf16[1,256,256]{2,1,0:T(8,128)(2,1)S(1)} collective-permute-done((bf16[1,256,256]{2,1,0:T(8,128)(2,1)S(1)}, bf16[1,256,256]{2,1,0:T(8,128)(2,1)S(1)}, u32[]{:S(2)}, u32[]{:S(2)}) %collective-permute-start.10) | collective-permute-done | bytes 131104 | tf_op jit(solution)/shard_map/ppermute | solution.py:17
  63.1 7.3 %collective-permute-done.9 = bf16[1,256,256]{2,1,0:T(8,128)(2,1)S(1)} collective-permute-done((bf16[1,256,256]{2,1,0:T(8,128)(2,1)S(1)}, bf16[1,256,256]{2,1,0:T(8,128)(2,1)S(1)}, u32[]{:S(2)}, u32[]{:S(2)}) %collective-permute-start.9) | collective-permute-done | bytes 131104 | tf_op jit(solution)/shard_map/ppermute | solution.py:17
  73.3 6.7 %fusion.3 = f32[256,448]{0,1:T(8,128)} fusion(bf16[256,7168]{1,0:T(8,128)(2,1)} %all-gather.2.cloned.1.call-done, bf16[896,7168]{1,0:T(8,128)(2,1)} %param.10), kind=kOutput, calls=%fused_computation.8 | convolution fusion | flops 1644167168 | bytes 10551296 | tf_op jit(solution)/shard_map/tk,jk->tj/dot_general | solution.py:95
  81.5 5.5 %fusion.1 = f32[256,448]{0,1:T(8,128)} fusion(bf16[256,7168]{1,0:T(8,128)(2,1)S(1)} %copy-done.1, bf16[896,7168]{1,0:T(8,128)(2,1)} %param.10), kind=kOutput, calls=%fused_computation.6 | convolution fusion | flops 1644167168 | bytes 10551296 | tf_op jit(solution)/shard_map/tk,jk->tj/dot_general | solution.py:95
  90.0 3.8 %collective-permute-done = f32[256,448]{0,1:T(8,128)} collective-permute-done((f32[256,448]{0,1:T(8,128)}, f32[256,448]{0,1:T(8,128)}, u32[]{:S(2)}, u32[]{:S(2)}) %collective-permute-start) | collective-permute-done | bytes 458784 | tf_op jit(solution)/shard_map/ppermute | solution.py:17
  93.8 8.6 %collective-permute-done.1 = f32[256,448]{0,1:T(8,128)} collective-permute-done((f32[256,448]{0,1:T(8,128)}, f32[256,448]{0,1:T(8,128)}, u32[]{:S(2)}, u32[]{:S(2)}) %collective-permute-start.1) | collective-permute-done | bytes 458784 | tf_op jit(solution)/shard_map/ppermute | solution.py:17
  102.3 1.7 %fusion.13 = (f32[1,256,448]{1,2,0:T(8,128)S(1)}, f32[1,256,448]{1,2,0:T(8,128)S(1)}) fusion(s32[]{:T(128)S(6)} %select_n.174, f32[1,256,448]{1,2,0:T(8,128)} %bitcast.3, s32[]{:T(128)S(6)} %select_n.173, f32[1,256,448]{1,2,0:T(8,128)} %bitcast.4, f32[1,256,448]{1,2,0:T(8,128)} %bitcast.1, f32[1,256,448]{1,2,0:T(8,128)} %bitcast), kind=kLoop, calls=%fused_computation.33 | loop fusion | flops 688128 | bytes 2752520 | tf_op jit(solution)/shard_map/add | solution.py:39
  105.2 6.9 %fusion.8 = f32[2,128]{1,0:T(2,128)S(1)} fusion(bf16[2,128,2048]{2,1,0:T(8,128)(2,1)S(1)} %reshape_reshape.7, f32[896,2048]{1,0:T(8,128)} %convert_element_type.42, f32[2,128,448]{2,1,0:T(8,128)S(1)} %bitcast.95, f32[2,128,448]{2,1,0:T(8,128)} %bitcast.96, f32[2,128]{1,0:T(2,128)S(1)} %compare_convert_fusion.1), kind=kOutput, calls=%fused_computation.12 | convolution fusion | flops 1889337088 | bytes 9308160 | tf_op jit(solution)/shard_map/stm,smn->stn/dot_general | solution.py:108
  112.2 1.9 %collective-permute-start.15 = (f32[2,128]{1,0:T(2,128)S(1)}, f32[2,128]{1,0:T(2,128)S(1)}, u32[]{:S(2)}, u32[]{:S(2)}) collective-permute-start(f32[2,128]{1,0:T(2,128)S(1)} %get-tuple-element.7), channel_id=1, source_target_pairs={{0,8},{1,9},{2,10},{3,11},{4,12},{5,13},{6,14},{7,15},{8,0},{9,1},... | collective-permute-start | bytes 3080 | tf_op jit(solution)/shard_map/ppermute | solution.py:17
  114.0 2.5 %collective-permute-start.17 = (f32[2,128]{1,0:T(2,128)S(1)}, f32[2,128]{1,0:T(2,128)S(1)}, u32[]{:S(2)}, u32[]{:S(2)}) collective-permute-start(f32[2,128]{1,0:T(2,128)S(1)} %get-tuple-element.7), channel_id=1, source_target_pairs={{0,12},{1,13},{2,14},{3,15},{4,8},{5,9},{6,10},{7,11},{8,4},{9,5},... | collective-permute-start | bytes 3080 | tf_op jit(solution)/shard_map/ppermute | solution.py:17
  116.7 2.7 %collective-permute-done.17 = f32[2,128]{1,0:T(2,128)S(1)} collective-permute-done((f32[2,128]{1,0:T(2,128)S(1)}, f32[2,128]{1,0:T(2,128)S(1)}, u32[]{:S(2)}, u32[]{:S(2)}) %collective-permute-start.17) | collective-permute-done | bytes 1056 | tf_op jit(solution)/shard_map/ppermute | solution.py:17
  119.5 1.7 %collective-permute-start.19 = (f32[2,128]{1,0:T(2,128)S(1)}, f32[2,128]{1,0:T(2,128)S(1)}, u32[]{:S(2)}, u32[]{:S(2)}) collective-permute-start(f32[2,128]{1,0:T(2,128)S(1)} %fusion.52), channel_id=1, source_target_pairs={{0,1},{1,0},{2,3},{3,2},{4,5},{5,4},{6,7},{7,6},{8,9},{9,8},{10,11... | collective-permute-start | bytes 3080 | tf_op jit(solution)/shard_map/ppermute | solution.py:17
  122.5 2.2 %collective-permute-done.18 = f32[2,128]{1,0:T(2,128)S(1)} collective-permute-done((f32[2,128]{1,0:T(2,128)S(1)}, f32[2,128]{1,0:T(2,128)S(1)}, u32[]{:S(2)}, u32[]{:S(2)}) %collective-permute-start.18) | collective-permute-done | bytes 1056 | tf_op jit(solution)/shard_map/ppermute | solution.py:17
  124.7 1.5 %collective-permute-start.21 = (f32[2,128]{1,0:T(2,128)S(1)}, f32[2,128]{1,0:T(2,128)S(1)}, u32[]{:S(2)}, u32[]{:S(2)}) collective-permute-start(f32[2,128]{1,0:T(2,128)S(1)} %fusion.51), channel_id=1, source_target_pairs={{0,16},{16,0},{1,17},{17,1},{2,18},{18,2},{3,19},{19,3},{4,20},{20... | collective-permute-start | bytes 3080 | tf_op jit(solution)/shard_map/ppermute | solution.py:17
  126.3 2.1 %collective-permute-done.21 = f32[2,128]{1,0:T(2,128)S(1)} collective-permute-done((f32[2,128]{1,0:T(2,128)S(1)}, f32[2,128]{1,0:T(2,128)S(1)}, u32[]{:S(2)}, u32[]{:S(2)}) %collective-permute-start.21) | collective-permute-done | bytes 1056 | tf_op jit(solution)/shard_map/ppermute | solution.py:17
  (80 shorter events, 22.9 us)
Async XLA Ops:
  7.2 31.0 %copy-start = (bf16[256,2048]{1,0:T(8,128)(2,1)S(1)}, bf16[256,2048]{1,0:T(8,128)(2,1)}, u32[]{:S(2)}) copy-start(bf16[256,2048]{1,0:T(8,128)(2,1)} %param.9) | copy-start | bytes 3145732
  7.2 66.1 %all-gather.2.cloned.1.call-start = ((), (), s32[]{:S(2)}) async-start(), calls=%async_computation | async-start | bytes 3899392 | tf_op jit(solution)/shard_map/all_gather | solution.py:84
  7.9 8.7 %collective-permute-start.4 = (bf16[1,16,2048]{2,1,0:T(8,128)(2,1)}, bf16[1,16,2048]{2,1,0:T(8,128)(2,1)S(1)}, u32[]{:S(2)}, u32[]{:S(2)}) collective-permute-start(bf16[1,16,2048]{2,1,0:T(8,128)(2,1)} %bitcast.107), channel_id=1, source_target_pairs={{0,12},{1,13},{2,14},{3,15},{4,8},{5,9},{6,10},{7,11},{8,4},{9,5},... | collective-permute-start | bytes 196616 | tf_op jit(solution)/shard_map/ppermute | solution.py:17
  13.0 4.9 %collective-permute-start.3 = (bf16[1,16,2048]{2,1,0:T(8,128)(2,1)}, bf16[1,16,2048]{2,1,0:T(8,128)(2,1)S(1)}, u32[]{:S(2)}, u32[]{:S(2)}) collective-permute-start(bf16[1,16,2048]{2,1,0:T(8,128)(2,1)} %bitcast.108), channel_id=1, source_target_pairs={{0,4},{1,5},{2,6},{3,7},{4,0},{5,1},{6,2},{7,3},{8,12},{9,13},{10,... | collective-permute-start | bytes 196616 | tf_op jit(solution)/shard_map/ppermute | solution.py:17
  13.0 5.8 %collective-permute-start.2 = (bf16[1,16,2048]{2,1,0:T(8,128)(2,1)}, bf16[1,16,2048]{2,1,0:T(8,128)(2,1)S(1)}, u32[]{:S(2)}, u32[]{:S(2)}) collective-permute-start(bf16[1,16,2048]{2,1,0:T(8,128)(2,1)} %bitcast.109), channel_id=1, source_target_pairs={{0,8},{1,9},{2,10},{3,11},{4,12},{5,13},{6,14},{7,15},{8,0},{9,1},... | collective-permute-start | bytes 196616 | tf_op jit(solution)/shard_map/ppermute | solution.py:17
  20.4 11.1 %collective-permute-start.7 = (bf16[4,16,2048]{2,1,0:T(8,128)(2,1)S(1)}, bf16[4,16,2048]{2,1,0:T(8,128)(2,1)S(1)}, u32[]{:S(2)}, u32[]{:S(2)}) collective-permute-start(bf16[4,16,2048]{2,1,0:T(8,128)(2,1)S(1)} %broadcast_select_fusion.1), channel_id=1, source_target_pairs={{0,3},{1,2},{2,1},{3,0},{4,7},{5,6},{6,5},{7,4},{8,11},{9,10},{10,... | collective-permute-start | bytes 786440 | tf_op jit(solution)/shard_map/ppermute | solution.py:17
  20.5 11.0 %collective-permute-start.6 = (bf16[4,16,2048]{2,1,0:T(8,128)(2,1)S(1)}, bf16[4,16,2048]{2,1,0:T(8,128)(2,1)S(1)}, u32[]{:S(2)}, u32[]{:S(2)}) collective-permute-start(bf16[4,16,2048]{2,1,0:T(8,128)(2,1)S(1)} %broadcast_select_fusion.1), channel_id=1, source_target_pairs={{0,1},{1,0},{2,3},{3,2},{4,5},{5,4},{6,7},{7,6},{8,9},{9,8},{10,11... | collective-permute-start | bytes 786440 | tf_op jit(solution)/shard_map/ppermute | solution.py:17
  22.1 15.0 %collective-permute-start.5 = (bf16[4,16,2048]{2,1,0:T(8,128)(2,1)S(1)}, bf16[4,16,2048]{2,1,0:T(8,128)(2,1)S(1)}, u32[]{:S(2)}, u32[]{:S(2)}) collective-permute-start(bf16[4,16,2048]{2,1,0:T(8,128)(2,1)S(1)} %broadcast_select_fusion.1), channel_id=1, source_target_pairs={{0,2},{1,3},{2,0},{3,1},{4,6},{5,7},{6,4},{7,5},{8,10},{9,11},{10,... | collective-permute-start | bytes 786440 | tf_op jit(solution)/shard_map/ppermute | solution.py:17
  38.7 8.3 %collective-permute-start.8 = (f32[256,256]{1,0:T(8,128)S(1)}, f32[256,256]{1,0:T(8,128)S(1)}, u32[]{:S(2)}, u32[]{:S(2)}) collective-permute-start(f32[256,256]{1,0:T(8,128)S(1)} %fusion.45), channel_id=1, source_target_pairs={{0,16},{16,0},{1,17},{17,1},{2,18},{18,2},{3,19},{19,3},{4,20},{20... | collective-permute-start | bytes 786440 | tf_op jit(solution)/shard_map/ppermute | solution.py:17
  47.2 11.0 %collective-permute-start.11 = (bf16[1,256,256]{2,1,0:T(8,128)(2,1)S(1)}, bf16[1,256,256]{2,1,0:T(8,128)(2,1)S(1)}, u32[]{:S(2)}, u32[]{:S(2)}) collective-permute-start(bf16[1,256,256]{2,1,0:T(8,128)(2,1)S(1)} %multiply_convert_fusion), channel_id=1, source_target_pairs={{0,12},{1,13},{2,14},{3,15},{4,8},{5,9},{6,10},{7,11},{8,4},{9,5},... | collective-permute-start | bytes 393224 | tf_op jit(solution)/shard_map/ppermute | solution.py:17
  49.5 13.7 %collective-permute-start.10 = (bf16[1,256,256]{2,1,0:T(8,128)(2,1)S(1)}, bf16[1,256,256]{2,1,0:T(8,128)(2,1)S(1)}, u32[]{:S(2)}, u32[]{:S(2)}) collective-permute-start(bf16[1,256,256]{2,1,0:T(8,128)(2,1)S(1)} %multiply_convert_fusion), channel_id=1, source_target_pairs={{0,4},{1,5},{2,6},{3,7},{4,0},{5,1},{6,2},{7,3},{8,12},{9,13},{10,... | collective-permute-start | bytes 393224 | tf_op jit(solution)/shard_map/ppermute | solution.py:17
  49.8 20.6 %collective-permute-start.9 = (bf16[1,256,256]{2,1,0:T(8,128)(2,1)S(1)}, bf16[1,256,256]{2,1,0:T(8,128)(2,1)S(1)}, u32[]{:S(2)}, u32[]{:S(2)}) collective-permute-start(bf16[1,256,256]{2,1,0:T(8,128)(2,1)S(1)} %multiply_convert_fusion), channel_id=1, source_target_pairs={{0,8},{1,9},{2,10},{3,11},{4,12},{5,13},{6,14},{7,15},{8,0},{9,1},... | collective-permute-start | bytes 393224 | tf_op jit(solution)/shard_map/ppermute | solution.py:17
  71.1 16.5 %collective-permute-start.14 = (bf16[2,256,256]{2,1,0:T(8,128)(2,1)S(1)}, bf16[2,256,256]{2,1,0:T(8,128)(2,1)S(1)}, u32[]{:S(2)}, u32[]{:S(2)}) collective-permute-start(bf16[2,256,256]{2,1,0:T(8,128)(2,1)S(1)} %broadcast_select_fusion), channel_id=1, source_target_pairs={{0,3},{1,2},{2,1},{3,0},{4,7},{5,6},{6,5},{7,4},{8,11},{9,10},{10,... | collective-permute-start | bytes 786440 | tf_op jit(solution)/shard_map/ppermute | solution.py:17
  72.2 15.5 %collective-permute-start.13 = (bf16[2,256,256]{2,1,0:T(8,128)(2,1)S(1)}, bf16[2,256,256]{2,1,0:T(8,128)(2,1)S(1)}, u32[]{:S(2)}, u32[]{:S(2)}) collective-permute-start(bf16[2,256,256]{2,1,0:T(8,128)(2,1)S(1)} %broadcast_select_fusion), channel_id=1, source_target_pairs={{0,1},{1,0},{2,3},{3,2},{4,5},{5,4},{6,7},{7,6},{8,9},{9,8},{10,11... | collective-permute-start | bytes 786440 | tf_op jit(solution)/shard_map/ppermute | solution.py:17
  72.8 14.9 %collective-permute-start.12 = (bf16[2,256,256]{2,1,0:T(8,128)(2,1)S(1)}, bf16[2,256,256]{2,1,0:T(8,128)(2,1)S(1)}, u32[]{:S(2)}, u32[]{:S(2)}) collective-permute-start(bf16[2,256,256]{2,1,0:T(8,128)(2,1)S(1)} %broadcast_select_fusion), channel_id=1, source_target_pairs={{0,2},{1,3},{2,0},{3,1},{4,6},{5,7},{6,4},{7,5},{8,10},{9,11},{10,... | collective-permute-start | bytes 786440 | tf_op jit(solution)/shard_map/ppermute | solution.py:17
  80.0 13.7 %collective-permute-start = (f32[256,448]{0,1:T(8,128)}, f32[256,448]{0,1:T(8,128)}, u32[]{:S(2)}, u32[]{:S(2)}) collective-permute-start(f32[256,448]{0,1:T(8,128)} %fusion.3), channel_id=1, source_target_pairs={{0,16},{16,0},{1,17},{17,1},{2,18},{18,2},{3,19},{19,3},{4,20},{20... | collective-permute-start | bytes 1376264 | tf_op jit(solution)/shard_map/ppermute | solution.py:17
  87.0 15.4 %collective-permute-start.1 = (f32[256,448]{0,1:T(8,128)}, f32[256,448]{0,1:T(8,128)}, u32[]{:S(2)}, u32[]{:S(2)}) collective-permute-start(f32[256,448]{0,1:T(8,128)} %fusion.1), channel_id=1, source_target_pairs={{0,16},{16,0},{1,17},{17,1},{2,18},{18,2},{3,19},{19,3},{4,20},{20... | collective-permute-start | bytes 1376264 | tf_op jit(solution)/shard_map/ppermute | solution.py:17
  112.1 4.5 %collective-permute-start.16 = (f32[2,128]{1,0:T(2,128)S(1)}, f32[2,128]{1,0:T(2,128)S(1)}, u32[]{:S(2)}, u32[]{:S(2)}) collective-permute-start(f32[2,128]{1,0:T(2,128)S(1)} %get-tuple-element.7), channel_id=1, source_target_pairs={{0,4},{1,5},{2,6},{3,7},{4,0},{5,1},{6,2},{7,3},{8,12},{9,13},{10,... | collective-permute-start | bytes 3080 | tf_op jit(solution)/shard_map/ppermute | solution.py:17
  112.2 4.5 %collective-permute-start.15 = (f32[2,128]{1,0:T(2,128)S(1)}, f32[2,128]{1,0:T(2,128)S(1)}, u32[]{:S(2)}, u32[]{:S(2)}) collective-permute-start(f32[2,128]{1,0:T(2,128)S(1)} %get-tuple-element.7), channel_id=1, source_target_pairs={{0,8},{1,9},{2,10},{3,11},{4,12},{5,13},{6,14},{7,15},{8,0},{9,1},... | collective-permute-start | bytes 3080 | tf_op jit(solution)/shard_map/ppermute | solution.py:17
  114.0 5.4 %collective-permute-start.17 = (f32[2,128]{1,0:T(2,128)S(1)}, f32[2,128]{1,0:T(2,128)S(1)}, u32[]{:S(2)}, u32[]{:S(2)}) collective-permute-start(f32[2,128]{1,0:T(2,128)S(1)} %get-tuple-element.7), channel_id=1, source_target_pairs={{0,12},{1,13},{2,14},{3,15},{4,8},{5,9},{6,10},{7,11},{8,4},{9,5},... | collective-permute-start | bytes 3080 | tf_op jit(solution)/shard_map/ppermute | solution.py:17
  119.4 3.1 %collective-permute-start.20 = (f32[2,128]{1,0:T(2,128)S(1)}, f32[2,128]{1,0:T(2,128)S(1)}, u32[]{:S(2)}, u32[]{:S(2)}) collective-permute-start(f32[2,128]{1,0:T(2,128)S(1)} %fusion.52), channel_id=1, source_target_pairs={{0,3},{1,2},{2,1},{3,0},{4,7},{5,6},{6,5},{7,4},{8,11},{9,10},{10,... | collective-permute-start | bytes 3080 | tf_op jit(solution)/shard_map/ppermute | solution.py:17
  119.5 3.0 %collective-permute-start.19 = (f32[2,128]{1,0:T(2,128)S(1)}, f32[2,128]{1,0:T(2,128)S(1)}, u32[]{:S(2)}, u32[]{:S(2)}) collective-permute-start(f32[2,128]{1,0:T(2,128)S(1)} %fusion.52), channel_id=1, source_target_pairs={{0,1},{1,0},{2,3},{3,2},{4,5},{5,4},{6,7},{7,6},{8,9},{9,8},{10,11... | collective-permute-start | bytes 3080 | tf_op jit(solution)/shard_map/ppermute | solution.py:17
  121.2 3.6 %collective-permute-start.18 = (f32[2,128]{1,0:T(2,128)S(1)}, f32[2,128]{1,0:T(2,128)S(1)}, u32[]{:S(2)}, u32[]{:S(2)}) collective-permute-start(f32[2,128]{1,0:T(2,128)S(1)} %fusion.52), channel_id=1, source_target_pairs={{0,2},{1,3},{2,0},{3,1},{4,6},{5,7},{6,4},{7,5},{8,10},{9,11},{10,... | collective-permute-start | bytes 3080 | tf_op jit(solution)/shard_map/ppermute | solution.py:17
  124.7 3.6 %collective-permute-start.21 = (f32[2,128]{1,0:T(2,128)S(1)}, f32[2,128]{1,0:T(2,128)S(1)}, u32[]{:S(2)}, u32[]{:S(2)}) collective-permute-start(f32[2,128]{1,0:T(2,128)S(1)} %fusion.51), channel_id=1, source_target_pairs={{0,16},{16,0},{1,17},{17,1},{2,18},{18,2},{3,19},{19,3},{4,20},{20... | collective-permute-start | bytes 3080 | tf_op jit(solution)/shard_map/ppermute | solution.py:17
  (2 other events, 31.5 us)
Sparse Core Ops, SparseCore 0:
  10.3 60.4 all-gather.1

commit v7 on v5

--- a/solution.py
+++ b/solution.py
@@ -64,6 +64,26 @@
     return held
 
 
+def row_rounds(rows_block, readers):
+    bits = [1 << k for k in range(readers.bit_length() - 1)][::-1]
+    groups = bit_groups([bit for bit in bits if bit >= 4]) + [[bit] for bit in bits if bit < 4]
+    held = rows_block[None]
+    offsets = [0]
+    pieces = [(held, [0])]
+    for group in groups:
+        received = []
+        new_offsets = []
+        for count in range(1, 1 << len(group)):
+            c = sum(bit for k, bit in enumerate(group) if count >> k & 1)
+            received.append(lax.ppermute(held, "reader", [(i, i ^ c) for i in range(readers)]))
+            new_offsets += [c ^ o for o in offsets]
+        piece = jnp.concatenate(received, axis=0)
+        pieces.append((piece, new_offsets))
+        held = jnp.concatenate([held, piece], axis=0)
+        offsets = offsets + new_offsets
+    return pieces, offsets
+
+
 def half_gather(block, owners, readers):
     held = ordered_gather(block, owners, readers)
     return jnp.transpose(held, (1, 0, 2)).reshape(block.shape[0], -1)
@@ -81,16 +101,29 @@
     dim_ff = m_block * readers
     dim_d = width * owners
 
-    all_g = lax.all_gather(grads, "reader", axis=0, tiled=True)
-    all_a = ordered_gather(acts, 1, readers).reshape(rows, acts.shape[1])
+    joined = jnp.concatenate([grads, acts], axis=1)
+    pieces, offsets = row_rounds(joined, readers)
+    width_g = grads.shape[1]
+    summed = []
+    for piece, _ in pieces:
+        flat = piece.reshape(-1, piece.shape[-1])
+        part_a = jnp.einsum("tk,jk->tj", flat[:, width_g:], basis_a, preferred_element_type=jnp.float32)
+        part_g = jnp.einsum("tk,jk->tj", flat[:, :width_g], basis_g, preferred_element_type=jnp.float32)
+        part = jnp.concatenate([part_g, part_a], axis=1)
+        summed.append(xor_sum(part, "owner", owners))
+    whole = jnp.concatenate(summed, axis=0).reshape(readers, acts.shape[0], -1)
+    position = [0] * readers
+    for p, off in enumerate(offsets):
+        position[off] = p
+    reader_index = lax.axis_index("reader")
+    order = jnp.asarray(position, jnp.int32)[reader_index ^ jnp.arange(readers, dtype=jnp.int32)]
+    whole = jnp.take(whole, order, axis=0).reshape(rows, -1)
 
     token = jnp.arange(rows, dtype=jnp.int32)
     live = ((token % SEQ) < lengths[token // SEQ]).astype(jnp.float32)
-
-    part_a = jnp.einsum("tk,jk->tj", all_a, basis_a, preferred_element_type=jnp.float32)
-    rot_a_block = (xor_sum(part_a, "owner", owners) * live[:, None]).astype(jnp.bfloat16)
-    part_g = jnp.einsum("tk,jk->tj", all_g, basis_g, preferred_element_type=jnp.float32)
-    rot_g = (xor_sum(part_g, "owner", owners) * live[:, None]).astype(jnp.bfloat16)
+    rot = (whole * live[:, None]).astype(jnp.bfloat16)
+    rot_g = rot[:, :m_block]
+    rot_a_block = rot[:, m_block:]
 
     rot_a = half_gather(rot_a_block, owners, readers)
 

time: 138 us -> 162 us (1.17)
  matrix products: 17.8 us -> 41.3 us
  between operations: 14.3 us -> 1.09 us
  starting transfers between devices: 26 us -> 35.3 us
  waiting for transfers between devices: 61.4 us -> 55.6 us
  other arithmetic: 12.2 us -> 17.9 us
  local copies, waits for them, and re-layouts: 5.67 us -> 10.4 us
    ppermute x21 -> x17, waiting for transfers between devices: 60.7 us -> 28.6 us  [xor_round(): parts.append(lax.ppermute(held, axis, [(i, i ^ c) for i in range(size)]))]
    ppermute x0 -> x5, waiting for transfers between devices: none -> 27 us  [row_rounds(): lax.ppermute(held, 'reader', [(i, i ^ c) for i in range(readers)])]
    dot_general x2 -> x8, matrix products: 11.2 us -> 34.2 us  [the longest x4 31.3 us: local(): jnp.einsum('tk,jk->tj', flat[:, :width_g], basis_g, preferred_element_typ...]
    ppermute x0 -> x5, starting transfers between devices: none -> 7.28 us  [row_rounds(): lax.ppermute(held, 'reader', [(i, i ^ c) for i in range(readers)])]
    unnamed x4 -> x35, local copies, waits for them, and re-layouts: 0.02 us -> 3.01 us
    concatenate x0 -> x7, other arithmetic: none -> 2.65 us  [the longest x4 2.32 us: local(): part = jnp.concatenate([part_g, part_a], axis=1)]
    ppermute x21 -> x17, starting transfers between devices: 26 us -> 28 us  [xor_round(): parts.append(lax.ppermute(held, axis, [(i, i ^ c) for i in range(size)]))]
    add x5 -> x8, other arithmetic: 1.7 us -> 3.39 us  [xor_sum(): terms = [terms[i] + terms[i + 1] for i in range(0, len(terms), 2)]]
  transfers between devices with their start and end apart: 22 -> 22, of which waited for: 17 -> 11; matrix products, arithmetic and copies ran while one was open for 11% -> 33% of each run, Pallas kernels for 0% -> 0%
where the time goes in v7:
time: 162 us
  waiting for transfers between devices  55.6 us (34%)
  matrix products  41.3 us (25%)
  starting transfers between devices  35.3 us (22%)
  other arithmetic  17.9 us (11%)
  local copies, waits for them, and re-layouts  10.4 us (6%)
    dot_general x4, matrix products, local(): jnp.einsum('tk,jk->tj', flat[:, :width_g], basis_g, preferred_element_typ...  31.3 us
    ppermute x17, waiting for transfers between devices, xor_round(): parts.append(lax.ppermute(held, axis, [(i, i ^ c) for i in range(size)]))  28.6 us
    ppermute x17, starting transfers between devices, xor_round(): parts.append(lax.ppermute(held, axis, [(i, i ^ c) for i in range(size)]))  28 us
    ppermute x5, waiting for transfers between devices, row_rounds(): lax.ppermute(held, 'reader', [(i, i ^ c) for i in range(readers)])  27 us
    ppermute x5, starting transfers between devices, row_rounds(): lax.ppermute(held, 'reader', [(i, i ^ c) for i in range(readers)])  7.28 us
    dot_general x1, matrix products, local(): jnp.einsum('stm,smn->stn', g_rows, scaled, preferred_element_type=jnp.flo...  7.14 us
    convert_element_type x1, other arithmetic, local(): denom = eigvals.astype(jnp.float32)  5.87 us
    add x8, other arithmetic, xor_sum(): terms = [terms[i] + terms[i + 1] for i in range(0, len(terms), 2)]  3.39 us
  transfers between devices with their start and end apart: 22, of which 11 were waited for; matrix products, arithmetic and copies ran while one was open for 33% of the time, Pallas kernels for 0%

profile of v7, /device:TPU:0, one launch (start us, length us, event | category | flops | bytes accessed | tf_op | source)
XLA Modules:
  0.0 161.5 jit_solution(11807808816896400296)
XLA Ops:
  1.8 4.1 %collective-permute-start.1 = (bf16[1,16,9216]{2,1,0:T(8,128)(2,1)S(1)}, bf16[1,16,9216]{2,1,0:T(8,128)(2,1)S(1)}, u32[]{:S(2)}, u32[]{:S(2)}) collective-permute-start(bf16[1,16,9216]{2,1,0:T(8,128)(2,1)S(1)} %maximum_bitcast_fusion.1), channel_id=1, source_target_pairs={{0,8},{1,9},{2,10},{3,11},{4,12},{5,13},{6,14},{7,15},{8,0},{9,1},... | collective-permute-start | bytes 884744 | tf_op jit(solution)/shard_map/ppermute | solution.py:78
  5.9 1.6 collective-permute-start.2
  7.4 8.2 %fusion.58 = f32[16,896]{1,0:T(8,128)S(1)} fusion(bf16[16,7168]{1,0:T(8,128)(2,1)} %param.9, bf16[896,7168]{1,0:T(8,128)(2,1)} %param.11), kind=kOutput, calls=%fused_computation.138 | convolution fusion | flops 205520896 | bytes 13131776 | tf_op jit(solution)/shard_map/tk,jk->tj/dot_general | solution.py:111
  16.7 1.7 %collective-permute-start = (f32[16,1152]{1,0:T(8,128)}, f32[16,1152]{1,0:T(8,128)}, u32[]{:S(2)}, u32[]{:S(2)}) collective-permute-start(f32[16,1152]{1,0:T(8,128)} %get-tuple-element.12), channel_id=1, source_target_pairs={{0,16},{16,0},{1,17},{17,1},{2,18},{18,2},{3,19},{19,3},{4,20},{20... | collective-permute-start | bytes 221192 | tf_op jit(solution)/shard_map/ppermute | solution.py:17
  22.7 4.0 %collective-permute-done.3 = bf16[1,16,9216]{2,1,0:T(8,128)(2,1)S(1)} collective-permute-done((bf16[1,16,9216]{2,1,0:T(8,128)(2,1)S(1)}, bf16[1,16,9216]{2,1,0:T(8,128)(2,1)S(1)}, u32[]{:S(2)}, u32[]{:S(2)}) %collective-permute-start.3) | collective-permute-done | bytes 294944 | tf_op jit(solution)/shard_map/ppermute | solution.py:78
  26.9 1.6 collective-permute-start.5
  30.8 22.9 %collective-permute-done.5 = bf16[4,16,9216]{2,1,0:T(8,128)(2,1)S(1)} collective-permute-done((bf16[4,16,9216]{2,1,0:T(8,128)(2,1)S(1)}, bf16[4,16,9216]{2,1,0:T(8,128)(2,1)S(1)}, u32[]{:S(2)}, u32[]{:S(2)}) %collective-permute-start.5) | collective-permute-done | bytes 1179680 | tf_op jit(solution)/shard_map/ppermute | solution.py:78
  55.3 8.7 %fusion.11 = f32[48,896]{1,0:T(8,128)S(1)} fusion(bf16[896,7168]{1,0:T(8,128)(2,1)} %param.11, bf16[48,9216]{1,0:T(8,128)(2,1)S(1)} %bitcast.114), kind=kOutput, calls=%fused_computation.29 | convolution fusion | flops 616562688 | bytes 13705216 | tf_op jit(solution)/shard_map/tk,jk->tj/dot_general | solution.py:111
  66.8 8.9 %fusion.9 = f32[64,896]{1,0:T(8,128)S(1)} fusion(bf16[896,7168]{1,0:T(8,128)(2,1)} %param.11, bf16[64,9216]{1,0:T(8,128)(2,1)S(1)} %bitcast.111), kind=kOutput, calls=%fused_computation.22 | convolution fusion | flops 822083584 | bytes 13991936 | tf_op jit(solution)/shard_map/tk,jk->tj/dot_general | solution.py:111
  77.0 5.6 %fusion.4 = f32[128,896]{1,0:T(8,128)S(1)} fusion(bf16[896,7168]{1,0:T(8,128)(2,1)S(1)} %bitcast.108, bf16[128,9216]{1,0:T(8,128)(2,1)} %bitcast.13), kind=kOutput, calls=%fused_computation.8 | convolution fusion | flops 1644167168 | bytes 15138816 | tf_op jit(solution)/shard_map/tk,jk->tj/dot_general | solution.py:111
  82.6 1.6 fusion.17
  84.3 1.6 collective-permute-start.8
  89.0 10.5 %collective-permute-done.8 = f32[128,1152]{1,0:T(8,128)S(1)} collective-permute-done((f32[128,1152]{1,0:T(8,128)S(1)}, f32[128,1152]{1,0:T(8,128)S(1)}, u32[]{:S(2)}, u32[]{:S(2)}) %collective-permute-start.8) | collective-permute-done | bytes 589856 | tf_op jit(solution)/shard_map/ppermute | solution.py:17
  100.7 8.9 %collective-permute-start.9 = (bf16[1,256,256]{2,1,0:T(8,128)(2,1)S(1)}, bf16[1,256,256]{2,1,0:T(8,128)(2,1)S(1)}, u32[]{:S(2)}, u32[]{:S(2)}) collective-permute-start(bf16[1,256,256]{2,1,0:T(8,128)(2,1)S(1)} %get-tuple-element.5), channel_id=1, source_target_pairs={{0,8},{1,9},{2,10},{3,11},{4,12},{5,13},{6,14},{7,15},{8,0},{9,1},... | collective-permute-start | bytes 393224 | tf_op jit(solution)/shard_map/ppermute | solution.py:17
  111.2 5.6 %collective-permute-done.9 = bf16[1,256,256]{2,1,0:T(8,128)(2,1)S(1)} collective-permute-done((bf16[1,256,256]{2,1,0:T(8,128)(2,1)S(1)}, bf16[1,256,256]{2,1,0:T(8,128)(2,1)S(1)}, u32[]{:S(2)}, u32[]{:S(2)}) %collective-permute-start.9) | collective-permute-done | bytes 131104 | tf_op jit(solution)/shard_map/ppermute | solution.py:17
  116.8 2.4 %collective-permute-done.10 = bf16[1,256,256]{2,1,0:T(8,128)(2,1)S(1)} collective-permute-done((bf16[1,256,256]{2,1,0:T(8,128)(2,1)S(1)}, bf16[1,256,256]{2,1,0:T(8,128)(2,1)S(1)}, u32[]{:S(2)}, u32[]{:S(2)}) %collective-permute-start.10) | collective-permute-done | bytes 131104 | tf_op jit(solution)/shard_map/ppermute | solution.py:17
  119.9 1.6 collective-permute-start.12
  122.2 5.9 %convert_element_type.22 = f32[896,2048]{1,0:T(8,128)} convert(bf16[896,2048]{1,0:T(8,128)(2,1)} %param.12) | non-fusion elementwise | flops 1835008 | bytes 11010048 | tf_op jit(solution)/shard_map/convert_element_type | solution.py:130
  128.2 2.7 %collective-permute-done.14 = bf16[2,256,256]{2,1,0:T(8,128)(2,1)S(1)} collective-permute-done((bf16[2,256,256]{2,1,0:T(8,128)(2,1)S(1)}, bf16[2,256,256]{2,1,0:T(8,128)(2,1)S(1)}, u32[]{:S(2)}, u32[]{:S(2)}) %collective-permute-start.14) | collective-permute-done | bytes 262176 | tf_op jit(solution)/shard_map/ppermute | solution.py:17
  135.6 7.1 %fusion.6 = f32[2,128]{1,0:T(2,128)S(1)} fusion(bf16[2,128,2048]{2,1,0:T(8,128)(2,1)} %reshape_reshape.3, bf16[2,128,896]{2,1,0:T(8,128)(2,1)S(1)} %bitcast.115, f32[896,2048]{1,0:T(8,128)} %convert_element_type.22), kind=kOutput, calls=%fused_computation.14 | convolution fusion | flops 1887960832 | bytes 8848384 | tf_op jit(solution)/shard_map/stm,smn->stn/dot_general | solution.py:135
  142.7 3.0 %collective-permute-start.15 = (f32[2,128]{1,0:T(2,128)S(1)}, f32[2,128]{1,0:T(2,128)S(1)}, u32[]{:S(2)}, u32[]{:S(2)}) collective-permute-start(f32[2,128]{1,0:T(2,128)S(1)} %get-tuple-element.15), channel_id=1, source_target_pairs={{0,8},{1,9},{2,10},{3,11},{4,12},{5,13},{6,14},{7,15},{8,0},{9,1},... | collective-permute-start | bytes 3080 | tf_op jit(solution)/shard_map/ppermute | solution.py:17
  146.8 2.3 %collective-permute-start.17 = (f32[2,128]{1,0:T(2,128)S(1)}, f32[2,128]{1,0:T(2,128)S(1)}, u32[]{:S(2)}, u32[]{:S(2)}) collective-permute-start(f32[2,128]{1,0:T(2,128)S(1)} %get-tuple-element.15), channel_id=1, source_target_pairs={{0,12},{1,13},{2,14},{3,15},{4,8},{5,9},{6,10},{7,11},{8,4},{9,5},... | collective-permute-start | bytes 3080 | tf_op jit(solution)/shard_map/ppermute | solution.py:17
  149.3 2.9 %collective-permute-done.17 = f32[2,128]{1,0:T(2,128)S(1)} collective-permute-done((f32[2,128]{1,0:T(2,128)S(1)}, f32[2,128]{1,0:T(2,128)S(1)}, u32[]{:S(2)}, u32[]{:S(2)}) %collective-permute-start.17) | collective-permute-done | bytes 1056 | tf_op jit(solution)/shard_map/ppermute | solution.py:17
  158.2 2.1 %collective-permute-done.21 = f32[2,128]{1,0:T(2,128)S(1)} collective-permute-done((f32[2,128]{1,0:T(2,128)S(1)}, f32[2,128]{1,0:T(2,128)S(1)}, u32[]{:S(2)}, u32[]{:S(2)}) %collective-permute-start.21) | collective-permute-done | bytes 1056 | tf_op jit(solution)/shard_map/ppermute | solution.py:17
  (123 shorter events, 35.1 us)
Async XLA Ops:
  1.8 20.9 %collective-permute-start.1 = (bf16[1,16,9216]{2,1,0:T(8,128)(2,1)S(1)}, bf16[1,16,9216]{2,1,0:T(8,128)(2,1)S(1)}, u32[]{:S(2)}, u32[]{:S(2)}) collective-permute-start(bf16[1,16,9216]{2,1,0:T(8,128)(2,1)S(1)} %maximum_bitcast_fusion.1), channel_id=1, source_target_pairs={{0,8},{1,9},{2,10},{3,11},{4,12},{5,13},{6,14},{7,15},{8,0},{9,1},... | collective-permute-start | bytes 884744 | tf_op jit(solution)/shard_map/ppermute | solution.py:78
  5.9 16.9 %collective-permute-start.2 = (bf16[1,16,9216]{2,1,0:T(8,128)(2,1)S(1)}, bf16[1,16,9216]{2,1,0:T(8,128)(2,1)S(1)}, u32[]{:S(2)}, u32[]{:S(2)}) collective-permute-start(bf16[1,16,9216]{2,1,0:T(8,128)(2,1)S(1)} %maximum_bitcast_fusion.1), channel_id=1, source_target_pairs={{0,4},{1,5},{2,6},{3,7},{4,0},{5,1},{6,2},{7,3},{8,12},{9,13},{10,... | collective-permute-start | bytes 884744 | tf_op jit(solution)/shard_map/ppermute | solution.py:78
  7.4 19.3 %collective-permute-start.3 = (bf16[1,16,9216]{2,1,0:T(8,128)(2,1)S(1)}, bf16[1,16,9216]{2,1,0:T(8,128)(2,1)S(1)}, u32[]{:S(2)}, u32[]{:S(2)}) collective-permute-start(bf16[1,16,9216]{2,1,0:T(8,128)(2,1)S(1)} %maximum_bitcast_fusion.1), channel_id=1, source_target_pairs={{0,12},{1,13},{2,14},{3,15},{4,8},{5,9},{6,10},{7,11},{8,4},{9,5},... | collective-permute-start | bytes 884744 | tf_op jit(solution)/shard_map/ppermute | solution.py:78
  16.7 69.1 %collective-permute-start = (f32[16,1152]{1,0:T(8,128)}, f32[16,1152]{1,0:T(8,128)}, u32[]{:S(2)}, u32[]{:S(2)}) collective-permute-start(f32[16,1152]{1,0:T(8,128)} %get-tuple-element.12), channel_id=1, source_target_pairs={{0,16},{16,0},{1,17},{17,1},{2,18},{18,2},{3,19},{19,3},{4,20},{20... | collective-permute-start | bytes 221192 | tf_op jit(solution)/shard_map/ppermute | solution.py:17
  26.9 26.9 %collective-permute-start.5 = (bf16[4,16,9216]{2,1,0:T(8,128)(2,1)S(1)}, bf16[4,16,9216]{2,1,0:T(8,128)(2,1)S(1)}, u32[]{:S(2)}, u32[]{:S(2)}) collective-permute-start(bf16[4,16,9216]{2,1,0:T(8,128)(2,1)S(1)} %pad_maximum_fusion), channel_id=1, source_target_pairs={{0,2},{1,3},{2,0},{3,1},{4,6},{5,7},{6,4},{7,5},{8,10},{9,11},{10,... | collective-permute-start | bytes 3538952 | tf_op jit(solution)/shard_map/ppermute | solution.py:78
  54.9 22.1 %collective-permute-start.7 = (bf16[8,16,9216]{2,1,0:T(8,128)(2,1)}, bf16[8,16,9216]{2,1,0:T(8,128)(2,1)}, u32[]{:S(2)}, u32[]{:S(2)}) collective-permute-start(bf16[8,16,9216]{2,1,0:T(8,128)(2,1)} %constant_dynamic-update-slice_fusion), channel_id=1, source_target_pairs={{0,1},{1,0},{2,3},{3,2},{4,5},{5,4},{6,7},{7,6},{8,9},{9,8},{10,11... | collective-permute-start | bytes 7077896 | tf_op jit(solution)/shard_map/ppermute | solution.py:78
  64.8 22.1 %collective-permute-start.4 = (f32[48,1152]{1,0:T(8,128)}, f32[48,1152]{1,0:T(8,128)}, u32[]{:S(2)}, u32[]{:S(2)}) collective-permute-start(f32[48,1152]{1,0:T(8,128)} %get-tuple-element.10), channel_id=1, source_target_pairs={{0,16},{16,0},{1,17},{17,1},{2,18},{18,2},{3,19},{19,3},{4,20},{20... | collective-permute-start | bytes 663560 | tf_op jit(solution)/shard_map/ppermute | solution.py:17
  76.4 11.5 %collective-permute-start.6 = (f32[64,1152]{1,0:T(8,128)}, f32[64,1152]{1,0:T(8,128)}, u32[]{:S(2)}, u32[]{:S(2)}) collective-permute-start(f32[64,1152]{1,0:T(8,128)} %get-tuple-element.8), channel_id=1, source_target_pairs={{0,16},{16,0},{1,17},{17,1},{2,18},{18,2},{3,19},{19,3},{4,20},{20... | collective-permute-start | bytes 884744 | tf_op jit(solution)/shard_map/ppermute | solution.py:17
  84.3 15.2 %collective-permute-start.8 = (f32[128,1152]{1,0:T(8,128)S(1)}, f32[128,1152]{1,0:T(8,128)S(1)}, u32[]{:S(2)}, u32[]{:S(2)}) collective-permute-start(f32[128,1152]{1,0:T(8,128)S(1)} %get-tuple-element.6), channel_id=1, source_target_pairs={{0,16},{16,0},{1,17},{17,1},{2,18},{18,2},{3,19},{19,3},{4,20},{20... | collective-permute-start | bytes 1769480 | tf_op jit(solution)/shard_map/ppermute | solution.py:17
  100.6 27.4 %copy-start.2 = (bf16[256,1152]{1,0:T(8,128)(2,1)}, bf16[256,1152]{1,0:T(8,128)(2,1)S(1)}, u32[]{:S(2)}) copy-start(bf16[256,1152]{1,0:T(8,128)(2,1)S(1)} %fusion.8) | copy-start | bytes 1769476
  100.7 16.1 %collective-permute-start.9 = (bf16[1,256,256]{2,1,0:T(8,128)(2,1)S(1)}, bf16[1,256,256]{2,1,0:T(8,128)(2,1)S(1)}, u32[]{:S(2)}, u32[]{:S(2)}) collective-permute-start(bf16[1,256,256]{2,1,0:T(8,128)(2,1)S(1)} %get-tuple-element.5), channel_id=1, source_target_pairs={{0,8},{1,9},{2,10},{3,11},{4,12},{5,13},{6,14},{7,15},{8,0},{9,1},... | collective-permute-start | bytes 393224 | tf_op jit(solution)/shard_map/ppermute | solution.py:17
  109.6 9.6 %collective-permute-start.10 = (bf16[1,256,256]{2,1,0:T(8,128)(2,1)S(1)}, bf16[1,256,256]{2,1,0:T(8,128)(2,1)S(1)}, u32[]{:S(2)}, u32[]{:S(2)}) collective-permute-start(bf16[1,256,256]{2,1,0:T(8,128)(2,1)S(1)} %get-tuple-element.5), channel_id=1, source_target_pairs={{0,4},{1,5},{2,6},{3,7},{4,0},{5,1},{6,2},{7,3},{8,12},{9,13},{10,... | collective-permute-start | bytes 393224 | tf_op jit(solution)/shard_map/ppermute | solution.py:17
  109.6 9.6 %collective-permute-start.11 = (bf16[1,256,256]{2,1,0:T(8,128)(2,1)S(1)}, bf16[1,256,256]{2,1,0:T(8,128)(2,1)S(1)}, u32[]{:S(2)}, u32[]{:S(2)}) collective-permute-start(bf16[1,256,256]{2,1,0:T(8,128)(2,1)S(1)} %get-tuple-element.5), channel_id=1, source_target_pairs={{0,12},{1,13},{2,14},{3,15},{4,8},{5,9},{6,10},{7,11},{8,4},{9,5},... | collective-permute-start | bytes 393224 | tf_op jit(solution)/shard_map/ppermute | solution.py:17
  119.9 8.3 %collective-permute-start.12 = (bf16[2,256,256]{2,1,0:T(8,128)(2,1)S(1)}, bf16[2,256,256]{2,1,0:T(8,128)(2,1)S(1)}, u32[]{:S(2)}, u32[]{:S(2)}) collective-permute-start(bf16[2,256,256]{2,1,0:T(8,128)(2,1)S(1)} %broadcast_select_fusion), channel_id=1, source_target_pairs={{0,2},{1,3},{2,0},{3,1},{4,6},{5,7},{6,4},{7,5},{8,10},{9,11},{10,... | collective-permute-start | bytes 786440 | tf_op jit(solution)/shard_map/ppermute | solution.py:17
  121.5 6.7 %collective-permute-start.13 = (bf16[2,256,256]{2,1,0:T(8,128)(2,1)S(1)}, bf16[2,256,256]{2,1,0:T(8,128)(2,1)S(1)}, u32[]{:S(2)}, u32[]{:S(2)}) collective-permute-start(bf16[2,256,256]{2,1,0:T(8,128)(2,1)S(1)} %broadcast_select_fusion), channel_id=1, source_target_pairs={{0,1},{1,0},{2,3},{3,2},{4,5},{5,4},{6,7},{7,6},{8,9},{9,8},{10,11... | collective-permute-start | bytes 786440 | tf_op jit(solution)/shard_map/ppermute | solution.py:17
  121.5 9.4 %collective-permute-start.14 = (bf16[2,256,256]{2,1,0:T(8,128)(2,1)S(1)}, bf16[2,256,256]{2,1,0:T(8,128)(2,1)S(1)}, u32[]{:S(2)}, u32[]{:S(2)}) collective-permute-start(bf16[2,256,256]{2,1,0:T(8,128)(2,1)S(1)} %broadcast_select_fusion), channel_id=1, source_target_pairs={{0,3},{1,2},{2,1},{3,0},{4,7},{5,6},{6,5},{7,4},{8,11},{9,10},{10,... | collective-permute-start | bytes 786440 | tf_op jit(solution)/shard_map/ppermute | solution.py:17
  135.6 25.3 %copy-start.11 = (s32[2]{0:T(128)S(1)}, s32[2]{0:T(128)}, u32[]{:S(2)}) copy-start(s32[2]{0:T(128)} %param.14) | copy-start | bytes 28
  142.7 6.4 %collective-permute-start.15 = (f32[2,128]{1,0:T(2,128)S(1)}, f32[2,128]{1,0:T(2,128)S(1)}, u32[]{:S(2)}, u32[]{:S(2)}) collective-permute-start(f32[2,128]{1,0:T(2,128)S(1)} %get-tuple-element.15), channel_id=1, source_target_pairs={{0,8},{1,9},{2,10},{3,11},{4,12},{5,13},{6,14},{7,15},{8,0},{9,1},... | collective-permute-start | bytes 3080 | tf_op jit(solution)/shard_map/ppermute | solution.py:17
  145.7 3.6 %collective-permute-start.16 = (f32[2,128]{1,0:T(2,128)S(1)}, f32[2,128]{1,0:T(2,128)S(1)}, u32[]{:S(2)}, u32[]{:S(2)}) collective-permute-start(f32[2,128]{1,0:T(2,128)S(1)} %get-tuple-element.15), channel_id=1, source_target_pairs={{0,4},{1,5},{2,6},{3,7},{4,0},{5,1},{6,2},{7,3},{8,12},{9,13},{10,... | collective-permute-start | bytes 3080 | tf_op jit(solution)/shard_map/ppermute | solution.py:17
  146.8 5.4 %collective-permute-start.17 = (f32[2,128]{1,0:T(2,128)S(1)}, f32[2,128]{1,0:T(2,128)S(1)}, u32[]{:S(2)}, u32[]{:S(2)}) collective-permute-start(f32[2,128]{1,0:T(2,128)S(1)} %get-tuple-element.15), channel_id=1, source_target_pairs={{0,12},{1,13},{2,14},{3,15},{4,8},{5,9},{6,10},{7,11},{8,4},{9,5},... | collective-permute-start | bytes 3080 | tf_op jit(solution)/shard_map/ppermute | solution.py:17
  152.2 3.6 %collective-permute-start.18 = (f32[2,128]{1,0:T(2,128)S(1)}, f32[2,128]{1,0:T(2,128)S(1)}, u32[]{:S(2)}, u32[]{:S(2)}) collective-permute-start(f32[2,128]{1,0:T(2,128)S(1)} %fusion.74), channel_id=1, source_target_pairs={{0,2},{1,3},{2,0},{3,1},{4,6},{5,7},{6,4},{7,5},{8,10},{9,11},{10,... | collective-permute-start | bytes 3080 | tf_op jit(solution)/shard_map/ppermute | solution.py:17
  153.6 2.2 %collective-permute-start.19 = (f32[2,128]{1,0:T(2,128)S(1)}, f32[2,128]{1,0:T(2,128)S(1)}, u32[]{:S(2)}, u32[]{:S(2)}) collective-permute-start(f32[2,128]{1,0:T(2,128)S(1)} %fusion.74), channel_id=1, source_target_pairs={{0,1},{1,0},{2,3},{3,2},{4,5},{5,4},{6,7},{7,6},{8,9},{9,8},{10,11... | collective-permute-start | bytes 3080 | tf_op jit(solution)/shard_map/ppermute | solution.py:17
  153.6 3.0 %collective-permute-start.20 = (f32[2,128]{1,0:T(2,128)S(1)}, f32[2,128]{1,0:T(2,128)S(1)}, u32[]{:S(2)}, u32[]{:S(2)}) collective-permute-start(f32[2,128]{1,0:T(2,128)S(1)} %fusion.74), channel_id=1, source_target_pairs={{0,3},{1,2},{2,1},{3,0},{4,7},{5,6},{6,5},{7,4},{8,11},{9,10},{10,... | collective-permute-start | bytes 3080 | tf_op jit(solution)/shard_map/ppermute | solution.py:17
  156.7 3.6 %collective-permute-start.21 = (f32[2,128]{1,0:T(2,128)S(1)}, f32[2,128]{1,0:T(2,128)S(1)}, u32[]{:S(2)}, u32[]{:S(2)}) collective-permute-start(f32[2,128]{1,0:T(2,128)S(1)} %fusion.73), channel_id=1, source_target_pairs={{0,16},{16,0},{1,17},{17,1},{2,18},{18,2},{3,19},{19,3},{4,20},{20... | collective-permute-start | bytes 3080 | tf_op jit(solution)/shard_map/ppermute | solution.py:17
  (15 other events, 145.9 us)

commit v8 on v6

--- a/solution.py
+++ b/solution.py
@@ -90,13 +90,13 @@
     part_a = jnp.einsum("tk,jk->tj", all_a, basis_a, preferred_element_type=jnp.float32)
     rot_a_block = (xor_sum(part_a, "owner", owners) * live[:, None]).astype(jnp.bfloat16)
     pieces = []
-    step = m_block // 2
+    step = m_block // 4
     for start in range(0, m_block, step):
         part_g = jnp.einsum(
             "tk,jk->tj", all_g, basis_g[start:start + step], preferred_element_type=jnp.float32
         )
-        pieces.append(xor_sum(part_g, "owner", owners))
-    rot_g = (jnp.concatenate(pieces, axis=1) * live[:, None]).astype(jnp.bfloat16)
+        pieces.append((xor_sum(part_g, "owner", owners) * live[:, None]).astype(jnp.bfloat16))
+    rot_g = jnp.concatenate(pieces, axis=1)
 
     rot_a = half_gather(rot_a_block, owners, readers)
 

time: 137 us -> 147 us (1.073)
  waiting for transfers between devices: 57.2 us -> 63.8 us
  starting transfers between devices: 26.4 us -> 28.7 us
    ppermute x22 -> x24, waiting for transfers between devices: 56.5 us -> 63.1 us  [xor_round(): parts.append(lax.ppermute(held, axis, [(i, i ^ c) for i in range(size)]))]
    ppermute x22 -> x24, starting transfers between devices: 26.4 us -> 28.6 us  [xor_round(): parts.append(lax.ppermute(held, axis, [(i, i ^ c) for i in range(size)]))]
    dot_general x2 -> x4, matrix products: 12.2 us -> 14.1 us  [local(): jnp.einsum('tk,jk->tj', all_g, basis_g[start:start + step], preferred_ele...]
  transfers between devices with their start and end apart: 23 -> 25, of which waited for: 15 -> 17; matrix products, arithmetic and copies ran while one was open for 20% -> 18% of each run, Pallas kernels for 0% -> 0%
where the time goes in v8:
time: 147 us
  waiting for transfers between devices  63.8 us (43%)
  starting transfers between devices  28.7 us (20%)
  matrix products  20.9 us (14%)
  between operations  14.4 us (10%)
  other arithmetic  12.8 us (9%)
  local copies, waits for them, and re-layouts  6.15 us (4%)
    ppermute x24, waiting for transfers between devices, xor_round(): parts.append(lax.ppermute(held, axis, [(i, i ^ c) for i in range(size)]))  63.1 us
    ppermute x24, starting transfers between devices, xor_round(): parts.append(lax.ppermute(held, axis, [(i, i ^ c) for i in range(size)]))  28.6 us
    dot_general x4, matrix products, local(): jnp.einsum('tk,jk->tj', all_g, basis_g[start:start + step], preferred_ele...  14.1 us
    dot_general x1, matrix products, local(): jnp.einsum('stm,smn->stn', g_rows, scaled, preferred_element_type=jnp.flo...  6.37 us
    convert_element_type x1, other arithmetic, local(): denom = eigvals.astype(jnp.float32)  5.91 us
  transfers between devices with their start and end apart: 25, of which 17 were waited for; matrix products, arithmetic and copies ran while one was open for 18% of the time, Pallas kernels for 0%

profile of v8, /device:TPU:0, one launch (start us, length us, event | category | flops | bytes accessed | tf_op | source)
XLA Modules:
  0.0 146.7 jit_solution(1411168641226494671)
XLA Ops:
  7.9 5.1 %collective-permute-start.6 = (bf16[1,16,2048]{2,1,0:T(8,128)(2,1)}, bf16[1,16,2048]{2,1,0:T(8,128)(2,1)S(1)}, u32[]{:S(2)}, u32[]{:S(2)}) collective-permute-start(bf16[1,16,2048]{2,1,0:T(8,128)(2,1)} %bitcast.123), channel_id=1, source_target_pairs={{0,12},{1,13},{2,14},{3,15},{4,8},{5,9},{6,10},{7,11},{8,4},{9,5},... | collective-permute-start | bytes 196616 | tf_op jit(solution)/shard_map/ppermute | solution.py:17
  22.7 8.7 %collective-permute-done.9 = bf16[4,16,2048]{2,1,0:T(8,128)(2,1)S(1)} collective-permute-done((bf16[4,16,2048]{2,1,0:T(8,128)(2,1)S(1)}, bf16[4,16,2048]{2,1,0:T(8,128)(2,1)S(1)}, u32[]{:S(2)}, u32[]{:S(2)}) %collective-permute-start.9) | collective-permute-done | bytes 262176 | tf_op jit(solution)/shard_map/ppermute | solution.py:17
  31.5 5.7 %collective-permute-done.7 = bf16[4,16,2048]{2,1,0:T(8,128)(2,1)S(1)} collective-permute-done((bf16[4,16,2048]{2,1,0:T(8,128)(2,1)S(1)}, bf16[4,16,2048]{2,1,0:T(8,128)(2,1)S(1)}, u32[]{:S(2)}, u32[]{:S(2)}) %collective-permute-start.7) | collective-permute-done | bytes 262176 | tf_op jit(solution)/shard_map/ppermute | solution.py:17
  40.3 6.7 %collective-permute-done.10 = f32[256,256]{1,0:T(8,128)S(1)} collective-permute-done((f32[256,256]{1,0:T(8,128)S(1)}, f32[256,256]{1,0:T(8,128)S(1)}, u32[]{:S(2)}, u32[]{:S(2)}) %collective-permute-start.10) | collective-permute-done | bytes 262176 | tf_op jit(solution)/shard_map/ppermute | solution.py:17
  47.2 2.2 %collective-permute-start.13 = (bf16[1,256,256]{2,1,0:T(8,128)(2,1)S(1)}, bf16[1,256,256]{2,1,0:T(8,128)(2,1)S(1)}, u32[]{:S(2)}, u32[]{:S(2)}) collective-permute-start(bf16[1,256,256]{2,1,0:T(8,128)(2,1)S(1)} %multiply_convert_fusion), channel_id=1, source_target_pairs={{0,12},{1,13},{2,14},{3,15},{4,8},{5,9},{6,10},{7,11},{8,4},{9,5},... | collective-permute-start | bytes 393224 | tf_op jit(solution)/shard_map/ppermute | solution.py:17
  49.8 1.9 %collective-permute-start.11 = (bf16[1,256,256]{2,1,0:T(8,128)(2,1)S(1)}, bf16[1,256,256]{2,1,0:T(8,128)(2,1)S(1)}, u32[]{:S(2)}, u32[]{:S(2)}) collective-permute-start(bf16[1,256,256]{2,1,0:T(8,128)(2,1)S(1)} %multiply_convert_fusion), channel_id=1, source_target_pairs={{0,8},{1,9},{2,10},{3,11},{4,12},{5,13},{6,14},{7,15},{8,0},{9,1},... | collective-permute-start | bytes 393224 | tf_op jit(solution)/shard_map/ppermute | solution.py:17
  51.8 6.5 %collective-permute-done.13 = bf16[1,256,256]{2,1,0:T(8,128)(2,1)S(1)} collective-permute-done((bf16[1,256,256]{2,1,0:T(8,128)(2,1)S(1)}, bf16[1,256,256]{2,1,0:T(8,128)(2,1)S(1)}, u32[]{:S(2)}, u32[]{:S(2)}) %collective-permute-start.13) | collective-permute-done | bytes 131104 | tf_op jit(solution)/shard_map/ppermute | solution.py:17
  58.2 4.9 %collective-permute-done.12 = bf16[1,256,256]{2,1,0:T(8,128)(2,1)S(1)} collective-permute-done((bf16[1,256,256]{2,1,0:T(8,128)(2,1)S(1)}, bf16[1,256,256]{2,1,0:T(8,128)(2,1)S(1)}, u32[]{:S(2)}, u32[]{:S(2)}) %collective-permute-start.12) | collective-permute-done | bytes 131104 | tf_op jit(solution)/shard_map/ppermute | solution.py:17
  63.1 7.3 %collective-permute-done.11 = bf16[1,256,256]{2,1,0:T(8,128)(2,1)S(1)} collective-permute-done((bf16[1,256,256]{2,1,0:T(8,128)(2,1)S(1)}, bf16[1,256,256]{2,1,0:T(8,128)(2,1)S(1)}, u32[]{:S(2)}, u32[]{:S(2)}) %collective-permute-start.11) | collective-permute-done | bytes 131104 | tf_op jit(solution)/shard_map/ppermute | solution.py:17
  73.3 5.9 %convert_element_type.57 = f32[896,2048]{1,0:T(8,128)} convert(bf16[896,2048]{1,0:T(8,128)(2,1)} %param.11) | non-fusion elementwise | flops 1835008 | bytes 11010048 | tf_op jit(solution)/shard_map/convert_element_type | solution.py:103
  79.8 5.6 %collective-permute-done.14 = bf16[2,256,256]{2,1,0:T(8,128)(2,1)S(1)} collective-permute-done((bf16[2,256,256]{2,1,0:T(8,128)(2,1)S(1)}, bf16[2,256,256]{2,1,0:T(8,128)(2,1)S(1)}, u32[]{:S(2)}, u32[]{:S(2)}) %collective-permute-start.14) | collective-permute-done | bytes 262176 | tf_op jit(solution)/shard_map/ppermute | solution.py:17
  87.8 4.4 %fusion.9 = f32[256,224]{0,1:T(8,128)S(1)} fusion(bf16[256,7168]{1,0:T(8,128)(2,1)} %all-gather.2.cloned.1.call-done, bf16[896,7168]{1,0:T(8,128)(2,1)} %param.10), kind=kOutput, calls=%fused_computation.13 | convolution fusion | flops 822083584 | bytes 7110656 | tf_op jit(solution)/shard_map/tk,jk->tj/dot_general | solution.py:95
  93.7 3.2 %fusion.7 = f32[256,224]{0,1:T(8,128)S(1)} fusion(bf16[256,7168]{1,0:T(8,128)(2,1)S(1)} %copy-done.1, bf16[896,7168]{1,0:T(8,128)(2,1)} %param.10), kind=kOutput, calls=%fused_computation.11 | convolution fusion | flops 822083584 | bytes 7110656 | tf_op jit(solution)/shard_map/tk,jk->tj/dot_general | solution.py:95
  97.6 3.2 %fusion.5 = f32[256,224]{0,1:T(8,128)S(1)} fusion(bf16[256,7168]{1,0:T(8,128)(2,1)S(1)} %copy-done.1, bf16[896,7168]{1,0:T(8,128)(2,1)} %param.10), kind=kOutput, calls=%fused_computation.9 | convolution fusion | flops 822083584 | bytes 7110656 | tf_op jit(solution)/shard_map/tk,jk->tj/dot_general | solution.py:95
  102.3 3.2 %fusion.3 = f32[256,224]{0,1:T(8,128)S(1)} fusion(bf16[256,7168]{1,0:T(8,128)(2,1)S(1)} %copy-done.1, bf16[896,7168]{1,0:T(8,128)(2,1)} %param.10), kind=kOutput, calls=%fused_computation.7 | convolution fusion | flops 822083584 | bytes 7110656 | tf_op jit(solution)/shard_map/tk,jk->tj/dot_general | solution.py:95
  106.6 3.9 %collective-permute-done.2 = f32[256,224]{0,1:T(8,128)} collective-permute-done((f32[256,224]{0,1:T(8,128)S(1)}, f32[256,224]{0,1:T(8,128)}, u32[]{:S(2)}, u32[]{:S(2)}) %collective-permute-start.2) | collective-permute-done | bytes 229408 | tf_op jit(solution)/shard_map/ppermute | solution.py:17
  111.7 3.0 %collective-permute-done.3 = f32[256,224]{0,1:T(8,128)} collective-permute-done((f32[256,224]{0,1:T(8,128)S(1)}, f32[256,224]{0,1:T(8,128)}, u32[]{:S(2)}, u32[]{:S(2)}) %collective-permute-start.3) | collective-permute-done | bytes 229408 | tf_op jit(solution)/shard_map/ppermute | solution.py:17
  115.9 6.4 %fusion.12 = f32[2,128]{1,0:T(2,128)S(1)} fusion(bf16[2,128,2048]{2,1,0:T(8,128)(2,1)S(1)} %reshape_reshape.7, f32[896,2048]{1,0:T(8,128)} %convert_element_type.57, bf16[2,128,224]{1,2,0:T(8,128)(2,1)S(1)} %get-tuple-element.11, bf16[2,128,224]{1,2,0:T(8,128)(2,1)S(1)} %get-tuple-element.10, bf16[2,128,224]{1,2,0:T(8,128)(2,1)S(1)} %get-tuple-element.9, ...), kind=kOutput, calls=%fused_computation.16 | convolution fusion | flops 1891630848 | bytes 8848384 | tf_op jit(solution)/shard_map/stm,smn->stn/dot_general | solution.py:108
  122.4 1.6 %collective-permute-start.17 = (f32[2,128]{1,0:T(2,128)S(1)}, f32[2,128]{1,0:T(2,128)S(1)}, u32[]{:S(2)}, u32[]{:S(2)}) collective-permute-start(f32[2,128]{1,0:T(2,128)S(1)} %get-tuple-element.7), channel_id=1, source_target_pairs={{0,8},{1,9},{2,10},{3,11},{4,12},{5,13},{6,14},{7,15},{8,0},{9,1},... | collective-permute-start | bytes 3080 | tf_op jit(solution)/shard_map/ppermute | solution.py:17
  124.1 2.7 %collective-permute-start.19 = (f32[2,128]{1,0:T(2,128)S(1)}, f32[2,128]{1,0:T(2,128)S(1)}, u32[]{:S(2)}, u32[]{:S(2)}) collective-permute-start(f32[2,128]{1,0:T(2,128)S(1)} %get-tuple-element.7), channel_id=1, source_target_pairs={{0,12},{1,13},{2,14},{3,15},{4,8},{5,9},{6,10},{7,11},{8,4},{9,5},... | collective-permute-start | bytes 3080 | tf_op jit(solution)/shard_map/ppermute | solution.py:17
  127.0 2.5 %collective-permute-done.19 = f32[2,128]{1,0:T(2,128)S(1)} collective-permute-done((f32[2,128]{1,0:T(2,128)S(1)}, f32[2,128]{1,0:T(2,128)S(1)}, u32[]{:S(2)}, u32[]{:S(2)}) %collective-permute-start.19) | collective-permute-done | bytes 1056 | tf_op jit(solution)/shard_map/ppermute | solution.py:17
  129.5 1.8 %collective-permute-start.21 = (f32[2,128]{1,0:T(2,128)S(1)}, f32[2,128]{1,0:T(2,128)S(1)}, u32[]{:S(2)}, u32[]{:S(2)}) collective-permute-start(f32[2,128]{1,0:T(2,128)S(1)} %fusion.77), channel_id=1, source_target_pairs={{0,1},{1,0},{2,3},{3,2},{4,5},{5,4},{6,7},{7,6},{8,9},{9,8},{10,11... | collective-permute-start | bytes 3080 | tf_op jit(solution)/shard_map/ppermute | solution.py:17
  132.5 2.4 %collective-permute-done.20 = f32[2,128]{1,0:T(2,128)S(1)} collective-permute-done((f32[2,128]{1,0:T(2,128)S(1)}, f32[2,128]{1,0:T(2,128)S(1)}, u32[]{:S(2)}, u32[]{:S(2)}) %collective-permute-start.20) | collective-permute-done | bytes 1056 | tf_op jit(solution)/shard_map/ppermute | solution.py:17
  136.5 2.1 %collective-permute-done.23 = f32[2,128]{1,0:T(2,128)S(1)} collective-permute-done((f32[2,128]{1,0:T(2,128)S(1)}, f32[2,128]{1,0:T(2,128)S(1)}, u32[]{:S(2)}, u32[]{:S(2)}) %collective-permute-start.23) | collective-permute-done | bytes 1056 | tf_op jit(solution)/shard_map/ppermute | solution.py:17
  (92 shorter events, 31.2 us)
Async XLA Ops:
  7.2 80.6 %all-gather.2.cloned.1.call-start = ((), (), s32[]{:S(2)}) async-start(), calls=%async_computation | async-start | bytes 3899392 | tf_op jit(solution)/shard_map/all_gather | solution.py:84
  7.9 8.6 %collective-permute-start.6 = (bf16[1,16,2048]{2,1,0:T(8,128)(2,1)}, bf16[1,16,2048]{2,1,0:T(8,128)(2,1)S(1)}, u32[]{:S(2)}, u32[]{:S(2)}) collective-permute-start(bf16[1,16,2048]{2,1,0:T(8,128)(2,1)} %bitcast.123), channel_id=1, source_target_pairs={{0,12},{1,13},{2,14},{3,15},{4,8},{5,9},{6,10},{7,11},{8,4},{9,5},... | collective-permute-start | bytes 196616 | tf_op jit(solution)/shard_map/ppermute | solution.py:17
  13.0 4.9 %collective-permute-start.5 = (bf16[1,16,2048]{2,1,0:T(8,128)(2,1)}, bf16[1,16,2048]{2,1,0:T(8,128)(2,1)S(1)}, u32[]{:S(2)}, u32[]{:S(2)}) collective-permute-start(bf16[1,16,2048]{2,1,0:T(8,128)(2,1)} %bitcast.124), channel_id=1, source_target_pairs={{0,4},{1,5},{2,6},{3,7},{4,0},{5,1},{6,2},{7,3},{8,12},{9,13},{10,... | collective-permute-start | bytes 196616 | tf_op jit(solution)/shard_map/ppermute | solution.py:17
  13.0 5.8 %collective-permute-start.4 = (bf16[1,16,2048]{2,1,0:T(8,128)(2,1)}, bf16[1,16,2048]{2,1,0:T(8,128)(2,1)S(1)}, u32[]{:S(2)}, u32[]{:S(2)}) collective-permute-start(bf16[1,16,2048]{2,1,0:T(8,128)(2,1)} %bitcast.125), channel_id=1, source_target_pairs={{0,8},{1,9},{2,10},{3,11},{4,12},{5,13},{6,14},{7,15},{8,0},{9,1},... | collective-permute-start | bytes 196616 | tf_op jit(solution)/shard_map/ppermute | solution.py:17
  20.4 11.1 %collective-permute-start.9 = (bf16[4,16,2048]{2,1,0:T(8,128)(2,1)S(1)}, bf16[4,16,2048]{2,1,0:T(8,128)(2,1)S(1)}, u32[]{:S(2)}, u32[]{:S(2)}) collective-permute-start(bf16[4,16,2048]{2,1,0:T(8,128)(2,1)S(1)} %broadcast_select_fusion.1), channel_id=1, source_target_pairs={{0,3},{1,2},{2,1},{3,0},{4,7},{5,6},{6,5},{7,4},{8,11},{9,10},{10,... | collective-permute-start | bytes 786440 | tf_op jit(solution)/shard_map/ppermute | solution.py:17
  20.5 11.0 %collective-permute-start.8 = (bf16[4,16,2048]{2,1,0:T(8,128)(2,1)S(1)}, bf16[4,16,2048]{2,1,0:T(8,128)(2,1)S(1)}, u32[]{:S(2)}, u32[]{:S(2)}) collective-permute-start(bf16[4,16,2048]{2,1,0:T(8,128)(2,1)S(1)} %broadcast_select_fusion.1), channel_id=1, source_target_pairs={{0,1},{1,0},{2,3},{3,2},{4,5},{5,4},{6,7},{7,6},{8,9},{9,8},{10,11... | collective-permute-start | bytes 786440 | tf_op jit(solution)/shard_map/ppermute | solution.py:17
  22.1 15.0 %collective-permute-start.7 = (bf16[4,16,2048]{2,1,0:T(8,128)(2,1)S(1)}, bf16[4,16,2048]{2,1,0:T(8,128)(2,1)S(1)}, u32[]{:S(2)}, u32[]{:S(2)}) collective-permute-start(bf16[4,16,2048]{2,1,0:T(8,128)(2,1)S(1)} %broadcast_select_fusion.1), channel_id=1, source_target_pairs={{0,2},{1,3},{2,0},{3,1},{4,6},{5,7},{6,4},{7,5},{8,10},{9,11},{10,... | collective-permute-start | bytes 786440 | tf_op jit(solution)/shard_map/ppermute | solution.py:17
  38.7 8.3 %collective-permute-start.10 = (f32[256,256]{1,0:T(8,128)S(1)}, f32[256,256]{1,0:T(8,128)S(1)}, u32[]{:S(2)}, u32[]{:S(2)}) collective-permute-start(f32[256,256]{1,0:T(8,128)S(1)} %fusion.68), channel_id=1, source_target_pairs={{0,16},{16,0},{1,17},{17,1},{2,18},{18,2},{3,19},{19,3},{4,20},{20... | collective-permute-start | bytes 786440 | tf_op jit(solution)/shard_map/ppermute | solution.py:17
  47.2 11.0 %collective-permute-start.13 = (bf16[1,256,256]{2,1,0:T(8,128)(2,1)S(1)}, bf16[1,256,256]{2,1,0:T(8,128)(2,1)S(1)}, u32[]{:S(2)}, u32[]{:S(2)}) collective-permute-start(bf16[1,256,256]{2,1,0:T(8,128)(2,1)S(1)} %multiply_convert_fusion), channel_id=1, source_target_pairs={{0,12},{1,13},{2,14},{3,15},{4,8},{5,9},{6,10},{7,11},{8,4},{9,5},... | collective-permute-start | bytes 393224 | tf_op jit(solution)/shard_map/ppermute | solution.py:17
  49.5 13.6 %collective-permute-start.12 = (bf16[1,256,256]{2,1,0:T(8,128)(2,1)S(1)}, bf16[1,256,256]{2,1,0:T(8,128)(2,1)S(1)}, u32[]{:S(2)}, u32[]{:S(2)}) collective-permute-start(bf16[1,256,256]{2,1,0:T(8,128)(2,1)S(1)} %multiply_convert_fusion), channel_id=1, source_target_pairs={{0,4},{1,5},{2,6},{3,7},{4,0},{5,1},{6,2},{7,3},{8,12},{9,13},{10,... | collective-permute-start | bytes 393224 | tf_op jit(solution)/shard_map/ppermute | solution.py:17
  49.8 20.6 %collective-permute-start.11 = (bf16[1,256,256]{2,1,0:T(8,128)(2,1)S(1)}, bf16[1,256,256]{2,1,0:T(8,128)(2,1)S(1)}, u32[]{:S(2)}, u32[]{:S(2)}) collective-permute-start(bf16[1,256,256]{2,1,0:T(8,128)(2,1)S(1)} %multiply_convert_fusion), channel_id=1, source_target_pairs={{0,8},{1,9},{2,10},{3,11},{4,12},{5,13},{6,14},{7,15},{8,0},{9,1},... | collective-permute-start | bytes 393224 | tf_op jit(solution)/shard_map/ppermute | solution.py:17
  71.1 8.6 %collective-permute-start.16 = (bf16[2,256,256]{2,1,0:T(8,128)(2,1)S(1)}, bf16[2,256,256]{2,1,0:T(8,128)(2,1)S(1)}, u32[]{:S(2)}, u32[]{:S(2)}) collective-permute-start(bf16[2,256,256]{2,1,0:T(8,128)(2,1)S(1)} %broadcast_select_fusion), channel_id=1, source_target_pairs={{0,3},{1,2},{2,1},{3,0},{4,7},{5,6},{6,5},{7,4},{8,11},{9,10},{10,... | collective-permute-start | bytes 786440 | tf_op jit(solution)/shard_map/ppermute | solution.py:17
  72.2 7.6 %collective-permute-start.15 = (bf16[2,256,256]{2,1,0:T(8,128)(2,1)S(1)}, bf16[2,256,256]{2,1,0:T(8,128)(2,1)S(1)}, u32[]{:S(2)}, u32[]{:S(2)}) collective-permute-start(bf16[2,256,256]{2,1,0:T(8,128)(2,1)S(1)} %broadcast_select_fusion), channel_id=1, source_target_pairs={{0,1},{1,0},{2,3},{3,2},{4,5},{5,4},{6,7},{7,6},{8,9},{9,8},{10,11... | collective-permute-start | bytes 786440 | tf_op jit(solution)/shard_map/ppermute | solution.py:17
  72.8 12.6 %collective-permute-start.14 = (bf16[2,256,256]{2,1,0:T(8,128)(2,1)S(1)}, bf16[2,256,256]{2,1,0:T(8,128)(2,1)S(1)}, u32[]{:S(2)}, u32[]{:S(2)}) collective-permute-start(bf16[2,256,256]{2,1,0:T(8,128)(2,1)S(1)} %broadcast_select_fusion), channel_id=1, source_target_pairs={{0,2},{1,3},{2,0},{3,1},{4,6},{5,7},{6,4},{7,5},{8,10},{9,11},{10,... | collective-permute-start | bytes 786440 | tf_op jit(solution)/shard_map/ppermute | solution.py:17
  92.2 13.9 %collective-permute-start = (f32[256,224]{0,1:T(8,128)S(1)}, f32[256,224]{0,1:T(8,128)S(1)}, u32[]{:S(2)}, u32[]{:S(2)}) collective-permute-start(f32[256,224]{0,1:T(8,128)S(1)} %fusion.9), channel_id=1, source_target_pairs={{0,16},{16,0},{1,17},{17,1},{2,18},{18,2},{3,19},{19,3},{4,20},{20... | collective-permute-start | bytes 688136 | tf_op jit(solution)/shard_map/ppermute | solution.py:17
  97.0 9.4 %collective-permute-start.1 = (f32[256,224]{0,1:T(8,128)S(1)}, f32[256,224]{0,1:T(8,128)S(1)}, u32[]{:S(2)}, u32[]{:S(2)}) collective-permute-start(f32[256,224]{0,1:T(8,128)S(1)} %fusion.7), channel_id=1, source_target_pairs={{0,16},{16,0},{1,17},{17,1},{2,18},{18,2},{3,19},{19,3},{4,20},{20... | collective-permute-start | bytes 688136 | tf_op jit(solution)/shard_map/ppermute | solution.py:17
  100.8 9.8 %collective-permute-start.2 = (f32[256,224]{0,1:T(8,128)S(1)}, f32[256,224]{0,1:T(8,128)}, u32[]{:S(2)}, u32[]{:S(2)}) collective-permute-start(f32[256,224]{0,1:T(8,128)S(1)} %fusion.5), channel_id=1, source_target_pairs={{0,16},{16,0},{1,17},{17,1},{2,18},{18,2},{3,19},{19,3},{4,20},{20... | collective-permute-start | bytes 688136 | tf_op jit(solution)/shard_map/ppermute | solution.py:17
  105.5 9.2 %collective-permute-start.3 = (f32[256,224]{0,1:T(8,128)S(1)}, f32[256,224]{0,1:T(8,128)}, u32[]{:S(2)}, u32[]{:S(2)}) collective-permute-start(f32[256,224]{0,1:T(8,128)S(1)} %fusion.3), channel_id=1, source_target_pairs={{0,16},{16,0},{1,17},{17,1},{2,18},{18,2},{3,19},{19,3},{4,20},{20... | collective-permute-start | bytes 688136 | tf_op jit(solution)/shard_map/ppermute | solution.py:17
  122.3 4.5 %collective-permute-start.18 = (f32[2,128]{1,0:T(2,128)S(1)}, f32[2,128]{1,0:T(2,128)S(1)}, u32[]{:S(2)}, u32[]{:S(2)}) collective-permute-start(f32[2,128]{1,0:T(2,128)S(1)} %get-tuple-element.7), channel_id=1, source_target_pairs={{0,4},{1,5},{2,6},{3,7},{4,0},{5,1},{6,2},{7,3},{8,12},{9,13},{10,... | collective-permute-start | bytes 3080 | tf_op jit(solution)/shard_map/ppermute | solution.py:17
  122.4 4.5 %collective-permute-start.17 = (f32[2,128]{1,0:T(2,128)S(1)}, f32[2,128]{1,0:T(2,128)S(1)}, u32[]{:S(2)}, u32[]{:S(2)}) collective-permute-start(f32[2,128]{1,0:T(2,128)S(1)} %get-tuple-element.7), channel_id=1, source_target_pairs={{0,8},{1,9},{2,10},{3,11},{4,12},{5,13},{6,14},{7,15},{8,0},{9,1},... | collective-permute-start | bytes 3080 | tf_op jit(solution)/shard_map/ppermute | solution.py:17
  124.1 5.4 %collective-permute-start.19 = (f32[2,128]{1,0:T(2,128)S(1)}, f32[2,128]{1,0:T(2,128)S(1)}, u32[]{:S(2)}, u32[]{:S(2)}) collective-permute-start(f32[2,128]{1,0:T(2,128)S(1)} %get-tuple-element.7), channel_id=1, source_target_pairs={{0,12},{1,13},{2,14},{3,15},{4,8},{5,9},{6,10},{7,11},{8,4},{9,5},... | collective-permute-start | bytes 3080 | tf_op jit(solution)/shard_map/ppermute | solution.py:17
  129.4 3.1 %collective-permute-start.22 = (f32[2,128]{1,0:T(2,128)S(1)}, f32[2,128]{1,0:T(2,128)S(1)}, u32[]{:S(2)}, u32[]{:S(2)}) collective-permute-start(f32[2,128]{1,0:T(2,128)S(1)} %fusion.77), channel_id=1, source_target_pairs={{0,3},{1,2},{2,1},{3,0},{4,7},{5,6},{6,5},{7,4},{8,11},{9,10},{10,... | collective-permute-start | bytes 3080 | tf_op jit(solution)/shard_map/ppermute | solution.py:17
  131.4 3.6 %collective-permute-start.20 = (f32[2,128]{1,0:T(2,128)S(1)}, f32[2,128]{1,0:T(2,128)S(1)}, u32[]{:S(2)}, u32[]{:S(2)}) collective-permute-start(f32[2,128]{1,0:T(2,128)S(1)} %fusion.77), channel_id=1, source_target_pairs={{0,2},{1,3},{2,0},{3,1},{4,6},{5,7},{6,4},{7,5},{8,10},{9,11},{10,... | collective-permute-start | bytes 3080 | tf_op jit(solution)/shard_map/ppermute | solution.py:17
  134.9 3.6 %collective-permute-start.23 = (f32[2,128]{1,0:T(2,128)S(1)}, f32[2,128]{1,0:T(2,128)S(1)}, u32[]{:S(2)}, u32[]{:S(2)}) collective-permute-start(f32[2,128]{1,0:T(2,128)S(1)} %fusion.76), channel_id=1, source_target_pairs={{0,16},{16,0},{1,17},{17,1},{2,18},{18,2},{3,19},{19,3},{4,20},{20... | collective-permute-start | bytes 3080 | tf_op jit(solution)/shard_map/ppermute | solution.py:17
  (4 other events, 62.8 us)
Sparse Core Ops, SparseCore 0:
  10.3 60.4 all-gather.1

commit v9 on v5

--- a/solution.py
+++ b/solution.py
@@ -41,16 +41,19 @@
     return x
 
 
-def ordered_gather(block, owners, readers):
+def ordered_gather(block, owners, readers, after=None):
     reader_index = lax.axis_index("reader")
     owner_index = lax.axis_index("owner") if owners > 1 else 0
     group_size = readers // owners
     bits = [1 << k for k in range(readers.bit_length() - 1)][::-1]
     target = owner_index * group_size
     held = block[None]
-    for group in bit_groups(bits):
+    groups = bit_groups(bits)
+    for group in groups:
         high = sum(bit for bit in group if bit >= group_size)
         low = [bit for bit in group if bit < group_size]
+        if after is not None and group is groups[-1]:
+            held, _ = lax.optimization_barrier((held, after))
         stacked = xor_round(held, "reader", readers, group)
         c_high = (reader_index ^ target) & high
         picks = []
@@ -64,8 +67,8 @@
     return held
 
 
-def half_gather(block, owners, readers):
-    held = ordered_gather(block, owners, readers)
+def half_gather(block, owners, readers, after):
+    held = ordered_gather(block, owners, readers, after)
     return jnp.transpose(held, (1, 0, 2)).reshape(block.shape[0], -1)
 
 
@@ -89,12 +92,18 @@
 
     part_a = jnp.einsum("tk,jk->tj", all_a, basis_a, preferred_element_type=jnp.float32)
     rot_a_block = (xor_sum(part_a, "owner", owners) * live[:, None]).astype(jnp.bfloat16)
-    part_g = jnp.einsum("tk,jk->tj", all_g, basis_g, preferred_element_type=jnp.float32)
-    rot_g = (xor_sum(part_g, "owner", owners) * live[:, None]).astype(jnp.bfloat16)
+    step = m_block // 4
+    parts_g = [
+        jnp.einsum("tk,jk->tj", all_g, basis_g[start:start + step], preferred_element_type=jnp.float32)
+        for start in range(0, m_block, step)
+    ]
+    parts_g[0], eig_after = lax.optimization_barrier((parts_g[0], eigvals))
+    pieces = [(xor_sum(part_g, "owner", owners) * live[:, None]).astype(jnp.bfloat16) for part_g in parts_g]
+    rot_g = jnp.concatenate(pieces, axis=1)
 
-    rot_a = half_gather(rot_a_block, owners, readers)
+    rot_a = half_gather(rot_a_block, owners, readers, parts_g[0])
 
-    denom = eigvals.astype(jnp.float32)
+    denom = eig_after.astype(jnp.float32)
     g_rows = rot_g.reshape(slots, SEQ, m_block)
     a_rows = rot_a.reshape(slots, SEQ, width)
     outer = jnp.einsum("smt,smn->stn", g_rows, a_rows, preferred_element_type=jnp.float32)

time: 138 us -> 140 us (1.014)
  matrix products: 17.8 us -> 21.2 us
  other arithmetic: 12.2 us -> 9.47 us
  starting transfers between devices: 26 us -> 28.6 us
    dot_general x1 -> x4, matrix products: 10.7 us -> 14.2 us  [local(): jnp.einsum('tk,jk->tj', all_g, basis_g[start:start + step], preferred_ele...]
    ppermute x21 -> x24, starting transfers between devices: 26 us -> 28.5 us  [xor_round(): parts.append(lax.ppermute(held, axis, [(i, i ^ c) for i in range(size)]))]
    convert_element_type x1 -> x2, other arithmetic: 5.92 us -> 4.61 us  [the longest x1 3.84 us: local(): denom = eig_after.astype(jnp.float32)]
    ppermute x21 -> x24, waiting for transfers between devices: 60.7 us -> 59.6 us  [xor_round(): parts.append(lax.ppermute(held, axis, [(i, i ^ c) for i in range(size)]))]
  transfers between devices with their start and end apart: 22 -> 25, of which waited for: 17 -> 15; matrix products, arithmetic and copies ran while one was open for 11% -> 16% of each run, Pallas kernels for 0% -> 0%
where the time goes in v9:
time: 140 us
  waiting for transfers between devices  60.3 us (43%)
  starting transfers between devices  28.6 us (20%)
  matrix products  21.2 us (15%)
  between operations  14.4 us (10%)
  other arithmetic  9.47 us (7%)
  local copies, waits for them, and re-layouts  6.16 us (4%)
    ppermute x24, waiting for transfers between devices, xor_round(): parts.append(lax.ppermute(held, axis, [(i, i ^ c) for i in range(size)]))  59.6 us
    ppermute x24, starting transfers between devices, xor_round(): parts.append(lax.ppermute(held, axis, [(i, i ^ c) for i in range(size)]))  28.5 us
    dot_general x4, matrix products, local(): jnp.einsum('tk,jk->tj', all_g, basis_g[start:start + step], preferred_ele...  14.2 us
    dot_general x1, matrix products, local(): jnp.einsum('stm,smn->stn', g_rows, scaled, preferred_element_type=jnp.flo...  6.52 us
    convert_element_type x1, other arithmetic, local(): denom = eig_after.astype(jnp.float32)  3.84 us
  transfers between devices with their start and end apart: 25, of which 15 were waited for; matrix products, arithmetic and copies ran while one was open for 16% of the time, Pallas kernels for 0%

profile of v9, /device:TPU:0, one launch (start us, length us, event | category | flops | bytes accessed | tf_op | source)
XLA Modules:
  0.0 140.1 jit_solution(5780877801302214896)
XLA Ops:
  7.9 5.1 %collective-permute-start.6 = (bf16[1,16,2048]{2,1,0:T(8,128)(2,1)}, bf16[1,16,2048]{2,1,0:T(8,128)(2,1)S(1)}, u32[]{:S(2)}, u32[]{:S(2)}) collective-permute-start(bf16[1,16,2048]{2,1,0:T(8,128)(2,1)} %bitcast.125), channel_id=1, source_target_pairs={{0,12},{1,13},{2,14},{3,15},{4,8},{5,9},{6,10},{7,11},{8,4},{9,5},... | collective-permute-start | bytes 196616 | tf_op jit(solution)/shard_map/ppermute | solution.py:17
  20.5 1.6 %collective-permute-start.8 = (bf16[4,16,2048]{2,1,0:T(8,128)(2,1)S(1)}, bf16[4,16,2048]{2,1,0:T(8,128)(2,1)S(1)}, u32[]{:S(2)}, u32[]{:S(2)}) collective-permute-start(bf16[4,16,2048]{2,1,0:T(8,128)(2,1)S(1)} %broadcast_select_fusion), channel_id=1, source_target_pairs={{0,1},{1,0},{2,3},{3,2},{4,5},{5,4},{6,7},{7,6},{8,9},{9,8},{10,11... | collective-permute-start | bytes 786440 | tf_op jit(solution)/shard_map/ppermute | solution.py:17
  22.7 8.7 %collective-permute-done.9 = bf16[4,16,2048]{2,1,0:T(8,128)(2,1)S(1)} collective-permute-done((bf16[4,16,2048]{2,1,0:T(8,128)(2,1)S(1)}, bf16[4,16,2048]{2,1,0:T(8,128)(2,1)S(1)}, u32[]{:S(2)}, u32[]{:S(2)}) %collective-permute-start.9) | collective-permute-done | bytes 262176 | tf_op jit(solution)/shard_map/ppermute | solution.py:17
  31.5 5.7 %collective-permute-done.7 = bf16[4,16,2048]{2,1,0:T(8,128)(2,1)S(1)} collective-permute-done((bf16[4,16,2048]{2,1,0:T(8,128)(2,1)S(1)}, bf16[4,16,2048]{2,1,0:T(8,128)(2,1)S(1)}, u32[]{:S(2)}, u32[]{:S(2)}) %collective-permute-start.7) | collective-permute-done | bytes 262176 | tf_op jit(solution)/shard_map/ppermute | solution.py:17
  40.3 6.7 %collective-permute-done.10 = f32[256,256]{1,0:T(8,128)S(1)} collective-permute-done((f32[256,256]{1,0:T(8,128)S(1)}, f32[256,256]{1,0:T(8,128)S(1)}, u32[]{:S(2)}, u32[]{:S(2)}) %collective-permute-start.10) | collective-permute-done | bytes 262176 | tf_op jit(solution)/shard_map/ppermute | solution.py:17
  47.2 2.2 %collective-permute-start.13 = (bf16[1,256,256]{2,1,0:T(8,128)(2,1)S(1)}, bf16[1,256,256]{2,1,0:T(8,128)(2,1)S(1)}, u32[]{:S(2)}, u32[]{:S(2)}) collective-permute-start(bf16[1,256,256]{2,1,0:T(8,128)(2,1)S(1)} %multiply_convert_fusion), channel_id=1, source_target_pairs={{0,12},{1,13},{2,14},{3,15},{4,8},{5,9},{6,10},{7,11},{8,4},{9,5},... | collective-permute-start | bytes 393224 | tf_op jit(solution)/shard_map/ppermute | solution.py:17
  49.8 1.9 %collective-permute-start.11 = (bf16[1,256,256]{2,1,0:T(8,128)(2,1)S(1)}, bf16[1,256,256]{2,1,0:T(8,128)(2,1)S(1)}, u32[]{:S(2)}, u32[]{:S(2)}) collective-permute-start(bf16[1,256,256]{2,1,0:T(8,128)(2,1)S(1)} %multiply_convert_fusion), channel_id=1, source_target_pairs={{0,8},{1,9},{2,10},{3,11},{4,12},{5,13},{6,14},{7,15},{8,0},{9,1},... | collective-permute-start | bytes 393224 | tf_op jit(solution)/shard_map/ppermute | solution.py:17
  51.8 6.5 %collective-permute-done.13 = bf16[1,256,256]{2,1,0:T(8,128)(2,1)S(1)} collective-permute-done((bf16[1,256,256]{2,1,0:T(8,128)(2,1)S(1)}, bf16[1,256,256]{2,1,0:T(8,128)(2,1)S(1)}, u32[]{:S(2)}, u32[]{:S(2)}) %collective-permute-start.13) | collective-permute-done | bytes 131104 | tf_op jit(solution)/shard_map/ppermute | solution.py:17
  58.2 4.9 %collective-permute-done.12 = bf16[1,256,256]{2,1,0:T(8,128)(2,1)S(1)} collective-permute-done((bf16[1,256,256]{2,1,0:T(8,128)(2,1)S(1)}, bf16[1,256,256]{2,1,0:T(8,128)(2,1)S(1)}, u32[]{:S(2)}, u32[]{:S(2)}) %collective-permute-start.12) | collective-permute-done | bytes 131104 | tf_op jit(solution)/shard_map/ppermute | solution.py:17
  63.1 7.3 %collective-permute-done.11 = bf16[1,256,256]{2,1,0:T(8,128)(2,1)S(1)} collective-permute-done((bf16[1,256,256]{2,1,0:T(8,128)(2,1)S(1)}, bf16[1,256,256]{2,1,0:T(8,128)(2,1)S(1)}, u32[]{:S(2)}, u32[]{:S(2)}) %collective-permute-start.11) | collective-permute-done | bytes 131104 | tf_op jit(solution)/shard_map/ppermute | solution.py:17
  71.2 4.4 %fusion.9 = f32[256,224]{0,1:T(8,128)S(1)} fusion(bf16[256,7168]{1,0:T(8,128)(2,1)} %all-gather.2.cloned.1.call-done, bf16[896,7168]{1,0:T(8,128)(2,1)} %param.10), kind=kOutput, calls=%fused_computation.13 | convolution fusion | flops 822083584 | bytes 7110656 | tf_op jit(solution)/shard_map/tk,jk->tj/dot_general | solution.py:97
  79.3 3.2 %fusion.7 = f32[256,224]{0,1:T(8,128)S(1)} fusion(bf16[256,7168]{1,0:T(8,128)(2,1)S(1)} %copy-done.4, bf16[896,7168]{1,0:T(8,128)(2,1)} %param.10), kind=kOutput, calls=%fused_computation.11 | convolution fusion | flops 822083584 | bytes 7110656 | tf_op jit(solution)/shard_map/tk,jk->tj/dot_general | solution.py:97
  83.1 3.2 %fusion.3 = f32[256,224]{0,1:T(8,128)S(1)} fusion(bf16[256,7168]{1,0:T(8,128)(2,1)S(1)} %copy-done.4, bf16[896,7168]{1,0:T(8,128)(2,1)} %param.10), kind=kOutput, calls=%fused_computation.7 | convolution fusion | flops 822083584 | bytes 7110656 | tf_op jit(solution)/shard_map/tk,jk->tj/dot_general | solution.py:97
  86.3 3.4 %fusion.5 = f32[256,224]{0,1:T(8,128)S(1)} fusion(bf16[256,7168]{1,0:T(8,128)(2,1)S(1)} %copy-done.4, bf16[896,7168]{1,0:T(8,128)(2,1)} %param.10), kind=kOutput, calls=%fused_computation.9 | convolution fusion | flops 822083584 | bytes 7110656 | tf_op jit(solution)/shard_map/tk,jk->tj/dot_general | solution.py:97
  89.7 3.8 %convert_element_type.57 = f32[896,2048]{1,0:T(8,128)} convert(bf16[896,2048]{1,0:T(8,128)(2,1)S(1)} %copy-done.1) | non-fusion elementwise | flops 1835008 | bytes 11010048 | tf_op jit(solution)/shard_map/convert_element_type | solution.py:106
  95.8 6.3 %collective-permute-done.2 = f32[256,224]{0,1:T(8,128)S(1)} collective-permute-done((f32[256,224]{0,1:T(8,128)S(1)}, f32[256,224]{0,1:T(8,128)S(1)}, u32[]{:S(2)}, u32[]{:S(2)}) %collective-permute-start.2) | collective-permute-done | bytes 229408 | tf_op jit(solution)/shard_map/ppermute | solution.py:17
  102.2 3.2 %collective-permute-done.3 = f32[256,224]{0,1:T(8,128)S(1)} collective-permute-done((f32[256,224]{0,1:T(8,128)S(1)}, f32[256,224]{0,1:T(8,128)S(1)}, u32[]{:S(2)}, u32[]{:S(2)}) %collective-permute-start.3) | collective-permute-done | bytes 229408 | tf_op jit(solution)/shard_map/ppermute | solution.py:17
  109.2 6.5 %fusion.12 = f32[2,128]{1,0:T(2,128)S(1)} fusion(bf16[2,128,2048]{2,1,0:T(8,128)(2,1)S(1)} %reshape_reshape.7, f32[896,2048]{1,0:T(8,128)} %convert_element_type.57, bf16[2,128,224]{1,2,0:T(8,128)(2,1)} %get-tuple-element.17, bf16[2,128,224]{1,2,0:T(8,128)(2,1)S(1)} %copy-done.3, bf16[2,128,224]{1,2,0:T(8,128)(2,1)S(1)} %copy-done.2, ...), kind=kOutput, calls=%fused_computation.16 | convolution fusion | flops 1891630848 | bytes 8848384 | tf_op jit(solution)/shard_map/stm,smn->stn/dot_general | solution.py:111
  115.8 1.8 %collective-permute-start.17 = (f32[2,128]{1,0:T(2,128)S(1)}, f32[2,128]{1,0:T(2,128)S(1)}, u32[]{:S(2)}, u32[]{:S(2)}) collective-permute-start(f32[2,128]{1,0:T(2,128)S(1)} %get-tuple-element.13), channel_id=1, source_target_pairs={{0,8},{1,9},{2,10},{3,11},{4,12},{5,13},{6,14},{7,15},{8,0},{9,1},... | collective-permute-start | bytes 3080 | tf_op jit(solution)/shard_map/ppermute | solution.py:17
  117.6 2.6 %collective-permute-start.19 = (f32[2,128]{1,0:T(2,128)S(1)}, f32[2,128]{1,0:T(2,128)S(1)}, u32[]{:S(2)}, u32[]{:S(2)}) collective-permute-start(f32[2,128]{1,0:T(2,128)S(1)} %get-tuple-element.13), channel_id=1, source_target_pairs={{0,12},{1,13},{2,14},{3,15},{4,8},{5,9},{6,10},{7,11},{8,4},{9,5},... | collective-permute-start | bytes 3080 | tf_op jit(solution)/shard_map/ppermute | solution.py:17
  120.3 2.6 %collective-permute-done.19 = f32[2,128]{1,0:T(2,128)S(1)} collective-permute-done((f32[2,128]{1,0:T(2,128)S(1)}, f32[2,128]{1,0:T(2,128)S(1)}, u32[]{:S(2)}, u32[]{:S(2)}) %collective-permute-start.19) | collective-permute-done | bytes 1056 | tf_op jit(solution)/shard_map/ppermute | solution.py:17
  123.0 1.7 %collective-permute-start.21 = (f32[2,128]{1,0:T(2,128)S(1)}, f32[2,128]{1,0:T(2,128)S(1)}, u32[]{:S(2)}, u32[]{:S(2)}) collective-permute-start(f32[2,128]{1,0:T(2,128)S(1)} %fusion.77), channel_id=1, source_target_pairs={{0,1},{1,0},{2,3},{3,2},{4,5},{5,4},{6,7},{7,6},{8,9},{9,8},{10,11... | collective-permute-start | bytes 3080 | tf_op jit(solution)/shard_map/ppermute | solution.py:17
  126.0 2.3 %collective-permute-done.20 = f32[2,128]{1,0:T(2,128)S(1)} collective-permute-done((f32[2,128]{1,0:T(2,128)S(1)}, f32[2,128]{1,0:T(2,128)S(1)}, u32[]{:S(2)}, u32[]{:S(2)}) %collective-permute-start.20) | collective-permute-done | bytes 1056 | tf_op jit(solution)/shard_map/ppermute | solution.py:17
  129.9 2.1 %collective-permute-done.23 = f32[2,128]{1,0:T(2,128)S(1)} collective-permute-done((f32[2,128]{1,0:T(2,128)S(1)}, f32[2,128]{1,0:T(2,128)S(1)}, u32[]{:S(2)}, u32[]{:S(2)}) %collective-permute-start.23) | collective-permute-done | bytes 1056 | tf_op jit(solution)/shard_map/ppermute | solution.py:17
  (97 shorter events, 27.9 us)
Async XLA Ops:
  7.2 64.0 %all-gather.2.cloned.1.call-start = ((), (), s32[]{:S(2)}) async-start(), calls=%async_computation | async-start | bytes 3899392 | tf_op jit(solution)/shard_map/all_gather | solution.py:87
  7.9 8.7 %collective-permute-start.6 = (bf16[1,16,2048]{2,1,0:T(8,128)(2,1)}, bf16[1,16,2048]{2,1,0:T(8,128)(2,1)S(1)}, u32[]{:S(2)}, u32[]{:S(2)}) collective-permute-start(bf16[1,16,2048]{2,1,0:T(8,128)(2,1)} %bitcast.125), channel_id=1, source_target_pairs={{0,12},{1,13},{2,14},{3,15},{4,8},{5,9},{6,10},{7,11},{8,4},{9,5},... | collective-permute-start | bytes 196616 | tf_op jit(solution)/shard_map/ppermute | solution.py:17
  13.0 4.9 %collective-permute-start.5 = (bf16[1,16,2048]{2,1,0:T(8,128)(2,1)}, bf16[1,16,2048]{2,1,0:T(8,128)(2,1)S(1)}, u32[]{:S(2)}, u32[]{:S(2)}) collective-permute-start(bf16[1,16,2048]{2,1,0:T(8,128)(2,1)} %bitcast.126), channel_id=1, source_target_pairs={{0,4},{1,5},{2,6},{3,7},{4,0},{5,1},{6,2},{7,3},{8,12},{9,13},{10,... | collective-permute-start | bytes 196616 | tf_op jit(solution)/shard_map/ppermute | solution.py:17
  13.0 5.8 %collective-permute-start.4 = (bf16[1,16,2048]{2,1,0:T(8,128)(2,1)}, bf16[1,16,2048]{2,1,0:T(8,128)(2,1)S(1)}, u32[]{:S(2)}, u32[]{:S(2)}) collective-permute-start(bf16[1,16,2048]{2,1,0:T(8,128)(2,1)} %bitcast.127), channel_id=1, source_target_pairs={{0,8},{1,9},{2,10},{3,11},{4,12},{5,13},{6,14},{7,15},{8,0},{9,1},... | collective-permute-start | bytes 196616 | tf_op jit(solution)/shard_map/ppermute | solution.py:17
  20.4 11.1 %collective-permute-start.9 = (bf16[4,16,2048]{2,1,0:T(8,128)(2,1)S(1)}, bf16[4,16,2048]{2,1,0:T(8,128)(2,1)S(1)}, u32[]{:S(2)}, u32[]{:S(2)}) collective-permute-start(bf16[4,16,2048]{2,1,0:T(8,128)(2,1)S(1)} %broadcast_select_fusion), channel_id=1, source_target_pairs={{0,3},{1,2},{2,1},{3,0},{4,7},{5,6},{6,5},{7,4},{8,11},{9,10},{10,... | collective-permute-start | bytes 786440 | tf_op jit(solution)/shard_map/ppermute | solution.py:17
  20.5 11.0 %collective-permute-start.8 = (bf16[4,16,2048]{2,1,0:T(8,128)(2,1)S(1)}, bf16[4,16,2048]{2,1,0:T(8,128)(2,1)S(1)}, u32[]{:S(2)}, u32[]{:S(2)}) collective-permute-start(bf16[4,16,2048]{2,1,0:T(8,128)(2,1)S(1)} %broadcast_select_fusion), channel_id=1, source_target_pairs={{0,1},{1,0},{2,3},{3,2},{4,5},{5,4},{6,7},{7,6},{8,9},{9,8},{10,11... | collective-permute-start | bytes 786440 | tf_op jit(solution)/shard_map/ppermute | solution.py:17
  22.1 15.0 %collective-permute-start.7 = (bf16[4,16,2048]{2,1,0:T(8,128)(2,1)S(1)}, bf16[4,16,2048]{2,1,0:T(8,128)(2,1)S(1)}, u32[]{:S(2)}, u32[]{:S(2)}) collective-permute-start(bf16[4,16,2048]{2,1,0:T(8,128)(2,1)S(1)} %broadcast_select_fusion), channel_id=1, source_target_pairs={{0,2},{1,3},{2,0},{3,1},{4,6},{5,7},{6,4},{7,5},{8,10},{9,11},{10,... | collective-permute-start | bytes 786440 | tf_op jit(solution)/shard_map/ppermute | solution.py:17
  38.7 8.3 %collective-permute-start.10 = (f32[256,256]{1,0:T(8,128)S(1)}, f32[256,256]{1,0:T(8,128)S(1)}, u32[]{:S(2)}, u32[]{:S(2)}) collective-permute-start(f32[256,256]{1,0:T(8,128)S(1)} %fusion.68), channel_id=1, source_target_pairs={{0,16},{16,0},{1,17},{17,1},{2,18},{18,2},{3,19},{19,3},{4,20},{20... | collective-permute-start | bytes 786440 | tf_op jit(solution)/shard_map/ppermute | solution.py:17
  47.2 11.0 %collective-permute-start.13 = (bf16[1,256,256]{2,1,0:T(8,128)(2,1)S(1)}, bf16[1,256,256]{2,1,0:T(8,128)(2,1)S(1)}, u32[]{:S(2)}, u32[]{:S(2)}) collective-permute-start(bf16[1,256,256]{2,1,0:T(8,128)(2,1)S(1)} %multiply_convert_fusion), channel_id=1, source_target_pairs={{0,12},{1,13},{2,14},{3,15},{4,8},{5,9},{6,10},{7,11},{8,4},{9,5},... | collective-permute-start | bytes 393224 | tf_op jit(solution)/shard_map/ppermute | solution.py:17
  49.5 13.7 %collective-permute-start.12 = (bf16[1,256,256]{2,1,0:T(8,128)(2,1)S(1)}, bf16[1,256,256]{2,1,0:T(8,128)(2,1)S(1)}, u32[]{:S(2)}, u32[]{:S(2)}) collective-permute-start(bf16[1,256,256]{2,1,0:T(8,128)(2,1)S(1)} %multiply_convert_fusion), channel_id=1, source_target_pairs={{0,4},{1,5},{2,6},{3,7},{4,0},{5,1},{6,2},{7,3},{8,12},{9,13},{10,... | collective-permute-start | bytes 393224 | tf_op jit(solution)/shard_map/ppermute | solution.py:17
  49.8 20.6 %collective-permute-start.11 = (bf16[1,256,256]{2,1,0:T(8,128)(2,1)S(1)}, bf16[1,256,256]{2,1,0:T(8,128)(2,1)S(1)}, u32[]{:S(2)}, u32[]{:S(2)}) collective-permute-start(bf16[1,256,256]{2,1,0:T(8,128)(2,1)S(1)} %multiply_convert_fusion), channel_id=1, source_target_pairs={{0,8},{1,9},{2,10},{3,11},{4,12},{5,13},{6,14},{7,15},{8,0},{9,1},... | collective-permute-start | bytes 393224 | tf_op jit(solution)/shard_map/ppermute | solution.py:17
  75.6 17.9 %collective-permute-start = (f32[256,224]{0,1:T(8,128)S(1)}, f32[256,224]{0,1:T(8,128)S(1)}, u32[]{:S(2)}, u32[]{:S(2)}) collective-permute-start(f32[256,224]{0,1:T(8,128)S(1)} %fusion.9), channel_id=1, source_target_pairs={{0,16},{16,0},{1,17},{17,1},{2,18},{18,2},{3,19},{19,3},{4,20},{20... | collective-permute-start | bytes 688136 | tf_op jit(solution)/shard_map/ppermute | solution.py:17
  77.1 29.6 %collective-permute-start.16 = (bf16[2,256,256]{2,1,0:T(8,128)(2,1)S(1)}, bf16[2,256,256]{2,1,0:T(8,128)(2,1)S(1)}, u32[]{:S(2)}, u32[]{:S(2)}) collective-permute-start(bf16[2,256,256]{2,1,0:T(8,128)(2,1)S(1)} %broadcast_select_fusion.1), channel_id=1, source_target_pairs={{0,3},{1,2},{2,1},{3,0},{4,7},{5,6},{6,5},{7,4},{8,11},{9,10},{10,... | collective-permute-start | bytes 786440 | tf_op jit(solution)/shard_map/ppermute | solution.py:17
  78.2 28.6 %collective-permute-start.15 = (bf16[2,256,256]{2,1,0:T(8,128)(2,1)S(1)}, bf16[2,256,256]{2,1,0:T(8,128)(2,1)S(1)}, u32[]{:S(2)}, u32[]{:S(2)}) collective-permute-start(bf16[2,256,256]{2,1,0:T(8,128)(2,1)S(1)} %broadcast_select_fusion.1), channel_id=1, source_target_pairs={{0,1},{1,0},{2,3},{3,2},{4,5},{5,4},{6,7},{7,6},{8,9},{9,8},{10,11... | collective-permute-start | bytes 786440 | tf_op jit(solution)/shard_map/ppermute | solution.py:17
  78.8 28.0 %collective-permute-start.14 = (bf16[2,256,256]{2,1,0:T(8,128)(2,1)S(1)}, bf16[2,256,256]{2,1,0:T(8,128)(2,1)S(1)}, u32[]{:S(2)}, u32[]{:S(2)}) collective-permute-start(bf16[2,256,256]{2,1,0:T(8,128)(2,1)S(1)} %broadcast_select_fusion.1), channel_id=1, source_target_pairs={{0,2},{1,3},{2,0},{3,1},{4,6},{5,7},{6,4},{7,5},{8,10},{9,11},{10,... | collective-permute-start | bytes 786440 | tf_op jit(solution)/shard_map/ppermute | solution.py:17
  82.5 12.6 %collective-permute-start.1 = (f32[256,224]{0,1:T(8,128)S(1)}, f32[256,224]{0,1:T(8,128)S(1)}, u32[]{:S(2)}, u32[]{:S(2)}) collective-permute-start(f32[256,224]{0,1:T(8,128)S(1)} %fusion.7), channel_id=1, source_target_pairs={{0,16},{16,0},{1,17},{17,1},{2,18},{18,2},{3,19},{19,3},{4,20},{20... | collective-permute-start | bytes 688136 | tf_op jit(solution)/shard_map/ppermute | solution.py:17
  93.5 8.5 %collective-permute-start.2 = (f32[256,224]{0,1:T(8,128)S(1)}, f32[256,224]{0,1:T(8,128)S(1)}, u32[]{:S(2)}, u32[]{:S(2)}) collective-permute-start(f32[256,224]{0,1:T(8,128)S(1)} %fusion.5), channel_id=1, source_target_pairs={{0,16},{16,0},{1,17},{17,1},{2,18},{18,2},{3,19},{19,3},{4,20},{20... | collective-permute-start | bytes 688136 | tf_op jit(solution)/shard_map/ppermute | solution.py:17
  95.1 10.3 %collective-permute-start.3 = (f32[256,224]{0,1:T(8,128)S(1)}, f32[256,224]{0,1:T(8,128)S(1)}, u32[]{:S(2)}, u32[]{:S(2)}) collective-permute-start(f32[256,224]{0,1:T(8,128)S(1)} %fusion.3), channel_id=1, source_target_pairs={{0,16},{16,0},{1,17},{17,1},{2,18},{18,2},{3,19},{19,3},{4,20},{20... | collective-permute-start | bytes 688136 | tf_op jit(solution)/shard_map/ppermute | solution.py:17
  115.7 4.5 %collective-permute-start.18 = (f32[2,128]{1,0:T(2,128)S(1)}, f32[2,128]{1,0:T(2,128)S(1)}, u32[]{:S(2)}, u32[]{:S(2)}) collective-permute-start(f32[2,128]{1,0:T(2,128)S(1)} %get-tuple-element.13), channel_id=1, source_target_pairs={{0,4},{1,5},{2,6},{3,7},{4,0},{5,1},{6,2},{7,3},{8,12},{9,13},{10,... | collective-permute-start | bytes 3080 | tf_op jit(solution)/shard_map/ppermute | solution.py:17
  115.8 4.5 %collective-permute-start.17 = (f32[2,128]{1,0:T(2,128)S(1)}, f32[2,128]{1,0:T(2,128)S(1)}, u32[]{:S(2)}, u32[]{:S(2)}) collective-permute-start(f32[2,128]{1,0:T(2,128)S(1)} %get-tuple-element.13), channel_id=1, source_target_pairs={{0,8},{1,9},{2,10},{3,11},{4,12},{5,13},{6,14},{7,15},{8,0},{9,1},... | collective-permute-start | bytes 3080 | tf_op jit(solution)/shard_map/ppermute | solution.py:17
  117.6 5.4 %collective-permute-start.19 = (f32[2,128]{1,0:T(2,128)S(1)}, f32[2,128]{1,0:T(2,128)S(1)}, u32[]{:S(2)}, u32[]{:S(2)}) collective-permute-start(f32[2,128]{1,0:T(2,128)S(1)} %get-tuple-element.13), channel_id=1, source_target_pairs={{0,12},{1,13},{2,14},{3,15},{4,8},{5,9},{6,10},{7,11},{8,4},{9,5},... | collective-permute-start | bytes 3080 | tf_op jit(solution)/shard_map/ppermute | solution.py:17
  122.9 3.1 %collective-permute-start.22 = (f32[2,128]{1,0:T(2,128)S(1)}, f32[2,128]{1,0:T(2,128)S(1)}, u32[]{:S(2)}, u32[]{:S(2)}) collective-permute-start(f32[2,128]{1,0:T(2,128)S(1)} %fusion.77), channel_id=1, source_target_pairs={{0,3},{1,2},{2,1},{3,0},{4,7},{5,6},{6,5},{7,4},{8,11},{9,10},{10,... | collective-permute-start | bytes 3080 | tf_op jit(solution)/shard_map/ppermute | solution.py:17
  124.8 3.6 %collective-permute-start.20 = (f32[2,128]{1,0:T(2,128)S(1)}, f32[2,128]{1,0:T(2,128)S(1)}, u32[]{:S(2)}, u32[]{:S(2)}) collective-permute-start(f32[2,128]{1,0:T(2,128)S(1)} %fusion.77), channel_id=1, source_target_pairs={{0,2},{1,3},{2,0},{3,1},{4,6},{5,7},{6,4},{7,5},{8,10},{9,11},{10,... | collective-permute-start | bytes 3080 | tf_op jit(solution)/shard_map/ppermute | solution.py:17
  128.3 3.6 %collective-permute-start.23 = (f32[2,128]{1,0:T(2,128)S(1)}, f32[2,128]{1,0:T(2,128)S(1)}, u32[]{:S(2)}, u32[]{:S(2)}) collective-permute-start(f32[2,128]{1,0:T(2,128)S(1)} %fusion.76), channel_id=1, source_target_pairs={{0,16},{16,0},{1,17},{17,1},{2,18},{18,2},{3,19},{19,3},{4,20},{20... | collective-permute-start | bytes 3080 | tf_op jit(solution)/shard_map/ppermute | solution.py:17
  (7 other events, 71.3 us)
Sparse Core Ops, SparseCore 0:
  10.3 60.4 all-gather.1

commit v10 on v6

--- a/solution.py
+++ b/solution.py
@@ -4,6 +4,7 @@
 from jax.sharding import PartitionSpec as P
 
 SEQ = 128
+READER = ("rz", "rc")
 
 
 def bit_groups(bits):
@@ -42,7 +43,7 @@
 
 
 def ordered_gather(block, owners, readers):
-    reader_index = lax.axis_index("reader")
+    reader_index = lax.axis_index(READER)
     owner_index = lax.axis_index("owner") if owners > 1 else 0
     group_size = readers // owners
     bits = [1 << k for k in range(readers.bit_length() - 1)][::-1]
@@ -51,7 +52,7 @@
     for group in bit_groups(bits):
         high = sum(bit for bit in group if bit >= group_size)
         low = [bit for bit in group if bit < group_size]
-        stacked = xor_round(held, "reader", readers, group)
+        stacked = xor_round(held, READER, readers, group)
         c_high = (reader_index ^ target) & high
         picks = []
         values = sorted(sum(bit for k, bit in enumerate(low) if count >> k & 1) for count in range(1 << len(low)))
@@ -71,7 +72,8 @@
 
 def local(acts, grads, basis_a, basis_g, eigvals, lengths, shuffle):
     owners = lax.axis_size("owner")
-    readers = lax.axis_size("reader")
+    halves = lax.axis_size("rc")
+    readers = lax.axis_size("rz") * halves
     owner_index = lax.axis_index("owner")
     rows = acts.shape[0] * readers
     slots = rows // SEQ
@@ -81,14 +83,30 @@
     dim_ff = m_block * readers
     dim_d = width * owners
 
-    all_g = lax.all_gather(grads, "reader", axis=0, tiled=True)
-    all_a = ordered_gather(acts, 1, readers).reshape(rows, acts.shape[1])
+    joined = jnp.concatenate([grads, acts], axis=1)
+    near = lax.all_gather(joined, "rz", axis=0, tiled=True)
+    parts = [near] + [
+        lax.ppermute(near, "rc", [(i, (i + shift) % halves) for i in range(halves)])
+        for shift in range(1, halves)
+    ]
+    rel = jnp.concatenate(parts, axis=0)
+    all_g = rel[:, : grads.shape[1]]
+    all_a = rel[:, grads.shape[1]:]
 
-    token = jnp.arange(rows, dtype=jnp.int32)
+    half_index = lax.axis_index("rc")
+    block = jnp.arange(readers, dtype=jnp.int32)
+    rz_of = block % (readers // halves)
+    rc_of = (half_index - block // (readers // halves)) % halves
+    source = rz_of * halves + rc_of
+    token = (source[:, None] * acts.shape[0] + jnp.arange(acts.shape[0], dtype=jnp.int32)[None, :]).reshape(rows)
     live = ((token % SEQ) < lengths[token // SEQ]).astype(jnp.float32)
+    position = ((half_index - block % halves) % halves) * (readers // halves) + block // halves
+
+    def in_token_order(x):
+        return jnp.take(x.reshape(readers, acts.shape[0], -1), position, axis=0).reshape(rows, -1)
 
     part_a = jnp.einsum("tk,jk->tj", all_a, basis_a, preferred_element_type=jnp.float32)
-    rot_a_block = (xor_sum(part_a, "owner", owners) * live[:, None]).astype(jnp.bfloat16)
+    rot_a_block = in_token_order((xor_sum(part_a, "owner", owners) * live[:, None]).astype(jnp.bfloat16))
     pieces = []
     step = m_block // 2
     for start in range(0, m_block, step):
@@ -96,7 +114,7 @@
             "tk,jk->tj", all_g, basis_g[start:start + step], preferred_element_type=jnp.float32
         )
         pieces.append(xor_sum(part_g, "owner", owners))
-    rot_g = (jnp.concatenate(pieces, axis=1) * live[:, None]).astype(jnp.bfloat16)
+    rot_g = in_token_order((jnp.concatenate(pieces, axis=1) * live[:, None]).astype(jnp.bfloat16))
 
     rot_a = half_gather(rot_a_block, owners, readers)
 
@@ -107,7 +125,7 @@
     scaled = (outer / denom[None]).astype(jnp.bfloat16)
     projected = jnp.einsum("stm,smn->stn", g_rows, scaled, preferred_element_type=jnp.float32)
     partial = jnp.sum(projected * a_rows.astype(jnp.float32), axis=2) / (dim_ff * dim_d)
-    scores = xor_sum(xor_sum(partial, "reader", readers), "owner", owners)
+    scores = xor_sum(xor_sum(partial, READER, readers), "owner", owners)
 
     token_score = lax.dynamic_index_in_dim(scores, owner_index, 0, keepdims=False)
     slot_mean = jnp.sum(scores, axis=1) / SEQ
@@ -117,18 +135,13 @@
 
 
 def solution(mesh):
+    owners, readers = mesh.devices.shape
+    split = jax.sharding.Mesh(mesh.devices.reshape(owners, readers // 2, 2), ("owner",) + READER)
+    rows = P(READER, "owner")
     return jax.shard_map(
         local,
-        mesh=mesh,
-        in_specs=(
-            P("reader", "owner"),
-            P("reader", "owner"),
-            P("reader", "owner"),
-            P("reader", "owner"),
-            P("reader", "owner"),
-            P(),
-            P(),
-        ),
+        mesh=split,
+        in_specs=(rows, rows, rows, rows, rows, P(), P()),
         out_specs=(P("owner"), P()),
         check_vma=False,
     )

time: 137 us -> 147 us (1.073)
  waiting for transfers between devices: 57.2 us -> 75.4 us
  starting transfers between devices: 26.4 us -> 18.2 us
  matrix products: 19.5 us -> 14 us
  other arithmetic: 12.2 us -> 15.9 us
  local copies, waits for them, and re-layouts: 6.85 us -> 9.06 us
    all_gather x1, waiting for transfers between devices: 0.01 us -> 53.2 us  [local(): near = lax.all_gather(joined, 'rz', axis=0, tiled=True)]
    ppermute x22 -> x16, waiting for transfers between devices: 56.5 us -> 22.2 us  [xor_round(): parts.append(lax.ppermute(held, axis, [(i, i ^ c) for i in range(size)]))]
    ppermute x22 -> x16, starting transfers between devices: 26.4 us -> 18.2 us  [xor_round(): parts.append(lax.ppermute(held, axis, [(i, i ^ c) for i in range(size)]))]
    dot_general x2, matrix products: 12.2 us -> 6.76 us  [local(): jnp.einsum('tk,jk->tj', all_g, basis_g[start:start + step], preferred_ele...]
    concatenate x0 -> x1, local copies, waits for them, and re-layouts: none -> 1.97 us  [local(): rel = jnp.concatenate(parts, axis=0)]
    concatenate x0 -> x1, other arithmetic: none -> 1.77 us  [local(): joined = jnp.concatenate([grads, acts], axis=1)]
  transfers between devices with their start and end apart: 23 -> 18, of which waited for: 15 -> 11; matrix products, arithmetic and copies ran while one was open for 20% -> 16% of each run, Pallas kernels for 0% -> 0%
where the time goes in v10:
time: 147 us
  waiting for transfers between devices  75.4 us (51%)
  starting transfers between devices  18.2 us (12%)
  other arithmetic  15.9 us (11%)
  between operations  14.4 us (10%)
  matrix products  14 us (10%)
  local copies, waits for them, and re-layouts  9.06 us (6%)
    all_gather x1, waiting for transfers between devices, local(): near = lax.all_gather(joined, 'rz', axis=0, tiled=True)  53.2 us
    ppermute x16, waiting for transfers between devices, xor_round(): parts.append(lax.ppermute(held, axis, [(i, i ^ c) for i in range(size)]))  22.2 us
    ppermute x16, starting transfers between devices, xor_round(): parts.append(lax.ppermute(held, axis, [(i, i ^ c) for i in range(size)]))  18.2 us
    dot_general x2, matrix products, local(): jnp.einsum('tk,jk->tj', all_g, basis_g[start:start + step], preferred_ele...  6.76 us
    dot_general x1, matrix products, local(): jnp.einsum('stm,smn->stn', g_rows, scaled, preferred_element_type=jnp.flo...  6.72 us
    convert_element_type x1, other arithmetic, local(): denom = eigvals.astype(jnp.float32)  6.06 us
  transfers between devices with their start and end apart: 18, of which 11 were waited for; matrix products, arithmetic and copies ran while one was open for 16% of the time, Pallas kernels for 0%

profile of v10, /device:TPU:0, one launch (start us, length us, event | category | flops | bytes accessed | tf_op | source)
XLA Modules:
  0.0 147.1 jit_solution(4299674765832277275)
XLA Ops:
  7.2 1.8 %pad_maximum_fusion.1 = bf16[16,9216]{1,0:T(8,128)(2,1)} fusion(bf16[16,2048]{1,0:T(8,128)(2,1)} %param.7, bf16[16,7168]{1,0:T(8,128)(2,1)} %param.8), kind=kLoop, calls=%fused_computation.41 | loop fusion | flops 589824 | bytes 589824 | tf_op jit(solution)/shard_map/concatenate | solution.py:86
  10.5 1.3 fusion.31
  11.8 53.2 %all-gather.2.cloned.1.call-done = bf16[128,9216]{1,0:T(8,128)(2,1)} async-done(((bf16[16,9216]{1,0:T(8,128)(2,1)}), bf16[128,9216]{1,0:T(8,128)(2,1)}) %all-gather.2.cloned.1.call-update) | async-done | bytes 2359312 | tf_op jit(solution)/shard_map/all_gather | solution.py:87
  65.5 6.1 %convert_element_type.28 = f32[896,2048]{1,0:T(8,128)} convert(bf16[896,2048]{1,0:T(8,128)(2,1)} %param.11) | non-fusion elementwise | flops 1835008 | bytes 11010048 | tf_op jit(solution)/shard_map/convert_element_type | solution.py:121
  72.2 2.0 %constant_dynamic-update-slice_fusion = bf16[256,9216]{1,0:T(8,128)(2,1)S(1)} fusion(bf16[256,9216]{1,0:T(8,128)(2,1)S(1)} %constant_dynamic-update-slice_fusion.1, bf16[128,9216]{1,0:T(8,128)(2,1)} %collective-permute-done), kind=kLoop, calls=%fused_computation.74 | loop fusion | bytes 4718592 | tf_op jit(solution)/shard_map/concatenate | solution.py:92
  74.8 1.5 %collective-permute-start.3 = (f32[256,256]{1,0:T(8,128)S(1)}, f32[256,256]{1,0:T(8,128)S(1)}, u32[]{:S(2)}, u32[]{:S(2)}) collective-permute-start(f32[256,256]{1,0:T(8,128)S(1)} %fusion.11), channel_id=1, source_target_pairs={{0,16},{16,0},{1,17},{17,1},{2,18},{18,2},{3,19},{19,3},{4,20},{20... | collective-permute-start | bytes 786440 | tf_op jit(solution)/shard_map/ppermute | solution.py:18
  76.3 4.9 %fusion.3 = f32[256,448]{0,1:T(8,128)S(1)} fusion(bf16[896,7168]{1,0:T(8,128)(2,1)} %param.10, bf16[256,9216]{1,0:T(8,128)(2,1)S(1)} %constant_dynamic-update-slice_fusion), kind=kOutput, calls=%fused_computation.8 | convolution fusion | flops 1644167168 | bytes 10551296 | tf_op jit(solution)/shard_map/tk,jk->tj/dot_general | solution.py:113
  81.3 1.9 %fusion.1 = f32[256,448]{0,1:T(8,128)S(1)} fusion(bf16[896,7168]{1,0:T(8,128)(2,1)S(1)} %bitcast.93, bf16[256,9216]{1,0:T(8,128)(2,1)S(1)} %constant_dynamic-update-slice_fusion), kind=kOutput, calls=%fused_computation.6 | convolution fusion | flops 1644167168 | bytes 10551296 | tf_op jit(solution)/shard_map/tk,jk->tj/dot_general | solution.py:113
  86.2 1.9 %collective-permute-start.4 = (bf16[1,256,256]{2,1,0:T(8,128)(2,1)S(1)}, bf16[1,256,256]{2,1,0:T(8,128)(2,1)S(1)}, u32[]{:S(2)}, u32[]{:S(2)}) collective-permute-start(bf16[1,256,256]{2,1,0:T(8,128)(2,1)S(1)} %bitcast_select_fusion.2), channel_id=1, source_target_pairs={{0,8},{1,9},{2,10},{3,11},{4,12},{5,13},{6,14},{7,15},{8,0},{9,1},... | collective-permute-start | bytes 393224 | tf_op jit(solution)/shard_map/ppermute | solution.py:18
  88.6 2.0 %collective-permute-start.6 = (bf16[1,256,256]{2,1,0:T(8,128)(2,1)S(1)}, bf16[1,256,256]{2,1,0:T(8,128)(2,1)S(1)}, u32[]{:S(2)}, u32[]{:S(2)}) collective-permute-start(bf16[1,256,256]{2,1,0:T(8,128)(2,1)S(1)} %bitcast_select_fusion.2), channel_id=1, source_target_pairs={{0,12},{1,13},{2,14},{3,15},{4,8},{5,9},{6,10},{7,11},{8,4},{9,5},... | collective-permute-start | bytes 393224 | tf_op jit(solution)/shard_map/ppermute | solution.py:18
  90.7 6.6 %collective-permute-done.4 = bf16[1,256,256]{2,1,0:T(8,128)(2,1)S(1)} collective-permute-done((bf16[1,256,256]{2,1,0:T(8,128)(2,1)S(1)}, bf16[1,256,256]{2,1,0:T(8,128)(2,1)S(1)}, u32[]{:S(2)}, u32[]{:S(2)}) %collective-permute-start.4) | collective-permute-done | bytes 131104 | tf_op jit(solution)/shard_map/ppermute | solution.py:18
  97.3 1.9 %collective-permute-done.6 = bf16[1,256,256]{2,1,0:T(8,128)(2,1)S(1)} collective-permute-done((bf16[1,256,256]{2,1,0:T(8,128)(2,1)S(1)}, bf16[1,256,256]{2,1,0:T(8,128)(2,1)S(1)}, u32[]{:S(2)}, u32[]{:S(2)}) %collective-permute-start.6) | collective-permute-done | bytes 131104 | tf_op jit(solution)/shard_map/ppermute | solution.py:18
  101.2 1.6 %collective-permute-start.9 = (bf16[2,256,256]{2,1,0:T(8,128)(2,1)}, bf16[2,256,256]{2,1,0:T(8,128)(2,1)}, u32[]{:S(2)}, u32[]{:S(2)}) collective-permute-start(bf16[2,256,256]{2,1,0:T(8,128)(2,1)} %broadcast_select_fusion), channel_id=1, source_target_pairs={{0,3},{1,2},{2,1},{3,0},{4,7},{5,6},{6,5},{7,4},{8,11},{9,10},{10,... | collective-permute-start | bytes 786440 | tf_op jit(solution)/shard_map/ppermute | solution.py:18
  102.9 3.2 %collective-permute-done.2 = f32[256,448]{0,1:T(8,128)} collective-permute-done((f32[256,448]{0,1:T(8,128)S(1)}, f32[256,448]{0,1:T(8,128)}, u32[]{:S(2)}, u32[]{:S(2)}) %collective-permute-start.2) | collective-permute-done | bytes 458784 | tf_op jit(solution)/shard_map/ppermute | solution.py:18
  106.1 1.5 %fusion.15 = (f32[1,256,448]{1,2,0:T(8,128)S(1)}, f32[1,256,448]{1,2,0:T(8,128)S(1)}) fusion(s32[]{:T(128)S(6)} %select_n.259, f32[1,256,448]{1,2,0:T(8,128)} %bitcast.78, s32[]{:T(128)S(6)} %select_n.258, f32[1,256,448]{1,2,0:T(8,128)} %bitcast.4, f32[1,256,448]{1,2,0:T(8,128)} %bitcast.79, f32[1,256,448]{1,2,0:T(8,128)S(1)} %bitcast.77), kind=kLoop, calls=%fused_computation.35 | loop fusion | flops 688128 | bytes 2752520 | tf_op jit(solution)/shard_map/add | solution.py:40
  110.2 1.7 %collective-permute-done.9 = bf16[2,256,256]{2,1,0:T(8,128)(2,1)} collective-permute-done((bf16[2,256,256]{2,1,0:T(8,128)(2,1)}, bf16[2,256,256]{2,1,0:T(8,128)(2,1)}, u32[]{:S(2)}, u32[]{:S(2)}) %collective-permute-start.9) | collective-permute-done | bytes 262176 | tf_op jit(solution)/shard_map/ppermute | solution.py:18
  115.7 6.7 %fusion.10 = f32[2,128]{1,0:T(2,128)S(1)} fusion(bf16[2,128,2048]{2,1,0:T(8,128)(2,1)S(1)} %reshape_reshape.4, bf16[2,128,896]{2,1,0:T(8,128)(2,1)} %bitcast_select_fusion, f32[896,2048]{1,0:T(8,128)} %convert_element_type.28), kind=kOutput, calls=%fused_computation.14 | convolution fusion | flops 1887960832 | bytes 8848384 | tf_op jit(solution)/shard_map/stm,smn->stn/dot_general | solution.py:126
  122.5 3.0 %collective-permute-start.10 = (f32[2,128]{1,0:T(2,128)S(1)}, f32[2,128]{1,0:T(2,128)S(1)}, u32[]{:S(2)}, u32[]{:S(2)}) collective-permute-start(f32[2,128]{1,0:T(2,128)S(1)} %get-tuple-element.5), channel_id=1, source_target_pairs={{0,8},{1,9},{2,10},{3,11},{4,12},{5,13},{6,14},{7,15},{8,0},{9,1},... | collective-permute-start | bytes 3080 | tf_op jit(solution)/shard_map/ppermute | solution.py:18
  125.5 2.0 %collective-permute-start.12 = (f32[2,128]{1,0:T(2,128)S(1)}, f32[2,128]{1,0:T(2,128)S(1)}, u32[]{:S(2)}, u32[]{:S(2)}) collective-permute-start(f32[2,128]{1,0:T(2,128)S(1)} %get-tuple-element.5), channel_id=1, source_target_pairs={{0,12},{1,13},{2,14},{3,15},{4,8},{5,9},{6,10},{7,11},{8,4},{9,5},... | collective-permute-start | bytes 3080 | tf_op jit(solution)/shard_map/ppermute | solution.py:18
  127.5 1.6 %collective-permute-done.11 = f32[2,128]{1,0:T(2,128)S(1)} collective-permute-done((f32[2,128]{1,0:T(2,128)S(1)}, f32[2,128]{1,0:T(2,128)S(1)}, u32[]{:S(2)}, u32[]{:S(2)}) %collective-permute-start.11) | collective-permute-done | bytes 1056 | tf_op jit(solution)/shard_map/ppermute | solution.py:18
  129.1 1.8 %collective-permute-done.12 = f32[2,128]{1,0:T(2,128)S(1)} collective-permute-done((f32[2,128]{1,0:T(2,128)S(1)}, f32[2,128]{1,0:T(2,128)S(1)}, u32[]{:S(2)}, u32[]{:S(2)}) %collective-permute-start.12) | collective-permute-done | bytes 1056 | tf_op jit(solution)/shard_map/ppermute | solution.py:18
  130.9 1.4 collective-permute-start.13
  133.1 1.4 collective-permute-done.13
  136.1 2.9 %collective-permute-done.16 = f32[2,128]{1,0:T(2,128)S(1)} collective-permute-done((f32[2,128]{1,0:T(2,128)S(1)}, f32[2,128]{1,0:T(2,128)S(1)}, u32[]{:S(2)}, u32[]{:S(2)}) %collective-permute-start.16) | collective-permute-done | bytes 1056 | tf_op jit(solution)/shard_map/ppermute | solution.py:18
  (93 shorter events, 18.8 us)
Async XLA Ops:
  7.2 67.1 %copy-start = (bf16[256,2048]{1,0:T(8,128)(2,1)S(1)}, bf16[256,2048]{1,0:T(8,128)(2,1)}, u32[]{:S(2)}) copy-start(bf16[256,2048]{1,0:T(8,128)(2,1)} %param.9) | copy-start | bytes 3145732
  7.2 57.8 %all-gather.2.cloned.1.call-start = ((), (), s32[]{:S(2)}) async-start(), calls=%async_computation | async-start | bytes 2654208 | tf_op jit(solution)/shard_map/all_gather | solution.py:87
  65.0 7.2 %collective-permute-start = (bf16[128,9216]{1,0:T(8,128)(2,1)}, bf16[128,9216]{1,0:T(8,128)(2,1)}, u32[]{:S(2)}, u32[]{:S(2)}) collective-permute-start(bf16[128,9216]{1,0:T(8,128)(2,1)} %all-gather.2.cloned.1.call-done), channel_id=1, source_target_pairs={{0,1},{1,0},{2,3},{3,2},{4,5},{5,4},{6,7},{7,6},{8,9},{9,8},{10,11... | collective-permute-start | bytes 7077896 | tf_op jit(solution)/shard_map/ppermute | solution.py:89
  65.5 6.5 %copy-start.1 = (bf16[128,9216]{1,0:T(8,128)(2,1)S(1)}, bf16[128,9216]{1,0:T(8,128)(2,1)}, u32[]{:S(2)}) copy-start(bf16[128,9216]{1,0:T(8,128)(2,1)} %all-gather.2.cloned.1.call-done) | copy-start | bytes 7077892
  72.0 9.2 %slice-start = ((s8[12845056]{0:T(1024)(128)(4,1)}), s8[4194304]{0:T(1024)(128)(4,1)S(1)}, s32[]{:S(2)}) async-start(s8[12845056]{0:T(1024)(128)(4,1)} %bitcast.92), calls=%async_computation.1 | async-start | bytes 8388608
  72.2 9.1 %slice-start.1 = ((s8[12845056]{0:T(1024)(128)(4,1)}), s8[4194304]{0:T(1024)(128)(4,1)S(1)}, s32[]{:S(2)}) async-start(s8[12845056]{0:T(1024)(128)(4,1)} %bitcast.92), calls=%async_computation.2 | async-start | bytes 8388608
  74.8 10.5 %collective-permute-start.3 = (f32[256,256]{1,0:T(8,128)S(1)}, f32[256,256]{1,0:T(8,128)S(1)}, u32[]{:S(2)}, u32[]{:S(2)}) collective-permute-start(f32[256,256]{1,0:T(8,128)S(1)} %fusion.11), channel_id=1, source_target_pairs={{0,16},{16,0},{1,17},{17,1},{2,18},{18,2},{3,19},{19,3},{4,20},{20... | collective-permute-start | bytes 786440 | tf_op jit(solution)/shard_map/ppermute | solution.py:18
  83.2 22.9 %copy-start.2 = (f32[256,448]{0,1:T(8,128)}, f32[256,448]{0,1:T(8,128)S(1)}, u32[]{:S(2)}) copy-start(f32[256,448]{0,1:T(8,128)S(1)} %fusion.1) | copy-start | bytes 1376260
  83.2 19.7 %collective-permute-start.1 = (f32[256,448]{0,1:T(8,128)S(1)}, f32[256,448]{0,1:T(8,128)S(1)}, u32[]{:S(2)}, u32[]{:S(2)}) collective-permute-start(f32[256,448]{0,1:T(8,128)S(1)} %fusion.3), channel_id=1, source_target_pairs={{0,16},{16,0},{1,17},{17,1},{2,18},{18,2},{3,19},{19,3},{4,20},{20... | collective-permute-start | bytes 1376264 | tf_op jit(solution)/shard_map/ppermute | solution.py:18
  84.4 21.8 %collective-permute-start.2 = (f32[256,448]{0,1:T(8,128)S(1)}, f32[256,448]{0,1:T(8,128)}, u32[]{:S(2)}, u32[]{:S(2)}) collective-permute-start(f32[256,448]{0,1:T(8,128)S(1)} %fusion.1), channel_id=1, source_target_pairs={{0,16},{16,0},{1,17},{17,1},{2,18},{18,2},{3,19},{19,3},{4,20},{20... | collective-permute-start | bytes 1376264 | tf_op jit(solution)/shard_map/ppermute | solution.py:18
  86.2 11.1 %collective-permute-start.4 = (bf16[1,256,256]{2,1,0:T(8,128)(2,1)S(1)}, bf16[1,256,256]{2,1,0:T(8,128)(2,1)S(1)}, u32[]{:S(2)}, u32[]{:S(2)}) collective-permute-start(bf16[1,256,256]{2,1,0:T(8,128)(2,1)S(1)} %bitcast_select_fusion.2), channel_id=1, source_target_pairs={{0,8},{1,9},{2,10},{3,11},{4,12},{5,13},{6,14},{7,15},{8,0},{9,1},... | collective-permute-start | bytes 393224 | tf_op jit(solution)/shard_map/ppermute | solution.py:18
  88.1 9.2 %collective-permute-start.5 = (bf16[1,256,256]{2,1,0:T(8,128)(2,1)S(1)}, bf16[1,256,256]{2,1,0:T(8,128)(2,1)S(1)}, u32[]{:S(2)}, u32[]{:S(2)}) collective-permute-start(bf16[1,256,256]{2,1,0:T(8,128)(2,1)S(1)} %bitcast_select_fusion.2), channel_id=1, source_target_pairs={{0,4},{1,5},{2,6},{3,7},{4,0},{5,1},{6,2},{7,3},{8,12},{9,13},{10,... | collective-permute-start | bytes 393224 | tf_op jit(solution)/shard_map/ppermute | solution.py:18
  88.6 10.5 %collective-permute-start.6 = (bf16[1,256,256]{2,1,0:T(8,128)(2,1)S(1)}, bf16[1,256,256]{2,1,0:T(8,128)(2,1)S(1)}, u32[]{:S(2)}, u32[]{:S(2)}) collective-permute-start(bf16[1,256,256]{2,1,0:T(8,128)(2,1)S(1)} %bitcast_select_fusion.2), channel_id=1, source_target_pairs={{0,12},{1,13},{2,14},{3,15},{4,8},{5,9},{6,10},{7,11},{8,4},{9,5},... | collective-permute-start | bytes 393224 | tf_op jit(solution)/shard_map/ppermute | solution.py:18
  100.6 9.6 %collective-permute-start.7 = (bf16[2,256,256]{2,1,0:T(8,128)(2,1)}, bf16[2,256,256]{2,1,0:T(8,128)(2,1)}, u32[]{:S(2)}, u32[]{:S(2)}) collective-permute-start(bf16[2,256,256]{2,1,0:T(8,128)(2,1)} %broadcast_select_fusion), channel_id=1, source_target_pairs={{0,2},{1,3},{2,0},{3,1},{4,6},{5,7},{6,4},{7,5},{8,10},{9,11},{10,... | collective-permute-start | bytes 786440 | tf_op jit(solution)/shard_map/ppermute | solution.py:18
  101.2 9.0 %collective-permute-start.8 = (bf16[2,256,256]{2,1,0:T(8,128)(2,1)}, bf16[2,256,256]{2,1,0:T(8,128)(2,1)}, u32[]{:S(2)}, u32[]{:S(2)}) collective-permute-start(bf16[2,256,256]{2,1,0:T(8,128)(2,1)} %broadcast_select_fusion), channel_id=1, source_target_pairs={{0,1},{1,0},{2,3},{3,2},{4,5},{5,4},{6,7},{7,6},{8,9},{9,8},{10,11... | collective-permute-start | bytes 786440 | tf_op jit(solution)/shard_map/ppermute | solution.py:18
  101.2 10.7 %collective-permute-start.9 = (bf16[2,256,256]{2,1,0:T(8,128)(2,1)}, bf16[2,256,256]{2,1,0:T(8,128)(2,1)}, u32[]{:S(2)}, u32[]{:S(2)}) collective-permute-start(bf16[2,256,256]{2,1,0:T(8,128)(2,1)} %broadcast_select_fusion), channel_id=1, source_target_pairs={{0,3},{1,2},{2,1},{3,0},{4,7},{5,6},{6,5},{7,4},{8,11},{9,10},{10,... | collective-permute-start | bytes 786440 | tf_op jit(solution)/shard_map/ppermute | solution.py:18
  115.7 23.9 %copy-start.4 = (s32[2]{0:T(128)S(1)}, s32[2]{0:T(128)}, u32[]{:S(2)}) copy-start(s32[2]{0:T(128)} %param.13) | copy-start | bytes 28
  122.5 5.0 %collective-permute-start.10 = (f32[2,128]{1,0:T(2,128)S(1)}, f32[2,128]{1,0:T(2,128)S(1)}, u32[]{:S(2)}, u32[]{:S(2)}) collective-permute-start(f32[2,128]{1,0:T(2,128)S(1)} %get-tuple-element.5), channel_id=1, source_target_pairs={{0,8},{1,9},{2,10},{3,11},{4,12},{5,13},{6,14},{7,15},{8,0},{9,1},... | collective-permute-start | bytes 3080 | tf_op jit(solution)/shard_map/ppermute | solution.py:18
  125.5 3.6 %collective-permute-start.11 = (f32[2,128]{1,0:T(2,128)S(1)}, f32[2,128]{1,0:T(2,128)S(1)}, u32[]{:S(2)}, u32[]{:S(2)}) collective-permute-start(f32[2,128]{1,0:T(2,128)S(1)} %get-tuple-element.5), channel_id=1, source_target_pairs={{0,4},{1,5},{2,6},{3,7},{4,0},{5,1},{6,2},{7,3},{8,12},{9,13},{10,... | collective-permute-start | bytes 3080 | tf_op jit(solution)/shard_map/ppermute | solution.py:18
  125.5 5.4 %collective-permute-start.12 = (f32[2,128]{1,0:T(2,128)S(1)}, f32[2,128]{1,0:T(2,128)S(1)}, u32[]{:S(2)}, u32[]{:S(2)}) collective-permute-start(f32[2,128]{1,0:T(2,128)S(1)} %get-tuple-element.5), channel_id=1, source_target_pairs={{0,12},{1,13},{2,14},{3,15},{4,8},{5,9},{6,10},{7,11},{8,4},{9,5},... | collective-permute-start | bytes 3080 | tf_op jit(solution)/shard_map/ppermute | solution.py:18
  130.9 3.6 %collective-permute-start.13 = (f32[2,128]{1,0:T(2,128)S(1)}, f32[2,128]{1,0:T(2,128)S(1)}, u32[]{:S(2)}, u32[]{:S(2)}) collective-permute-start(f32[2,128]{1,0:T(2,128)S(1)} %fusion.68), channel_id=1, source_target_pairs={{0,2},{1,3},{2,0},{3,1},{4,6},{5,7},{6,4},{7,5},{8,10},{9,11},{10,... | collective-permute-start | bytes 3080 | tf_op jit(solution)/shard_map/ppermute | solution.py:18
  132.3 2.2 %collective-permute-start.14 = (f32[2,128]{1,0:T(2,128)S(1)}, f32[2,128]{1,0:T(2,128)S(1)}, u32[]{:S(2)}, u32[]{:S(2)}) collective-permute-start(f32[2,128]{1,0:T(2,128)S(1)} %fusion.68), channel_id=1, source_target_pairs={{0,1},{1,0},{2,3},{3,2},{4,5},{5,4},{6,7},{7,6},{8,9},{9,8},{10,11... | collective-permute-start | bytes 3080 | tf_op jit(solution)/shard_map/ppermute | solution.py:18
  132.3 3.0 %collective-permute-start.15 = (f32[2,128]{1,0:T(2,128)S(1)}, f32[2,128]{1,0:T(2,128)S(1)}, u32[]{:S(2)}, u32[]{:S(2)}) collective-permute-start(f32[2,128]{1,0:T(2,128)S(1)} %fusion.68), channel_id=1, source_target_pairs={{0,3},{1,2},{2,1},{3,0},{4,7},{5,6},{6,5},{7,4},{8,11},{9,10},{10,... | collective-permute-start | bytes 3080 | tf_op jit(solution)/shard_map/ppermute | solution.py:18
  135.3 3.6 %collective-permute-start.16 = (f32[2,128]{1,0:T(2,128)S(1)}, f32[2,128]{1,0:T(2,128)S(1)}, u32[]{:S(2)}, u32[]{:S(2)}) collective-permute-start(f32[2,128]{1,0:T(2,128)S(1)} %fusion.67), channel_id=1, source_target_pairs={{0,16},{16,0},{1,17},{17,1},{2,18},{18,2},{3,19},{19,3},{4,20},{20... | collective-permute-start | bytes 3080 | tf_op jit(solution)/shard_map/ppermute | solution.py:18
  (3 other events, 16.2 us)
Sparse Core Ops, SparseCore 0:
  10.2 54.7 all-gather.1

commit v11 on v8

--- a/solution.py
+++ b/solution.py
@@ -90,7 +90,7 @@
     part_a = jnp.einsum("tk,jk->tj", all_a, basis_a, preferred_element_type=jnp.float32)
     rot_a_block = (xor_sum(part_a, "owner", owners) * live[:, None]).astype(jnp.bfloat16)
     pieces = []
-    step = m_block // 4
+    step = m_block // 2
     for start in range(0, m_block, step):
         part_g = jnp.einsum(
             "tk,jk->tj", all_g, basis_g[start:start + step], preferred_element_type=jnp.float32

time: 147 us -> 135 us (0.918)
  waiting for transfers between devices: 63.8 us -> 55.8 us
  starting transfers between devices: 28.7 us -> 26.4 us
  matrix products: 20.9 us -> 19.1 us
    ppermute x24 -> x22, waiting for transfers between devices: 63.1 us -> 55.1 us  [xor_round(): parts.append(lax.ppermute(held, axis, [(i, i ^ c) for i in range(size)]))]
    ppermute x24 -> x22, starting transfers between devices: 28.6 us -> 26.4 us  [xor_round(): parts.append(lax.ppermute(held, axis, [(i, i ^ c) for i in range(size)]))]
    dot_general x4 -> x2, matrix products: 14.1 us -> 12.2 us  [local(): jnp.einsum('tk,jk->tj', all_g, basis_g[start:start + step], preferred_ele...]
  transfers between devices with their start and end apart: 25 -> 23, of which waited for: 17 -> 15; matrix products, arithmetic and copies ran while one was open for 18% -> 22% of each run, Pallas kernels for 0% -> 0%
where the time goes in v11:
time: 135 us
  waiting for transfers between devices  55.8 us (41%)
  starting transfers between devices  26.4 us (20%)
  matrix products  19.1 us (14%)
  between operations  14.3 us (11%)
  other arithmetic  13.2 us (10%)
  local copies, waits for them, and re-layouts  6.15 us (5%)
    ppermute x22, waiting for transfers between devices, xor_round(): parts.append(lax.ppermute(held, axis, [(i, i ^ c) for i in range(size)]))  55.1 us
    ppermute x22, starting transfers between devices, xor_round(): parts.append(lax.ppermute(held, axis, [(i, i ^ c) for i in range(size)]))  26.4 us
    dot_general x2, matrix products, local(): jnp.einsum('tk,jk->tj', all_g, basis_g[start:start + step], preferred_ele...  12.2 us
    dot_general x1, matrix products, local(): jnp.einsum('stm,smn->stn', g_rows, scaled, preferred_element_type=jnp.flo...  6.48 us
    convert_element_type x1, other arithmetic, local(): denom = eigvals.astype(jnp.float32)  5.91 us
  transfers between devices with their start and end apart: 23, of which 15 were waited for; matrix products, arithmetic and copies ran while one was open for 22% of the time, Pallas kernels for 0%

profile of v11, /device:TPU:0, one launch (start us, length us, event | category | flops | bytes accessed | tf_op | source)
XLA Modules:
  0.0 135.0 jit_solution(8957338972333505539)
XLA Ops:
  7.9 5.1 %collective-permute-start.4 = (bf16[1,16,2048]{2,1,0:T(8,128)(2,1)}, bf16[1,16,2048]{2,1,0:T(8,128)(2,1)S(1)}, u32[]{:S(2)}, u32[]{:S(2)}) collective-permute-start(bf16[1,16,2048]{2,1,0:T(8,128)(2,1)} %bitcast.107), channel_id=1, source_target_pairs={{0,12},{1,13},{2,14},{3,15},{4,8},{5,9},{6,10},{7,11},{8,4},{9,5},... | collective-permute-start | bytes 196616 | tf_op jit(solution)/shard_map/ppermute | solution.py:17
  20.5 1.6 %collective-permute-start.6 = (bf16[4,16,2048]{2,1,0:T(8,128)(2,1)S(1)}, bf16[4,16,2048]{2,1,0:T(8,128)(2,1)S(1)}, u32[]{:S(2)}, u32[]{:S(2)}) collective-permute-start(bf16[4,16,2048]{2,1,0:T(8,128)(2,1)S(1)} %broadcast_select_fusion.1), channel_id=1, source_target_pairs={{0,1},{1,0},{2,3},{3,2},{4,5},{5,4},{6,7},{7,6},{8,9},{9,8},{10,11... | collective-permute-start | bytes 786440 | tf_op jit(solution)/shard_map/ppermute | solution.py:17
  22.7 8.7 %collective-permute-done.7 = bf16[4,16,2048]{2,1,0:T(8,128)(2,1)S(1)} collective-permute-done((bf16[4,16,2048]{2,1,0:T(8,128)(2,1)S(1)}, bf16[4,16,2048]{2,1,0:T(8,128)(2,1)S(1)}, u32[]{:S(2)}, u32[]{:S(2)}) %collective-permute-start.7) | collective-permute-done | bytes 262176 | tf_op jit(solution)/shard_map/ppermute | solution.py:17
  31.5 5.7 %collective-permute-done.5 = bf16[4,16,2048]{2,1,0:T(8,128)(2,1)S(1)} collective-permute-done((bf16[4,16,2048]{2,1,0:T(8,128)(2,1)S(1)}, bf16[4,16,2048]{2,1,0:T(8,128)(2,1)S(1)}, u32[]{:S(2)}, u32[]{:S(2)}) %collective-permute-start.5) | collective-permute-done | bytes 262176 | tf_op jit(solution)/shard_map/ppermute | solution.py:17
  38.7 1.6 %collective-permute-start.8 = (f32[256,256]{1,0:T(8,128)S(1)}, f32[256,256]{1,0:T(8,128)S(1)}, u32[]{:S(2)}, u32[]{:S(2)}) collective-permute-start(f32[256,256]{1,0:T(8,128)S(1)} %fusion.48), channel_id=1, source_target_pairs={{0,16},{16,0},{1,17},{17,1},{2,18},{18,2},{3,19},{19,3},{4,20},{20... | collective-permute-start | bytes 786440 | tf_op jit(solution)/shard_map/ppermute | solution.py:17
  40.3 6.7 %collective-permute-done.8 = f32[256,256]{1,0:T(8,128)S(1)} collective-permute-done((f32[256,256]{1,0:T(8,128)S(1)}, f32[256,256]{1,0:T(8,128)S(1)}, u32[]{:S(2)}, u32[]{:S(2)}) %collective-permute-start.8) | collective-permute-done | bytes 262176 | tf_op jit(solution)/shard_map/ppermute | solution.py:17
  47.2 2.2 %collective-permute-start.11 = (bf16[1,256,256]{2,1,0:T(8,128)(2,1)S(1)}, bf16[1,256,256]{2,1,0:T(8,128)(2,1)S(1)}, u32[]{:S(2)}, u32[]{:S(2)}) collective-permute-start(bf16[1,256,256]{2,1,0:T(8,128)(2,1)S(1)} %multiply_convert_fusion), channel_id=1, source_target_pairs={{0,12},{1,13},{2,14},{3,15},{4,8},{5,9},{6,10},{7,11},{8,4},{9,5},... | collective-permute-start | bytes 393224 | tf_op jit(solution)/shard_map/ppermute | solution.py:17
  49.8 1.9 %collective-permute-start.9 = (bf16[1,256,256]{2,1,0:T(8,128)(2,1)S(1)}, bf16[1,256,256]{2,1,0:T(8,128)(2,1)S(1)}, u32[]{:S(2)}, u32[]{:S(2)}) collective-permute-start(bf16[1,256,256]{2,1,0:T(8,128)(2,1)S(1)} %multiply_convert_fusion), channel_id=1, source_target_pairs={{0,8},{1,9},{2,10},{3,11},{4,12},{5,13},{6,14},{7,15},{8,0},{9,1},... | collective-permute-start | bytes 393224 | tf_op jit(solution)/shard_map/ppermute | solution.py:17
  51.8 5.9 %convert_element_type.47 = f32[896,2048]{1,0:T(8,128)} convert(bf16[896,2048]{1,0:T(8,128)(2,1)} %param.11) | non-fusion elementwise | flops 1835008 | bytes 11010048 | tf_op jit(solution)/shard_map/convert_element_type | solution.py:103
  58.2 4.9 %collective-permute-done.10 = bf16[1,256,256]{2,1,0:T(8,128)(2,1)S(1)} collective-permute-done((bf16[1,256,256]{2,1,0:T(8,128)(2,1)S(1)}, bf16[1,256,256]{2,1,0:T(8,128)(2,1)S(1)}, u32[]{:S(2)}, u32[]{:S(2)}) %collective-permute-start.10) | collective-permute-done | bytes 131104 | tf_op jit(solution)/shard_map/ppermute | solution.py:17
  63.1 7.2 %collective-permute-done.9 = bf16[1,256,256]{2,1,0:T(8,128)(2,1)S(1)} collective-permute-done((bf16[1,256,256]{2,1,0:T(8,128)(2,1)S(1)}, bf16[1,256,256]{2,1,0:T(8,128)(2,1)S(1)}, u32[]{:S(2)}, u32[]{:S(2)}) %collective-permute-start.9) | collective-permute-done | bytes 131104 | tf_op jit(solution)/shard_map/ppermute | solution.py:17
  73.5 6.7 %fusion.3 = f32[256,448]{0,1:T(8,128)} fusion(bf16[256,7168]{1,0:T(8,128)(2,1)} %all-gather.2.cloned.1.call-done, bf16[896,7168]{1,0:T(8,128)(2,1)} %param.10), kind=kOutput, calls=%fused_computation.8 | convolution fusion | flops 1644167168 | bytes 10551296 | tf_op jit(solution)/shard_map/tk,jk->tj/dot_general | solution.py:95
  80.2 1.5 %collective-permute-start = (f32[256,448]{0,1:T(8,128)}, f32[256,448]{0,1:T(8,128)}, u32[]{:S(2)}, u32[]{:S(2)}) collective-permute-start(f32[256,448]{0,1:T(8,128)} %fusion.3), channel_id=1, source_target_pairs={{0,16},{16,0},{1,17},{17,1},{2,18},{18,2},{3,19},{19,3},{4,20},{20... | collective-permute-start | bytes 1376264 | tf_op jit(solution)/shard_map/ppermute | solution.py:17
  81.6 5.5 %fusion.1 = f32[256,448]{0,1:T(8,128)} fusion(bf16[256,7168]{1,0:T(8,128)(2,1)S(1)} %copy-done.1, bf16[896,7168]{1,0:T(8,128)(2,1)} %param.10), kind=kOutput, calls=%fused_computation.6 | convolution fusion | flops 1644167168 | bytes 10551296 | tf_op jit(solution)/shard_map/tk,jk->tj/dot_general | solution.py:95
  90.0 3.9 %collective-permute-done = f32[256,448]{0,1:T(8,128)} collective-permute-done((f32[256,448]{0,1:T(8,128)}, f32[256,448]{0,1:T(8,128)}, u32[]{:S(2)}, u32[]{:S(2)}) %collective-permute-start) | collective-permute-done | bytes 458784 | tf_op jit(solution)/shard_map/ppermute | solution.py:17
  95.4 7.0 %collective-permute-done.1 = f32[256,448]{0,1:T(8,128)} collective-permute-done((f32[256,448]{0,1:T(8,128)}, f32[256,448]{0,1:T(8,128)}, u32[]{:S(2)}, u32[]{:S(2)}) %collective-permute-start.1) | collective-permute-done | bytes 458784 | tf_op jit(solution)/shard_map/ppermute | solution.py:17
  104.1 6.5 %fusion.8 = f32[2,128]{1,0:T(2,128)S(1)} fusion(bf16[2,128,2048]{2,1,0:T(8,128)(2,1)S(1)} %reshape_reshape.7, f32[896,2048]{1,0:T(8,128)} %convert_element_type.47, bf16[2,128,448]{1,2,0:T(8,128)(2,1)S(1)} %get-tuple-element.9, bf16[2,128,448]{1,2,0:T(8,128)(2,1)S(1)} %get-tuple-element.8), kind=kOutput, calls=%fused_computation.12 | convolution fusion | flops 1889795840 | bytes 8848384 | tf_op jit(solution)/shard_map/stm,smn->stn/dot_general | solution.py:108
  110.7 1.9 %collective-permute-start.15 = (f32[2,128]{1,0:T(2,128)S(1)}, f32[2,128]{1,0:T(2,128)S(1)}, u32[]{:S(2)}, u32[]{:S(2)}) collective-permute-start(f32[2,128]{1,0:T(2,128)S(1)} %get-tuple-element.7), channel_id=1, source_target_pairs={{0,8},{1,9},{2,10},{3,11},{4,12},{5,13},{6,14},{7,15},{8,0},{9,1},... | collective-permute-start | bytes 3080 | tf_op jit(solution)/shard_map/ppermute | solution.py:17
  112.5 2.5 %collective-permute-start.17 = (f32[2,128]{1,0:T(2,128)S(1)}, f32[2,128]{1,0:T(2,128)S(1)}, u32[]{:S(2)}, u32[]{:S(2)}) collective-permute-start(f32[2,128]{1,0:T(2,128)S(1)} %get-tuple-element.7), channel_id=1, source_target_pairs={{0,12},{1,13},{2,14},{3,15},{4,8},{5,9},{6,10},{7,11},{8,4},{9,5},... | collective-permute-start | bytes 3080 | tf_op jit(solution)/shard_map/ppermute | solution.py:17
  115.2 2.7 %collective-permute-done.17 = f32[2,128]{1,0:T(2,128)S(1)} collective-permute-done((f32[2,128]{1,0:T(2,128)S(1)}, f32[2,128]{1,0:T(2,128)S(1)}, u32[]{:S(2)}, u32[]{:S(2)}) %collective-permute-start.17) | collective-permute-done | bytes 1056 | tf_op jit(solution)/shard_map/ppermute | solution.py:17
  118.0 1.7 %collective-permute-start.19 = (f32[2,128]{1,0:T(2,128)S(1)}, f32[2,128]{1,0:T(2,128)S(1)}, u32[]{:S(2)}, u32[]{:S(2)}) collective-permute-start(f32[2,128]{1,0:T(2,128)S(1)} %fusion.55), channel_id=1, source_target_pairs={{0,1},{1,0},{2,3},{3,2},{4,5},{5,4},{6,7},{7,6},{8,9},{9,8},{10,11... | collective-permute-start | bytes 3080 | tf_op jit(solution)/shard_map/ppermute | solution.py:17
  121.0 2.2 %collective-permute-done.18 = f32[2,128]{1,0:T(2,128)S(1)} collective-permute-done((f32[2,128]{1,0:T(2,128)S(1)}, f32[2,128]{1,0:T(2,128)S(1)}, u32[]{:S(2)}, u32[]{:S(2)}) %collective-permute-start.18) | collective-permute-done | bytes 1056 | tf_op jit(solution)/shard_map/ppermute | solution.py:17
  123.2 1.5 %collective-permute-start.21 = (f32[2,128]{1,0:T(2,128)S(1)}, f32[2,128]{1,0:T(2,128)S(1)}, u32[]{:S(2)}, u32[]{:S(2)}) collective-permute-start(f32[2,128]{1,0:T(2,128)S(1)} %fusion.54), channel_id=1, source_target_pairs={{0,16},{16,0},{1,17},{17,1},{2,18},{18,2},{3,19},{19,3},{4,20},{20... | collective-permute-start | bytes 3080 | tf_op jit(solution)/shard_map/ppermute | solution.py:17
  124.8 2.1 %collective-permute-done.21 = f32[2,128]{1,0:T(2,128)S(1)} collective-permute-done((f32[2,128]{1,0:T(2,128)S(1)}, f32[2,128]{1,0:T(2,128)S(1)}, u32[]{:S(2)}, u32[]{:S(2)}) %collective-permute-start.21) | collective-permute-done | bytes 1056 | tf_op jit(solution)/shard_map/ppermute | solution.py:17
  (82 shorter events, 23.4 us)
Async XLA Ops:
  7.2 31.0 %copy-start = (bf16[256,2048]{1,0:T(8,128)(2,1)S(1)}, bf16[256,2048]{1,0:T(8,128)(2,1)}, u32[]{:S(2)}) copy-start(bf16[256,2048]{1,0:T(8,128)(2,1)} %param.9) | copy-start | bytes 3145732
  7.2 66.3 %all-gather.2.cloned.1.call-start = ((), (), s32[]{:S(2)}) async-start(), calls=%async_computation | async-start | bytes 3899392 | tf_op jit(solution)/shard_map/all_gather | solution.py:84
  7.9 8.7 %collective-permute-start.4 = (bf16[1,16,2048]{2,1,0:T(8,128)(2,1)}, bf16[1,16,2048]{2,1,0:T(8,128)(2,1)S(1)}, u32[]{:S(2)}, u32[]{:S(2)}) collective-permute-start(bf16[1,16,2048]{2,1,0:T(8,128)(2,1)} %bitcast.107), channel_id=1, source_target_pairs={{0,12},{1,13},{2,14},{3,15},{4,8},{5,9},{6,10},{7,11},{8,4},{9,5},... | collective-permute-start | bytes 196616 | tf_op jit(solution)/shard_map/ppermute | solution.py:17
  13.0 4.9 %collective-permute-start.3 = (bf16[1,16,2048]{2,1,0:T(8,128)(2,1)}, bf16[1,16,2048]{2,1,0:T(8,128)(2,1)S(1)}, u32[]{:S(2)}, u32[]{:S(2)}) collective-permute-start(bf16[1,16,2048]{2,1,0:T(8,128)(2,1)} %bitcast.108), channel_id=1, source_target_pairs={{0,4},{1,5},{2,6},{3,7},{4,0},{5,1},{6,2},{7,3},{8,12},{9,13},{10,... | collective-permute-start | bytes 196616 | tf_op jit(solution)/shard_map/ppermute | solution.py:17
  13.0 5.8 %collective-permute-start.2 = (bf16[1,16,2048]{2,1,0:T(8,128)(2,1)}, bf16[1,16,2048]{2,1,0:T(8,128)(2,1)S(1)}, u32[]{:S(2)}, u32[]{:S(2)}) collective-permute-start(bf16[1,16,2048]{2,1,0:T(8,128)(2,1)} %bitcast.109), channel_id=1, source_target_pairs={{0,8},{1,9},{2,10},{3,11},{4,12},{5,13},{6,14},{7,15},{8,0},{9,1},... | collective-permute-start | bytes 196616 | tf_op jit(solution)/shard_map/ppermute | solution.py:17
  20.4 11.1 %collective-permute-start.7 = (bf16[4,16,2048]{2,1,0:T(8,128)(2,1)S(1)}, bf16[4,16,2048]{2,1,0:T(8,128)(2,1)S(1)}, u32[]{:S(2)}, u32[]{:S(2)}) collective-permute-start(bf16[4,16,2048]{2,1,0:T(8,128)(2,1)S(1)} %broadcast_select_fusion.1), channel_id=1, source_target_pairs={{0,3},{1,2},{2,1},{3,0},{4,7},{5,6},{6,5},{7,4},{8,11},{9,10},{10,... | collective-permute-start | bytes 786440 | tf_op jit(solution)/shard_map/ppermute | solution.py:17
  20.5 11.0 %collective-permute-start.6 = (bf16[4,16,2048]{2,1,0:T(8,128)(2,1)S(1)}, bf16[4,16,2048]{2,1,0:T(8,128)(2,1)S(1)}, u32[]{:S(2)}, u32[]{:S(2)}) collective-permute-start(bf16[4,16,2048]{2,1,0:T(8,128)(2,1)S(1)} %broadcast_select_fusion.1), channel_id=1, source_target_pairs={{0,1},{1,0},{2,3},{3,2},{4,5},{5,4},{6,7},{7,6},{8,9},{9,8},{10,11... | collective-permute-start | bytes 786440 | tf_op jit(solution)/shard_map/ppermute | solution.py:17
  22.1 15.0 %collective-permute-start.5 = (bf16[4,16,2048]{2,1,0:T(8,128)(2,1)S(1)}, bf16[4,16,2048]{2,1,0:T(8,128)(2,1)S(1)}, u32[]{:S(2)}, u32[]{:S(2)}) collective-permute-start(bf16[4,16,2048]{2,1,0:T(8,128)(2,1)S(1)} %broadcast_select_fusion.1), channel_id=1, source_target_pairs={{0,2},{1,3},{2,0},{3,1},{4,6},{5,7},{6,4},{7,5},{8,10},{9,11},{10,... | collective-permute-start | bytes 786440 | tf_op jit(solution)/shard_map/ppermute | solution.py:17
  38.7 8.3 %collective-permute-start.8 = (f32[256,256]{1,0:T(8,128)S(1)}, f32[256,256]{1,0:T(8,128)S(1)}, u32[]{:S(2)}, u32[]{:S(2)}) collective-permute-start(f32[256,256]{1,0:T(8,128)S(1)} %fusion.48), channel_id=1, source_target_pairs={{0,16},{16,0},{1,17},{17,1},{2,18},{18,2},{3,19},{19,3},{4,20},{20... | collective-permute-start | bytes 786440 | tf_op jit(solution)/shard_map/ppermute | solution.py:17
  47.2 11.0 %collective-permute-start.11 = (bf16[1,256,256]{2,1,0:T(8,128)(2,1)S(1)}, bf16[1,256,256]{2,1,0:T(8,128)(2,1)S(1)}, u32[]{:S(2)}, u32[]{:S(2)}) collective-permute-start(bf16[1,256,256]{2,1,0:T(8,128)(2,1)S(1)} %multiply_convert_fusion), channel_id=1, source_target_pairs={{0,12},{1,13},{2,14},{3,15},{4,8},{5,9},{6,10},{7,11},{8,4},{9,5},... | collective-permute-start | bytes 393224 | tf_op jit(solution)/shard_map/ppermute | solution.py:17
  49.5 13.7 %collective-permute-start.10 = (bf16[1,256,256]{2,1,0:T(8,128)(2,1)S(1)}, bf16[1,256,256]{2,1,0:T(8,128)(2,1)S(1)}, u32[]{:S(2)}, u32[]{:S(2)}) collective-permute-start(bf16[1,256,256]{2,1,0:T(8,128)(2,1)S(1)} %multiply_convert_fusion), channel_id=1, source_target_pairs={{0,4},{1,5},{2,6},{3,7},{4,0},{5,1},{6,2},{7,3},{8,12},{9,13},{10,... | collective-permute-start | bytes 393224 | tf_op jit(solution)/shard_map/ppermute | solution.py:17
  49.8 20.6 %collective-permute-start.9 = (bf16[1,256,256]{2,1,0:T(8,128)(2,1)S(1)}, bf16[1,256,256]{2,1,0:T(8,128)(2,1)S(1)}, u32[]{:S(2)}, u32[]{:S(2)}) collective-permute-start(bf16[1,256,256]{2,1,0:T(8,128)(2,1)S(1)} %multiply_convert_fusion), channel_id=1, source_target_pairs={{0,8},{1,9},{2,10},{3,11},{4,12},{5,13},{6,14},{7,15},{8,0},{9,1},... | collective-permute-start | bytes 393224 | tf_op jit(solution)/shard_map/ppermute | solution.py:17
  71.1 16.5 %collective-permute-start.14 = (bf16[2,256,256]{2,1,0:T(8,128)(2,1)S(1)}, bf16[2,256,256]{2,1,0:T(8,128)(2,1)S(1)}, u32[]{:S(2)}, u32[]{:S(2)}) collective-permute-start(bf16[2,256,256]{2,1,0:T(8,128)(2,1)S(1)} %broadcast_select_fusion), channel_id=1, source_target_pairs={{0,3},{1,2},{2,1},{3,0},{4,7},{5,6},{6,5},{7,4},{8,11},{9,10},{10,... | collective-permute-start | bytes 786440 | tf_op jit(solution)/shard_map/ppermute | solution.py:17
  72.2 15.5 %collective-permute-start.13 = (bf16[2,256,256]{2,1,0:T(8,128)(2,1)S(1)}, bf16[2,256,256]{2,1,0:T(8,128)(2,1)S(1)}, u32[]{:S(2)}, u32[]{:S(2)}) collective-permute-start(bf16[2,256,256]{2,1,0:T(8,128)(2,1)S(1)} %broadcast_select_fusion), channel_id=1, source_target_pairs={{0,1},{1,0},{2,3},{3,2},{4,5},{5,4},{6,7},{7,6},{8,9},{9,8},{10,11... | collective-permute-start | bytes 786440 | tf_op jit(solution)/shard_map/ppermute | solution.py:17
  72.8 14.9 %collective-permute-start.12 = (bf16[2,256,256]{2,1,0:T(8,128)(2,1)S(1)}, bf16[2,256,256]{2,1,0:T(8,128)(2,1)S(1)}, u32[]{:S(2)}, u32[]{:S(2)}) collective-permute-start(bf16[2,256,256]{2,1,0:T(8,128)(2,1)S(1)} %broadcast_select_fusion), channel_id=1, source_target_pairs={{0,2},{1,3},{2,0},{3,1},{4,6},{5,7},{6,4},{7,5},{8,10},{9,11},{10,... | collective-permute-start | bytes 786440 | tf_op jit(solution)/shard_map/ppermute | solution.py:17
  80.2 13.7 %collective-permute-start = (f32[256,448]{0,1:T(8,128)}, f32[256,448]{0,1:T(8,128)}, u32[]{:S(2)}, u32[]{:S(2)}) collective-permute-start(f32[256,448]{0,1:T(8,128)} %fusion.3), channel_id=1, source_target_pairs={{0,16},{16,0},{1,17},{17,1},{2,18},{18,2},{3,19},{19,3},{4,20},{20... | collective-permute-start | bytes 1376264 | tf_op jit(solution)/shard_map/ppermute | solution.py:17
  87.1 15.4 %collective-permute-start.1 = (f32[256,448]{0,1:T(8,128)}, f32[256,448]{0,1:T(8,128)}, u32[]{:S(2)}, u32[]{:S(2)}) collective-permute-start(f32[256,448]{0,1:T(8,128)} %fusion.1), channel_id=1, source_target_pairs={{0,16},{16,0},{1,17},{17,1},{2,18},{18,2},{3,19},{19,3},{4,20},{20... | collective-permute-start | bytes 1376264 | tf_op jit(solution)/shard_map/ppermute | solution.py:17
  110.6 4.5 %collective-permute-start.16 = (f32[2,128]{1,0:T(2,128)S(1)}, f32[2,128]{1,0:T(2,128)S(1)}, u32[]{:S(2)}, u32[]{:S(2)}) collective-permute-start(f32[2,128]{1,0:T(2,128)S(1)} %get-tuple-element.7), channel_id=1, source_target_pairs={{0,4},{1,5},{2,6},{3,7},{4,0},{5,1},{6,2},{7,3},{8,12},{9,13},{10,... | collective-permute-start | bytes 3080 | tf_op jit(solution)/shard_map/ppermute | solution.py:17
  110.7 4.5 %collective-permute-start.15 = (f32[2,128]{1,0:T(2,128)S(1)}, f32[2,128]{1,0:T(2,128)S(1)}, u32[]{:S(2)}, u32[]{:S(2)}) collective-permute-start(f32[2,128]{1,0:T(2,128)S(1)} %get-tuple-element.7), channel_id=1, source_target_pairs={{0,8},{1,9},{2,10},{3,11},{4,12},{5,13},{6,14},{7,15},{8,0},{9,1},... | collective-permute-start | bytes 3080 | tf_op jit(solution)/shard_map/ppermute | solution.py:17
  112.5 5.4 %collective-permute-start.17 = (f32[2,128]{1,0:T(2,128)S(1)}, f32[2,128]{1,0:T(2,128)S(1)}, u32[]{:S(2)}, u32[]{:S(2)}) collective-permute-start(f32[2,128]{1,0:T(2,128)S(1)} %get-tuple-element.7), channel_id=1, source_target_pairs={{0,12},{1,13},{2,14},{3,15},{4,8},{5,9},{6,10},{7,11},{8,4},{9,5},... | collective-permute-start | bytes 3080 | tf_op jit(solution)/shard_map/ppermute | solution.py:17
  117.9 3.1 %collective-permute-start.20 = (f32[2,128]{1,0:T(2,128)S(1)}, f32[2,128]{1,0:T(2,128)S(1)}, u32[]{:S(2)}, u32[]{:S(2)}) collective-permute-start(f32[2,128]{1,0:T(2,128)S(1)} %fusion.55), channel_id=1, source_target_pairs={{0,3},{1,2},{2,1},{3,0},{4,7},{5,6},{6,5},{7,4},{8,11},{9,10},{10,... | collective-permute-start | bytes 3080 | tf_op jit(solution)/shard_map/ppermute | solution.py:17
  118.0 3.0 %collective-permute-start.19 = (f32[2,128]{1,0:T(2,128)S(1)}, f32[2,128]{1,0:T(2,128)S(1)}, u32[]{:S(2)}, u32[]{:S(2)}) collective-permute-start(f32[2,128]{1,0:T(2,128)S(1)} %fusion.55), channel_id=1, source_target_pairs={{0,1},{1,0},{2,3},{3,2},{4,5},{5,4},{6,7},{7,6},{8,9},{9,8},{10,11... | collective-permute-start | bytes 3080 | tf_op jit(solution)/shard_map/ppermute | solution.py:17
  119.6 3.6 %collective-permute-start.18 = (f32[2,128]{1,0:T(2,128)S(1)}, f32[2,128]{1,0:T(2,128)S(1)}, u32[]{:S(2)}, u32[]{:S(2)}) collective-permute-start(f32[2,128]{1,0:T(2,128)S(1)} %fusion.55), channel_id=1, source_target_pairs={{0,2},{1,3},{2,0},{3,1},{4,6},{5,7},{6,4},{7,5},{8,10},{9,11},{10,... | collective-permute-start | bytes 3080 | tf_op jit(solution)/shard_map/ppermute | solution.py:17
  123.2 3.6 %collective-permute-start.21 = (f32[2,128]{1,0:T(2,128)S(1)}, f32[2,128]{1,0:T(2,128)S(1)}, u32[]{:S(2)}, u32[]{:S(2)}) collective-permute-start(f32[2,128]{1,0:T(2,128)S(1)} %fusion.54), channel_id=1, source_target_pairs={{0,16},{16,0},{1,17},{17,1},{2,18},{18,2},{3,19},{19,3},{4,20},{20... | collective-permute-start | bytes 3080 | tf_op jit(solution)/shard_map/ppermute | solution.py:17
  (2 other events, 31.1 us)
Sparse Core Ops, SparseCore 0:
  10.3 60.4 all-gather.1

commit v12 on v11

--- a/solution.py
+++ b/solution.py
@@ -100,13 +100,15 @@
 
     rot_a = half_gather(rot_a_block, owners, readers)
 
-    denom = eigvals.astype(jnp.float32)
     g_rows = rot_g.reshape(slots, SEQ, m_block)
     a_rows = rot_a.reshape(slots, SEQ, width)
-    outer = jnp.einsum("smt,smn->stn", g_rows, a_rows, preferred_element_type=jnp.float32)
-    scaled = (outer / denom[None]).astype(jnp.bfloat16)
-    projected = jnp.einsum("stm,smn->stn", g_rows, scaled, preferred_element_type=jnp.float32)
-    partial = jnp.sum(projected * a_rows.astype(jnp.float32), axis=2) / (dim_ff * dim_d)
+    partials = []
+    for slot in range(slots):
+        outer = jnp.dot(g_rows[slot].T, a_rows[slot], preferred_element_type=jnp.float32)
+        scaled = (outer / eigvals.astype(jnp.float32)).astype(jnp.bfloat16)
+        projected = jnp.dot(g_rows[slot], scaled, preferred_element_type=jnp.float32)
+        partials.append(jnp.sum(projected * a_rows[slot].astype(jnp.float32), axis=1))
+    partial = jnp.stack(partials) / (dim_ff * dim_d)
     scores = xor_sum(xor_sum(partial, "reader", readers), "owner", owners)
 
     token_score = lax.dynamic_index_in_dim(scores, owner_index, 0, keepdims=False)

time: 135 us -> 146 us (1.081)
  waiting for transfers between devices: 55.8 us -> 76.4 us
  other arithmetic: 13.2 us -> 4.92 us
  local copies, waits for them, and re-layouts: 6.15 us -> 4.55 us
    ppermute x22, waiting for transfers between devices: 55.1 us -> 75.7 us  [xor_round(): parts.append(lax.ppermute(held, axis, [(i, i ^ c) for i in range(size)]))]
    convert_element_type x1 -> x0, other arithmetic: 5.91 us -> none  [local(): denom = eigvals.astype(jnp.float32)]
    add x6 -> x4, other arithmetic: 2.59 us -> 0.03 us  [xor_sum(): terms = [terms[i] + terms[i + 1] for i in range(0, len(terms), 2)]]
    dot_general x2, matrix products: 12.2 us -> 10.6 us  [local(): jnp.einsum('tk,jk->tj', all_g, basis_g[start:start + step], preferred_ele...]
    dot_general x1 -> x2, matrix products: 6.48 us -> 7.89 us  [local(): jnp.dot(g_rows[slot], scaled, preferred_element_type=jnp.float32)]
  transfers between devices with their start and end apart: 23 -> 23, of which waited for: 15 -> 17; matrix products, arithmetic and copies ran while one was open for 22% -> 9% of each run, Pallas kernels for 0% -> 0%
where the time goes in v12:
time: 146 us
  waiting for transfers between devices  76.4 us (52%)
  starting transfers between devices  26.5 us (18%)
  matrix products  19 us (13%)
  between operations  14.3 us (10%)
  other arithmetic  4.92 us (3%)
  local copies, waits for them, and re-layouts  4.55 us (3%)
    ppermute x22, waiting for transfers between devices, xor_round(): parts.append(lax.ppermute(held, axis, [(i, i ^ c) for i in range(size)]))  75.7 us
    ppermute x22, starting transfers between devices, xor_round(): parts.append(lax.ppermute(held, axis, [(i, i ^ c) for i in range(size)]))  26.5 us
    dot_general x2, matrix products, local(): jnp.einsum('tk,jk->tj', all_g, basis_g[start:start + step], preferred_ele...  10.6 us
    dot_general x2, matrix products, local(): jnp.dot(g_rows[slot], scaled, preferred_element_type=jnp.float32)  7.89 us
  transfers between devices with their start and end apart: 23, of which 17 were waited for; matrix products, arithmetic and copies ran while one was open for 9% of the time, Pallas kernels for 0%

profile of v12, /device:TPU:0, one launch (start us, length us, event | category | flops | bytes accessed | tf_op | source)
XLA Modules:
  0.0 145.7 jit_solution(14931675554609656768)
XLA Ops:
  7.9 5.1 %collective-permute-start.4 = (bf16[1,16,2048]{2,1,0:T(8,128)(2,1)}, bf16[1,16,2048]{2,1,0:T(8,128)(2,1)S(1)}, u32[]{:S(2)}, u32[]{:S(2)}) collective-permute-start(bf16[1,16,2048]{2,1,0:T(8,128)(2,1)} %bitcast.129), channel_id=1, source_target_pairs={{0,12},{1,13},{2,14},{3,15},{4,8},{5,9},{6,10},{7,11},{8,4},{9,5},... | collective-permute-start | bytes 196616 | tf_op jit(solution)/shard_map/ppermute | solution.py:17
  20.5 1.6 %collective-permute-start.6 = (bf16[4,16,2048]{2,1,0:T(8,128)(2,1)S(1)}, bf16[4,16,2048]{2,1,0:T(8,128)(2,1)S(1)}, u32[]{:S(2)}, u32[]{:S(2)}) collective-permute-start(bf16[4,16,2048]{2,1,0:T(8,128)(2,1)S(1)} %broadcast_select_fusion.1), channel_id=1, source_target_pairs={{0,1},{1,0},{2,3},{3,2},{4,5},{5,4},{6,7},{7,6},{8,9},{9,8},{10,11... | collective-permute-start | bytes 786440 | tf_op jit(solution)/shard_map/ppermute | solution.py:17
  22.7 8.7 %collective-permute-done.7 = bf16[4,16,2048]{2,1,0:T(8,128)(2,1)S(1)} collective-permute-done((bf16[4,16,2048]{2,1,0:T(8,128)(2,1)S(1)}, bf16[4,16,2048]{2,1,0:T(8,128)(2,1)S(1)}, u32[]{:S(2)}, u32[]{:S(2)}) %collective-permute-start.7) | collective-permute-done | bytes 262176 | tf_op jit(solution)/shard_map/ppermute | solution.py:17
  31.5 5.7 %collective-permute-done.5 = bf16[4,16,2048]{2,1,0:T(8,128)(2,1)S(1)} collective-permute-done((bf16[4,16,2048]{2,1,0:T(8,128)(2,1)S(1)}, bf16[4,16,2048]{2,1,0:T(8,128)(2,1)S(1)}, u32[]{:S(2)}, u32[]{:S(2)}) %collective-permute-start.5) | collective-permute-done | bytes 262176 | tf_op jit(solution)/shard_map/ppermute | solution.py:17
  38.7 1.6 %collective-permute-start.8 = (f32[256,256]{1,0:T(8,128)S(1)}, f32[256,256]{1,0:T(8,128)S(1)}, u32[]{:S(2)}, u32[]{:S(2)}) collective-permute-start(f32[256,256]{1,0:T(8,128)S(1)} %fusion.69), channel_id=1, source_target_pairs={{0,16},{16,0},{1,17},{17,1},{2,18},{18,2},{3,19},{19,3},{4,20},{20... | collective-permute-start | bytes 786440 | tf_op jit(solution)/shard_map/ppermute | solution.py:17
  40.3 6.7 %collective-permute-done.8 = f32[256,256]{1,0:T(8,128)S(1)} collective-permute-done((f32[256,256]{1,0:T(8,128)S(1)}, f32[256,256]{1,0:T(8,128)S(1)}, u32[]{:S(2)}, u32[]{:S(2)}) %collective-permute-start.8) | collective-permute-done | bytes 262176 | tf_op jit(solution)/shard_map/ppermute | solution.py:17
  47.2 2.2 %collective-permute-start.11 = (bf16[1,256,256]{2,1,0:T(8,128)(2,1)S(1)}, bf16[1,256,256]{2,1,0:T(8,128)(2,1)S(1)}, u32[]{:S(2)}, u32[]{:S(2)}) collective-permute-start(bf16[1,256,256]{2,1,0:T(8,128)(2,1)S(1)} %multiply_convert_fusion), channel_id=1, source_target_pairs={{0,12},{1,13},{2,14},{3,15},{4,8},{5,9},{6,10},{7,11},{8,4},{9,5},... | collective-permute-start | bytes 393224 | tf_op jit(solution)/shard_map/ppermute | solution.py:17
  49.8 1.9 %collective-permute-start.9 = (bf16[1,256,256]{2,1,0:T(8,128)(2,1)S(1)}, bf16[1,256,256]{2,1,0:T(8,128)(2,1)S(1)}, u32[]{:S(2)}, u32[]{:S(2)}) collective-permute-start(bf16[1,256,256]{2,1,0:T(8,128)(2,1)S(1)} %multiply_convert_fusion), channel_id=1, source_target_pairs={{0,8},{1,9},{2,10},{3,11},{4,12},{5,13},{6,14},{7,15},{8,0},{9,1},... | collective-permute-start | bytes 393224 | tf_op jit(solution)/shard_map/ppermute | solution.py:17
  51.8 6.5 %collective-permute-done.11 = bf16[1,256,256]{2,1,0:T(8,128)(2,1)S(1)} collective-permute-done((bf16[1,256,256]{2,1,0:T(8,128)(2,1)S(1)}, bf16[1,256,256]{2,1,0:T(8,128)(2,1)S(1)}, u32[]{:S(2)}, u32[]{:S(2)}) %collective-permute-start.11) | collective-permute-done | bytes 131104 | tf_op jit(solution)/shard_map/ppermute | solution.py:17
  58.2 4.9 %collective-permute-done.10 = bf16[1,256,256]{2,1,0:T(8,128)(2,1)S(1)} collective-permute-done((bf16[1,256,256]{2,1,0:T(8,128)(2,1)S(1)}, bf16[1,256,256]{2,1,0:T(8,128)(2,1)S(1)}, u32[]{:S(2)}, u32[]{:S(2)}) %collective-permute-start.10) | collective-permute-done | bytes 131104 | tf_op jit(solution)/shard_map/ppermute | solution.py:17
  63.1 7.3 %collective-permute-done.9 = bf16[1,256,256]{2,1,0:T(8,128)(2,1)S(1)} collective-permute-done((bf16[1,256,256]{2,1,0:T(8,128)(2,1)S(1)}, bf16[1,256,256]{2,1,0:T(8,128)(2,1)S(1)}, u32[]{:S(2)}, u32[]{:S(2)}) %collective-permute-start.9) | collective-permute-done | bytes 131104 | tf_op jit(solution)/shard_map/ppermute | solution.py:17
  73.4 6.3 %collective-permute-done.14 = bf16[2,256,256]{2,1,0:T(8,128)(2,1)S(1)} collective-permute-done((bf16[2,256,256]{2,1,0:T(8,128)(2,1)S(1)}, bf16[2,256,256]{2,1,0:T(8,128)(2,1)S(1)}, u32[]{:S(2)}, u32[]{:S(2)}) %collective-permute-start.14) | collective-permute-done | bytes 262176 | tf_op jit(solution)/shard_map/ppermute | solution.py:17
  79.8 5.6 %collective-permute-done.12 = bf16[2,256,256]{2,1,0:T(8,128)(2,1)S(1)} collective-permute-done((bf16[2,256,256]{2,1,0:T(8,128)(2,1)S(1)}, bf16[2,256,256]{2,1,0:T(8,128)(2,1)S(1)}, u32[]{:S(2)}, u32[]{:S(2)}) %collective-permute-start.12) | collective-permute-done | bytes 262176 | tf_op jit(solution)/shard_map/ppermute | solution.py:17
  86.2 5.9 %fusion.4 = f32[256,448]{0,1:T(8,128)S(1)} fusion(bf16[256,7168]{1,0:T(8,128)(2,1)} %all-gather.2.cloned.1.call-done, bf16[896,7168]{1,0:T(8,128)(2,1)} %param.10), kind=kOutput, calls=%fused_computation.10 | convolution fusion | flops 1644167168 | bytes 10551296 | tf_op jit(solution)/shard_map/tk,jk->tj/dot_general | solution.py:95
  92.1 1.5 %collective-permute-start = (f32[256,448]{0,1:T(8,128)S(1)}, f32[256,448]{0,1:T(8,128)S(1)}, u32[]{:S(2)}, u32[]{:S(2)}) collective-permute-start(f32[256,448]{0,1:T(8,128)S(1)} %fusion.4), channel_id=1, source_target_pairs={{0,16},{16,0},{1,17},{17,1},{2,18},{18,2},{3,19},{19,3},{4,20},{20... | collective-permute-start | bytes 1376264 | tf_op jit(solution)/shard_map/ppermute | solution.py:17
  93.7 4.7 %fusion.2 = f32[256,448]{0,1:T(8,128)S(1)} fusion(bf16[256,7168]{1,0:T(8,128)(2,1)S(1)} %copy-done.1, bf16[896,7168]{1,0:T(8,128)(2,1)} %param.10), kind=kOutput, calls=%fused_computation.8 | convolution fusion | flops 1644167168 | bytes 10551296 | tf_op jit(solution)/shard_map/tk,jk->tj/dot_general | solution.py:95
  99.4 6.1 %collective-permute-done = f32[256,448]{0,1:T(8,128)S(1)} collective-permute-done((f32[256,448]{0,1:T(8,128)S(1)}, f32[256,448]{0,1:T(8,128)S(1)}, u32[]{:S(2)}, u32[]{:S(2)}) %collective-permute-start) | collective-permute-done | bytes 458784 | tf_op jit(solution)/shard_map/ppermute | solution.py:17
  105.6 9.0 %collective-permute-done.1 = f32[256,448]{0,1:T(8,128)S(1)} collective-permute-done((f32[256,448]{0,1:T(8,128)S(1)}, f32[256,448]{0,1:T(8,128)S(1)}, u32[]{:S(2)}, u32[]{:S(2)}) %collective-permute-start.1) | collective-permute-done | bytes 458784 | tf_op jit(solution)/shard_map/ppermute | solution.py:17
  114.8 3.9 %fusion.23 = f32[128]{0:T(128)S(1)} fusion(bf16[896,2048]{1,0:T(8,128)(2,1)} %param.11, bf16[128,2048]{1,0:T(8,128)(2,1)S(1)} %bitcast.113, bf16[256,448]{0,1:T(8,128)(2,1)S(1)} %get-tuple-element.8, bf16[256,448]{0,1:T(8,128)(2,1)S(1)} %get-tuple-element.9), kind=kOutput, calls=%fused_computation.19 | convolution fusion | flops 946732928 | bytes 5636608 | tf_op jit(solution)/shard_map/dot_general | solution.py:109
  118.8 3.9 %fusion.20 = f32[128]{0:T(128)S(1)} fusion(bf16[896,2048]{1,0:T(8,128)(2,1)} %param.11, bf16[128,2048]{1,0:T(8,128)(2,1)S(1)} %bitcast.114, bf16[256,448]{0,1:T(8,128)(2,1)S(1)} %get-tuple-element.9, bf16[256,448]{0,1:T(8,128)(2,1)S(1)} %get-tuple-element.8), kind=kOutput, calls=%fused_computation.18 | convolution fusion | flops 946732928 | bytes 4653568 | tf_op jit(solution)/shard_map/dot_general | solution.py:109
  123.9 3.3 %collective-permute-start.15 = (f32[2,128]{1,0:T(2,128)S(1)}, f32[2,128]{1,0:T(2,128)S(1)}, u32[]{:S(2)}, u32[]{:S(2)}) collective-permute-start(f32[2,128]{1,0:T(2,128)S(1)} %maximum_multiply_fusion.1), channel_id=1, source_target_pairs={{0,8},{1,9},{2,10},{3,11},{4,12},{5,13},{6,14},{7,15},{8,0},{9,1},... | collective-permute-start | bytes 3080 | tf_op jit(solution)/shard_map/ppermute | solution.py:17
  131.8 2.1 %collective-permute-done.18 = f32[2,128]{1,0:T(2,128)S(1)} collective-permute-done((f32[2,128]{1,0:T(2,128)S(1)}, f32[2,128]{1,0:T(2,128)S(1)}, u32[]{:S(2)}, u32[]{:S(2)}) %collective-permute-start.18) | collective-permute-done | bytes 1056 | tf_op jit(solution)/shard_map/ppermute | solution.py:17
  134.0 1.5 %collective-permute-start.21 = (f32[2,128]{1,0:T(2,128)S(1)}, f32[2,128]{1,0:T(2,128)S(1)}, u32[]{:S(2)}, u32[]{:S(2)}) collective-permute-start(f32[2,128]{1,0:T(2,128)S(1)} %fusion.76), channel_id=1, source_target_pairs={{0,16},{16,0},{1,17},{17,1},{2,18},{18,2},{3,19},{19,3},{4,20},{20... | collective-permute-start | bytes 3080 | tf_op jit(solution)/shard_map/ppermute | solution.py:17
  135.5 2.1 %collective-permute-done.21 = f32[2,128]{1,0:T(2,128)S(1)} collective-permute-done((f32[2,128]{1,0:T(2,128)S(1)}, f32[2,128]{1,0:T(2,128)S(1)}, u32[]{:S(2)}, u32[]{:S(2)}) %collective-permute-start.21) | collective-permute-done | bytes 1056 | tf_op jit(solution)/shard_map/ppermute | solution.py:17
  (79 shorter events, 23.1 us)
Async XLA Ops:
  7.2 31.0 %copy-start = (bf16[256,2048]{1,0:T(8,128)(2,1)S(1)}, bf16[256,2048]{1,0:T(8,128)(2,1)}, u32[]{:S(2)}) copy-start(bf16[256,2048]{1,0:T(8,128)(2,1)} %param.9) | copy-start | bytes 3145732
  7.2 79.0 %all-gather.2.cloned.1.call-start = ((), (), s32[]{:S(2)}) async-start(), calls=%async_computation | async-start | bytes 3899392 | tf_op jit(solution)/shard_map/all_gather | solution.py:84
  7.9 8.6 %collective-permute-start.4 = (bf16[1,16,2048]{2,1,0:T(8,128)(2,1)}, bf16[1,16,2048]{2,1,0:T(8,128)(2,1)S(1)}, u32[]{:S(2)}, u32[]{:S(2)}) collective-permute-start(bf16[1,16,2048]{2,1,0:T(8,128)(2,1)} %bitcast.129), channel_id=1, source_target_pairs={{0,12},{1,13},{2,14},{3,15},{4,8},{5,9},{6,10},{7,11},{8,4},{9,5},... | collective-permute-start | bytes 196616 | tf_op jit(solution)/shard_map/ppermute | solution.py:17
  13.0 4.9 %collective-permute-start.3 = (bf16[1,16,2048]{2,1,0:T(8,128)(2,1)}, bf16[1,16,2048]{2,1,0:T(8,128)(2,1)S(1)}, u32[]{:S(2)}, u32[]{:S(2)}) collective-permute-start(bf16[1,16,2048]{2,1,0:T(8,128)(2,1)} %bitcast.130), channel_id=1, source_target_pairs={{0,4},{1,5},{2,6},{3,7},{4,0},{5,1},{6,2},{7,3},{8,12},{9,13},{10,... | collective-permute-start | bytes 196616 | tf_op jit(solution)/shard_map/ppermute | solution.py:17
  13.0 5.8 %collective-permute-start.2 = (bf16[1,16,2048]{2,1,0:T(8,128)(2,1)}, bf16[1,16,2048]{2,1,0:T(8,128)(2,1)S(1)}, u32[]{:S(2)}, u32[]{:S(2)}) collective-permute-start(bf16[1,16,2048]{2,1,0:T(8,128)(2,1)} %bitcast.131), channel_id=1, source_target_pairs={{0,8},{1,9},{2,10},{3,11},{4,12},{5,13},{6,14},{7,15},{8,0},{9,1},... | collective-permute-start | bytes 196616 | tf_op jit(solution)/shard_map/ppermute | solution.py:17
  20.4 11.1 %collective-permute-start.7 = (bf16[4,16,2048]{2,1,0:T(8,128)(2,1)S(1)}, bf16[4,16,2048]{2,1,0:T(8,128)(2,1)S(1)}, u32[]{:S(2)}, u32[]{:S(2)}) collective-permute-start(bf16[4,16,2048]{2,1,0:T(8,128)(2,1)S(1)} %broadcast_select_fusion.1), channel_id=1, source_target_pairs={{0,3},{1,2},{2,1},{3,0},{4,7},{5,6},{6,5},{7,4},{8,11},{9,10},{10,... | collective-permute-start | bytes 786440 | tf_op jit(solution)/shard_map/ppermute | solution.py:17
  20.5 11.0 %collective-permute-start.6 = (bf16[4,16,2048]{2,1,0:T(8,128)(2,1)S(1)}, bf16[4,16,2048]{2,1,0:T(8,128)(2,1)S(1)}, u32[]{:S(2)}, u32[]{:S(2)}) collective-permute-start(bf16[4,16,2048]{2,1,0:T(8,128)(2,1)S(1)} %broadcast_select_fusion.1), channel_id=1, source_target_pairs={{0,1},{1,0},{2,3},{3,2},{4,5},{5,4},{6,7},{7,6},{8,9},{9,8},{10,11... | collective-permute-start | bytes 786440 | tf_op jit(solution)/shard_map/ppermute | solution.py:17
  22.1 15.0 %collective-permute-start.5 = (bf16[4,16,2048]{2,1,0:T(8,128)(2,1)S(1)}, bf16[4,16,2048]{2,1,0:T(8,128)(2,1)S(1)}, u32[]{:S(2)}, u32[]{:S(2)}) collective-permute-start(bf16[4,16,2048]{2,1,0:T(8,128)(2,1)S(1)} %broadcast_select_fusion.1), channel_id=1, source_target_pairs={{0,2},{1,3},{2,0},{3,1},{4,6},{5,7},{6,4},{7,5},{8,10},{9,11},{10,... | collective-permute-start | bytes 786440 | tf_op jit(solution)/shard_map/ppermute | solution.py:17
  38.7 8.3 %collective-permute-start.8 = (f32[256,256]{1,0:T(8,128)S(1)}, f32[256,256]{1,0:T(8,128)S(1)}, u32[]{:S(2)}, u32[]{:S(2)}) collective-permute-start(f32[256,256]{1,0:T(8,128)S(1)} %fusion.69), channel_id=1, source_target_pairs={{0,16},{16,0},{1,17},{17,1},{2,18},{18,2},{3,19},{19,3},{4,20},{20... | collective-permute-start | bytes 786440 | tf_op jit(solution)/shard_map/ppermute | solution.py:17
  47.2 11.0 %collective-permute-start.11 = (bf16[1,256,256]{2,1,0:T(8,128)(2,1)S(1)}, bf16[1,256,256]{2,1,0:T(8,128)(2,1)S(1)}, u32[]{:S(2)}, u32[]{:S(2)}) collective-permute-start(bf16[1,256,256]{2,1,0:T(8,128)(2,1)S(1)} %multiply_convert_fusion), channel_id=1, source_target_pairs={{0,12},{1,13},{2,14},{3,15},{4,8},{5,9},{6,10},{7,11},{8,4},{9,5},... | collective-permute-start | bytes 393224 | tf_op jit(solution)/shard_map/ppermute | solution.py:17
  49.5 13.7 %collective-permute-start.10 = (bf16[1,256,256]{2,1,0:T(8,128)(2,1)S(1)}, bf16[1,256,256]{2,1,0:T(8,128)(2,1)S(1)}, u32[]{:S(2)}, u32[]{:S(2)}) collective-permute-start(bf16[1,256,256]{2,1,0:T(8,128)(2,1)S(1)} %multiply_convert_fusion), channel_id=1, source_target_pairs={{0,4},{1,5},{2,6},{3,7},{4,0},{5,1},{6,2},{7,3},{8,12},{9,13},{10,... | collective-permute-start | bytes 393224 | tf_op jit(solution)/shard_map/ppermute | solution.py:17
  49.8 20.6 %collective-permute-start.9 = (bf16[1,256,256]{2,1,0:T(8,128)(2,1)S(1)}, bf16[1,256,256]{2,1,0:T(8,128)(2,1)S(1)}, u32[]{:S(2)}, u32[]{:S(2)}) collective-permute-start(bf16[1,256,256]{2,1,0:T(8,128)(2,1)S(1)} %multiply_convert_fusion), channel_id=1, source_target_pairs={{0,8},{1,9},{2,10},{3,11},{4,12},{5,13},{6,14},{7,15},{8,0},{9,1},... | collective-permute-start | bytes 393224 | tf_op jit(solution)/shard_map/ppermute | solution.py:17
  71.1 8.6 %collective-permute-start.14 = (bf16[2,256,256]{2,1,0:T(8,128)(2,1)S(1)}, bf16[2,256,256]{2,1,0:T(8,128)(2,1)S(1)}, u32[]{:S(2)}, u32[]{:S(2)}) collective-permute-start(bf16[2,256,256]{2,1,0:T(8,128)(2,1)S(1)} %broadcast_select_fusion), channel_id=1, source_target_pairs={{0,3},{1,2},{2,1},{3,0},{4,7},{5,6},{6,5},{7,4},{8,11},{9,10},{10,... | collective-permute-start | bytes 786440 | tf_op jit(solution)/shard_map/ppermute | solution.py:17
  72.2 7.6 %collective-permute-start.13 = (bf16[2,256,256]{2,1,0:T(8,128)(2,1)S(1)}, bf16[2,256,256]{2,1,0:T(8,128)(2,1)S(1)}, u32[]{:S(2)}, u32[]{:S(2)}) collective-permute-start(bf16[2,256,256]{2,1,0:T(8,128)(2,1)S(1)} %broadcast_select_fusion), channel_id=1, source_target_pairs={{0,1},{1,0},{2,3},{3,2},{4,5},{5,4},{6,7},{7,6},{8,9},{9,8},{10,11... | collective-permute-start | bytes 786440 | tf_op jit(solution)/shard_map/ppermute | solution.py:17
  72.8 12.6 %collective-permute-start.12 = (bf16[2,256,256]{2,1,0:T(8,128)(2,1)S(1)}, bf16[2,256,256]{2,1,0:T(8,128)(2,1)S(1)}, u32[]{:S(2)}, u32[]{:S(2)}) collective-permute-start(bf16[2,256,256]{2,1,0:T(8,128)(2,1)S(1)} %broadcast_select_fusion), channel_id=1, source_target_pairs={{0,2},{1,3},{2,0},{3,1},{4,6},{5,7},{6,4},{7,5},{8,10},{9,11},{10,... | collective-permute-start | bytes 786440 | tf_op jit(solution)/shard_map/ppermute | solution.py:17
  92.1 13.4 %collective-permute-start = (f32[256,448]{0,1:T(8,128)S(1)}, f32[256,448]{0,1:T(8,128)S(1)}, u32[]{:S(2)}, u32[]{:S(2)}) collective-permute-start(f32[256,448]{0,1:T(8,128)S(1)} %fusion.4), channel_id=1, source_target_pairs={{0,16},{16,0},{1,17},{17,1},{2,18},{18,2},{3,19},{19,3},{4,20},{20... | collective-permute-start | bytes 1376264 | tf_op jit(solution)/shard_map/ppermute | solution.py:17
  98.4 16.2 %collective-permute-start.1 = (f32[256,448]{0,1:T(8,128)S(1)}, f32[256,448]{0,1:T(8,128)S(1)}, u32[]{:S(2)}, u32[]{:S(2)}) collective-permute-start(f32[256,448]{0,1:T(8,128)S(1)} %fusion.2), channel_id=1, source_target_pairs={{0,16},{16,0},{1,17},{17,1},{2,18},{18,2},{3,19},{19,3},{4,20},{20... | collective-permute-start | bytes 1376264 | tf_op jit(solution)/shard_map/ppermute | solution.py:17
  122.8 5.4 %collective-permute-start.17 = (f32[2,128]{1,0:T(2,128)S(1)}, f32[2,128]{1,0:T(2,128)S(1)}, u32[]{:S(2)}, u32[]{:S(2)}) collective-permute-start(f32[2,128]{1,0:T(2,128)S(1)} %maximum_multiply_fusion.1), channel_id=1, source_target_pairs={{0,12},{1,13},{2,14},{3,15},{4,8},{5,9},{6,10},{7,11},{8,4},{9,5},... | collective-permute-start | bytes 3080 | tf_op jit(solution)/shard_map/ppermute | solution.py:17
  123.9 4.3 %collective-permute-start.16 = (f32[2,128]{1,0:T(2,128)S(1)}, f32[2,128]{1,0:T(2,128)S(1)}, u32[]{:S(2)}, u32[]{:S(2)}) collective-permute-start(f32[2,128]{1,0:T(2,128)S(1)} %maximum_multiply_fusion.1), channel_id=1, source_target_pairs={{0,4},{1,5},{2,6},{3,7},{4,0},{5,1},{6,2},{7,3},{8,12},{9,13},{10,... | collective-permute-start | bytes 3080 | tf_op jit(solution)/shard_map/ppermute | solution.py:17
  123.9 4.8 %collective-permute-start.15 = (f32[2,128]{1,0:T(2,128)S(1)}, f32[2,128]{1,0:T(2,128)S(1)}, u32[]{:S(2)}, u32[]{:S(2)}) collective-permute-start(f32[2,128]{1,0:T(2,128)S(1)} %maximum_multiply_fusion.1), channel_id=1, source_target_pairs={{0,8},{1,9},{2,10},{3,11},{4,12},{5,13},{6,14},{7,15},{8,0},{9,1},... | collective-permute-start | bytes 3080 | tf_op jit(solution)/shard_map/ppermute | solution.py:17
  128.8 3.1 %collective-permute-start.20 = (f32[2,128]{1,0:T(2,128)S(1)}, f32[2,128]{1,0:T(2,128)S(1)}, u32[]{:S(2)}, u32[]{:S(2)}) collective-permute-start(f32[2,128]{1,0:T(2,128)S(1)} %fusion.77), channel_id=1, source_target_pairs={{0,3},{1,2},{2,1},{3,0},{4,7},{5,6},{6,5},{7,4},{8,11},{9,10},{10,... | collective-permute-start | bytes 3080 | tf_op jit(solution)/shard_map/ppermute | solution.py:17
  128.9 3.0 %collective-permute-start.19 = (f32[2,128]{1,0:T(2,128)S(1)}, f32[2,128]{1,0:T(2,128)S(1)}, u32[]{:S(2)}, u32[]{:S(2)}) collective-permute-start(f32[2,128]{1,0:T(2,128)S(1)} %fusion.77), channel_id=1, source_target_pairs={{0,1},{1,0},{2,3},{3,2},{4,5},{5,4},{6,7},{7,6},{8,9},{9,8},{10,11... | collective-permute-start | bytes 3080 | tf_op jit(solution)/shard_map/ppermute | solution.py:17
  130.4 3.6 %collective-permute-start.18 = (f32[2,128]{1,0:T(2,128)S(1)}, f32[2,128]{1,0:T(2,128)S(1)}, u32[]{:S(2)}, u32[]{:S(2)}) collective-permute-start(f32[2,128]{1,0:T(2,128)S(1)} %fusion.77), channel_id=1, source_target_pairs={{0,2},{1,3},{2,0},{3,1},{4,6},{5,7},{6,4},{7,5},{8,10},{9,11},{10,... | collective-permute-start | bytes 3080 | tf_op jit(solution)/shard_map/ppermute | solution.py:17
  134.0 3.6 %collective-permute-start.21 = (f32[2,128]{1,0:T(2,128)S(1)}, f32[2,128]{1,0:T(2,128)S(1)}, u32[]{:S(2)}, u32[]{:S(2)}) collective-permute-start(f32[2,128]{1,0:T(2,128)S(1)} %fusion.76), channel_id=1, source_target_pairs={{0,16},{16,0},{1,17},{17,1},{2,18},{18,2},{3,19},{19,3},{4,20},{20... | collective-permute-start | bytes 3080 | tf_op jit(solution)/shard_map/ppermute | solution.py:17
  (2 other events, 26.4 us)
Sparse Core Ops, SparseCore 0:
  10.3 60.4 all-gather.1

commit v13 on v9

--- a/solution.py
+++ b/solution.py
@@ -92,10 +92,10 @@
 
     part_a = jnp.einsum("tk,jk->tj", all_a, basis_a, preferred_element_type=jnp.float32)
     rot_a_block = (xor_sum(part_a, "owner", owners) * live[:, None]).astype(jnp.bfloat16)
-    step = m_block // 4
+    first = min(256, m_block // 2)
     parts_g = [
-        jnp.einsum("tk,jk->tj", all_g, basis_g[start:start + step], preferred_element_type=jnp.float32)
-        for start in range(0, m_block, step)
+        jnp.einsum("tk,jk->tj", all_g, basis_g[start:stop], preferred_element_type=jnp.float32)
+        for start, stop in ((0, first), (first, m_block))
     ]
     parts_g[0], eig_after = lax.optimization_barrier((parts_g[0], eigvals))
     pieces = [(xor_sum(part_g, "owner", owners) * live[:, None]).astype(jnp.bfloat16) for part_g in parts_g]

time: 140 us -> 136 us (0.971)
  starting transfers between devices: 28.6 us -> 25.5 us
  matrix products: 21.2 us -> 18.9 us
    ppermute x24 -> x22, starting transfers between devices: 28.5 us -> 25.5 us  [xor_round(): parts.append(lax.ppermute(held, axis, [(i, i ^ c) for i in range(size)]))]
    dot_general x4 -> x2, matrix products: 14.2 us -> 12.1 us  [local(): jnp.einsum('tk,jk->tj', all_g, basis_g[start:stop], preferred_element_typ...]
    ppermute x24 -> x22, waiting for transfers between devices: 59.6 us -> 59.9 us  [xor_round(): parts.append(lax.ppermute(held, axis, [(i, i ^ c) for i in range(size)]))]
  transfers between devices with their start and end apart: 25 -> 23, of which waited for: 15 -> 14; matrix products, arithmetic and copies ran while one was open for 16% -> 16% of each run, Pallas kernels for 0% -> 0%
where the time goes in v13:
time: 136 us
  waiting for transfers between devices  60.6 us (45%)
  starting transfers between devices  25.5 us (19%)
  matrix products  18.9 us (14%)
  between operations  14.3 us (11%)
  other arithmetic  10 us (7%)
  local copies, waits for them, and re-layouts  6.76 us (5%)
    ppermute x22, waiting for transfers between devices, xor_round(): parts.append(lax.ppermute(held, axis, [(i, i ^ c) for i in range(size)]))  59.9 us
    ppermute x22, starting transfers between devices, xor_round(): parts.append(lax.ppermute(held, axis, [(i, i ^ c) for i in range(size)]))  25.5 us
    dot_general x2, matrix products, local(): jnp.einsum('tk,jk->tj', all_g, basis_g[start:stop], preferred_element_typ...  12.1 us
    dot_general x1, matrix products, local(): jnp.einsum('stm,smn->stn', g_rows, scaled, preferred_element_type=jnp.flo...  6.38 us
    convert_element_type x1, other arithmetic, local(): denom = eig_after.astype(jnp.float32)  3.86 us
  transfers between devices with their start and end apart: 23, of which 14 were waited for; matrix products, arithmetic and copies ran while one was open for 16% of the time, Pallas kernels for 0%

profile of v13, /device:TPU:0, one launch (start us, length us, event | category | flops | bytes accessed | tf_op | source)
XLA Modules:
  0.0 136.1 jit_solution(3383461568087134634)
XLA Ops:
  7.9 5.1 %collective-permute-start.4 = (bf16[1,16,2048]{2,1,0:T(8,128)(2,1)}, bf16[1,16,2048]{2,1,0:T(8,128)(2,1)S(1)}, u32[]{:S(2)}, u32[]{:S(2)}) collective-permute-start(bf16[1,16,2048]{2,1,0:T(8,128)(2,1)} %bitcast.109), channel_id=1, source_target_pairs={{0,12},{1,13},{2,14},{3,15},{4,8},{5,9},{6,10},{7,11},{8,4},{9,5},... | collective-permute-start | bytes 196616 | tf_op jit(solution)/shard_map/ppermute | solution.py:17
  20.5 1.6 %collective-permute-start.6 = (bf16[4,16,2048]{2,1,0:T(8,128)(2,1)S(1)}, bf16[4,16,2048]{2,1,0:T(8,128)(2,1)S(1)}, u32[]{:S(2)}, u32[]{:S(2)}) collective-permute-start(bf16[4,16,2048]{2,1,0:T(8,128)(2,1)S(1)} %broadcast_select_fusion), channel_id=1, source_target_pairs={{0,1},{1,0},{2,3},{3,2},{4,5},{5,4},{6,7},{7,6},{8,9},{9,8},{10,11... | collective-permute-start | bytes 786440 | tf_op jit(solution)/shard_map/ppermute | solution.py:17
  22.7 8.7 %collective-permute-done.7 = bf16[4,16,2048]{2,1,0:T(8,128)(2,1)S(1)} collective-permute-done((bf16[4,16,2048]{2,1,0:T(8,128)(2,1)S(1)}, bf16[4,16,2048]{2,1,0:T(8,128)(2,1)S(1)}, u32[]{:S(2)}, u32[]{:S(2)}) %collective-permute-start.7) | collective-permute-done | bytes 262176 | tf_op jit(solution)/shard_map/ppermute | solution.py:17
  31.5 5.7 %collective-permute-done.5 = bf16[4,16,2048]{2,1,0:T(8,128)(2,1)S(1)} collective-permute-done((bf16[4,16,2048]{2,1,0:T(8,128)(2,1)S(1)}, bf16[4,16,2048]{2,1,0:T(8,128)(2,1)S(1)}, u32[]{:S(2)}, u32[]{:S(2)}) %collective-permute-start.5) | collective-permute-done | bytes 262176 | tf_op jit(solution)/shard_map/ppermute | solution.py:17
  38.7 1.6 %collective-permute-start.8 = (f32[256,256]{1,0:T(8,128)S(1)}, f32[256,256]{1,0:T(8,128)S(1)}, u32[]{:S(2)}, u32[]{:S(2)}) collective-permute-start(f32[256,256]{1,0:T(8,128)S(1)} %fusion.46), channel_id=1, source_target_pairs={{0,16},{16,0},{1,17},{17,1},{2,18},{18,2},{3,19},{19,3},{4,20},{20... | collective-permute-start | bytes 786440 | tf_op jit(solution)/shard_map/ppermute | solution.py:17
  40.3 6.7 %collective-permute-done.8 = f32[256,256]{1,0:T(8,128)S(1)} collective-permute-done((f32[256,256]{1,0:T(8,128)S(1)}, f32[256,256]{1,0:T(8,128)S(1)}, u32[]{:S(2)}, u32[]{:S(2)}) %collective-permute-start.8) | collective-permute-done | bytes 262176 | tf_op jit(solution)/shard_map/ppermute | solution.py:17
  47.2 2.2 %collective-permute-start.11 = (bf16[1,256,256]{2,1,0:T(8,128)(2,1)S(1)}, bf16[1,256,256]{2,1,0:T(8,128)(2,1)S(1)}, u32[]{:S(2)}, u32[]{:S(2)}) collective-permute-start(bf16[1,256,256]{2,1,0:T(8,128)(2,1)S(1)} %multiply_convert_fusion.1), channel_id=1, source_target_pairs={{0,12},{1,13},{2,14},{3,15},{4,8},{5,9},{6,10},{7,11},{8,4},{9,5},... | collective-permute-start | bytes 393224 | tf_op jit(solution)/shard_map/ppermute | solution.py:17
  49.8 1.9 %collective-permute-start.9 = (bf16[1,256,256]{2,1,0:T(8,128)(2,1)S(1)}, bf16[1,256,256]{2,1,0:T(8,128)(2,1)S(1)}, u32[]{:S(2)}, u32[]{:S(2)}) collective-permute-start(bf16[1,256,256]{2,1,0:T(8,128)(2,1)S(1)} %multiply_convert_fusion.1), channel_id=1, source_target_pairs={{0,8},{1,9},{2,10},{3,11},{4,12},{5,13},{6,14},{7,15},{8,0},{9,1},... | collective-permute-start | bytes 393224 | tf_op jit(solution)/shard_map/ppermute | solution.py:17
  51.8 6.5 %collective-permute-done.11 = bf16[1,256,256]{2,1,0:T(8,128)(2,1)S(1)} collective-permute-done((bf16[1,256,256]{2,1,0:T(8,128)(2,1)S(1)}, bf16[1,256,256]{2,1,0:T(8,128)(2,1)S(1)}, u32[]{:S(2)}, u32[]{:S(2)}) %collective-permute-start.11) | collective-permute-done | bytes 131104 | tf_op jit(solution)/shard_map/ppermute | solution.py:17
  58.2 4.9 %collective-permute-done.10 = bf16[1,256,256]{2,1,0:T(8,128)(2,1)S(1)} collective-permute-done((bf16[1,256,256]{2,1,0:T(8,128)(2,1)S(1)}, bf16[1,256,256]{2,1,0:T(8,128)(2,1)S(1)}, u32[]{:S(2)}, u32[]{:S(2)}) %collective-permute-start.10) | collective-permute-done | bytes 131104 | tf_op jit(solution)/shard_map/ppermute | solution.py:17
  63.1 7.3 %collective-permute-done.9 = bf16[1,256,256]{2,1,0:T(8,128)(2,1)S(1)} collective-permute-done((bf16[1,256,256]{2,1,0:T(8,128)(2,1)S(1)}, bf16[1,256,256]{2,1,0:T(8,128)(2,1)S(1)}, u32[]{:S(2)}, u32[]{:S(2)}) %collective-permute-start.9) | collective-permute-done | bytes 131104 | tf_op jit(solution)/shard_map/ppermute | solution.py:17
  71.2 4.4 %fusion.5 = f32[256,256]{1,0:T(8,128)S(1)} fusion(bf16[256,7168]{1,0:T(8,128)(2,1)} %all-gather.2.cloned.1.call-done, bf16[896,7168]{1,0:T(8,128)(2,1)} %param.10), kind=kOutput, calls=%fused_computation.9 | convolution fusion | flops 939524096 | bytes 7602176 | tf_op jit(solution)/shard_map/tk,jk->tj/dot_general | solution.py:97
  75.6 1.5 %collective-permute-start = (f32[256,256]{1,0:T(8,128)S(1)}, f32[256,256]{1,0:T(8,128)S(1)}, u32[]{:S(2)}, u32[]{:S(2)}) collective-permute-start(f32[256,256]{1,0:T(8,128)S(1)} %fusion.5), channel_id=1, source_target_pairs={{0,16},{16,0},{1,17},{17,1},{2,18},{18,2},{3,19},{19,3},{4,20},{20... | collective-permute-start | bytes 786440 | tf_op jit(solution)/shard_map/ppermute | solution.py:17
  79.3 7.6 %fusion = f32[256,640]{1,0:T(8,128)} fusion(bf16[256,7168]{1,0:T(8,128)(2,1)S(1)} %copy-done.3, bf16[896,7168]{1,0:T(8,128)(2,1)} %param.10), kind=kOutput, calls=%fused_computation.5 | convolution fusion | flops 2348810240 | bytes 13500416 | tf_op jit(solution)/shard_map/tk,jk->tj/dot_general | solution.py:97
  87.5 3.9 %convert_element_type.47 = f32[896,2048]{1,0:T(8,128)} convert(bf16[896,2048]{1,0:T(8,128)(2,1)S(1)} %copy-done.1) | non-fusion elementwise | flops 1835008 | bytes 11010048 | tf_op jit(solution)/shard_map/convert_element_type | solution.py:106
  94.7 8.9 %collective-permute-done.1 = f32[256,640]{1,0:T(8,128)} collective-permute-done((f32[256,640]{1,0:T(8,128)}, f32[256,640]{1,0:T(8,128)}, u32[]{:S(2)}, u32[]{:S(2)}) %collective-permute-start.1) | collective-permute-done | bytes 655392 | tf_op jit(solution)/shard_map/ppermute | solution.py:17
  103.6 1.4 %fusion.10 = f32[1,256,640]{2,1,0:T(8,128)S(1)} fusion(s32[]{:T(128)S(6)} %select_n.165, f32[1,256,640]{2,1,0:T(8,128)} %bitcast.6, s32[]{:T(128)S(6)} %select_n.164, f32[1,256,640]{2,1,0:T(8,128)} %bitcast.7), kind=kLoop, calls=%fused_computation.22 | loop fusion | flops 491520 | bytes 1966088 | tf_op jit(solution)/shard_map/add | solution.py:39
  105.3 6.4 %fusion.8 = f32[2,128]{1,0:T(2,128)S(1)} fusion(bf16[2,128,2048]{2,1,0:T(8,128)(2,1)S(1)} %reshape_reshape.7, f32[896,2048]{1,0:T(8,128)} %convert_element_type.47, bf16[2,128,640]{1,2,0:T(8,128)(2,1)S(1)} %multiply_convert_fusion, bf16[2,128,256]{1,2,0:T(8,128)(2,1)S(1)} %multiply_convert_fusion.2), kind=kOutput, calls=%fused_computation.16 | convolution fusion | flops 1889795840 | bytes 8848384 | tf_op jit(solution)/shard_map/stm,smn->stn/dot_general | solution.py:111
  111.8 2.0 %collective-permute-start.15 = (f32[2,128]{1,0:T(2,128)S(1)}, f32[2,128]{1,0:T(2,128)S(1)}, u32[]{:S(2)}, u32[]{:S(2)}) collective-permute-start(f32[2,128]{1,0:T(2,128)S(1)} %get-tuple-element.13), channel_id=1, source_target_pairs={{0,8},{1,9},{2,10},{3,11},{4,12},{5,13},{6,14},{7,15},{8,0},{9,1},... | collective-permute-start | bytes 3080 | tf_op jit(solution)/shard_map/ppermute | solution.py:17
  113.8 2.4 %collective-permute-start.17 = (f32[2,128]{1,0:T(2,128)S(1)}, f32[2,128]{1,0:T(2,128)S(1)}, u32[]{:S(2)}, u32[]{:S(2)}) collective-permute-start(f32[2,128]{1,0:T(2,128)S(1)} %get-tuple-element.13), channel_id=1, source_target_pairs={{0,12},{1,13},{2,14},{3,15},{4,8},{5,9},{6,10},{7,11},{8,4},{9,5},... | collective-permute-start | bytes 3080 | tf_op jit(solution)/shard_map/ppermute | solution.py:17
  116.3 2.8 %collective-permute-done.17 = f32[2,128]{1,0:T(2,128)S(1)} collective-permute-done((f32[2,128]{1,0:T(2,128)S(1)}, f32[2,128]{1,0:T(2,128)S(1)}, u32[]{:S(2)}, u32[]{:S(2)}) %collective-permute-start.17) | collective-permute-done | bytes 1056 | tf_op jit(solution)/shard_map/ppermute | solution.py:17
  119.2 1.6 %collective-permute-start.19 = (f32[2,128]{1,0:T(2,128)S(1)}, f32[2,128]{1,0:T(2,128)S(1)}, u32[]{:S(2)}, u32[]{:S(2)}) collective-permute-start(f32[2,128]{1,0:T(2,128)S(1)} %fusion.53), channel_id=1, source_target_pairs={{0,1},{1,0},{2,3},{3,2},{4,5},{5,4},{6,7},{7,6},{8,9},{9,8},{10,11... | collective-permute-start | bytes 3080 | tf_op jit(solution)/shard_map/ppermute | solution.py:17
  122.2 2.2 %collective-permute-done.18 = f32[2,128]{1,0:T(2,128)S(1)} collective-permute-done((f32[2,128]{1,0:T(2,128)S(1)}, f32[2,128]{1,0:T(2,128)S(1)}, u32[]{:S(2)}, u32[]{:S(2)}) %collective-permute-start.18) | collective-permute-done | bytes 1056 | tf_op jit(solution)/shard_map/ppermute | solution.py:17
  125.0 3.0 %collective-permute-done.21 = f32[2,128]{1,0:T(2,128)S(1)} collective-permute-done((f32[2,128]{1,0:T(2,128)S(1)}, f32[2,128]{1,0:T(2,128)S(1)}, u32[]{:S(2)}, u32[]{:S(2)}) %collective-permute-start.21) | collective-permute-done | bytes 1056 | tf_op jit(solution)/shard_map/ppermute | solution.py:17
  (86 shorter events, 21.6 us)
Async XLA Ops:
  7.2 31.0 %copy-start = (bf16[256,2048]{1,0:T(8,128)(2,1)S(1)}, bf16[256,2048]{1,0:T(8,128)(2,1)}, u32[]{:S(2)}) copy-start(bf16[256,2048]{1,0:T(8,128)(2,1)} %param.9) | copy-start | bytes 3145732
  7.2 64.0 %all-gather.2.cloned.1.call-start = ((), (), s32[]{:S(2)}) async-start(), calls=%async_computation | async-start | bytes 3899392 | tf_op jit(solution)/shard_map/all_gather | solution.py:87
  7.9 8.7 %collective-permute-start.4 = (bf16[1,16,2048]{2,1,0:T(8,128)(2,1)}, bf16[1,16,2048]{2,1,0:T(8,128)(2,1)S(1)}, u32[]{:S(2)}, u32[]{:S(2)}) collective-permute-start(bf16[1,16,2048]{2,1,0:T(8,128)(2,1)} %bitcast.109), channel_id=1, source_target_pairs={{0,12},{1,13},{2,14},{3,15},{4,8},{5,9},{6,10},{7,11},{8,4},{9,5},... | collective-permute-start | bytes 196616 | tf_op jit(solution)/shard_map/ppermute | solution.py:17
  13.0 4.9 %collective-permute-start.3 = (bf16[1,16,2048]{2,1,0:T(8,128)(2,1)}, bf16[1,16,2048]{2,1,0:T(8,128)(2,1)S(1)}, u32[]{:S(2)}, u32[]{:S(2)}) collective-permute-start(bf16[1,16,2048]{2,1,0:T(8,128)(2,1)} %bitcast.110), channel_id=1, source_target_pairs={{0,4},{1,5},{2,6},{3,7},{4,0},{5,1},{6,2},{7,3},{8,12},{9,13},{10,... | collective-permute-start | bytes 196616 | tf_op jit(solution)/shard_map/ppermute | solution.py:17
  13.0 5.8 %collective-permute-start.2 = (bf16[1,16,2048]{2,1,0:T(8,128)(2,1)}, bf16[1,16,2048]{2,1,0:T(8,128)(2,1)S(1)}, u32[]{:S(2)}, u32[]{:S(2)}) collective-permute-start(bf16[1,16,2048]{2,1,0:T(8,128)(2,1)} %bitcast.111), channel_id=1, source_target_pairs={{0,8},{1,9},{2,10},{3,11},{4,12},{5,13},{6,14},{7,15},{8,0},{9,1},... | collective-permute-start | bytes 196616 | tf_op jit(solution)/shard_map/ppermute | solution.py:17
  20.4 11.1 %collective-permute-start.7 = (bf16[4,16,2048]{2,1,0:T(8,128)(2,1)S(1)}, bf16[4,16,2048]{2,1,0:T(8,128)(2,1)S(1)}, u32[]{:S(2)}, u32[]{:S(2)}) collective-permute-start(bf16[4,16,2048]{2,1,0:T(8,128)(2,1)S(1)} %broadcast_select_fusion), channel_id=1, source_target_pairs={{0,3},{1,2},{2,1},{3,0},{4,7},{5,6},{6,5},{7,4},{8,11},{9,10},{10,... | collective-permute-start | bytes 786440 | tf_op jit(solution)/shard_map/ppermute | solution.py:17
  20.5 11.0 %collective-permute-start.6 = (bf16[4,16,2048]{2,1,0:T(8,128)(2,1)S(1)}, bf16[4,16,2048]{2,1,0:T(8,128)(2,1)S(1)}, u32[]{:S(2)}, u32[]{:S(2)}) collective-permute-start(bf16[4,16,2048]{2,1,0:T(8,128)(2,1)S(1)} %broadcast_select_fusion), channel_id=1, source_target_pairs={{0,1},{1,0},{2,3},{3,2},{4,5},{5,4},{6,7},{7,6},{8,9},{9,8},{10,11... | collective-permute-start | bytes 786440 | tf_op jit(solution)/shard_map/ppermute | solution.py:17
  22.1 15.0 %collective-permute-start.5 = (bf16[4,16,2048]{2,1,0:T(8,128)(2,1)S(1)}, bf16[4,16,2048]{2,1,0:T(8,128)(2,1)S(1)}, u32[]{:S(2)}, u32[]{:S(2)}) collective-permute-start(bf16[4,16,2048]{2,1,0:T(8,128)(2,1)S(1)} %broadcast_select_fusion), channel_id=1, source_target_pairs={{0,2},{1,3},{2,0},{3,1},{4,6},{5,7},{6,4},{7,5},{8,10},{9,11},{10,... | collective-permute-start | bytes 786440 | tf_op jit(solution)/shard_map/ppermute | solution.py:17
  38.7 8.3 %collective-permute-start.8 = (f32[256,256]{1,0:T(8,128)S(1)}, f32[256,256]{1,0:T(8,128)S(1)}, u32[]{:S(2)}, u32[]{:S(2)}) collective-permute-start(f32[256,256]{1,0:T(8,128)S(1)} %fusion.46), channel_id=1, source_target_pairs={{0,16},{16,0},{1,17},{17,1},{2,18},{18,2},{3,19},{19,3},{4,20},{20... | collective-permute-start | bytes 786440 | tf_op jit(solution)/shard_map/ppermute | solution.py:17
  47.2 11.0 %collective-permute-start.11 = (bf16[1,256,256]{2,1,0:T(8,128)(2,1)S(1)}, bf16[1,256,256]{2,1,0:T(8,128)(2,1)S(1)}, u32[]{:S(2)}, u32[]{:S(2)}) collective-permute-start(bf16[1,256,256]{2,1,0:T(8,128)(2,1)S(1)} %multiply_convert_fusion.1), channel_id=1, source_target_pairs={{0,12},{1,13},{2,14},{3,15},{4,8},{5,9},{6,10},{7,11},{8,4},{9,5},... | collective-permute-start | bytes 393224 | tf_op jit(solution)/shard_map/ppermute | solution.py:17
  49.5 13.6 %collective-permute-start.10 = (bf16[1,256,256]{2,1,0:T(8,128)(2,1)S(1)}, bf16[1,256,256]{2,1,0:T(8,128)(2,1)S(1)}, u32[]{:S(2)}, u32[]{:S(2)}) collective-permute-start(bf16[1,256,256]{2,1,0:T(8,128)(2,1)S(1)} %multiply_convert_fusion.1), channel_id=1, source_target_pairs={{0,4},{1,5},{2,6},{3,7},{4,0},{5,1},{6,2},{7,3},{8,12},{9,13},{10,... | collective-permute-start | bytes 393224 | tf_op jit(solution)/shard_map/ppermute | solution.py:17
  49.8 20.6 %collective-permute-start.9 = (bf16[1,256,256]{2,1,0:T(8,128)(2,1)S(1)}, bf16[1,256,256]{2,1,0:T(8,128)(2,1)S(1)}, u32[]{:S(2)}, u32[]{:S(2)}) collective-permute-start(bf16[1,256,256]{2,1,0:T(8,128)(2,1)S(1)} %multiply_convert_fusion.1), channel_id=1, source_target_pairs={{0,8},{1,9},{2,10},{3,11},{4,12},{5,13},{6,14},{7,15},{8,0},{9,1},... | collective-permute-start | bytes 393224 | tf_op jit(solution)/shard_map/ppermute | solution.py:17
  75.6 15.7 %collective-permute-start = (f32[256,256]{1,0:T(8,128)S(1)}, f32[256,256]{1,0:T(8,128)S(1)}, u32[]{:S(2)}, u32[]{:S(2)}) collective-permute-start(f32[256,256]{1,0:T(8,128)S(1)} %fusion.5), channel_id=1, source_target_pairs={{0,16},{16,0},{1,17},{17,1},{2,18},{18,2},{3,19},{19,3},{4,20},{20... | collective-permute-start | bytes 786440 | tf_op jit(solution)/shard_map/ppermute | solution.py:17
  77.1 15.2 %collective-permute-start.14 = (bf16[2,256,256]{2,1,0:T(8,128)(2,1)S(1)}, bf16[2,256,256]{2,1,0:T(8,128)(2,1)S(1)}, u32[]{:S(2)}, u32[]{:S(2)}) collective-permute-start(bf16[2,256,256]{2,1,0:T(8,128)(2,1)S(1)} %broadcast_select_fusion.1), channel_id=1, source_target_pairs={{0,3},{1,2},{2,1},{3,0},{4,7},{5,6},{6,5},{7,4},{8,11},{9,10},{10,... | collective-permute-start | bytes 786440 | tf_op jit(solution)/shard_map/ppermute | solution.py:17
  78.2 14.1 %collective-permute-start.13 = (bf16[2,256,256]{2,1,0:T(8,128)(2,1)S(1)}, bf16[2,256,256]{2,1,0:T(8,128)(2,1)S(1)}, u32[]{:S(2)}, u32[]{:S(2)}) collective-permute-start(bf16[2,256,256]{2,1,0:T(8,128)(2,1)S(1)} %broadcast_select_fusion.1), channel_id=1, source_target_pairs={{0,1},{1,0},{2,3},{3,2},{4,5},{5,4},{6,7},{7,6},{8,9},{9,8},{10,11... | collective-permute-start | bytes 786440 | tf_op jit(solution)/shard_map/ppermute | solution.py:17
  78.8 13.5 %collective-permute-start.12 = (bf16[2,256,256]{2,1,0:T(8,128)(2,1)S(1)}, bf16[2,256,256]{2,1,0:T(8,128)(2,1)S(1)}, u32[]{:S(2)}, u32[]{:S(2)}) collective-permute-start(bf16[2,256,256]{2,1,0:T(8,128)(2,1)S(1)} %broadcast_select_fusion.1), channel_id=1, source_target_pairs={{0,2},{1,3},{2,0},{3,1},{4,6},{5,7},{6,4},{7,5},{8,10},{9,11},{10,... | collective-permute-start | bytes 786440 | tf_op jit(solution)/shard_map/ppermute | solution.py:17
  86.9 16.7 %collective-permute-start.1 = (f32[256,640]{1,0:T(8,128)}, f32[256,640]{1,0:T(8,128)}, u32[]{:S(2)}, u32[]{:S(2)}) collective-permute-start(f32[256,640]{1,0:T(8,128)} %fusion), channel_id=1, source_target_pairs={{0,16},{16,0},{1,17},{17,1},{2,18},{18,2},{3,19},{19,3},{4,20},{20... | collective-permute-start | bytes 1966088 | tf_op jit(solution)/shard_map/ppermute | solution.py:17
  111.7 4.5 %collective-permute-start.16 = (f32[2,128]{1,0:T(2,128)S(1)}, f32[2,128]{1,0:T(2,128)S(1)}, u32[]{:S(2)}, u32[]{:S(2)}) collective-permute-start(f32[2,128]{1,0:T(2,128)S(1)} %get-tuple-element.13), channel_id=1, source_target_pairs={{0,4},{1,5},{2,6},{3,7},{4,0},{5,1},{6,2},{7,3},{8,12},{9,13},{10,... | collective-permute-start | bytes 3080 | tf_op jit(solution)/shard_map/ppermute | solution.py:17
  111.8 4.5 %collective-permute-start.15 = (f32[2,128]{1,0:T(2,128)S(1)}, f32[2,128]{1,0:T(2,128)S(1)}, u32[]{:S(2)}, u32[]{:S(2)}) collective-permute-start(f32[2,128]{1,0:T(2,128)S(1)} %get-tuple-element.13), channel_id=1, source_target_pairs={{0,8},{1,9},{2,10},{3,11},{4,12},{5,13},{6,14},{7,15},{8,0},{9,1},... | collective-permute-start | bytes 3080 | tf_op jit(solution)/shard_map/ppermute | solution.py:17
  113.8 5.4 %collective-permute-start.17 = (f32[2,128]{1,0:T(2,128)S(1)}, f32[2,128]{1,0:T(2,128)S(1)}, u32[]{:S(2)}, u32[]{:S(2)}) collective-permute-start(f32[2,128]{1,0:T(2,128)S(1)} %get-tuple-element.13), channel_id=1, source_target_pairs={{0,12},{1,13},{2,14},{3,15},{4,8},{5,9},{6,10},{7,11},{8,4},{9,5},... | collective-permute-start | bytes 3080 | tf_op jit(solution)/shard_map/ppermute | solution.py:17
  119.2 3.1 %collective-permute-start.20 = (f32[2,128]{1,0:T(2,128)S(1)}, f32[2,128]{1,0:T(2,128)S(1)}, u32[]{:S(2)}, u32[]{:S(2)}) collective-permute-start(f32[2,128]{1,0:T(2,128)S(1)} %fusion.53), channel_id=1, source_target_pairs={{0,3},{1,2},{2,1},{3,0},{4,7},{5,6},{6,5},{7,4},{8,11},{9,10},{10,... | collective-permute-start | bytes 3080 | tf_op jit(solution)/shard_map/ppermute | solution.py:17
  119.2 3.0 %collective-permute-start.19 = (f32[2,128]{1,0:T(2,128)S(1)}, f32[2,128]{1,0:T(2,128)S(1)}, u32[]{:S(2)}, u32[]{:S(2)}) collective-permute-start(f32[2,128]{1,0:T(2,128)S(1)} %fusion.53), channel_id=1, source_target_pairs={{0,1},{1,0},{2,3},{3,2},{4,5},{5,4},{6,7},{7,6},{8,9},{9,8},{10,11... | collective-permute-start | bytes 3080 | tf_op jit(solution)/shard_map/ppermute | solution.py:17
  120.8 3.6 %collective-permute-start.18 = (f32[2,128]{1,0:T(2,128)S(1)}, f32[2,128]{1,0:T(2,128)S(1)}, u32[]{:S(2)}, u32[]{:S(2)}) collective-permute-start(f32[2,128]{1,0:T(2,128)S(1)} %fusion.53), channel_id=1, source_target_pairs={{0,2},{1,3},{2,0},{3,1},{4,6},{5,7},{6,4},{7,5},{8,10},{9,11},{10,... | collective-permute-start | bytes 3080 | tf_op jit(solution)/shard_map/ppermute | solution.py:17
  124.4 3.6 %collective-permute-start.21 = (f32[2,128]{1,0:T(2,128)S(1)}, f32[2,128]{1,0:T(2,128)S(1)}, u32[]{:S(2)}, u32[]{:S(2)}) collective-permute-start(f32[2,128]{1,0:T(2,128)S(1)} %fusion.52), channel_id=1, source_target_pairs={{0,16},{16,0},{1,17},{17,1},{2,18},{18,2},{3,19},{19,3},{4,20},{20... | collective-permute-start | bytes 3080 | tf_op jit(solution)/shard_map/ppermute | solution.py:17
  (4 other events, 44.4 us)
Sparse Core Ops, SparseCore 0:
  10.3 60.4 all-gather.1

commit v14 on v11

--- a/solution.py
+++ b/solution.py
@@ -69,6 +69,24 @@
     return jnp.transpose(held, (1, 0, 2)).reshape(block.shape[0], -1)
 
 
+def owner_rounded(part, live, owners):
+    if owners != 2:
+        return (xor_sum(part, "owner", owners) * live[:, None]).astype(jnp.bfloat16)
+    owner_index = lax.axis_index("owner")
+    half = part.shape[0] // 2
+    mine = lax.dynamic_slice_in_dim(part, owner_index * half, half, axis=0)
+    theirs = lax.dynamic_slice_in_dim(part, (1 - owner_index) * half, half, axis=0)
+    received = lax.ppermute(theirs, "owner", [(0, 1), (1, 0)])
+    first = jnp.where(owner_index == 0, mine, received)
+    second = jnp.where(owner_index == 0, received, mine)
+    live_mine = lax.dynamic_slice_in_dim(live, owner_index * half, half, axis=0)
+    rounded = ((first + second) * live_mine[:, None]).astype(jnp.bfloat16)
+    other = lax.ppermute(rounded, "owner", [(0, 1), (1, 0)])
+    low = jnp.where(owner_index == 0, rounded, other)
+    high = jnp.where(owner_index == 0, other, rounded)
+    return jnp.concatenate([low, high], axis=0)
+
+
 def local(acts, grads, basis_a, basis_g, eigvals, lengths, shuffle):
     owners = lax.axis_size("owner")
     readers = lax.axis_size("reader")
@@ -95,7 +113,7 @@
         part_g = jnp.einsum(
             "tk,jk->tj", all_g, basis_g[start:start + step], preferred_element_type=jnp.float32
         )
-        pieces.append((xor_sum(part_g, "owner", owners) * live[:, None]).astype(jnp.bfloat16))
+        pieces.append(owner_rounded(part_g, live, owners))
     rot_g = jnp.concatenate(pieces, axis=1)
 
     rot_a = half_gather(rot_a_block, owners, readers)

time: 135 us -> 139 us (1.030)
  waiting for transfers between devices: 55.8 us -> 59.4 us
  matrix products: 19.1 us -> 17.5 us
    ppermute x0 -> x4, waiting for transfers between devices: none -> 13.7 us  [the longest x2 9.53 us: owner_rounded(): received = lax.ppermute(theirs, 'owner', [(0, 1), (1, 0)])]
    ppermute x22 -> x20, waiting for transfers between devices: 55.1 us -> 45 us  [xor_round(): parts.append(lax.ppermute(held, axis, [(i, i ^ c) for i in range(size)]))]
    ppermute x0 -> x4, starting transfers between devices: none -> 4.18 us  [the longest x2 2.16 us: owner_rounded(): other = lax.ppermute(rounded, 'owner', [(0, 1), (1, 0)])]
    ppermute x22 -> x20, starting transfers between devices: 26.4 us -> 23.5 us  [xor_round(): parts.append(lax.ppermute(held, axis, [(i, i ^ c) for i in range(size)]))]
    add x6 -> x4, other arithmetic: 2.59 us -> 0.03 us  [xor_sum(): terms = [terms[i] + terms[i + 1] for i in range(0, len(terms), 2)]]
    dynamic_slice x0 -> x3, local copies, waits for them, and re-layouts: none -> 1.62 us  [the longest x2 1.54 us: owner_rounded(): lax.dynamic_slice_in_dim(part, (1 - owner_index) * half, half, axis=0)]
    dot_general x2, matrix products: 12.2 us -> 10.6 us  [local(): jnp.einsum('tk,jk->tj', all_g, basis_g[start:start + step], preferred_ele...]
  transfers between devices with their start and end apart: 23 -> 25, of which waited for: 15 -> 17; matrix products, arithmetic and copies ran while one was open for 22% -> 20% of each run, Pallas kernels for 0% -> 0%
where the time goes in v14:
time: 139 us; the launch traced here: 138 us
  waiting for transfers between devices  59.4 us (43%)
  starting transfers between devices  27.7 us (20%)
  matrix products  17.5 us (13%)
  between operations  14.4 us (10%)
  other arithmetic  11.9 us (9%)
  local copies, waits for them, and re-layouts  7.54 us (5%)
    ppermute x20, waiting for transfers between devices, xor_round(): parts.append(lax.ppermute(held, axis, [(i, i ^ c) for i in range(size)]))  45 us
    ppermute x20, starting transfers between devices, xor_round(): parts.append(lax.ppermute(held, axis, [(i, i ^ c) for i in range(size)]))  23.5 us
    dot_general x2, matrix products, local(): jnp.einsum('tk,jk->tj', all_g, basis_g[start:start + step], preferred_ele...  10.6 us
    ppermute x2, waiting for transfers between devices, owner_rounded(): received = lax.ppermute(theirs, 'owner', [(0, 1), (1, 0)])  9.53 us
    dot_general x1, matrix products, local(): jnp.einsum('stm,smn->stn', g_rows, scaled, preferred_element_type=jnp.flo...  6.41 us
    convert_element_type x1, other arithmetic, local(): denom = eigvals.astype(jnp.float32)  5.89 us
    ppermute x2, waiting for transfers between devices, owner_rounded(): other = lax.ppermute(rounded, 'owner', [(0, 1), (1, 0)])  4.21 us
  transfers between devices with their start and end apart: 25, of which 17 were waited for; matrix products, arithmetic and copies ran while one was open for 20% of the time, Pallas kernels for 0%

profile of v14, /device:TPU:0, one launch (start us, length us, event | category | flops | bytes accessed | tf_op | source)
XLA Modules:
  0.0 138.5 jit_solution(3035441227578218578)
XLA Ops:
  7.9 5.1 %collective-permute-start.6 = (bf16[1,16,2048]{2,1,0:T(8,128)(2,1)}, bf16[1,16,2048]{2,1,0:T(8,128)(2,1)S(1)}, u32[]{:S(2)}, u32[]{:S(2)}) collective-permute-start(bf16[1,16,2048]{2,1,0:T(8,128)(2,1)} %bitcast.102), channel_id=1, source_target_pairs={{0,12},{1,13},{2,14},{3,15},{4,8},{5,9},{6,10},{7,11},{8,4},{9,5},... | collective-permute-start | bytes 196616 | tf_op jit(solution)/shard_map/ppermute | solution.py:17
  20.5 1.6 %collective-permute-start.8 = (bf16[4,16,2048]{2,1,0:T(8,128)(2,1)S(1)}, bf16[4,16,2048]{2,1,0:T(8,128)(2,1)S(1)}, u32[]{:S(2)}, u32[]{:S(2)}) collective-permute-start(bf16[4,16,2048]{2,1,0:T(8,128)(2,1)S(1)} %broadcast_select_fusion.1), channel_id=1, source_target_pairs={{0,1},{1,0},{2,3},{3,2},{4,5},{5,4},{6,7},{7,6},{8,9},{9,8},{10,11... | collective-permute-start | bytes 786440 | tf_op jit(solution)/shard_map/ppermute | solution.py:17
  22.7 8.7 %collective-permute-done.9 = bf16[4,16,2048]{2,1,0:T(8,128)(2,1)S(1)} collective-permute-done((bf16[4,16,2048]{2,1,0:T(8,128)(2,1)S(1)}, bf16[4,16,2048]{2,1,0:T(8,128)(2,1)S(1)}, u32[]{:S(2)}, u32[]{:S(2)}) %collective-permute-start.9) | collective-permute-done | bytes 262176 | tf_op jit(solution)/shard_map/ppermute | solution.py:17
  31.5 5.7 %collective-permute-done.7 = bf16[4,16,2048]{2,1,0:T(8,128)(2,1)S(1)} collective-permute-done((bf16[4,16,2048]{2,1,0:T(8,128)(2,1)S(1)}, bf16[4,16,2048]{2,1,0:T(8,128)(2,1)S(1)}, u32[]{:S(2)}, u32[]{:S(2)}) %collective-permute-start.7) | collective-permute-done | bytes 262176 | tf_op jit(solution)/shard_map/ppermute | solution.py:17
  38.7 1.6 %collective-permute-start.10 = (f32[256,256]{1,0:T(8,128)S(1)}, f32[256,256]{1,0:T(8,128)S(1)}, u32[]{:S(2)}, u32[]{:S(2)}) collective-permute-start(f32[256,256]{1,0:T(8,128)S(1)} %fusion.32), channel_id=1, source_target_pairs={{0,16},{16,0},{1,17},{17,1},{2,18},{18,2},{3,19},{19,3},{4,20},{20... | collective-permute-start | bytes 786440 | tf_op jit(solution)/shard_map/ppermute | solution.py:17
  40.3 6.7 %collective-permute-done.10 = f32[256,256]{1,0:T(8,128)S(1)} collective-permute-done((f32[256,256]{1,0:T(8,128)S(1)}, f32[256,256]{1,0:T(8,128)S(1)}, u32[]{:S(2)}, u32[]{:S(2)}) %collective-permute-start.10) | collective-permute-done | bytes 262176 | tf_op jit(solution)/shard_map/ppermute | solution.py:17
  47.2 2.2 %collective-permute-start.13 = (bf16[1,256,256]{2,1,0:T(8,128)(2,1)S(1)}, bf16[1,256,256]{2,1,0:T(8,128)(2,1)S(1)}, u32[]{:S(2)}, u32[]{:S(2)}) collective-permute-start(bf16[1,256,256]{2,1,0:T(8,128)(2,1)S(1)} %multiply_convert_fusion), channel_id=1, source_target_pairs={{0,12},{1,13},{2,14},{3,15},{4,8},{5,9},{6,10},{7,11},{8,4},{9,5},... | collective-permute-start | bytes 393224 | tf_op jit(solution)/shard_map/ppermute | solution.py:17
  49.8 1.9 %collective-permute-start.11 = (bf16[1,256,256]{2,1,0:T(8,128)(2,1)S(1)}, bf16[1,256,256]{2,1,0:T(8,128)(2,1)S(1)}, u32[]{:S(2)}, u32[]{:S(2)}) collective-permute-start(bf16[1,256,256]{2,1,0:T(8,128)(2,1)S(1)} %multiply_convert_fusion), channel_id=1, source_target_pairs={{0,8},{1,9},{2,10},{3,11},{4,12},{5,13},{6,14},{7,15},{8,0},{9,1},... | collective-permute-start | bytes 393224 | tf_op jit(solution)/shard_map/ppermute | solution.py:17
  51.8 5.9 %convert_element_type.41 = f32[896,2048]{1,0:T(8,128)} convert(bf16[896,2048]{1,0:T(8,128)(2,1)} %param.11) | non-fusion elementwise | flops 1835008 | bytes 11010048 | tf_op jit(solution)/shard_map/convert_element_type | solution.py:121
  58.2 4.9 %collective-permute-done.12 = bf16[1,256,256]{2,1,0:T(8,128)(2,1)S(1)} collective-permute-done((bf16[1,256,256]{2,1,0:T(8,128)(2,1)S(1)}, bf16[1,256,256]{2,1,0:T(8,128)(2,1)S(1)}, u32[]{:S(2)}, u32[]{:S(2)}) %collective-permute-start.12) | collective-permute-done | bytes 131104 | tf_op jit(solution)/shard_map/ppermute | solution.py:17
  63.1 7.3 %collective-permute-done.11 = bf16[1,256,256]{2,1,0:T(8,128)(2,1)S(1)} collective-permute-done((bf16[1,256,256]{2,1,0:T(8,128)(2,1)S(1)}, bf16[1,256,256]{2,1,0:T(8,128)(2,1)S(1)}, u32[]{:S(2)}, u32[]{:S(2)}) %collective-permute-start.11) | collective-permute-done | bytes 131104 | tf_op jit(solution)/shard_map/ppermute | solution.py:17
  73.3 5.9 %fusion.3 = f32[256,448]{0,1:T(8,128)S(1)} fusion(bf16[256,7168]{1,0:T(8,128)(2,1)} %all-gather.2.cloned.1.call-done, bf16[896,7168]{1,0:T(8,128)(2,1)} %param.10), kind=kOutput, calls=%fused_computation.8 | convolution fusion | flops 1644167168 | bytes 10551296 | tf_op jit(solution)/shard_map/tk,jk->tj/dot_general | solution.py:113
  80.0 4.7 %fusion.1 = f32[256,448]{0,1:T(8,128)S(1)} fusion(bf16[256,7168]{1,0:T(8,128)(2,1)S(1)} %copy-done.3, bf16[896,7168]{1,0:T(8,128)(2,1)} %param.10), kind=kOutput, calls=%fused_computation.6 | convolution fusion | flops 1644167168 | bytes 10551296 | tf_op jit(solution)/shard_map/tk,jk->tj/dot_general | solution.py:113
  88.5 5.9 %collective-permute-done.2 = f32[128,448]{0,1:T(8,128)} collective-permute-done((f32[128,448]{0,1:T(8,128)}, f32[128,448]{0,1:T(8,128)}, u32[]{:S(2)}, u32[]{:S(2)}) %collective-permute-start.2) | collective-permute-done | bytes 229408 | tf_op jit(solution)/shard_map/ppermute | solution.py:79
  94.4 3.6 %collective-permute-done = f32[128,448]{0,1:T(8,128)} collective-permute-done((f32[128,448]{0,1:T(8,128)}, f32[128,448]{0,1:T(8,128)}, u32[]{:S(2)}, u32[]{:S(2)}) %collective-permute-start) | collective-permute-done | bytes 229408 | tf_op jit(solution)/shard_map/ppermute | solution.py:79
  103.1 1.8 %collective-permute-done.1 = bf16[128,448]{0,1:T(8,128)(2,1)S(1)} collective-permute-done((bf16[128,448]{0,1:T(8,128)(2,1)S(1)}, bf16[128,448]{0,1:T(8,128)(2,1)S(1)}, u32[]{:S(2)}, u32[]{:S(2)}) %collective-permute-start.1) | collective-permute-done | bytes 114720 | tf_op jit(solution)/shard_map/ppermute | solution.py:84
  104.8 2.5 %collective-permute-done.3 = bf16[128,448]{0,1:T(8,128)(2,1)S(1)} collective-permute-done((bf16[128,448]{0,1:T(8,128)(2,1)S(1)}, bf16[128,448]{0,1:T(8,128)(2,1)S(1)}, u32[]{:S(2)}, u32[]{:S(2)}) %collective-permute-start.3) | collective-permute-done | bytes 114720 | tf_op jit(solution)/shard_map/ppermute | solution.py:84
  107.6 6.4 %fusion.8 = f32[2,128]{1,0:T(2,128)S(1)} fusion(bf16[2,128,2048]{2,1,0:T(8,128)(2,1)S(1)} %reshape_reshape.7, bf16[2,128,896]{2,1,0:T(8,128)(2,1)S(1)} %bitcast.91, f32[896,2048]{1,0:T(8,128)} %convert_element_type.41), kind=kOutput, calls=%fused_computation.12 | convolution fusion | flops 1887960832 | bytes 8848384 | tf_op jit(solution)/shard_map/stm,smn->stn/dot_general | solution.py:126
  114.2 2.0 %collective-permute-start.17 = (f32[2,128]{1,0:T(2,128)S(1)}, f32[2,128]{1,0:T(2,128)S(1)}, u32[]{:S(2)}, u32[]{:S(2)}) collective-permute-start(f32[2,128]{1,0:T(2,128)S(1)} %get-tuple-element.11), channel_id=1, source_target_pairs={{0,8},{1,9},{2,10},{3,11},{4,12},{5,13},{6,14},{7,15},{8,0},{9,1},... | collective-permute-start | bytes 3080 | tf_op jit(solution)/shard_map/ppermute | solution.py:17
  116.1 2.4 %collective-permute-start.19 = (f32[2,128]{1,0:T(2,128)S(1)}, f32[2,128]{1,0:T(2,128)S(1)}, u32[]{:S(2)}, u32[]{:S(2)}) collective-permute-start(f32[2,128]{1,0:T(2,128)S(1)} %get-tuple-element.11), channel_id=1, source_target_pairs={{0,12},{1,13},{2,14},{3,15},{4,8},{5,9},{6,10},{7,11},{8,4},{9,5},... | collective-permute-start | bytes 3080 | tf_op jit(solution)/shard_map/ppermute | solution.py:17
  118.7 2.8 %collective-permute-done.19 = f32[2,128]{1,0:T(2,128)S(1)} collective-permute-done((f32[2,128]{1,0:T(2,128)S(1)}, f32[2,128]{1,0:T(2,128)S(1)}, u32[]{:S(2)}, u32[]{:S(2)}) %collective-permute-start.19) | collective-permute-done | bytes 1056 | tf_op jit(solution)/shard_map/ppermute | solution.py:17
  121.6 1.6 %collective-permute-start.21 = (f32[2,128]{1,0:T(2,128)S(1)}, f32[2,128]{1,0:T(2,128)S(1)}, u32[]{:S(2)}, u32[]{:S(2)}) collective-permute-start(f32[2,128]{1,0:T(2,128)S(1)} %fusion.41), channel_id=1, source_target_pairs={{0,1},{1,0},{2,3},{3,2},{4,5},{5,4},{6,7},{7,6},{8,9},{9,8},{10,11... | collective-permute-start | bytes 3080 | tf_op jit(solution)/shard_map/ppermute | solution.py:17
  124.6 2.2 %collective-permute-done.20 = f32[2,128]{1,0:T(2,128)S(1)} collective-permute-done((f32[2,128]{1,0:T(2,128)S(1)}, f32[2,128]{1,0:T(2,128)S(1)}, u32[]{:S(2)}, u32[]{:S(2)}) %collective-permute-start.20) | collective-permute-done | bytes 1056 | tf_op jit(solution)/shard_map/ppermute | solution.py:17
  127.4 3.0 %collective-permute-done.23 = f32[2,128]{1,0:T(2,128)S(1)} collective-permute-done((f32[2,128]{1,0:T(2,128)S(1)}, f32[2,128]{1,0:T(2,128)S(1)}, u32[]{:S(2)}, u32[]{:S(2)}) %collective-permute-start.23) | collective-permute-done | bytes 1056 | tf_op jit(solution)/shard_map/ppermute | solution.py:17
  (92 shorter events, 27.9 us)
Async XLA Ops:
  7.2 66.1 %all-gather.2.cloned.1.call-start = ((), (), s32[]{:S(2)}) async-start(), calls=%async_computation | async-start | bytes 3899392 | tf_op jit(solution)/shard_map/all_gather | solution.py:102
  7.9 8.6 %collective-permute-start.6 = (bf16[1,16,2048]{2,1,0:T(8,128)(2,1)}, bf16[1,16,2048]{2,1,0:T(8,128)(2,1)S(1)}, u32[]{:S(2)}, u32[]{:S(2)}) collective-permute-start(bf16[1,16,2048]{2,1,0:T(8,128)(2,1)} %bitcast.102), channel_id=1, source_target_pairs={{0,12},{1,13},{2,14},{3,15},{4,8},{5,9},{6,10},{7,11},{8,4},{9,5},... | collective-permute-start | bytes 196616 | tf_op jit(solution)/shard_map/ppermute | solution.py:17
  13.0 4.9 %collective-permute-start.5 = (bf16[1,16,2048]{2,1,0:T(8,128)(2,1)}, bf16[1,16,2048]{2,1,0:T(8,128)(2,1)S(1)}, u32[]{:S(2)}, u32[]{:S(2)}) collective-permute-start(bf16[1,16,2048]{2,1,0:T(8,128)(2,1)} %bitcast.103), channel_id=1, source_target_pairs={{0,4},{1,5},{2,6},{3,7},{4,0},{5,1},{6,2},{7,3},{8,12},{9,13},{10,... | collective-permute-start | bytes 196616 | tf_op jit(solution)/shard_map/ppermute | solution.py:17
  13.0 5.8 %collective-permute-start.4 = (bf16[1,16,2048]{2,1,0:T(8,128)(2,1)}, bf16[1,16,2048]{2,1,0:T(8,128)(2,1)S(1)}, u32[]{:S(2)}, u32[]{:S(2)}) collective-permute-start(bf16[1,16,2048]{2,1,0:T(8,128)(2,1)} %bitcast.104), channel_id=1, source_target_pairs={{0,8},{1,9},{2,10},{3,11},{4,12},{5,13},{6,14},{7,15},{8,0},{9,1},... | collective-permute-start | bytes 196616 | tf_op jit(solution)/shard_map/ppermute | solution.py:17
  20.4 11.1 %collective-permute-start.9 = (bf16[4,16,2048]{2,1,0:T(8,128)(2,1)S(1)}, bf16[4,16,2048]{2,1,0:T(8,128)(2,1)S(1)}, u32[]{:S(2)}, u32[]{:S(2)}) collective-permute-start(bf16[4,16,2048]{2,1,0:T(8,128)(2,1)S(1)} %broadcast_select_fusion.1), channel_id=1, source_target_pairs={{0,3},{1,2},{2,1},{3,0},{4,7},{5,6},{6,5},{7,4},{8,11},{9,10},{10,... | collective-permute-start | bytes 786440 | tf_op jit(solution)/shard_map/ppermute | solution.py:17
  20.5 11.0 %collective-permute-start.8 = (bf16[4,16,2048]{2,1,0:T(8,128)(2,1)S(1)}, bf16[4,16,2048]{2,1,0:T(8,128)(2,1)S(1)}, u32[]{:S(2)}, u32[]{:S(2)}) collective-permute-start(bf16[4,16,2048]{2,1,0:T(8,128)(2,1)S(1)} %broadcast_select_fusion.1), channel_id=1, source_target_pairs={{0,1},{1,0},{2,3},{3,2},{4,5},{5,4},{6,7},{7,6},{8,9},{9,8},{10,11... | collective-permute-start | bytes 786440 | tf_op jit(solution)/shard_map/ppermute | solution.py:17
  22.1 15.0 %collective-permute-start.7 = (bf16[4,16,2048]{2,1,0:T(8,128)(2,1)S(1)}, bf16[4,16,2048]{2,1,0:T(8,128)(2,1)S(1)}, u32[]{:S(2)}, u32[]{:S(2)}) collective-permute-start(bf16[4,16,2048]{2,1,0:T(8,128)(2,1)S(1)} %broadcast_select_fusion.1), channel_id=1, source_target_pairs={{0,2},{1,3},{2,0},{3,1},{4,6},{5,7},{6,4},{7,5},{8,10},{9,11},{10,... | collective-permute-start | bytes 786440 | tf_op jit(solution)/shard_map/ppermute | solution.py:17
  38.7 8.3 %collective-permute-start.10 = (f32[256,256]{1,0:T(8,128)S(1)}, f32[256,256]{1,0:T(8,128)S(1)}, u32[]{:S(2)}, u32[]{:S(2)}) collective-permute-start(f32[256,256]{1,0:T(8,128)S(1)} %fusion.32), channel_id=1, source_target_pairs={{0,16},{16,0},{1,17},{17,1},{2,18},{18,2},{3,19},{19,3},{4,20},{20... | collective-permute-start | bytes 786440 | tf_op jit(solution)/shard_map/ppermute | solution.py:17
  47.2 11.0 %collective-permute-start.13 = (bf16[1,256,256]{2,1,0:T(8,128)(2,1)S(1)}, bf16[1,256,256]{2,1,0:T(8,128)(2,1)S(1)}, u32[]{:S(2)}, u32[]{:S(2)}) collective-permute-start(bf16[1,256,256]{2,1,0:T(8,128)(2,1)S(1)} %multiply_convert_fusion), channel_id=1, source_target_pairs={{0,12},{1,13},{2,14},{3,15},{4,8},{5,9},{6,10},{7,11},{8,4},{9,5},... | collective-permute-start | bytes 393224 | tf_op jit(solution)/shard_map/ppermute | solution.py:17
  49.5 13.7 %collective-permute-start.12 = (bf16[1,256,256]{2,1,0:T(8,128)(2,1)S(1)}, bf16[1,256,256]{2,1,0:T(8,128)(2,1)S(1)}, u32[]{:S(2)}, u32[]{:S(2)}) collective-permute-start(bf16[1,256,256]{2,1,0:T(8,128)(2,1)S(1)} %multiply_convert_fusion), channel_id=1, source_target_pairs={{0,4},{1,5},{2,6},{3,7},{4,0},{5,1},{6,2},{7,3},{8,12},{9,13},{10,... | collective-permute-start | bytes 393224 | tf_op jit(solution)/shard_map/ppermute | solution.py:17
  49.8 20.6 %collective-permute-start.11 = (bf16[1,256,256]{2,1,0:T(8,128)(2,1)S(1)}, bf16[1,256,256]{2,1,0:T(8,128)(2,1)S(1)}, u32[]{:S(2)}, u32[]{:S(2)}) collective-permute-start(bf16[1,256,256]{2,1,0:T(8,128)(2,1)S(1)} %multiply_convert_fusion), channel_id=1, source_target_pairs={{0,8},{1,9},{2,10},{3,11},{4,12},{5,13},{6,14},{7,15},{8,0},{9,1},... | collective-permute-start | bytes 393224 | tf_op jit(solution)/shard_map/ppermute | solution.py:17
  71.1 16.5 %collective-permute-start.16 = (bf16[2,256,256]{2,1,0:T(8,128)(2,1)S(1)}, bf16[2,256,256]{2,1,0:T(8,128)(2,1)S(1)}, u32[]{:S(2)}, u32[]{:S(2)}) collective-permute-start(bf16[2,256,256]{2,1,0:T(8,128)(2,1)S(1)} %broadcast_select_fusion), channel_id=1, source_target_pairs={{0,3},{1,2},{2,1},{3,0},{4,7},{5,6},{6,5},{7,4},{8,11},{9,10},{10,... | collective-permute-start | bytes 786440 | tf_op jit(solution)/shard_map/ppermute | solution.py:17
  72.2 15.5 %collective-permute-start.15 = (bf16[2,256,256]{2,1,0:T(8,128)(2,1)S(1)}, bf16[2,256,256]{2,1,0:T(8,128)(2,1)S(1)}, u32[]{:S(2)}, u32[]{:S(2)}) collective-permute-start(bf16[2,256,256]{2,1,0:T(8,128)(2,1)S(1)} %broadcast_select_fusion), channel_id=1, source_target_pairs={{0,1},{1,0},{2,3},{3,2},{4,5},{5,4},{6,7},{7,6},{8,9},{9,8},{10,11... | collective-permute-start | bytes 786440 | tf_op jit(solution)/shard_map/ppermute | solution.py:17
  72.8 14.9 %collective-permute-start.14 = (bf16[2,256,256]{2,1,0:T(8,128)(2,1)S(1)}, bf16[2,256,256]{2,1,0:T(8,128)(2,1)S(1)}, u32[]{:S(2)}, u32[]{:S(2)}) collective-permute-start(bf16[2,256,256]{2,1,0:T(8,128)(2,1)S(1)} %broadcast_select_fusion), channel_id=1, source_target_pairs={{0,2},{1,3},{2,0},{3,1},{4,6},{5,7},{6,4},{7,5},{8,10},{9,11},{10,... | collective-permute-start | bytes 786440 | tf_op jit(solution)/shard_map/ppermute | solution.py:17
  85.5 8.8 %collective-permute-start.2 = (f32[128,448]{0,1:T(8,128)}, f32[128,448]{0,1:T(8,128)}, u32[]{:S(2)}, u32[]{:S(2)}) collective-permute-start(f32[128,448]{0,1:T(8,128)} %constant_dynamic-slice_fusion.13), channel_id=1, source_target_pairs={{0,16},{16,0},{1,17},{17,1},{2,18},{18,2},{3,19},{19,3},{4,20},{20... | collective-permute-start | bytes 688136 | tf_op jit(solution)/shard_map/ppermute | solution.py:79
  87.0 11.0 %collective-permute-start = (f32[128,448]{0,1:T(8,128)}, f32[128,448]{0,1:T(8,128)}, u32[]{:S(2)}, u32[]{:S(2)}) collective-permute-start(f32[128,448]{0,1:T(8,128)} %constant_dynamic-slice_fusion.14), channel_id=1, source_target_pairs={{0,16},{16,0},{1,17},{17,1},{2,18},{18,2},{3,19},{19,3},{4,20},{20... | collective-permute-start | bytes 688136 | tf_op jit(solution)/shard_map/ppermute | solution.py:79
  99.4 5.5 %collective-permute-start.1 = (bf16[128,448]{0,1:T(8,128)(2,1)S(1)}, bf16[128,448]{0,1:T(8,128)(2,1)S(1)}, u32[]{:S(2)}, u32[]{:S(2)}) collective-permute-start(bf16[128,448]{0,1:T(8,128)(2,1)S(1)} %get-tuple-element.12), channel_id=1, source_target_pairs={{0,16},{16,0},{1,17},{17,1},{2,18},{18,2},{3,19},{19,3},{4,20},{20... | collective-permute-start | bytes 344072 | tf_op jit(solution)/shard_map/ppermute | solution.py:84
  102.4 4.9 %collective-permute-start.3 = (bf16[128,448]{0,1:T(8,128)(2,1)S(1)}, bf16[128,448]{0,1:T(8,128)(2,1)S(1)}, u32[]{:S(2)}, u32[]{:S(2)}) collective-permute-start(bf16[128,448]{0,1:T(8,128)(2,1)S(1)} %get-tuple-element.13), channel_id=1, source_target_pairs={{0,16},{16,0},{1,17},{17,1},{2,18},{18,2},{3,19},{19,3},{4,20},{20... | collective-permute-start | bytes 344072 | tf_op jit(solution)/shard_map/ppermute | solution.py:84
  114.1 4.5 %collective-permute-start.18 = (f32[2,128]{1,0:T(2,128)S(1)}, f32[2,128]{1,0:T(2,128)S(1)}, u32[]{:S(2)}, u32[]{:S(2)}) collective-permute-start(f32[2,128]{1,0:T(2,128)S(1)} %get-tuple-element.11), channel_id=1, source_target_pairs={{0,4},{1,5},{2,6},{3,7},{4,0},{5,1},{6,2},{7,3},{8,12},{9,13},{10,... | collective-permute-start | bytes 3080 | tf_op jit(solution)/shard_map/ppermute | solution.py:17
  114.2 4.5 %collective-permute-start.17 = (f32[2,128]{1,0:T(2,128)S(1)}, f32[2,128]{1,0:T(2,128)S(1)}, u32[]{:S(2)}, u32[]{:S(2)}) collective-permute-start(f32[2,128]{1,0:T(2,128)S(1)} %get-tuple-element.11), channel_id=1, source_target_pairs={{0,8},{1,9},{2,10},{3,11},{4,12},{5,13},{6,14},{7,15},{8,0},{9,1},... | collective-permute-start | bytes 3080 | tf_op jit(solution)/shard_map/ppermute | solution.py:17
  116.1 5.4 %collective-permute-start.19 = (f32[2,128]{1,0:T(2,128)S(1)}, f32[2,128]{1,0:T(2,128)S(1)}, u32[]{:S(2)}, u32[]{:S(2)}) collective-permute-start(f32[2,128]{1,0:T(2,128)S(1)} %get-tuple-element.11), channel_id=1, source_target_pairs={{0,12},{1,13},{2,14},{3,15},{4,8},{5,9},{6,10},{7,11},{8,4},{9,5},... | collective-permute-start | bytes 3080 | tf_op jit(solution)/shard_map/ppermute | solution.py:17
  121.5 3.1 %collective-permute-start.22 = (f32[2,128]{1,0:T(2,128)S(1)}, f32[2,128]{1,0:T(2,128)S(1)}, u32[]{:S(2)}, u32[]{:S(2)}) collective-permute-start(f32[2,128]{1,0:T(2,128)S(1)} %fusion.41), channel_id=1, source_target_pairs={{0,3},{1,2},{2,1},{3,0},{4,7},{5,6},{6,5},{7,4},{8,11},{9,10},{10,... | collective-permute-start | bytes 3080 | tf_op jit(solution)/shard_map/ppermute | solution.py:17
  123.1 3.6 %collective-permute-start.20 = (f32[2,128]{1,0:T(2,128)S(1)}, f32[2,128]{1,0:T(2,128)S(1)}, u32[]{:S(2)}, u32[]{:S(2)}) collective-permute-start(f32[2,128]{1,0:T(2,128)S(1)} %fusion.41), channel_id=1, source_target_pairs={{0,2},{1,3},{2,0},{3,1},{4,6},{5,7},{6,4},{7,5},{8,10},{9,11},{10,... | collective-permute-start | bytes 3080 | tf_op jit(solution)/shard_map/ppermute | solution.py:17
  126.7 3.6 %collective-permute-start.23 = (f32[2,128]{1,0:T(2,128)S(1)}, f32[2,128]{1,0:T(2,128)S(1)}, u32[]{:S(2)}, u32[]{:S(2)}) collective-permute-start(f32[2,128]{1,0:T(2,128)S(1)} %fusion.40), channel_id=1, source_target_pairs={{0,16},{16,0},{1,17},{17,1},{2,18},{18,2},{3,19},{19,3},{4,20},{20... | collective-permute-start | bytes 3080 | tf_op jit(solution)/shard_map/ppermute | solution.py:17
  (6 other events, 72.0 us)
Sparse Core Ops, SparseCore 0:
  10.3 60.4 all-gather.1

commit v15 on v11

--- a/solution.py
+++ b/solution.py
@@ -25,12 +25,12 @@
     return out
 
 
-def xor_sum(x, axis, size):
+def xor_sum(x, axis, size, radix_bits=2):
     if size & (size - 1):
         return lax.psum(x, axis)
     index = lax.axis_index(axis)
     bits = [1 << k for k in range(size.bit_length() - 1)][::-1]
-    for group in bit_groups(bits):
+    for group in [bits[i:i + radix_bits] for i in range(0, len(bits), radix_bits)]:
         mask = sum(group)
         stacked = xor_round(x, axis, size, group)
         order = [counter_of((v ^ (index & mask)), group) for v in range(mask + 1) if v & ~mask == 0]
@@ -107,7 +107,7 @@
     scaled = (outer / denom[None]).astype(jnp.bfloat16)
     projected = jnp.einsum("stm,smn->stn", g_rows, scaled, preferred_element_type=jnp.float32)
     partial = jnp.sum(projected * a_rows.astype(jnp.float32), axis=2) / (dim_ff * dim_d)
-    scores = xor_sum(xor_sum(partial, "reader", readers), "owner", owners)
+    scores = xor_sum(partial, ("owner", "reader"), owners * readers, radix_bits=3)
 
     token_score = lax.dynamic_index_in_dim(scores, owner_index, 0, keepdims=False)
     slot_mean = jnp.sum(scores, axis=1) / SEQ

time: 135 us -> 138 us (1.022)
  starting transfers between devices: 26.4 us -> 32 us
  waiting for transfers between devices: 55.8 us -> 52.5 us
    ppermute x22 -> x25, starting transfers between devices: 26.4 us -> 31.9 us  [xor_round(): parts.append(lax.ppermute(held, axis, [(i, i ^ c) for i in range(size)]))]
    ppermute x22 -> x25, waiting for transfers between devices: 55.1 us -> 50.7 us  [xor_round(): parts.append(lax.ppermute(held, axis, [(i, i ^ c) for i in range(size)]))]
  transfers between devices with their start and end apart: 23 -> 26, of which waited for: 15 -> 13; matrix products, arithmetic and copies ran while one was open for 22% -> 21% of each run, Pallas kernels for 0% -> 0%
where the time goes in v15:
time: 138 us; the launch traced here: 137 us
  waiting for transfers between devices  52.5 us (38%)
  starting transfers between devices  32 us (23%)
  matrix products  19.1 us (14%)
  between operations  14.3 us (10%)
  other arithmetic  13.2 us (10%)
  local copies, waits for them, and re-layouts  6.21 us (4%)
    ppermute x25, waiting for transfers between devices, xor_round(): parts.append(lax.ppermute(held, axis, [(i, i ^ c) for i in range(size)]))  50.7 us
    ppermute x25, starting transfers between devices, xor_round(): parts.append(lax.ppermute(held, axis, [(i, i ^ c) for i in range(size)]))  31.9 us
    dot_general x2, matrix products, local(): jnp.einsum('tk,jk->tj', all_g, basis_g[start:start + step], preferred_ele...  12.2 us
    dot_general x1, matrix products, local(): jnp.einsum('stm,smn->stn', g_rows, scaled, preferred_element_type=jnp.flo...  6.48 us
    convert_element_type x1, other arithmetic, local(): denom = eigvals.astype(jnp.float32)  5.91 us
  transfers between devices with their start and end apart: 26, of which 13 were waited for; matrix products, arithmetic and copies ran while one was open for 21% of the time, Pallas kernels for 0%

profile of v15, /device:TPU:0, one launch (start us, length us, event | category | flops | bytes accessed | tf_op | source)
XLA Modules:
  0.0 137.2 jit_solution(650814266752254080)
XLA Ops:
  7.9 4.1 %collective-permute-start.2 = (bf16[1,16,2048]{2,1,0:T(8,128)(2,1)}, bf16[1,16,2048]{2,1,0:T(8,128)(2,1)S(1)}, u32[]{:S(2)}, u32[]{:S(2)}) collective-permute-start(bf16[1,16,2048]{2,1,0:T(8,128)(2,1)} %bitcast.115), channel_id=1, source_target_pairs={{0,8},{1,9},{2,10},{3,11},{4,12},{5,13},{6,14},{7,15},{8,0},{9,1},... | collective-permute-start | bytes 196616 | tf_op jit(solution)/shard_map/ppermute | solution.py:17
  12.0 1.6 %collective-permute-start.3 = (bf16[1,16,2048]{2,1,0:T(8,128)(2,1)}, bf16[1,16,2048]{2,1,0:T(8,128)(2,1)S(1)}, u32[]{:S(2)}, u32[]{:S(2)}) collective-permute-start(bf16[1,16,2048]{2,1,0:T(8,128)(2,1)} %bitcast.116), channel_id=1, source_target_pairs={{0,4},{1,5},{2,6},{3,7},{4,0},{5,1},{6,2},{7,3},{8,12},{9,13},{10,... | collective-permute-start | bytes 196616 | tf_op jit(solution)/shard_map/ppermute | solution.py:17
  16.5 3.4 %collective-permute-done.4 = bf16[1,16,2048]{2,1,0:T(8,128)(2,1)S(1)} collective-permute-done((bf16[1,16,2048]{2,1,0:T(8,128)(2,1)}, bf16[1,16,2048]{2,1,0:T(8,128)(2,1)S(1)}, u32[]{:S(2)}, u32[]{:S(2)}) %collective-permute-start.4) | collective-permute-done | bytes 65568 | tf_op jit(solution)/shard_map/ppermute | solution.py:17
  21.4 1.6 %collective-permute-start.5 = (bf16[4,16,2048]{2,1,0:T(8,128)(2,1)S(1)}, bf16[4,16,2048]{2,1,0:T(8,128)(2,1)S(1)}, u32[]{:S(2)}, u32[]{:S(2)}) collective-permute-start(bf16[4,16,2048]{2,1,0:T(8,128)(2,1)S(1)} %broadcast_select_fusion.1), channel_id=1, source_target_pairs={{0,2},{1,3},{2,0},{3,1},{4,6},{5,7},{6,4},{7,5},{8,10},{9,11},{10,... | collective-permute-start | bytes 786440 | tf_op jit(solution)/shard_map/ppermute | solution.py:17
  23.7 8.4 %collective-permute-done.5 = bf16[4,16,2048]{2,1,0:T(8,128)(2,1)S(1)} collective-permute-done((bf16[4,16,2048]{2,1,0:T(8,128)(2,1)S(1)}, bf16[4,16,2048]{2,1,0:T(8,128)(2,1)S(1)}, u32[]{:S(2)}, u32[]{:S(2)}) %collective-permute-start.5) | collective-permute-done | bytes 262176 | tf_op jit(solution)/shard_map/ppermute | solution.py:17
  32.1 2.9 %collective-permute-done.7 = bf16[4,16,2048]{2,1,0:T(8,128)(2,1)S(1)} collective-permute-done((bf16[4,16,2048]{2,1,0:T(8,128)(2,1)S(1)}, bf16[4,16,2048]{2,1,0:T(8,128)(2,1)S(1)}, u32[]{:S(2)}, u32[]{:S(2)}) %collective-permute-start.7) | collective-permute-done | bytes 262176 | tf_op jit(solution)/shard_map/ppermute | solution.py:17
  36.6 1.6 %collective-permute-start.8 = (f32[256,256]{1,0:T(8,128)S(1)}, f32[256,256]{1,0:T(8,128)S(1)}, u32[]{:S(2)}, u32[]{:S(2)}) collective-permute-start(f32[256,256]{1,0:T(8,128)S(1)} %fusion.48), channel_id=1, source_target_pairs={{0,16},{16,0},{1,17},{17,1},{2,18},{18,2},{3,19},{19,3},{4,20},{20... | collective-permute-start | bytes 786440 | tf_op jit(solution)/shard_map/ppermute | solution.py:17
  38.2 7.4 %collective-permute-done.8 = f32[256,256]{1,0:T(8,128)S(1)} collective-permute-done((f32[256,256]{1,0:T(8,128)S(1)}, f32[256,256]{1,0:T(8,128)S(1)}, u32[]{:S(2)}, u32[]{:S(2)}) %collective-permute-start.8) | collective-permute-done | bytes 262176 | tf_op jit(solution)/shard_map/ppermute | solution.py:17
  45.8 2.8 %collective-permute-start.9 = (bf16[1,256,256]{2,1,0:T(8,128)(2,1)S(1)}, bf16[1,256,256]{2,1,0:T(8,128)(2,1)S(1)}, u32[]{:S(2)}, u32[]{:S(2)}) collective-permute-start(bf16[1,256,256]{2,1,0:T(8,128)(2,1)S(1)} %multiply_convert_fusion), channel_id=1, source_target_pairs={{0,8},{1,9},{2,10},{3,11},{4,12},{5,13},{6,14},{7,15},{8,0},{9,1},... | collective-permute-start | bytes 393224 | tf_op jit(solution)/shard_map/ppermute | solution.py:17
  48.7 1.6 %collective-permute-start.11 = (bf16[1,256,256]{2,1,0:T(8,128)(2,1)S(1)}, bf16[1,256,256]{2,1,0:T(8,128)(2,1)S(1)}, u32[]{:S(2)}, u32[]{:S(2)}) collective-permute-start(bf16[1,256,256]{2,1,0:T(8,128)(2,1)S(1)} %multiply_convert_fusion), channel_id=1, source_target_pairs={{0,12},{1,13},{2,14},{3,15},{4,8},{5,9},{6,10},{7,11},{8,4},{9,5},... | collective-permute-start | bytes 393224 | tf_op jit(solution)/shard_map/ppermute | solution.py:17
  50.4 5.9 %convert_element_type.47 = f32[896,2048]{1,0:T(8,128)} convert(bf16[896,2048]{1,0:T(8,128)(2,1)} %param.11) | non-fusion elementwise | flops 1835008 | bytes 11010048 | tf_op jit(solution)/shard_map/convert_element_type | solution.py:103
  56.3 4.8 %collective-permute-done.9 = bf16[1,256,256]{2,1,0:T(8,128)(2,1)S(1)} collective-permute-done((bf16[1,256,256]{2,1,0:T(8,128)(2,1)S(1)}, bf16[1,256,256]{2,1,0:T(8,128)(2,1)S(1)}, u32[]{:S(2)}, u32[]{:S(2)}) %collective-permute-start.9) | collective-permute-done | bytes 131104 | tf_op jit(solution)/shard_map/ppermute | solution.py:17
  61.0 6.2 %collective-permute-done.11 = bf16[1,256,256]{2,1,0:T(8,128)(2,1)S(1)} collective-permute-done((bf16[1,256,256]{2,1,0:T(8,128)(2,1)S(1)}, bf16[1,256,256]{2,1,0:T(8,128)(2,1)S(1)}, u32[]{:S(2)}, u32[]{:S(2)}) %collective-permute-start.11) | collective-permute-done | bytes 131104 | tf_op jit(solution)/shard_map/ppermute | solution.py:17
  71.4 6.7 %fusion.3 = f32[256,448]{0,1:T(8,128)} fusion(bf16[256,7168]{1,0:T(8,128)(2,1)} %all-gather.2.cloned.1.call-done, bf16[896,7168]{1,0:T(8,128)(2,1)} %param.10), kind=kOutput, calls=%fused_computation.8 | convolution fusion | flops 1644167168 | bytes 10551296 | tf_op jit(solution)/shard_map/tk,jk->tj/dot_general | solution.py:95
  79.6 5.4 %fusion.1 = f32[256,448]{0,1:T(8,128)} fusion(bf16[256,7168]{1,0:T(8,128)(2,1)S(1)} %copy-done.1, bf16[896,7168]{1,0:T(8,128)(2,1)} %param.10), kind=kOutput, calls=%fused_computation.6 | convolution fusion | flops 1644167168 | bytes 10551296 | tf_op jit(solution)/shard_map/tk,jk->tj/dot_general | solution.py:95
  87.9 3.9 %collective-permute-done = f32[256,448]{0,1:T(8,128)} collective-permute-done((f32[256,448]{0,1:T(8,128)}, f32[256,448]{0,1:T(8,128)}, u32[]{:S(2)}, u32[]{:S(2)}) %collective-permute-start) | collective-permute-done | bytes 458784 | tf_op jit(solution)/shard_map/ppermute | solution.py:17
  93.3 7.6 %collective-permute-done.1 = f32[256,448]{0,1:T(8,128)} collective-permute-done((f32[256,448]{0,1:T(8,128)}, f32[256,448]{0,1:T(8,128)}, u32[]{:S(2)}, u32[]{:S(2)}) %collective-permute-start.1) | collective-permute-done | bytes 458784 | tf_op jit(solution)/shard_map/ppermute | solution.py:17
  102.6 6.5 %fusion.8 = f32[2,128]{1,0:T(2,128)S(1)} fusion(bf16[2,128,2048]{2,1,0:T(8,128)(2,1)S(1)} %reshape_reshape.7, f32[896,2048]{1,0:T(8,128)} %convert_element_type.47, bf16[2,128,448]{1,2,0:T(8,128)(2,1)S(1)} %get-tuple-element.7, bf16[2,128,448]{1,2,0:T(8,128)(2,1)S(1)} %get-tuple-element.6), kind=kOutput, calls=%fused_computation.12 | convolution fusion | flops 1889795840 | bytes 8848384 | tf_op jit(solution)/shard_map/stm,smn->stn/dot_general | solution.py:108
  109.1 1.5 %collective-permute-start.15 = (f32[2,128]{1,0:T(2,128)S(1)}, f32[2,128]{1,0:T(2,128)S(1)}, u32[]{:S(2)}, u32[]{:S(2)}) collective-permute-start(f32[2,128]{1,0:T(2,128)S(1)} %broadcast_multiply_fusion), channel_id=1, source_target_pairs={{0,16},{1,17},{2,18},{3,19},{4,20},{5,21},{6,22},{7,23},{8,24},{9,... | collective-permute-start | bytes 3080 | tf_op jit(solution)/shard_map/ppermute | solution.py:17
  110.6 2.4 %collective-permute-start.16 = (f32[2,128]{1,0:T(2,128)S(1)}, f32[2,128]{1,0:T(2,128)S(1)}, u32[]{:S(2)}, u32[]{:S(2)}) collective-permute-start(f32[2,128]{1,0:T(2,128)S(1)} %broadcast_multiply_fusion), channel_id=1, source_target_pairs={{0,8},{1,9},{2,10},{3,11},{4,12},{5,13},{6,14},{7,15},{8,0},{9,1},... | collective-permute-start | bytes 3080 | tf_op jit(solution)/shard_map/ppermute | solution.py:17
  113.5 2.4 %collective-permute-start.18 = (f32[2,128]{1,0:T(2,128)S(1)}, f32[2,128]{1,0:T(2,128)S(1)}, u32[]{:S(2)}, u32[]{:S(2)}) collective-permute-start(f32[2,128]{1,0:T(2,128)S(1)} %broadcast_multiply_fusion), channel_id=1, source_target_pairs={{0,4},{1,5},{2,6},{3,7},{4,0},{5,1},{6,2},{7,3},{8,12},{9,13},{10,... | collective-permute-start | bytes 3080 | tf_op jit(solution)/shard_map/ppermute | solution.py:17
  118.3 2.4 %collective-permute-start.21 = (f32[2,128]{1,0:T(2,128)S(1)}, f32[2,128]{1,0:T(2,128)S(1)}, u32[]{:S(2)}, u32[]{:S(2)}) collective-permute-start(f32[2,128]{1,0:T(2,128)S(1)} %broadcast_multiply_fusion), channel_id=1, source_target_pairs={{0,28},{1,29},{2,30},{3,31},{4,24},{5,25},{6,26},{7,27},{8,20},{9,... | collective-permute-start | bytes 3080 | tf_op jit(solution)/shard_map/ppermute | solution.py:17
  122.2 2.4 %collective-permute-done.21 = f32[2,128]{1,0:T(2,128)S(1)} collective-permute-done((f32[2,128]{1,0:T(2,128)S(1)}, f32[2,128]{1,0:T(2,128)S(1)}, u32[]{:S(2)}, u32[]{:S(2)}) %collective-permute-start.21) | collective-permute-done | bytes 1056 | tf_op jit(solution)/shard_map/ppermute | solution.py:17
  124.6 1.5 %collective-permute-start.22 = (f32[2,128]{1,0:T(2,128)S(1)}, f32[2,128]{1,0:T(2,128)S(1)}, u32[]{:S(2)}, u32[]{:S(2)}) collective-permute-start(f32[2,128]{1,0:T(2,128)S(1)} %fusion.54), channel_id=1, source_target_pairs={{0,2},{1,3},{2,0},{3,1},{4,6},{5,7},{6,4},{7,5},{8,10},{9,11},{10,... | collective-permute-start | bytes 3080 | tf_op jit(solution)/shard_map/ppermute | solution.py:17
  (93 shorter events, 28.1 us)
Async XLA Ops:
  7.2 64.2 %all-gather.2.cloned.1.call-start = ((), (), s32[]{:S(2)}) async-start(), calls=%async_computation | async-start | bytes 3899392 | tf_op jit(solution)/shard_map/all_gather | solution.py:84
  7.9 8.6 %collective-permute-start.2 = (bf16[1,16,2048]{2,1,0:T(8,128)(2,1)}, bf16[1,16,2048]{2,1,0:T(8,128)(2,1)S(1)}, u32[]{:S(2)}, u32[]{:S(2)}) collective-permute-start(bf16[1,16,2048]{2,1,0:T(8,128)(2,1)} %bitcast.115), channel_id=1, source_target_pairs={{0,8},{1,9},{2,10},{3,11},{4,12},{5,13},{6,14},{7,15},{8,0},{9,1},... | collective-permute-start | bytes 196616 | tf_op jit(solution)/shard_map/ppermute | solution.py:17
  12.0 4.5 %collective-permute-start.3 = (bf16[1,16,2048]{2,1,0:T(8,128)(2,1)}, bf16[1,16,2048]{2,1,0:T(8,128)(2,1)S(1)}, u32[]{:S(2)}, u32[]{:S(2)}) collective-permute-start(bf16[1,16,2048]{2,1,0:T(8,128)(2,1)} %bitcast.116), channel_id=1, source_target_pairs={{0,4},{1,5},{2,6},{3,7},{4,0},{5,1},{6,2},{7,3},{8,12},{9,13},{10,... | collective-permute-start | bytes 196616 | tf_op jit(solution)/shard_map/ppermute | solution.py:17
  13.6 6.3 %collective-permute-start.4 = (bf16[1,16,2048]{2,1,0:T(8,128)(2,1)}, bf16[1,16,2048]{2,1,0:T(8,128)(2,1)S(1)}, u32[]{:S(2)}, u32[]{:S(2)}) collective-permute-start(bf16[1,16,2048]{2,1,0:T(8,128)(2,1)} %bitcast.117), channel_id=1, source_target_pairs={{0,12},{1,13},{2,14},{3,15},{4,8},{5,9},{6,10},{7,11},{8,4},{9,5},... | collective-permute-start | bytes 196616 | tf_op jit(solution)/shard_map/ppermute | solution.py:17
  21.4 10.7 %collective-permute-start.5 = (bf16[4,16,2048]{2,1,0:T(8,128)(2,1)S(1)}, bf16[4,16,2048]{2,1,0:T(8,128)(2,1)S(1)}, u32[]{:S(2)}, u32[]{:S(2)}) collective-permute-start(bf16[4,16,2048]{2,1,0:T(8,128)(2,1)S(1)} %broadcast_select_fusion.1), channel_id=1, source_target_pairs={{0,2},{1,3},{2,0},{3,1},{4,6},{5,7},{6,4},{7,5},{8,10},{9,11},{10,... | collective-permute-start | bytes 786440 | tf_op jit(solution)/shard_map/ppermute | solution.py:17
  23.0 9.1 %collective-permute-start.6 = (bf16[4,16,2048]{2,1,0:T(8,128)(2,1)S(1)}, bf16[4,16,2048]{2,1,0:T(8,128)(2,1)S(1)}, u32[]{:S(2)}, u32[]{:S(2)}) collective-permute-start(bf16[4,16,2048]{2,1,0:T(8,128)(2,1)S(1)} %broadcast_select_fusion.1), channel_id=1, source_target_pairs={{0,1},{1,0},{2,3},{3,2},{4,5},{5,4},{6,7},{7,6},{8,9},{9,8},{10,11... | collective-permute-start | bytes 786440 | tf_op jit(solution)/shard_map/ppermute | solution.py:17
  23.0 12.0 %collective-permute-start.7 = (bf16[4,16,2048]{2,1,0:T(8,128)(2,1)S(1)}, bf16[4,16,2048]{2,1,0:T(8,128)(2,1)S(1)}, u32[]{:S(2)}, u32[]{:S(2)}) collective-permute-start(bf16[4,16,2048]{2,1,0:T(8,128)(2,1)S(1)} %broadcast_select_fusion.1), channel_id=1, source_target_pairs={{0,3},{1,2},{2,1},{3,0},{4,7},{5,6},{6,5},{7,4},{8,11},{9,10},{10,... | collective-permute-start | bytes 786440 | tf_op jit(solution)/shard_map/ppermute | solution.py:17
  36.6 9.0 %collective-permute-start.8 = (f32[256,256]{1,0:T(8,128)S(1)}, f32[256,256]{1,0:T(8,128)S(1)}, u32[]{:S(2)}, u32[]{:S(2)}) collective-permute-start(f32[256,256]{1,0:T(8,128)S(1)} %fusion.48), channel_id=1, source_target_pairs={{0,16},{16,0},{1,17},{17,1},{2,18},{18,2},{3,19},{19,3},{4,20},{20... | collective-permute-start | bytes 786440 | tf_op jit(solution)/shard_map/ppermute | solution.py:17
  45.8 15.2 %collective-permute-start.9 = (bf16[1,256,256]{2,1,0:T(8,128)(2,1)S(1)}, bf16[1,256,256]{2,1,0:T(8,128)(2,1)S(1)}, u32[]{:S(2)}, u32[]{:S(2)}) collective-permute-start(bf16[1,256,256]{2,1,0:T(8,128)(2,1)S(1)} %multiply_convert_fusion), channel_id=1, source_target_pairs={{0,8},{1,9},{2,10},{3,11},{4,12},{5,13},{6,14},{7,15},{8,0},{9,1},... | collective-permute-start | bytes 393224 | tf_op jit(solution)/shard_map/ppermute | solution.py:17
  48.7 12.4 %collective-permute-start.10 = (bf16[1,256,256]{2,1,0:T(8,128)(2,1)S(1)}, bf16[1,256,256]{2,1,0:T(8,128)(2,1)S(1)}, u32[]{:S(2)}, u32[]{:S(2)}) collective-permute-start(bf16[1,256,256]{2,1,0:T(8,128)(2,1)S(1)} %multiply_convert_fusion), channel_id=1, source_target_pairs={{0,4},{1,5},{2,6},{3,7},{4,0},{5,1},{6,2},{7,3},{8,12},{9,13},{10,... | collective-permute-start | bytes 393224 | tf_op jit(solution)/shard_map/ppermute | solution.py:17
  48.7 18.6 %collective-permute-start.11 = (bf16[1,256,256]{2,1,0:T(8,128)(2,1)S(1)}, bf16[1,256,256]{2,1,0:T(8,128)(2,1)S(1)}, u32[]{:S(2)}, u32[]{:S(2)}) collective-permute-start(bf16[1,256,256]{2,1,0:T(8,128)(2,1)S(1)} %multiply_convert_fusion), channel_id=1, source_target_pairs={{0,12},{1,13},{2,14},{3,15},{4,8},{5,9},{6,10},{7,11},{8,4},{9,5},... | collective-permute-start | bytes 393224 | tf_op jit(solution)/shard_map/ppermute | solution.py:17
  68.0 17.6 %collective-permute-start.12 = (bf16[2,256,256]{2,1,0:T(8,128)(2,1)S(1)}, bf16[2,256,256]{2,1,0:T(8,128)(2,1)S(1)}, u32[]{:S(2)}, u32[]{:S(2)}) collective-permute-start(bf16[2,256,256]{2,1,0:T(8,128)(2,1)S(1)} %broadcast_select_fusion), channel_id=1, source_target_pairs={{0,2},{1,3},{2,0},{3,1},{4,6},{5,7},{6,4},{7,5},{8,10},{9,11},{10,... | collective-permute-start | bytes 786440 | tf_op jit(solution)/shard_map/ppermute | solution.py:17
  69.5 16.1 %collective-permute-start.13 = (bf16[2,256,256]{2,1,0:T(8,128)(2,1)S(1)}, bf16[2,256,256]{2,1,0:T(8,128)(2,1)S(1)}, u32[]{:S(2)}, u32[]{:S(2)}) collective-permute-start(bf16[2,256,256]{2,1,0:T(8,128)(2,1)S(1)} %broadcast_select_fusion), channel_id=1, source_target_pairs={{0,1},{1,0},{2,3},{3,2},{4,5},{5,4},{6,7},{7,6},{8,9},{9,8},{10,11... | collective-permute-start | bytes 786440 | tf_op jit(solution)/shard_map/ppermute | solution.py:17
  69.5 16.1 %collective-permute-start.14 = (bf16[2,256,256]{2,1,0:T(8,128)(2,1)S(1)}, bf16[2,256,256]{2,1,0:T(8,128)(2,1)S(1)}, u32[]{:S(2)}, u32[]{:S(2)}) collective-permute-start(bf16[2,256,256]{2,1,0:T(8,128)(2,1)S(1)} %broadcast_select_fusion), channel_id=1, source_target_pairs={{0,3},{1,2},{2,1},{3,0},{4,7},{5,6},{6,5},{7,4},{8,11},{9,10},{10,... | collective-permute-start | bytes 786440 | tf_op jit(solution)/shard_map/ppermute | solution.py:17
  78.1 13.7 %collective-permute-start = (f32[256,448]{0,1:T(8,128)}, f32[256,448]{0,1:T(8,128)}, u32[]{:S(2)}, u32[]{:S(2)}) collective-permute-start(f32[256,448]{0,1:T(8,128)} %fusion.3), channel_id=1, source_target_pairs={{0,16},{16,0},{1,17},{17,1},{2,18},{18,2},{3,19},{19,3},{4,20},{20... | collective-permute-start | bytes 1376264 | tf_op jit(solution)/shard_map/ppermute | solution.py:17
  85.0 15.9 %collective-permute-start.1 = (f32[256,448]{0,1:T(8,128)}, f32[256,448]{0,1:T(8,128)}, u32[]{:S(2)}, u32[]{:S(2)}) collective-permute-start(f32[256,448]{0,1:T(8,128)} %fusion.1), channel_id=1, source_target_pairs={{0,16},{16,0},{1,17},{17,1},{2,18},{18,2},{3,19},{19,3},{4,20},{20... | collective-permute-start | bytes 1376264 | tf_op jit(solution)/shard_map/ppermute | solution.py:17
  109.1 7.8 %collective-permute-start.15 = (f32[2,128]{1,0:T(2,128)S(1)}, f32[2,128]{1,0:T(2,128)S(1)}, u32[]{:S(2)}, u32[]{:S(2)}) collective-permute-start(f32[2,128]{1,0:T(2,128)S(1)} %broadcast_multiply_fusion), channel_id=1, source_target_pairs={{0,16},{1,17},{2,18},{3,19},{4,20},{5,21},{6,22},{7,23},{8,24},{9,... | collective-permute-start | bytes 3080 | tf_op jit(solution)/shard_map/ppermute | solution.py:17
  110.6 7.7 %collective-permute-start.16 = (f32[2,128]{1,0:T(2,128)S(1)}, f32[2,128]{1,0:T(2,128)S(1)}, u32[]{:S(2)}, u32[]{:S(2)}) collective-permute-start(f32[2,128]{1,0:T(2,128)S(1)} %broadcast_multiply_fusion), channel_id=1, source_target_pairs={{0,8},{1,9},{2,10},{3,11},{4,12},{5,13},{6,14},{7,15},{8,0},{9,1},... | collective-permute-start | bytes 3080 | tf_op jit(solution)/shard_map/ppermute | solution.py:17
  113.0 7.7 %collective-permute-start.17 = (f32[2,128]{1,0:T(2,128)S(1)}, f32[2,128]{1,0:T(2,128)S(1)}, u32[]{:S(2)}, u32[]{:S(2)}) collective-permute-start(f32[2,128]{1,0:T(2,128)S(1)} %broadcast_multiply_fusion), channel_id=1, source_target_pairs={{0,24},{1,25},{2,26},{3,27},{4,28},{5,29},{6,30},{7,31},{8,16},{9,... | collective-permute-start | bytes 3080 | tf_op jit(solution)/shard_map/ppermute | solution.py:17
  113.5 7.2 %collective-permute-start.18 = (f32[2,128]{1,0:T(2,128)S(1)}, f32[2,128]{1,0:T(2,128)S(1)}, u32[]{:S(2)}, u32[]{:S(2)}) collective-permute-start(f32[2,128]{1,0:T(2,128)S(1)} %broadcast_multiply_fusion), channel_id=1, source_target_pairs={{0,4},{1,5},{2,6},{3,7},{4,0},{5,1},{6,2},{7,3},{8,12},{9,13},{10,... | collective-permute-start | bytes 3080 | tf_op jit(solution)/shard_map/ppermute | solution.py:17
  115.9 4.8 %collective-permute-start.19 = (f32[2,128]{1,0:T(2,128)S(1)}, f32[2,128]{1,0:T(2,128)S(1)}, u32[]{:S(2)}, u32[]{:S(2)}) collective-permute-start(f32[2,128]{1,0:T(2,128)S(1)} %broadcast_multiply_fusion), channel_id=1, source_target_pairs={{0,20},{1,21},{2,22},{3,23},{4,16},{5,17},{6,18},{7,19},{8,28},{9,... | collective-permute-start | bytes 3080 | tf_op jit(solution)/shard_map/ppermute | solution.py:17
  116.8 5.4 %collective-permute-start.20 = (f32[2,128]{1,0:T(2,128)S(1)}, f32[2,128]{1,0:T(2,128)S(1)}, u32[]{:S(2)}, u32[]{:S(2)}) collective-permute-start(f32[2,128]{1,0:T(2,128)S(1)} %broadcast_multiply_fusion), channel_id=1, source_target_pairs={{0,12},{1,13},{2,14},{3,15},{4,8},{5,9},{6,10},{7,11},{8,4},{9,5},... | collective-permute-start | bytes 3080 | tf_op jit(solution)/shard_map/ppermute | solution.py:17
  118.3 6.3 %collective-permute-start.21 = (f32[2,128]{1,0:T(2,128)S(1)}, f32[2,128]{1,0:T(2,128)S(1)}, u32[]{:S(2)}, u32[]{:S(2)}) collective-permute-start(f32[2,128]{1,0:T(2,128)S(1)} %broadcast_multiply_fusion), channel_id=1, source_target_pairs={{0,28},{1,29},{2,30},{3,31},{4,24},{5,25},{6,26},{7,27},{8,20},{9,... | collective-permute-start | bytes 3080 | tf_op jit(solution)/shard_map/ppermute | solution.py:17
  124.6 3.6 %collective-permute-start.22 = (f32[2,128]{1,0:T(2,128)S(1)}, f32[2,128]{1,0:T(2,128)S(1)}, u32[]{:S(2)}, u32[]{:S(2)}) collective-permute-start(f32[2,128]{1,0:T(2,128)S(1)} %fusion.54), channel_id=1, source_target_pairs={{0,2},{1,3},{2,0},{3,1},{4,6},{5,7},{6,4},{7,5},{8,10},{9,11},{10,... | collective-permute-start | bytes 3080 | tf_op jit(solution)/shard_map/ppermute | solution.py:17
  (5 other events, 69.4 us)
Sparse Core Ops, SparseCore 0:
  10.3 61.0 all-gather.1

commit v16 on v13

--- a/solution.py
+++ b/solution.py
@@ -92,7 +92,7 @@
 
     part_a = jnp.einsum("tk,jk->tj", all_a, basis_a, preferred_element_type=jnp.float32)
     rot_a_block = (xor_sum(part_a, "owner", owners) * live[:, None]).astype(jnp.bfloat16)
-    first = min(256, m_block // 2)
+    first = m_block // 2
     parts_g = [
         jnp.einsum("tk,jk->tj", all_g, basis_g[start:stop], preferred_element_type=jnp.float32)
         for start, stop in ((0, first), (first, m_block))

time: 136 us -> 135 us (level)
  waiting for transfers between devices: 60.6 us -> 58 us
    ppermute x22, waiting for transfers between devices: 59.9 us -> 57.3 us  [xor_round(): parts.append(lax.ppermute(held, axis, [(i, i ^ c) for i in range(size)]))]
  transfers between devices with their start and end apart: 23 -> 23, of which waited for: 14 -> 15; matrix products, arithmetic and copies ran while one was open for 16% -> 15% of each run, Pallas kernels for 0% -> 0%
where the time goes in v16:
time: 135 us
  waiting for transfers between devices  58 us (43%)
  starting transfers between devices  26.3 us (19%)
  matrix products  19.1 us (14%)
  between operations  14.3 us (11%)
  other arithmetic  11.1 us (8%)
  local copies, waits for them, and re-layouts  6.15 us (5%)
    ppermute x22, waiting for transfers between devices, xor_round(): parts.append(lax.ppermute(held, axis, [(i, i ^ c) for i in range(size)]))  57.3 us
    ppermute x22, starting transfers between devices, xor_round(): parts.append(lax.ppermute(held, axis, [(i, i ^ c) for i in range(size)]))  26.3 us
    dot_general x2, matrix products, local(): jnp.einsum('tk,jk->tj', all_g, basis_g[start:stop], preferred_element_typ...  12.2 us
    dot_general x1, matrix products, local(): jnp.einsum('stm,smn->stn', g_rows, scaled, preferred_element_type=jnp.flo...  6.48 us
    convert_element_type x1, other arithmetic, local(): denom = eig_after.astype(jnp.float32)  3.88 us
  transfers between devices with their start and end apart: 23, of which 15 were waited for; matrix products, arithmetic and copies ran while one was open for 15% of the time, Pallas kernels for 0%

profile of v16, /device:TPU:0, one launch (start us, length us, event | category | flops | bytes accessed | tf_op | source)
XLA Modules:
  0.0 135.0 jit_solution(4965666997633822655)
XLA Ops:
  7.9 5.1 %collective-permute-start.4 = (bf16[1,16,2048]{2,1,0:T(8,128)(2,1)}, bf16[1,16,2048]{2,1,0:T(8,128)(2,1)S(1)}, u32[]{:S(2)}, u32[]{:S(2)}) collective-permute-start(bf16[1,16,2048]{2,1,0:T(8,128)(2,1)} %bitcast.107), channel_id=1, source_target_pairs={{0,12},{1,13},{2,14},{3,15},{4,8},{5,9},{6,10},{7,11},{8,4},{9,5},... | collective-permute-start | bytes 196616 | tf_op jit(solution)/shard_map/ppermute | solution.py:17
  20.5 1.6 %collective-permute-start.6 = (bf16[4,16,2048]{2,1,0:T(8,128)(2,1)S(1)}, bf16[4,16,2048]{2,1,0:T(8,128)(2,1)S(1)}, u32[]{:S(2)}, u32[]{:S(2)}) collective-permute-start(bf16[4,16,2048]{2,1,0:T(8,128)(2,1)S(1)} %broadcast_select_fusion), channel_id=1, source_target_pairs={{0,1},{1,0},{2,3},{3,2},{4,5},{5,4},{6,7},{7,6},{8,9},{9,8},{10,11... | collective-permute-start | bytes 786440 | tf_op jit(solution)/shard_map/ppermute | solution.py:17
  22.7 8.7 %collective-permute-done.7 = bf16[4,16,2048]{2,1,0:T(8,128)(2,1)S(1)} collective-permute-done((bf16[4,16,2048]{2,1,0:T(8,128)(2,1)S(1)}, bf16[4,16,2048]{2,1,0:T(8,128)(2,1)S(1)}, u32[]{:S(2)}, u32[]{:S(2)}) %collective-permute-start.7) | collective-permute-done | bytes 262176 | tf_op jit(solution)/shard_map/ppermute | solution.py:17
  31.5 5.7 %collective-permute-done.5 = bf16[4,16,2048]{2,1,0:T(8,128)(2,1)S(1)} collective-permute-done((bf16[4,16,2048]{2,1,0:T(8,128)(2,1)S(1)}, bf16[4,16,2048]{2,1,0:T(8,128)(2,1)S(1)}, u32[]{:S(2)}, u32[]{:S(2)}) %collective-permute-start.5) | collective-permute-done | bytes 262176 | tf_op jit(solution)/shard_map/ppermute | solution.py:17
  38.7 1.6 %collective-permute-start.8 = (f32[256,256]{1,0:T(8,128)S(1)}, f32[256,256]{1,0:T(8,128)S(1)}, u32[]{:S(2)}, u32[]{:S(2)}) collective-permute-start(f32[256,256]{1,0:T(8,128)S(1)} %fusion.48), channel_id=1, source_target_pairs={{0,16},{16,0},{1,17},{17,1},{2,18},{18,2},{3,19},{19,3},{4,20},{20... | collective-permute-start | bytes 786440 | tf_op jit(solution)/shard_map/ppermute | solution.py:17
  40.3 6.7 %collective-permute-done.8 = f32[256,256]{1,0:T(8,128)S(1)} collective-permute-done((f32[256,256]{1,0:T(8,128)S(1)}, f32[256,256]{1,0:T(8,128)S(1)}, u32[]{:S(2)}, u32[]{:S(2)}) %collective-permute-start.8) | collective-permute-done | bytes 262176 | tf_op jit(solution)/shard_map/ppermute | solution.py:17
  47.2 2.2 %collective-permute-start.11 = (bf16[1,256,256]{2,1,0:T(8,128)(2,1)S(1)}, bf16[1,256,256]{2,1,0:T(8,128)(2,1)S(1)}, u32[]{:S(2)}, u32[]{:S(2)}) collective-permute-start(bf16[1,256,256]{2,1,0:T(8,128)(2,1)S(1)} %multiply_convert_fusion), channel_id=1, source_target_pairs={{0,12},{1,13},{2,14},{3,15},{4,8},{5,9},{6,10},{7,11},{8,4},{9,5},... | collective-permute-start | bytes 393224 | tf_op jit(solution)/shard_map/ppermute | solution.py:17
  49.8 1.9 %collective-permute-start.9 = (bf16[1,256,256]{2,1,0:T(8,128)(2,1)S(1)}, bf16[1,256,256]{2,1,0:T(8,128)(2,1)S(1)}, u32[]{:S(2)}, u32[]{:S(2)}) collective-permute-start(bf16[1,256,256]{2,1,0:T(8,128)(2,1)S(1)} %multiply_convert_fusion), channel_id=1, source_target_pairs={{0,8},{1,9},{2,10},{3,11},{4,12},{5,13},{6,14},{7,15},{8,0},{9,1},... | collective-permute-start | bytes 393224 | tf_op jit(solution)/shard_map/ppermute | solution.py:17
  51.8 6.5 %collective-permute-done.11 = bf16[1,256,256]{2,1,0:T(8,128)(2,1)S(1)} collective-permute-done((bf16[1,256,256]{2,1,0:T(8,128)(2,1)S(1)}, bf16[1,256,256]{2,1,0:T(8,128)(2,1)S(1)}, u32[]{:S(2)}, u32[]{:S(2)}) %collective-permute-start.11) | collective-permute-done | bytes 131104 | tf_op jit(solution)/shard_map/ppermute | solution.py:17
  58.2 4.9 %collective-permute-done.10 = bf16[1,256,256]{2,1,0:T(8,128)(2,1)S(1)} collective-permute-done((bf16[1,256,256]{2,1,0:T(8,128)(2,1)S(1)}, bf16[1,256,256]{2,1,0:T(8,128)(2,1)S(1)}, u32[]{:S(2)}, u32[]{:S(2)}) %collective-permute-start.10) | collective-permute-done | bytes 131104 | tf_op jit(solution)/shard_map/ppermute | solution.py:17
  63.1 7.2 %collective-permute-done.9 = bf16[1,256,256]{2,1,0:T(8,128)(2,1)S(1)} collective-permute-done((bf16[1,256,256]{2,1,0:T(8,128)(2,1)S(1)}, bf16[1,256,256]{2,1,0:T(8,128)(2,1)S(1)}, u32[]{:S(2)}, u32[]{:S(2)}) %collective-permute-start.9) | collective-permute-done | bytes 131104 | tf_op jit(solution)/shard_map/ppermute | solution.py:17
  71.2 6.7 %fusion.3 = f32[256,448]{0,1:T(8,128)} fusion(bf16[256,7168]{1,0:T(8,128)(2,1)} %all-gather.2.cloned.1.call-done, bf16[896,7168]{1,0:T(8,128)(2,1)} %param.10), kind=kOutput, calls=%fused_computation.8 | convolution fusion | flops 1644167168 | bytes 10551296 | tf_op jit(solution)/shard_map/tk,jk->tj/dot_general | solution.py:97
  80.0 1.5 %collective-permute-start = (f32[256,448]{0,1:T(8,128)}, f32[256,448]{0,1:T(8,128)}, u32[]{:S(2)}, u32[]{:S(2)}) collective-permute-start(f32[256,448]{0,1:T(8,128)} %fusion.3), channel_id=1, source_target_pairs={{0,16},{16,0},{1,17},{17,1},{2,18},{18,2},{3,19},{19,3},{4,20},{20... | collective-permute-start | bytes 1376264 | tf_op jit(solution)/shard_map/ppermute | solution.py:17
  81.5 5.5 %fusion.1 = f32[256,448]{0,1:T(8,128)} fusion(bf16[256,7168]{1,0:T(8,128)(2,1)S(1)} %copy-done.2, bf16[896,7168]{1,0:T(8,128)(2,1)} %param.10), kind=kOutput, calls=%fused_computation.6 | convolution fusion | flops 1644167168 | bytes 10551296 | tf_op jit(solution)/shard_map/tk,jk->tj/dot_general | solution.py:97
  87.5 3.9 %convert_element_type.47 = f32[896,2048]{1,0:T(8,128)} convert(bf16[896,2048]{1,0:T(8,128)(2,1)S(1)} %copy-done.1) | non-fusion elementwise | flops 1835008 | bytes 11010048 | tf_op jit(solution)/shard_map/convert_element_type | solution.py:106
  95.9 6.4 %collective-permute-done.1 = f32[256,448]{0,1:T(8,128)} collective-permute-done((f32[256,448]{0,1:T(8,128)}, f32[256,448]{0,1:T(8,128)}, u32[]{:S(2)}, u32[]{:S(2)}) %collective-permute-start.1) | collective-permute-done | bytes 458784 | tf_op jit(solution)/shard_map/ppermute | solution.py:17
  103.9 6.5 %fusion.8 = f32[2,128]{1,0:T(2,128)S(1)} fusion(bf16[2,128,2048]{2,1,0:T(8,128)(2,1)S(1)} %reshape_reshape.7, f32[896,2048]{1,0:T(8,128)} %convert_element_type.47, bf16[2,128,448]{1,2,0:T(8,128)(2,1)S(1)} %get-tuple-element.15, bf16[2,128,448]{1,2,0:T(8,128)(2,1)S(1)} %get-tuple-element.14), kind=kOutput, calls=%fused_computation.12 | convolution fusion | flops 1889795840 | bytes 8848384 | tf_op jit(solution)/shard_map/stm,smn->stn/dot_general | solution.py:111
  110.5 1.9 %collective-permute-start.15 = (f32[2,128]{1,0:T(2,128)S(1)}, f32[2,128]{1,0:T(2,128)S(1)}, u32[]{:S(2)}, u32[]{:S(2)}) collective-permute-start(f32[2,128]{1,0:T(2,128)S(1)} %get-tuple-element.13), channel_id=1, source_target_pairs={{0,8},{1,9},{2,10},{3,11},{4,12},{5,13},{6,14},{7,15},{8,0},{9,1},... | collective-permute-start | bytes 3080 | tf_op jit(solution)/shard_map/ppermute | solution.py:17
  112.4 2.5 %collective-permute-start.17 = (f32[2,128]{1,0:T(2,128)S(1)}, f32[2,128]{1,0:T(2,128)S(1)}, u32[]{:S(2)}, u32[]{:S(2)}) collective-permute-start(f32[2,128]{1,0:T(2,128)S(1)} %get-tuple-element.13), channel_id=1, source_target_pairs={{0,12},{1,13},{2,14},{3,15},{4,8},{5,9},{6,10},{7,11},{8,4},{9,5},... | collective-permute-start | bytes 3080 | tf_op jit(solution)/shard_map/ppermute | solution.py:17
  115.0 2.7 %collective-permute-done.17 = f32[2,128]{1,0:T(2,128)S(1)} collective-permute-done((f32[2,128]{1,0:T(2,128)S(1)}, f32[2,128]{1,0:T(2,128)S(1)}, u32[]{:S(2)}, u32[]{:S(2)}) %collective-permute-start.17) | collective-permute-done | bytes 1056 | tf_op jit(solution)/shard_map/ppermute | solution.py:17
  117.8 1.8 %collective-permute-start.19 = (f32[2,128]{1,0:T(2,128)S(1)}, f32[2,128]{1,0:T(2,128)S(1)}, u32[]{:S(2)}, u32[]{:S(2)}) collective-permute-start(f32[2,128]{1,0:T(2,128)S(1)} %fusion.55), channel_id=1, source_target_pairs={{0,1},{1,0},{2,3},{3,2},{4,5},{5,4},{6,7},{7,6},{8,9},{9,8},{10,11... | collective-permute-start | bytes 3080 | tf_op jit(solution)/shard_map/ppermute | solution.py:17
  120.8 2.4 %collective-permute-done.18 = f32[2,128]{1,0:T(2,128)S(1)} collective-permute-done((f32[2,128]{1,0:T(2,128)S(1)}, f32[2,128]{1,0:T(2,128)S(1)}, u32[]{:S(2)}, u32[]{:S(2)}) %collective-permute-start.18) | collective-permute-done | bytes 1056 | tf_op jit(solution)/shard_map/ppermute | solution.py:17
  123.3 1.5 %collective-permute-start.21 = (f32[2,128]{1,0:T(2,128)S(1)}, f32[2,128]{1,0:T(2,128)S(1)}, u32[]{:S(2)}, u32[]{:S(2)}) collective-permute-start(f32[2,128]{1,0:T(2,128)S(1)} %fusion.54), channel_id=1, source_target_pairs={{0,16},{16,0},{1,17},{17,1},{2,18},{18,2},{3,19},{19,3},{4,20},{20... | collective-permute-start | bytes 3080 | tf_op jit(solution)/shard_map/ppermute | solution.py:17
  124.8 2.1 %collective-permute-done.21 = f32[2,128]{1,0:T(2,128)S(1)} collective-permute-done((f32[2,128]{1,0:T(2,128)S(1)}, f32[2,128]{1,0:T(2,128)S(1)}, u32[]{:S(2)}, u32[]{:S(2)}) %collective-permute-start.21) | collective-permute-done | bytes 1056 | tf_op jit(solution)/shard_map/ppermute | solution.py:17
  (83 shorter events, 23.2 us)
Async XLA Ops:
  7.2 31.0 %copy-start = (bf16[256,2048]{1,0:T(8,128)(2,1)S(1)}, bf16[256,2048]{1,0:T(8,128)(2,1)}, u32[]{:S(2)}) copy-start(bf16[256,2048]{1,0:T(8,128)(2,1)} %param.9) | copy-start | bytes 3145732
  7.2 64.0 %all-gather.2.cloned.1.call-start = ((), (), s32[]{:S(2)}) async-start(), calls=%async_computation | async-start | bytes 3899392 | tf_op jit(solution)/shard_map/all_gather | solution.py:87
  7.9 8.7 %collective-permute-start.4 = (bf16[1,16,2048]{2,1,0:T(8,128)(2,1)}, bf16[1,16,2048]{2,1,0:T(8,128)(2,1)S(1)}, u32[]{:S(2)}, u32[]{:S(2)}) collective-permute-start(bf16[1,16,2048]{2,1,0:T(8,128)(2,1)} %bitcast.107), channel_id=1, source_target_pairs={{0,12},{1,13},{2,14},{3,15},{4,8},{5,9},{6,10},{7,11},{8,4},{9,5},... | collective-permute-start | bytes 196616 | tf_op jit(solution)/shard_map/ppermute | solution.py:17
  13.0 4.9 %collective-permute-start.3 = (bf16[1,16,2048]{2,1,0:T(8,128)(2,1)}, bf16[1,16,2048]{2,1,0:T(8,128)(2,1)S(1)}, u32[]{:S(2)}, u32[]{:S(2)}) collective-permute-start(bf16[1,16,2048]{2,1,0:T(8,128)(2,1)} %bitcast.108), channel_id=1, source_target_pairs={{0,4},{1,5},{2,6},{3,7},{4,0},{5,1},{6,2},{7,3},{8,12},{9,13},{10,... | collective-permute-start | bytes 196616 | tf_op jit(solution)/shard_map/ppermute | solution.py:17
  13.0 5.8 %collective-permute-start.2 = (bf16[1,16,2048]{2,1,0:T(8,128)(2,1)}, bf16[1,16,2048]{2,1,0:T(8,128)(2,1)S(1)}, u32[]{:S(2)}, u32[]{:S(2)}) collective-permute-start(bf16[1,16,2048]{2,1,0:T(8,128)(2,1)} %bitcast.109), channel_id=1, source_target_pairs={{0,8},{1,9},{2,10},{3,11},{4,12},{5,13},{6,14},{7,15},{8,0},{9,1},... | collective-permute-start | bytes 196616 | tf_op jit(solution)/shard_map/ppermute | solution.py:17
  20.4 11.1 %collective-permute-start.7 = (bf16[4,16,2048]{2,1,0:T(8,128)(2,1)S(1)}, bf16[4,16,2048]{2,1,0:T(8,128)(2,1)S(1)}, u32[]{:S(2)}, u32[]{:S(2)}) collective-permute-start(bf16[4,16,2048]{2,1,0:T(8,128)(2,1)S(1)} %broadcast_select_fusion), channel_id=1, source_target_pairs={{0,3},{1,2},{2,1},{3,0},{4,7},{5,6},{6,5},{7,4},{8,11},{9,10},{10,... | collective-permute-start | bytes 786440 | tf_op jit(solution)/shard_map/ppermute | solution.py:17
  20.5 11.0 %collective-permute-start.6 = (bf16[4,16,2048]{2,1,0:T(8,128)(2,1)S(1)}, bf16[4,16,2048]{2,1,0:T(8,128)(2,1)S(1)}, u32[]{:S(2)}, u32[]{:S(2)}) collective-permute-start(bf16[4,16,2048]{2,1,0:T(8,128)(2,1)S(1)} %broadcast_select_fusion), channel_id=1, source_target_pairs={{0,1},{1,0},{2,3},{3,2},{4,5},{5,4},{6,7},{7,6},{8,9},{9,8},{10,11... | collective-permute-start | bytes 786440 | tf_op jit(solution)/shard_map/ppermute | solution.py:17
  22.1 15.0 %collective-permute-start.5 = (bf16[4,16,2048]{2,1,0:T(8,128)(2,1)S(1)}, bf16[4,16,2048]{2,1,0:T(8,128)(2,1)S(1)}, u32[]{:S(2)}, u32[]{:S(2)}) collective-permute-start(bf16[4,16,2048]{2,1,0:T(8,128)(2,1)S(1)} %broadcast_select_fusion), channel_id=1, source_target_pairs={{0,2},{1,3},{2,0},{3,1},{4,6},{5,7},{6,4},{7,5},{8,10},{9,11},{10,... | collective-permute-start | bytes 786440 | tf_op jit(solution)/shard_map/ppermute | solution.py:17
  38.7 8.3 %collective-permute-start.8 = (f32[256,256]{1,0:T(8,128)S(1)}, f32[256,256]{1,0:T(8,128)S(1)}, u32[]{:S(2)}, u32[]{:S(2)}) collective-permute-start(f32[256,256]{1,0:T(8,128)S(1)} %fusion.48), channel_id=1, source_target_pairs={{0,16},{16,0},{1,17},{17,1},{2,18},{18,2},{3,19},{19,3},{4,20},{20... | collective-permute-start | bytes 786440 | tf_op jit(solution)/shard_map/ppermute | solution.py:17
  47.2 11.0 %collective-permute-start.11 = (bf16[1,256,256]{2,1,0:T(8,128)(2,1)S(1)}, bf16[1,256,256]{2,1,0:T(8,128)(2,1)S(1)}, u32[]{:S(2)}, u32[]{:S(2)}) collective-permute-start(bf16[1,256,256]{2,1,0:T(8,128)(2,1)S(1)} %multiply_convert_fusion), channel_id=1, source_target_pairs={{0,12},{1,13},{2,14},{3,15},{4,8},{5,9},{6,10},{7,11},{8,4},{9,5},... | collective-permute-start | bytes 393224 | tf_op jit(solution)/shard_map/ppermute | solution.py:17
  49.5 13.7 %collective-permute-start.10 = (bf16[1,256,256]{2,1,0:T(8,128)(2,1)S(1)}, bf16[1,256,256]{2,1,0:T(8,128)(2,1)S(1)}, u32[]{:S(2)}, u32[]{:S(2)}) collective-permute-start(bf16[1,256,256]{2,1,0:T(8,128)(2,1)S(1)} %multiply_convert_fusion), channel_id=1, source_target_pairs={{0,4},{1,5},{2,6},{3,7},{4,0},{5,1},{6,2},{7,3},{8,12},{9,13},{10,... | collective-permute-start | bytes 393224 | tf_op jit(solution)/shard_map/ppermute | solution.py:17
  49.8 20.6 %collective-permute-start.9 = (bf16[1,256,256]{2,1,0:T(8,128)(2,1)S(1)}, bf16[1,256,256]{2,1,0:T(8,128)(2,1)S(1)}, u32[]{:S(2)}, u32[]{:S(2)}) collective-permute-start(bf16[1,256,256]{2,1,0:T(8,128)(2,1)S(1)} %multiply_convert_fusion), channel_id=1, source_target_pairs={{0,8},{1,9},{2,10},{3,11},{4,12},{5,13},{6,14},{7,15},{8,0},{9,1},... | collective-permute-start | bytes 393224 | tf_op jit(solution)/shard_map/ppermute | solution.py:17
  77.9 13.6 %collective-permute-start.14 = (bf16[2,256,256]{2,1,0:T(8,128)(2,1)S(1)}, bf16[2,256,256]{2,1,0:T(8,128)(2,1)S(1)}, u32[]{:S(2)}, u32[]{:S(2)}) collective-permute-start(bf16[2,256,256]{2,1,0:T(8,128)(2,1)S(1)} %broadcast_select_fusion.1), channel_id=1, source_target_pairs={{0,3},{1,2},{2,1},{3,0},{4,7},{5,6},{6,5},{7,4},{8,11},{9,10},{10,... | collective-permute-start | bytes 786440 | tf_op jit(solution)/shard_map/ppermute | solution.py:17
  79.2 12.2 %collective-permute-start.13 = (bf16[2,256,256]{2,1,0:T(8,128)(2,1)S(1)}, bf16[2,256,256]{2,1,0:T(8,128)(2,1)S(1)}, u32[]{:S(2)}, u32[]{:S(2)}) collective-permute-start(bf16[2,256,256]{2,1,0:T(8,128)(2,1)S(1)} %broadcast_select_fusion.1), channel_id=1, source_target_pairs={{0,1},{1,0},{2,3},{3,2},{4,5},{5,4},{6,7},{7,6},{8,9},{9,8},{10,11... | collective-permute-start | bytes 786440 | tf_op jit(solution)/shard_map/ppermute | solution.py:17
  79.5 12.6 %collective-permute-start.12 = (bf16[2,256,256]{2,1,0:T(8,128)(2,1)S(1)}, bf16[2,256,256]{2,1,0:T(8,128)(2,1)S(1)}, u32[]{:S(2)}, u32[]{:S(2)}) collective-permute-start(bf16[2,256,256]{2,1,0:T(8,128)(2,1)S(1)} %broadcast_select_fusion.1), channel_id=1, source_target_pairs={{0,2},{1,3},{2,0},{3,1},{4,6},{5,7},{6,4},{7,5},{8,10},{9,11},{10,... | collective-permute-start | bytes 786440 | tf_op jit(solution)/shard_map/ppermute | solution.py:17
  80.0 14.4 %collective-permute-start = (f32[256,448]{0,1:T(8,128)}, f32[256,448]{0,1:T(8,128)}, u32[]{:S(2)}, u32[]{:S(2)}) collective-permute-start(f32[256,448]{0,1:T(8,128)} %fusion.3), channel_id=1, source_target_pairs={{0,16},{16,0},{1,17},{17,1},{2,18},{18,2},{3,19},{19,3},{4,20},{20... | collective-permute-start | bytes 1376264 | tf_op jit(solution)/shard_map/ppermute | solution.py:17
  87.0 15.3 %collective-permute-start.1 = (f32[256,448]{0,1:T(8,128)}, f32[256,448]{0,1:T(8,128)}, u32[]{:S(2)}, u32[]{:S(2)}) collective-permute-start(f32[256,448]{0,1:T(8,128)} %fusion.1), channel_id=1, source_target_pairs={{0,16},{16,0},{1,17},{17,1},{2,18},{18,2},{3,19},{19,3},{4,20},{20... | collective-permute-start | bytes 1376264 | tf_op jit(solution)/shard_map/ppermute | solution.py:17
  110.4 4.5 %collective-permute-start.16 = (f32[2,128]{1,0:T(2,128)S(1)}, f32[2,128]{1,0:T(2,128)S(1)}, u32[]{:S(2)}, u32[]{:S(2)}) collective-permute-start(f32[2,128]{1,0:T(2,128)S(1)} %get-tuple-element.13), channel_id=1, source_target_pairs={{0,4},{1,5},{2,6},{3,7},{4,0},{5,1},{6,2},{7,3},{8,12},{9,13},{10,... | collective-permute-start | bytes 3080 | tf_op jit(solution)/shard_map/ppermute | solution.py:17
  110.5 4.5 %collective-permute-start.15 = (f32[2,128]{1,0:T(2,128)S(1)}, f32[2,128]{1,0:T(2,128)S(1)}, u32[]{:S(2)}, u32[]{:S(2)}) collective-permute-start(f32[2,128]{1,0:T(2,128)S(1)} %get-tuple-element.13), channel_id=1, source_target_pairs={{0,8},{1,9},{2,10},{3,11},{4,12},{5,13},{6,14},{7,15},{8,0},{9,1},... | collective-permute-start | bytes 3080 | tf_op jit(solution)/shard_map/ppermute | solution.py:17
  112.4 5.4 %collective-permute-start.17 = (f32[2,128]{1,0:T(2,128)S(1)}, f32[2,128]{1,0:T(2,128)S(1)}, u32[]{:S(2)}, u32[]{:S(2)}) collective-permute-start(f32[2,128]{1,0:T(2,128)S(1)} %get-tuple-element.13), channel_id=1, source_target_pairs={{0,12},{1,13},{2,14},{3,15},{4,8},{5,9},{6,10},{7,11},{8,4},{9,5},... | collective-permute-start | bytes 3080 | tf_op jit(solution)/shard_map/ppermute | solution.py:17
  117.8 3.1 %collective-permute-start.20 = (f32[2,128]{1,0:T(2,128)S(1)}, f32[2,128]{1,0:T(2,128)S(1)}, u32[]{:S(2)}, u32[]{:S(2)}) collective-permute-start(f32[2,128]{1,0:T(2,128)S(1)} %fusion.55), channel_id=1, source_target_pairs={{0,3},{1,2},{2,1},{3,0},{4,7},{5,6},{6,5},{7,4},{8,11},{9,10},{10,... | collective-permute-start | bytes 3080 | tf_op jit(solution)/shard_map/ppermute | solution.py:17
  117.8 3.0 %collective-permute-start.19 = (f32[2,128]{1,0:T(2,128)S(1)}, f32[2,128]{1,0:T(2,128)S(1)}, u32[]{:S(2)}, u32[]{:S(2)}) collective-permute-start(f32[2,128]{1,0:T(2,128)S(1)} %fusion.55), channel_id=1, source_target_pairs={{0,1},{1,0},{2,3},{3,2},{4,5},{5,4},{6,7},{7,6},{8,9},{9,8},{10,11... | collective-permute-start | bytes 3080 | tf_op jit(solution)/shard_map/ppermute | solution.py:17
  119.7 3.6 %collective-permute-start.18 = (f32[2,128]{1,0:T(2,128)S(1)}, f32[2,128]{1,0:T(2,128)S(1)}, u32[]{:S(2)}, u32[]{:S(2)}) collective-permute-start(f32[2,128]{1,0:T(2,128)S(1)} %fusion.55), channel_id=1, source_target_pairs={{0,2},{1,3},{2,0},{3,1},{4,6},{5,7},{6,4},{7,5},{8,10},{9,11},{10,... | collective-permute-start | bytes 3080 | tf_op jit(solution)/shard_map/ppermute | solution.py:17
  123.3 3.6 %collective-permute-start.21 = (f32[2,128]{1,0:T(2,128)S(1)}, f32[2,128]{1,0:T(2,128)S(1)}, u32[]{:S(2)}, u32[]{:S(2)}) collective-permute-start(f32[2,128]{1,0:T(2,128)S(1)} %fusion.54), channel_id=1, source_target_pairs={{0,16},{16,0},{1,17},{17,1},{2,18},{18,2},{3,19},{19,3},{4,20},{20... | collective-permute-start | bytes 3080 | tf_op jit(solution)/shard_map/ppermute | solution.py:17
  (3 other events, 43.1 us)
Sparse Core Ops, SparseCore 0:
  10.3 60.4 all-gather.1

commit v17 on v16

--- a/solution.py
+++ b/solution.py
@@ -49,10 +49,13 @@
     target = owner_index * group_size
     held = block[None]
     groups = bit_groups(bits)
-    for group in groups:
+    if after is not None:
+        groups = groups[:-1] + [[bit] for bit in groups[-1]]
+        gate_at = len(groups) - 2 if len(groups) > 1 and len(groups[-2]) == 1 else len(groups) - 1
+    for step, group in enumerate(groups):
         high = sum(bit for bit in group if bit >= group_size)
         low = [bit for bit in group if bit < group_size]
-        if after is not None and group is groups[-1]:
+        if after is not None and step == gate_at:
             held, _ = lax.optimization_barrier((held, after))
         stacked = xor_round(held, "reader", readers, group)
         c_high = (reader_index ^ target) & high

time: 135 us -> 138 us (1.022)
  other arithmetic: 11.1 us -> 15.2 us
  waiting for transfers between devices: 58 us -> 55.8 us
  local copies, waits for them, and re-layouts: 6.15 us -> 7.56 us
    ppermute x22 -> x21, waiting for transfers between devices: 57.3 us -> 55.1 us  [xor_round(): parts.append(lax.ppermute(held, axis, [(i, i ^ c) for i in range(size)]))]
    convert_element_type x1, other arithmetic: 3.88 us -> 5.91 us  [local(): denom = eig_after.astype(jnp.float32)]
    gather x4 -> x5, local copies, waits for them, and re-layouts: 2.36 us -> 2.94 us  [ordered_gather(): chosen = jnp.take(stacked, jnp.stack(picks), axis=0)]
    ppermute x22 -> x21, starting transfers between devices: 26.3 us -> 25.9 us  [xor_round(): parts.append(lax.ppermute(held, axis, [(i, i ^ c) for i in range(size)]))]
  transfers between devices with their start and end apart: 23 -> 22, of which waited for: 15 -> 15; matrix products, arithmetic and copies ran while one was open for 15% -> 17% of each run, Pallas kernels for 0% -> 0%
where the time goes in v17:
time: 138 us; the launch traced here: 137 us
  waiting for transfers between devices  55.8 us (40%)
  starting transfers between devices  25.9 us (19%)
  matrix products  18.5 us (13%)
  other arithmetic  15.2 us (11%)
  between operations  14.4 us (10%)
  local copies, waits for them, and re-layouts  7.56 us (5%)
    ppermute x21, waiting for transfers between devices, xor_round(): parts.append(lax.ppermute(held, axis, [(i, i ^ c) for i in range(size)]))  55.1 us
    ppermute x21, starting transfers between devices, xor_round(): parts.append(lax.ppermute(held, axis, [(i, i ^ c) for i in range(size)]))  25.9 us
    dot_general x2, matrix products, local(): jnp.einsum('tk,jk->tj', all_g, basis_g[start:stop], preferred_element_typ...  11.4 us
    dot_general x1, matrix products, local(): jnp.einsum('stm,smn->stn', g_rows, scaled, preferred_element_type=jnp.flo...  6.63 us
    convert_element_type x1, other arithmetic, local(): denom = eig_after.astype(jnp.float32)  5.91 us
    gather x5, local copies, waits for them, and re-layouts, ordered_gather(): chosen = jnp.take(stacked, jnp.stack(picks), axis=0)  2.94 us
  transfers between devices with their start and end apart: 22, of which 15 were waited for; matrix products, arithmetic and copies ran while one was open for 17% of the time, Pallas kernels for 0%

profile of v17, /device:TPU:0, one launch (start us, length us, event | category | flops | bytes accessed | tf_op | source)
XLA Modules:
  0.0 137.4 jit_solution(16140045666621942076)
XLA Ops:
  7.9 5.1 %collective-permute-start.4 = (bf16[1,16,2048]{2,1,0:T(8,128)(2,1)}, bf16[1,16,2048]{2,1,0:T(8,128)(2,1)S(1)}, u32[]{:S(2)}, u32[]{:S(2)}) collective-permute-start(bf16[1,16,2048]{2,1,0:T(8,128)(2,1)} %bitcast.124), channel_id=1, source_target_pairs={{0,12},{1,13},{2,14},{3,15},{4,8},{5,9},{6,10},{7,11},{8,4},{9,5},... | collective-permute-start | bytes 196616 | tf_op jit(solution)/shard_map/ppermute | solution.py:17
  20.5 1.6 %collective-permute-start.6 = (bf16[4,16,2048]{2,1,0:T(8,128)(2,1)S(1)}, bf16[4,16,2048]{2,1,0:T(8,128)(2,1)S(1)}, u32[]{:S(2)}, u32[]{:S(2)}) collective-permute-start(bf16[4,16,2048]{2,1,0:T(8,128)(2,1)S(1)} %broadcast_select_fusion), channel_id=1, source_target_pairs={{0,1},{1,0},{2,3},{3,2},{4,5},{5,4},{6,7},{7,6},{8,9},{9,8},{10,11... | collective-permute-start | bytes 786440 | tf_op jit(solution)/shard_map/ppermute | solution.py:17
  22.7 8.7 %collective-permute-done.7 = bf16[4,16,2048]{2,1,0:T(8,128)(2,1)S(1)} collective-permute-done((bf16[4,16,2048]{2,1,0:T(8,128)(2,1)S(1)}, bf16[4,16,2048]{2,1,0:T(8,128)(2,1)S(1)}, u32[]{:S(2)}, u32[]{:S(2)}) %collective-permute-start.7) | collective-permute-done | bytes 262176 | tf_op jit(solution)/shard_map/ppermute | solution.py:17
  31.5 5.7 %collective-permute-done.5 = bf16[4,16,2048]{2,1,0:T(8,128)(2,1)S(1)} collective-permute-done((bf16[4,16,2048]{2,1,0:T(8,128)(2,1)S(1)}, bf16[4,16,2048]{2,1,0:T(8,128)(2,1)S(1)}, u32[]{:S(2)}, u32[]{:S(2)}) %collective-permute-start.5) | collective-permute-done | bytes 262176 | tf_op jit(solution)/shard_map/ppermute | solution.py:17
  38.7 1.6 %collective-permute-start.8 = (f32[256,256]{1,0:T(8,128)S(1)}, f32[256,256]{1,0:T(8,128)S(1)}, u32[]{:S(2)}, u32[]{:S(2)}) collective-permute-start(f32[256,256]{1,0:T(8,128)S(1)} %fusion.50), channel_id=1, source_target_pairs={{0,16},{16,0},{1,17},{17,1},{2,18},{18,2},{3,19},{19,3},{4,20},{20... | collective-permute-start | bytes 786440 | tf_op jit(solution)/shard_map/ppermute | solution.py:17
  40.3 6.7 %collective-permute-done.8 = f32[256,256]{1,0:T(8,128)S(1)} collective-permute-done((f32[256,256]{1,0:T(8,128)S(1)}, f32[256,256]{1,0:T(8,128)S(1)}, u32[]{:S(2)}, u32[]{:S(2)}) %collective-permute-start.8) | collective-permute-done | bytes 262176 | tf_op jit(solution)/shard_map/ppermute | solution.py:17
  47.2 2.2 %collective-permute-start.11 = (bf16[1,256,256]{2,1,0:T(8,128)(2,1)S(1)}, bf16[1,256,256]{2,1,0:T(8,128)(2,1)S(1)}, u32[]{:S(2)}, u32[]{:S(2)}) collective-permute-start(bf16[1,256,256]{2,1,0:T(8,128)(2,1)S(1)} %multiply_convert_fusion), channel_id=1, source_target_pairs={{0,12},{1,13},{2,14},{3,15},{4,8},{5,9},{6,10},{7,11},{8,4},{9,5},... | collective-permute-start | bytes 393224 | tf_op jit(solution)/shard_map/ppermute | solution.py:17
  49.8 1.9 %collective-permute-start.9 = (bf16[1,256,256]{2,1,0:T(8,128)(2,1)S(1)}, bf16[1,256,256]{2,1,0:T(8,128)(2,1)S(1)}, u32[]{:S(2)}, u32[]{:S(2)}) collective-permute-start(bf16[1,256,256]{2,1,0:T(8,128)(2,1)S(1)} %multiply_convert_fusion), channel_id=1, source_target_pairs={{0,8},{1,9},{2,10},{3,11},{4,12},{5,13},{6,14},{7,15},{8,0},{9,1},... | collective-permute-start | bytes 393224 | tf_op jit(solution)/shard_map/ppermute | solution.py:17
  51.8 6.5 %collective-permute-done.11 = bf16[1,256,256]{2,1,0:T(8,128)(2,1)S(1)} collective-permute-done((bf16[1,256,256]{2,1,0:T(8,128)(2,1)S(1)}, bf16[1,256,256]{2,1,0:T(8,128)(2,1)S(1)}, u32[]{:S(2)}, u32[]{:S(2)}) %collective-permute-start.11) | collective-permute-done | bytes 131104 | tf_op jit(solution)/shard_map/ppermute | solution.py:17
  58.2 4.9 %collective-permute-done.10 = bf16[1,256,256]{2,1,0:T(8,128)(2,1)S(1)} collective-permute-done((bf16[1,256,256]{2,1,0:T(8,128)(2,1)S(1)}, bf16[1,256,256]{2,1,0:T(8,128)(2,1)S(1)}, u32[]{:S(2)}, u32[]{:S(2)}) %collective-permute-start.10) | collective-permute-done | bytes 131104 | tf_op jit(solution)/shard_map/ppermute | solution.py:17
  63.1 7.3 %collective-permute-done.9 = bf16[1,256,256]{2,1,0:T(8,128)(2,1)S(1)} collective-permute-done((bf16[1,256,256]{2,1,0:T(8,128)(2,1)S(1)}, bf16[1,256,256]{2,1,0:T(8,128)(2,1)S(1)}, u32[]{:S(2)}, u32[]{:S(2)}) %collective-permute-start.9) | collective-permute-done | bytes 131104 | tf_op jit(solution)/shard_map/ppermute | solution.py:17
  71.2 5.9 %fusion.3 = f32[256,448]{0,1:T(8,128)S(1)} fusion(bf16[256,7168]{1,0:T(8,128)(2,1)} %all-gather.2.cloned.1.call-done, bf16[896,7168]{1,0:T(8,128)(2,1)} %param.10), kind=kOutput, calls=%fused_computation.9 | convolution fusion | flops 1644167168 | bytes 10551296 | tf_op jit(solution)/shard_map/tk,jk->tj/dot_general | solution.py:100
  77.1 1.5 %collective-permute-start = (f32[256,448]{0,1:T(8,128)S(1)}, f32[256,448]{0,1:T(8,128)}, u32[]{:S(2)}, u32[]{:S(2)}) collective-permute-start(f32[256,448]{0,1:T(8,128)S(1)} %fusion.3), channel_id=1, source_target_pairs={{0,16},{16,0},{1,17},{17,1},{2,18},{18,2},{3,19},{19,3},{4,20},{20... | collective-permute-start | bytes 1376264 | tf_op jit(solution)/shard_map/ppermute | solution.py:17
  80.1 5.5 %fusion.1 = f32[256,448]{0,1:T(8,128)} fusion(bf16[256,7168]{1,0:T(8,128)(2,1)S(1)} %copy-done.3, bf16[896,7168]{1,0:T(8,128)(2,1)} %param.10), kind=kOutput, calls=%fused_computation.7 | convolution fusion | flops 1644167168 | bytes 10551296 | tf_op jit(solution)/shard_map/tk,jk->tj/dot_general | solution.py:100
  87.5 5.9 %convert_element_type.47 = f32[896,2048]{1,0:T(8,128)} convert(bf16[896,2048]{1,0:T(8,128)(2,1)} %param.11) | non-fusion elementwise | flops 1835008 | bytes 11010048 | tf_op jit(solution)/shard_map/convert_element_type | solution.py:109
  94.8 4.6 %collective-permute-done.1 = f32[256,448]{0,1:T(8,128)} collective-permute-done((f32[256,448]{0,1:T(8,128)}, f32[256,448]{0,1:T(8,128)}, u32[]{:S(2)}, u32[]{:S(2)}) %collective-permute-start.1) | collective-permute-done | bytes 458784 | tf_op jit(solution)/shard_map/ppermute | solution.py:17
  106.1 6.6 %fusion.8 = f32[2,128]{1,0:T(2,128)S(1)} fusion(bf16[2,128,2048]{2,1,0:T(8,128)(2,1)S(1)} %reshape_reshape.7, f32[896,2048]{1,0:T(8,128)} %convert_element_type.47, bf16[2,128,448]{1,2,0:T(8,128)(2,1)} %get-tuple-element.15, bf16[2,128,448]{1,2,0:T(8,128)(2,1)S(1)} %copy-done.2), kind=kOutput, calls=%fused_computation.13 | convolution fusion | flops 1889795840 | bytes 8848384 | tf_op jit(solution)/shard_map/stm,smn->stn/dot_general | solution.py:114
  112.8 1.7 %collective-permute-start.14 = (f32[2,128]{1,0:T(2,128)S(1)}, f32[2,128]{1,0:T(2,128)S(1)}, u32[]{:S(2)}, u32[]{:S(2)}) collective-permute-start(f32[2,128]{1,0:T(2,128)S(1)} %get-tuple-element.13), channel_id=1, source_target_pairs={{0,8},{1,9},{2,10},{3,11},{4,12},{5,13},{6,14},{7,15},{8,0},{9,1},... | collective-permute-start | bytes 3080 | tf_op jit(solution)/shard_map/ppermute | solution.py:17
  114.4 2.7 %collective-permute-start.16 = (f32[2,128]{1,0:T(2,128)S(1)}, f32[2,128]{1,0:T(2,128)S(1)}, u32[]{:S(2)}, u32[]{:S(2)}) collective-permute-start(f32[2,128]{1,0:T(2,128)S(1)} %get-tuple-element.13), channel_id=1, source_target_pairs={{0,12},{1,13},{2,14},{3,15},{4,8},{5,9},{6,10},{7,11},{8,4},{9,5},... | collective-permute-start | bytes 3080 | tf_op jit(solution)/shard_map/ppermute | solution.py:17
  117.3 2.5 %collective-permute-done.16 = f32[2,128]{1,0:T(2,128)S(1)} collective-permute-done((f32[2,128]{1,0:T(2,128)S(1)}, f32[2,128]{1,0:T(2,128)S(1)}, u32[]{:S(2)}, u32[]{:S(2)}) %collective-permute-start.16) | collective-permute-done | bytes 1056 | tf_op jit(solution)/shard_map/ppermute | solution.py:17
  119.9 2.2 %collective-permute-start.18 = (f32[2,128]{1,0:T(2,128)S(1)}, f32[2,128]{1,0:T(2,128)S(1)}, u32[]{:S(2)}, u32[]{:S(2)}) collective-permute-start(f32[2,128]{1,0:T(2,128)S(1)} %fusion.57), channel_id=1, source_target_pairs={{0,1},{1,0},{2,3},{3,2},{4,5},{5,4},{6,7},{7,6},{8,9},{9,8},{10,11... | collective-permute-start | bytes 3080 | tf_op jit(solution)/shard_map/ppermute | solution.py:17
  122.9 2.7 %collective-permute-done.17 = f32[2,128]{1,0:T(2,128)S(1)} collective-permute-done((f32[2,128]{1,0:T(2,128)S(1)}, f32[2,128]{1,0:T(2,128)S(1)}, u32[]{:S(2)}, u32[]{:S(2)}) %collective-permute-start.17) | collective-permute-done | bytes 1056 | tf_op jit(solution)/shard_map/ppermute | solution.py:17
  125.6 1.5 %collective-permute-start.20 = (f32[2,128]{1,0:T(2,128)S(1)}, f32[2,128]{1,0:T(2,128)S(1)}, u32[]{:S(2)}, u32[]{:S(2)}) collective-permute-start(f32[2,128]{1,0:T(2,128)S(1)} %fusion.56), channel_id=1, source_target_pairs={{0,16},{16,0},{1,17},{17,1},{2,18},{18,2},{3,19},{19,3},{4,20},{20... | collective-permute-start | bytes 3080 | tf_op jit(solution)/shard_map/ppermute | solution.py:17
  127.2 2.1 %collective-permute-done.20 = f32[2,128]{1,0:T(2,128)S(1)} collective-permute-done((f32[2,128]{1,0:T(2,128)S(1)}, f32[2,128]{1,0:T(2,128)S(1)}, u32[]{:S(2)}, u32[]{:S(2)}) %collective-permute-start.20) | collective-permute-done | bytes 1056 | tf_op jit(solution)/shard_map/ppermute | solution.py:17
  (92 shorter events, 25.4 us)
Async XLA Ops:
  7.2 31.0 %copy-start = (bf16[256,2048]{1,0:T(8,128)(2,1)S(1)}, bf16[256,2048]{1,0:T(8,128)(2,1)}, u32[]{:S(2)}) copy-start(bf16[256,2048]{1,0:T(8,128)(2,1)} %param.9) | copy-start | bytes 3145732
  7.2 64.0 %all-gather.2.cloned.1.call-start = ((), (), s32[]{:S(2)}) async-start(), calls=%async_computation | async-start | bytes 3899392 | tf_op jit(solution)/shard_map/all_gather | solution.py:90
  7.9 8.8 %collective-permute-start.4 = (bf16[1,16,2048]{2,1,0:T(8,128)(2,1)}, bf16[1,16,2048]{2,1,0:T(8,128)(2,1)S(1)}, u32[]{:S(2)}, u32[]{:S(2)}) collective-permute-start(bf16[1,16,2048]{2,1,0:T(8,128)(2,1)} %bitcast.124), channel_id=1, source_target_pairs={{0,12},{1,13},{2,14},{3,15},{4,8},{5,9},{6,10},{7,11},{8,4},{9,5},... | collective-permute-start | bytes 196616 | tf_op jit(solution)/shard_map/ppermute | solution.py:17
  13.0 4.9 %collective-permute-start.3 = (bf16[1,16,2048]{2,1,0:T(8,128)(2,1)}, bf16[1,16,2048]{2,1,0:T(8,128)(2,1)S(1)}, u32[]{:S(2)}, u32[]{:S(2)}) collective-permute-start(bf16[1,16,2048]{2,1,0:T(8,128)(2,1)} %bitcast.125), channel_id=1, source_target_pairs={{0,4},{1,5},{2,6},{3,7},{4,0},{5,1},{6,2},{7,3},{8,12},{9,13},{10,... | collective-permute-start | bytes 196616 | tf_op jit(solution)/shard_map/ppermute | solution.py:17
  13.0 5.8 %collective-permute-start.2 = (bf16[1,16,2048]{2,1,0:T(8,128)(2,1)}, bf16[1,16,2048]{2,1,0:T(8,128)(2,1)S(1)}, u32[]{:S(2)}, u32[]{:S(2)}) collective-permute-start(bf16[1,16,2048]{2,1,0:T(8,128)(2,1)} %bitcast.126), channel_id=1, source_target_pairs={{0,8},{1,9},{2,10},{3,11},{4,12},{5,13},{6,14},{7,15},{8,0},{9,1},... | collective-permute-start | bytes 196616 | tf_op jit(solution)/shard_map/ppermute | solution.py:17
  20.4 11.1 %collective-permute-start.7 = (bf16[4,16,2048]{2,1,0:T(8,128)(2,1)S(1)}, bf16[4,16,2048]{2,1,0:T(8,128)(2,1)S(1)}, u32[]{:S(2)}, u32[]{:S(2)}) collective-permute-start(bf16[4,16,2048]{2,1,0:T(8,128)(2,1)S(1)} %broadcast_select_fusion), channel_id=1, source_target_pairs={{0,3},{1,2},{2,1},{3,0},{4,7},{5,6},{6,5},{7,4},{8,11},{9,10},{10,... | collective-permute-start | bytes 786440 | tf_op jit(solution)/shard_map/ppermute | solution.py:17
  20.5 11.0 %collective-permute-start.6 = (bf16[4,16,2048]{2,1,0:T(8,128)(2,1)S(1)}, bf16[4,16,2048]{2,1,0:T(8,128)(2,1)S(1)}, u32[]{:S(2)}, u32[]{:S(2)}) collective-permute-start(bf16[4,16,2048]{2,1,0:T(8,128)(2,1)S(1)} %broadcast_select_fusion), channel_id=1, source_target_pairs={{0,1},{1,0},{2,3},{3,2},{4,5},{5,4},{6,7},{7,6},{8,9},{9,8},{10,11... | collective-permute-start | bytes 786440 | tf_op jit(solution)/shard_map/ppermute | solution.py:17
  22.1 15.0 %collective-permute-start.5 = (bf16[4,16,2048]{2,1,0:T(8,128)(2,1)S(1)}, bf16[4,16,2048]{2,1,0:T(8,128)(2,1)S(1)}, u32[]{:S(2)}, u32[]{:S(2)}) collective-permute-start(bf16[4,16,2048]{2,1,0:T(8,128)(2,1)S(1)} %broadcast_select_fusion), channel_id=1, source_target_pairs={{0,2},{1,3},{2,0},{3,1},{4,6},{5,7},{6,4},{7,5},{8,10},{9,11},{10,... | collective-permute-start | bytes 786440 | tf_op jit(solution)/shard_map/ppermute | solution.py:17
  38.7 8.3 %collective-permute-start.8 = (f32[256,256]{1,0:T(8,128)S(1)}, f32[256,256]{1,0:T(8,128)S(1)}, u32[]{:S(2)}, u32[]{:S(2)}) collective-permute-start(f32[256,256]{1,0:T(8,128)S(1)} %fusion.50), channel_id=1, source_target_pairs={{0,16},{16,0},{1,17},{17,1},{2,18},{18,2},{3,19},{19,3},{4,20},{20... | collective-permute-start | bytes 786440 | tf_op jit(solution)/shard_map/ppermute | solution.py:17
  47.2 11.0 %collective-permute-start.11 = (bf16[1,256,256]{2,1,0:T(8,128)(2,1)S(1)}, bf16[1,256,256]{2,1,0:T(8,128)(2,1)S(1)}, u32[]{:S(2)}, u32[]{:S(2)}) collective-permute-start(bf16[1,256,256]{2,1,0:T(8,128)(2,1)S(1)} %multiply_convert_fusion), channel_id=1, source_target_pairs={{0,12},{1,13},{2,14},{3,15},{4,8},{5,9},{6,10},{7,11},{8,4},{9,5},... | collective-permute-start | bytes 393224 | tf_op jit(solution)/shard_map/ppermute | solution.py:17
  49.5 13.6 %collective-permute-start.10 = (bf16[1,256,256]{2,1,0:T(8,128)(2,1)S(1)}, bf16[1,256,256]{2,1,0:T(8,128)(2,1)S(1)}, u32[]{:S(2)}, u32[]{:S(2)}) collective-permute-start(bf16[1,256,256]{2,1,0:T(8,128)(2,1)S(1)} %multiply_convert_fusion), channel_id=1, source_target_pairs={{0,4},{1,5},{2,6},{3,7},{4,0},{5,1},{6,2},{7,3},{8,12},{9,13},{10,... | collective-permute-start | bytes 393224 | tf_op jit(solution)/shard_map/ppermute | solution.py:17
  49.8 20.6 %collective-permute-start.9 = (bf16[1,256,256]{2,1,0:T(8,128)(2,1)S(1)}, bf16[1,256,256]{2,1,0:T(8,128)(2,1)S(1)}, u32[]{:S(2)}, u32[]{:S(2)}) collective-permute-start(bf16[1,256,256]{2,1,0:T(8,128)(2,1)S(1)} %multiply_convert_fusion), channel_id=1, source_target_pairs={{0,8},{1,9},{2,10},{3,11},{4,12},{5,13},{6,14},{7,15},{8,0},{9,1},... | collective-permute-start | bytes 393224 | tf_op jit(solution)/shard_map/ppermute | solution.py:17
  77.1 16.4 %collective-permute-start = (f32[256,448]{0,1:T(8,128)S(1)}, f32[256,448]{0,1:T(8,128)}, u32[]{:S(2)}, u32[]{:S(2)}) collective-permute-start(f32[256,448]{0,1:T(8,128)S(1)} %fusion.3), channel_id=1, source_target_pairs={{0,16},{16,0},{1,17},{17,1},{2,18},{18,2},{3,19},{19,3},{4,20},{20... | collective-permute-start | bytes 1376264 | tf_op jit(solution)/shard_map/ppermute | solution.py:17
  78.6 7.9 %collective-permute-start.12 = (bf16[2,256,256]{2,1,0:T(8,128)(2,1)S(1)}, bf16[2,256,256]{2,1,0:T(8,128)(2,1)S(1)}, u32[]{:S(2)}, u32[]{:S(2)}) collective-permute-start(bf16[2,256,256]{2,1,0:T(8,128)(2,1)S(1)} %broadcast_select_fusion.1), channel_id=1, source_target_pairs={{0,2},{1,3},{2,0},{3,1},{4,6},{5,7},{6,4},{7,5},{8,10},{9,11},{10,... | collective-permute-start | bytes 786440 | tf_op jit(solution)/shard_map/ppermute | solution.py:17
  85.6 13.8 %collective-permute-start.1 = (f32[256,448]{0,1:T(8,128)}, f32[256,448]{0,1:T(8,128)}, u32[]{:S(2)}, u32[]{:S(2)}) collective-permute-start(f32[256,448]{0,1:T(8,128)} %fusion.1), channel_id=1, source_target_pairs={{0,16},{16,0},{1,17},{17,1},{2,18},{18,2},{3,19},{19,3},{4,20},{20... | collective-permute-start | bytes 1376264 | tf_op jit(solution)/shard_map/ppermute | solution.py:17
  87.4 14.5 %collective-permute-start.13 = (bf16[4,256,256]{2,1,0:T(8,128)(2,1)S(1)}, bf16[4,256,256]{2,1,0:T(8,128)(2,1)S(1)}, u32[]{:S(2)}, u32[]{:S(2)}) collective-permute-start(bf16[4,256,256]{2,1,0:T(8,128)(2,1)S(1)} %bitcast.110), channel_id=1, source_target_pairs={{0,1},{1,0},{2,3},{3,2},{4,5},{5,4},{6,7},{7,6},{8,9},{9,8},{10,11... | collective-permute-start | bytes 1572872 | tf_op jit(solution)/shard_map/ppermute | solution.py:17
  106.0 23.4 %copy-start.4 = (s32[2]{0:T(128)S(1)}, s32[2]{0:T(128)}, u32[]{:S(2)}) copy-start(s32[2]{0:T(128)} %param.13) | copy-start | bytes 28
  112.7 4.5 %collective-permute-start.15 = (f32[2,128]{1,0:T(2,128)S(1)}, f32[2,128]{1,0:T(2,128)S(1)}, u32[]{:S(2)}, u32[]{:S(2)}) collective-permute-start(f32[2,128]{1,0:T(2,128)S(1)} %get-tuple-element.13), channel_id=1, source_target_pairs={{0,4},{1,5},{2,6},{3,7},{4,0},{5,1},{6,2},{7,3},{8,12},{9,13},{10,... | collective-permute-start | bytes 3080 | tf_op jit(solution)/shard_map/ppermute | solution.py:17
  112.8 4.5 %collective-permute-start.14 = (f32[2,128]{1,0:T(2,128)S(1)}, f32[2,128]{1,0:T(2,128)S(1)}, u32[]{:S(2)}, u32[]{:S(2)}) collective-permute-start(f32[2,128]{1,0:T(2,128)S(1)} %get-tuple-element.13), channel_id=1, source_target_pairs={{0,8},{1,9},{2,10},{3,11},{4,12},{5,13},{6,14},{7,15},{8,0},{9,1},... | collective-permute-start | bytes 3080 | tf_op jit(solution)/shard_map/ppermute | solution.py:17
  114.4 5.4 %collective-permute-start.16 = (f32[2,128]{1,0:T(2,128)S(1)}, f32[2,128]{1,0:T(2,128)S(1)}, u32[]{:S(2)}, u32[]{:S(2)}) collective-permute-start(f32[2,128]{1,0:T(2,128)S(1)} %get-tuple-element.13), channel_id=1, source_target_pairs={{0,12},{1,13},{2,14},{3,15},{4,8},{5,9},{6,10},{7,11},{8,4},{9,5},... | collective-permute-start | bytes 3080 | tf_op jit(solution)/shard_map/ppermute | solution.py:17
  119.8 3.1 %collective-permute-start.19 = (f32[2,128]{1,0:T(2,128)S(1)}, f32[2,128]{1,0:T(2,128)S(1)}, u32[]{:S(2)}, u32[]{:S(2)}) collective-permute-start(f32[2,128]{1,0:T(2,128)S(1)} %fusion.57), channel_id=1, source_target_pairs={{0,3},{1,2},{2,1},{3,0},{4,7},{5,6},{6,5},{7,4},{8,11},{9,10},{10,... | collective-permute-start | bytes 3080 | tf_op jit(solution)/shard_map/ppermute | solution.py:17
  119.9 3.0 %collective-permute-start.18 = (f32[2,128]{1,0:T(2,128)S(1)}, f32[2,128]{1,0:T(2,128)S(1)}, u32[]{:S(2)}, u32[]{:S(2)}) collective-permute-start(f32[2,128]{1,0:T(2,128)S(1)} %fusion.57), channel_id=1, source_target_pairs={{0,1},{1,0},{2,3},{3,2},{4,5},{5,4},{6,7},{7,6},{8,9},{9,8},{10,11... | collective-permute-start | bytes 3080 | tf_op jit(solution)/shard_map/ppermute | solution.py:17
  122.0 3.6 %collective-permute-start.17 = (f32[2,128]{1,0:T(2,128)S(1)}, f32[2,128]{1,0:T(2,128)S(1)}, u32[]{:S(2)}, u32[]{:S(2)}) collective-permute-start(f32[2,128]{1,0:T(2,128)S(1)} %fusion.57), channel_id=1, source_target_pairs={{0,2},{1,3},{2,0},{3,1},{4,6},{5,7},{6,4},{7,5},{8,10},{9,11},{10,... | collective-permute-start | bytes 3080 | tf_op jit(solution)/shard_map/ppermute | solution.py:17
  125.6 3.6 %collective-permute-start.20 = (f32[2,128]{1,0:T(2,128)S(1)}, f32[2,128]{1,0:T(2,128)S(1)}, u32[]{:S(2)}, u32[]{:S(2)}) collective-permute-start(f32[2,128]{1,0:T(2,128)S(1)} %fusion.56), channel_id=1, source_target_pairs={{0,16},{16,0},{1,17},{17,1},{2,18},{18,2},{3,19},{19,3},{4,20},{20... | collective-permute-start | bytes 3080 | tf_op jit(solution)/shard_map/ppermute | solution.py:17
  (3 other events, 13.1 us)
Sparse Core Ops, SparseCore 0:
  10.3 60.4 all-gather.1
